TPU v7x, 32 devices: a whole 2x2x4 slice. The times are simulated.
32 devices in a mesh: seq: 8 (over y, x, core), dec: 4 (over z).
Axes of the slice: x: 2, y: 2, z: 4, core: 2. Of those that a mesh axis runs over, the one named last changes fastest.
Arguments:
- tokens: bfloat16 [512, 8, 1536], P('dec', 'seq'), may hold values from -400 to 400
- norm_gain: float32 [1536], replicated, may hold values from 0.1 to 1.9
- lengths: int32 [8], replicated, may hold values from 0 to 1536
- w_query: bfloat16 [1536, 1536], P(None, 'dec'), may hold values from -0.3125 to 0.3125
- w_keyval: bfloat16 [1536, 1024], P(None, 'dec'), may hold values from -0.15625 to 0.15625
- w_out: bfloat16 [1536, 1536], P('dec'), may hold values from -0.75 to 0.75
- kv_cache: bfloat16 [8, 8, 1536, 128], P('seq', 'dec'), may hold values from -60 to 60
- prior_kv: bfloat16 [8, 2, 8, 2048, 128], P('seq', None, 'dec'), may hold values from -4 to 4
- owners: int32 [8, 3, 8, 16, 1], P('seq', None, 'dec'), may hold values from 0 to 7; in each aligned block of 32 rows (0 to 31, 32 to 63, ..., all dimensions but the last counted through in order) at most 4 rows name the same one
Outputs:
- attention_out: bfloat16 [512, 8, 1536], P('dec', 'seq')
- decode_pool: bfloat16 [8, 4, 3, 8, 4, 128, 128], P('seq', 'dec')
Inputs may be any that keep to these rules, and one draw needn't show every extreme that they name: `owners`: for one request, one layer and the 2 KV heads of one decode group (32 blocks, consecutive in the array), no owner is named more than 4 times.
All inputs are finite; a program needn't handle non-finite values.
Results may differ from a plain program's by a relative error of at most 0.012.
The roundings to bfloat16 on the way count: a program that leaves them out, or rounds other values in their place, can miss the bound.
Values may be sent and summed in bfloat16 or wider, within the bound.
No kernel may reach another device: no remote copies, remote signals or barrier semaphores. Data moves between devices by JAX's collectives and lax.ppermute only.
A program may use at most 128 MiB of HBM per device.

v0:
```python
import jax
import jax.numpy as jnp
from jax import lax
from jax.sharding import PartitionSpec as P

HD = 64
NEW_TOK = 512


EPSILON = 1e-06
ROPE_BASE = 10000.0


def rotate(values, angles):
    half_dim = values.shape[-1] // 2
    first_half = values[..., :half_dim]
    second_half = values[..., half_dim:]
    cosine = jnp.cos(angles)
    sine_part = jnp.sin(angles)
    return jnp.concatenate(
        [
            first_half * cosine - second_half * sine_part,
            second_half * cosine + first_half * sine_part,
        ],
        axis=-1,
    )


def route_blocks(dispatch_table, block_data):
    moved_blocks = jnp.einsum(
        "locr,lrf->olcf", dispatch_table, block_data, preferred_element_type=jnp.float32
    ).astype(jnp.bfloat16)
    return moved_blocks.reshape(
        moved_blocks.shape[0],
        moved_blocks.shape[1],
        1,
        moved_blocks.shape[2],
        moved_blocks.shape[3],
    )


def local(tokens, norm_gain, lengths, w_query, w_keyval, w_out, kv_cache, prior_kv, owners):
    query_cols = w_query.shape[1]
    heads_here = kv_cache.shape[1]
    layer_count = owners.shape[1]
    block_count = owners.shape[3]
    span_len = prior_kv.shape[3]
    block_len = span_len // block_count
    kv_width = 2 * HD
    rows_here = heads_here * block_count
    owner_count = lax.axis_size("seq")
    capacity = (rows_here + owner_count - 1) // owner_count
    req_length = lengths[lax.axis_index("seq")]
    slot_ids = jnp.arange(span_len, dtype=jnp.int32)
    zero_index = jnp.zeros((), jnp.int32)
    owner_rows = owners[0, :, :, :, 0].reshape(layer_count, rows_here)
    owner_hits = (owner_rows[:, :, None] == jnp.arange(owner_count, dtype=jnp.int32)).astype(
        jnp.int32
    )
    owner_rank = jnp.sum((jnp.cumsum(owner_hits, axis=1) - owner_hits) * owner_hits, axis=-1)
    slot_index = owner_rows * capacity + owner_rank
    dispatch = (
        slot_index[:, None, :] == jnp.arange(owner_count * capacity, dtype=jnp.int32)[None, :, None]
    ).astype(jnp.bfloat16)
    dispatch = dispatch.reshape(layer_count, owner_count, capacity, rows_here)
    live_mask = (slot_ids < req_length + NEW_TOK)[None, None, :, None]
    earlier = jnp.where(live_mask, prior_kv[0], jnp.zeros_like(prior_kv[0]))
    earlier_rows = earlier.reshape(layer_count - 1, rows_here, block_len * kv_width)
    widened = tokens.astype(jnp.float32)
    normed = (
        widened
        * lax.rsqrt(jnp.mean(widened * widened, axis=-1, keepdims=True) + EPSILON)
        * norm_gain
    ).astype(jnp.bfloat16)
    portion = lax.all_gather(normed, "dec", axis=0, tiled=True)
    flattened = portion.reshape(-1, portion.shape[-1])
    combined = jnp.concatenate(
        [
            jnp.dot(flattened, w_query, preferred_element_type=jnp.float32),
            jnp.dot(flattened, w_keyval, preferred_element_type=jnp.float32),
        ],
        axis=-1,
    )
    positions = (jnp.arange(NEW_TOK, dtype=jnp.int32) + req_length).astype(jnp.float32)
    inverse_freq = ROPE_BASE ** (-(jnp.arange(0, HD, 2, dtype=jnp.float32) / HD))
    angles = positions[:, None, None] * inverse_freq
    queries = rotate(
        combined[:, :query_cols].reshape(NEW_TOK, query_cols // HD, HD), angles
    ).astype(jnp.bfloat16)
    key_value = combined[:, query_cols:].reshape(NEW_TOK, heads_here, kv_width)
    key_value = jnp.concatenate(
        [rotate(key_value[..., :HD], angles), key_value[..., HD:]], axis=-1
    ).astype(jnp.bfloat16)
    cached = kv_cache[0]
    padded = jnp.pad(cached, ((0, 0), (0, span_len - cached.shape[1]), (0, 0)))
    kept_cache = jnp.where((slot_ids < req_length)[None, :, None], padded, jnp.zeros_like(padded))
    fresh_rows = jnp.transpose(key_value, (1, 0, 2))
    assembled = lax.dynamic_update_slice(
        kept_cache, fresh_rows, (zero_index, req_length, zero_index)
    )
    grouped = queries.reshape(NEW_TOK, heads_here, query_cols // HD // heads_here, HD)
    visible = slot_ids[None, :] <= (req_length + jnp.arange(NEW_TOK, dtype=jnp.int32))[:, None]
    score_scale = HD ** (-0.5)
    contexts = []
    for head_index in range(heads_here):
        key_part = assembled[head_index, :, :HD]
        value_part = assembled[head_index, :, HD:]
        scores = (
            jnp.einsum(
                "tjd,pd->jtp", grouped[:, head_index], key_part, preferred_element_type=jnp.float32
            )
            * score_scale
        )
        row_max = jnp.max(jnp.where(visible, scores, -jnp.inf), axis=-1, keepdims=True)
        weights = jnp.where(visible, jnp.exp(scores - row_max), 0.0)
        row_total = jnp.sum(weights, axis=-1, keepdims=True)
        mixed_rows = jnp.einsum(
            "jtp,pd->tjd",
            weights.astype(jnp.bfloat16),
            value_part,
            preferred_element_type=jnp.float32,
        )
        contexts.append((mixed_rows / jnp.transpose(row_total, (1, 0, 2))).astype(jnp.bfloat16))
    context = jnp.concatenate(contexts, axis=1).reshape(NEW_TOK, query_cols)
    product = jnp.dot(context, w_out, preferred_element_type=jnp.float32)
    summed = lax.psum_scatter(
        product.reshape(
            NEW_TOK // lax.axis_size("dec") * lax.axis_size("dec"), 1, product.shape[-1]
        ).astype(jnp.bfloat16),
        "dec",
        scatter_dimension=0,
        tiled=True,
    )
    current_rows = assembled.reshape(1, rows_here, block_len * kv_width)
    all_rows = jnp.concatenate([earlier_rows, current_rows], axis=0)
    received = lax.all_to_all(
        route_blocks(dispatch, all_rows), "seq", split_axis=0, concat_axis=2, tiled=True
    )
    decode_pool = received.reshape(1, 1, layer_count, owner_count, capacity, block_len, kv_width)
    return (summed, decode_pool)


def solution(mesh):
    in_specs = (
        P("dec", "seq", None),
        P(),
        P(),
        P(None, "dec"),
        P(None, "dec"),
        P("dec", None),
        P("seq", "dec", None, None),
        P("seq", None, "dec", None, None),
        P("seq", None, "dec", None, None),
    )
    out_specs = (P("dec", "seq", None), P("seq", "dec", None, None, None, None, None))
    return jax.shard_map(local, mesh=mesh, in_specs=in_specs, out_specs=out_specs, check_vma=False)
```

profile of v0, /device:TPU:0, one launch (start us, length us, event | category | flops | bytes accessed | tf_op | source)
XLA Modules:
  0.0 153.2 jit_solution(14484536433223254290)
XLA Ops:
  7.2 0.0 copy-start
  7.2 0.0 copy-start.5
  7.2 0.0 all-gather.2.cloned.1.call-start
  7.2 1.3 fusion.50
  8.6 1.9 %fusion.52 = bf16[128,1,1536]{2,0,1:T(8,128)(2,1)} fusion(bf16[128,1,1536]{2,0,1:T(8,128)(2,1)} %param.9, f32[1536]{0:T(1024)} %param.10, f32[128]{0:T(128)S(1)} %add_rsqrt_fusion), kind=kLoop, calls=%fused_computation.50 | loop fusion | flops 786432 | bytes 793088 | tf_op jit(solution)/shard_map/convert_element_type | solution.py:74
  10.5 0.0 all-gather.2.cloned.1.call-update
  10.5 0.0 reduce-scatter.2.cloned.1.call-start
  10.5 1.2 dynamic_slice.3
  11.8 0.6 iota_add_fusion
  12.4 0.6 iota_compare_fusion.3
  13.6 1.8 %iota_compare_fusion = pred[512,2048]{0,1:T(8,128)(4,1)} fusion(s32[512]{0:T(512)S(1)} %get-tuple-element.18), kind=kLoop, calls=%fused_computation.26 | loop fusion | flops 1048576 | bytes 1050624 | tf_op jit(solution)/shard_map/le | solution.py:102
  15.4 2.3 %copy.24 = bf16[1,2,1536,128]{2,3,1,0:T(8,128)(2,1)} copy(bf16[1,2,1536,128]{3,2,1,0:T(8,128)(2,1)} %param.15) | data formatting | bytes 1572864 | tf_op args[6]
  17.6 2.3 %copy.35 = bf16[256,1536]{1,0:T(8,128)(2,1)} copy(bf16[256,1536]{0,1:T(8,128)(2,1)} %bitcast.151) | data formatting | bytes 1572864 | tf_op jit(solution)/shard_map/dot_general | solution.py:80
  20.5 0.0 copy-done.5
  20.5 1.5 copy.26
  22.0 2.8 %squeeze.35 = bf16[2,32,16384]{2,1,0:T(8,128)(2,1)S(1)} reshape(bf16[1,2,2,2048,128]{4,3,2,1,0:T(8,128)(2,1)} %param.16) | data formatting | bytes 4194304 | tf_op jit(solution)/shard_map/squeeze | solution.py:67
  25.4 1.1 broadcast_in_dim.68
  26.6 2.2 %broadcast_in_dim.69 = pred[32,16384]{1,0:T(8,128)(4,1)} reshape(pred[2,2048,128]{2,1,0:T(8,128)(4,1)} %broadcast_in_dim.68) | data formatting | bytes 1048576 | tf_op jit(solution)/shard_map/jit(_where)/broadcast_in_dim | solution.py:67
  28.8 0.5 broadcast.110
  29.3 0.6 reduce.4
  29.9 0.1 reshape_squeeze.3
  29.9 0.1 fusion.58
  30.0 0.1 reduce_window_sum.11
  30.1 0.2 select_reduce_fusion
  30.3 2.3 %pad_select_fusion = bf16[2,2048,128]{1,2,0:T(8,128)(2,1)} fusion(bf16[2,1536,128]{1,2,0:T(8,128)(2,1)} %bitcast.148, pred[2048]{0:T(1024)(128)(4,1)S(1)} %iota_compare_fusion.3), kind=kLoop, calls=%fused_computation.45 | loop fusion | flops 524288 | bytes 1837056 | tf_op jit(solution)/shard_map/jit(_where)/select_n | solution.py:96
  32.6 1.0 multiply_cosine_fusion
  34.2 2.7 %broadcast_select_fusion = bf16[2,32,16384]{2,1,0:T(8,128)(2,1)} fusion(bf16[2,32,16384]{2,1,0:T(8,128)(2,1)S(1)} %squeeze.35, pred[32,16384]{1,0:T(8,128)(4,1)} %broadcast_in_dim.69), kind=kLoop, calls=%fused_computation.32 | loop fusion | flops 1048576 | bytes 4718592 | tf_op jit(solution)/shard_map/jit(_where)/select_n | solution.py:67
  36.9 13.6 %all-gather.2.cloned.1.call-done = bf16[512,1,1536]{2,0,1:T(8,128)(2,1)} async-done(((bf16[128,1,1536]{2,0,1:T(8,128)(2,1)}), bf16[512,1,1536]{2,0,1:T(8,128)(2,1)}) %all-gather.2.cloned.1.call-update) | async-done | bytes 1572880 | tf_op jit(solution)/shard_map/all_gather | solution.py:75
  50.4 2.2 %fusion.26 = f32[512,2,128]{0,2,1:T(8,128)S(1)} fusion(bf16[2,128,1536]{2,1,0:T(8,128)(2,1)} %bitcast.152, bf16[512,1,1536]{2,0,1:T(8,128)(2,1)} %all-gather.2.cloned.1.call-done), kind=kOutput, calls=%fused_computation.35 | convolution fusion | flops 402653184 | bytes 2883584 | tf_op jit(solution)/shard_map/dot_general | solution.py:80
  52.7 0.9 subtract_convert_fusion.1
  53.6 2.5 %fusion.24 = f32[512,6,64]{0,2,1:T(8,128)S(1)} fusion(bf16[6,64,1536]{2,1,0:T(8,128)(2,1)} %bitcast.150, bf16[512,1,1536]{2,0,1:T(8,128)(2,1)} %all-gather.2.cloned.1.call-done), kind=kOutput, calls=%fused_computation.33 | convolution fusion | flops 603979776 | bytes 3538944 | tf_op jit(solution)/shard_map/dot_general | solution.py:79
  56.2 0.9 subtract_convert_fusion
  57.0 1.5 dynamic_update_slice.3
  58.6 0.0 copy-start.9
  58.6 8.6 %fusion.80 = (f32[3,512]{1,0:T(4,128)S(1)}, bf16[3,512,2048]{1,2,0:T(8,128)(2,1)}) fusion(pred[512,2048]{0,1:T(8,128)(4,1)S(1)} %copy-done.6, bf16[2,2048,128]{1,2,0:T(8,128)(2,1)S(1)} %dynamic_update_slice.3, bf16[512,2,3,32]{0,3,2,1:T(8,128)(2,1)} %bitcast.155, bf16[512,2,3,32]{0,3,2,1:T(8,128)(2,1)} %bitcast.153), kind=kOutput, calls=%fused_computation.93 | convolution fusion | flops 828114944 | bytes 9705472 | tf_op jit(solution)/shard_map/sub | solution.py:115
  67.2 8.1 %fusion.85 = (f32[3,512]{1,0:T(4,128)S(1)}, bf16[3,512,2048]{1,2,0:T(8,128)(2,1)}) fusion(pred[512,2048]{0,1:T(8,128)(4,1)S(1)} %copy-done.6, bf16[2,2048,128]{1,2,0:T(8,128)(2,1)S(1)} %dynamic_update_slice.3, bf16[512,2,3,32]{0,3,2,1:T(8,128)(2,1)S(1)} %bitcast.154, bf16[512,2,3,32]{0,3,2,1:T(8,128)(2,1)} %bitcast.156), kind=kOutput, calls=%fused_computation.94 | convolution fusion | flops 828114944 | bytes 9705472 | tf_op jit(solution)/shard_map/sub | solution.py:115
  75.3 4.1 %fusion.47 = bf16[512,3,64]{0,2,1:T(8,128)(2,1)S(1)} fusion(bf16[3,512,2048]{1,2,0:T(8,128)(2,1)} %get-tuple-element.15, bf16[2,2048,128]{1,2,0:T(8,128)(2,1)S(1)} %dynamic_update_slice.3, f32[512,3]{0,1:T(4,128)S(1)} %bitcast.158), kind=kOutput, calls=%fused_computation.44 | convolution fusion | flops 402849792 | bytes 6758400 | tf_op jit(solution)/shard_map/jtp,pd->tjd/dot_general | solution.py:117
  79.4 0.5 copy-done.1
  79.9 1.2 fusion.44
  81.2 2.2 %fusion.23 = bf16[512,1,1536]{2,0,1:T(8,128)(2,1)} fusion(bf16[512,384]{0,1:T(8,128)(2,1)S(1)} %bitcast.149, bf16[384,1536]{1,0:T(8,128)(2,1)S(1)} %copy-done), kind=kOutput, calls=%fused_computation.31 | convolution fusion | flops 604766208 | bytes 3145728 | tf_op jit(solution)/shard_map/dot_general | solution.py:125
  83.3 0.0 reduce-scatter.2.cloned.1.call-update
  83.4 2.3 %copy.29 = bf16[2,2048,128]{2,1,0:T(8,128)(2,1)} copy(bf16[2,2048,128]{1,2,0:T(8,128)(2,1)} %copy-done.4) | data formatting | bytes 2097152 | tf_op jit(solution)/shard_map/dynamic_update_slice | solution.py:98
  85.7 2.3 %reshape.146 = bf16[1,32,16384]{2,1,0:T(8,128)(2,1)} reshape(bf16[2,2048,128]{2,1,0:T(8,128)(2,1)} %copy.29) | data formatting | bytes 2097152 | tf_op jit(solution)/shard_map/reshape | solution.py:134
  88.0 2.2 %fusion.2 = bf16[8,3,1,4,16384]{4,0,3,1,2:T(8,128)(2,1)S(1)} fusion(bf16[1,32,16384]{2,1,0:T(8,128)(2,1)} %reshape.146, bf16[2,32,16384]{2,1,0:T(8,128)(2,1)S(1)} %copy-done.2, s32[8,4]{0,1:T(4,128)S(1)} %multiply_add_fusion, s32[3,32]{1,0:T(4,128)S(1)} %multiply_add_fusion.1), kind=kOutput, calls=%fused_computation.3 | convolution fusion | flops 108530688 | bytes 6291968 | tf_op jit(solution)/shard_map/locr,lrf->olcf/dot_general | solution.py:30
  90.3 2.4 %copy.30 = bf16[8,3,1,4,16384]{4,3,1,2,0:T(4,128)(2,1)S(1)} copy(bf16[8,3,1,4,16384]{4,0,3,1,2:T(8,128)(2,1)S(1)} %fusion.2) | data formatting | bytes 6291456 | tf_op jit(solution)/shard_map/reshape | solution.py:33
  92.7 43.1 %all_to_all.15 = bf16[8,3,1,4,16384]{4,3,1,2,0:T(4,128)(2,1)} all-to-all(bf16[8,3,1,4,16384]{4,3,1,2,0:T(4,128)(2,1)S(1)} %copy.30), channel_id=1, replica_groups=mesh['seq'=8,'dec'=4] {'seq'}, dimensions={0} | all-to-all | bytes 6291456 | tf_op jit(solution)/shard_map/all_to_all | solution.py:136
  135.8 6.6 %reshape.148 = bf16[1,1,3,8,4,128,128]{6,5,4,2,3,1,0:T(8,128)(2,1)} reshape(bf16[1,3,8,1,4,16384]{5,4,1,2,3,0:T(4,128)(2,1)} %bitcast.147) | data formatting | bytes 6291456 | tf_op jit(solution)/shard_map/reshape | solution.py:139
  142.4 4.0 %copy.31 = bf16[1,1,3,8,4,128,128]{6,5,4,3,2,1,0:T(8,128)(2,1)} copy(bf16[1,1,3,8,4,128,128]{6,5,4,2,3,1,0:T(8,128)(2,1)} %reshape.148) | data formatting | bytes 6291456
  (26 shorter events, 0.1 us)
Async XLA Ops:
  7.2 74.0 %copy-start = (bf16[384,1536]{1,0:T(8,128)(2,1)S(1)}, bf16[384,1536]{1,0:T(8,128)(2,1)}, u32[]{:S(2)}) copy-start(bf16[384,1536]{1,0:T(8,128)(2,1)} %param.14) | copy-start | bytes 3538948
  7.2 13.4 %copy-start.5 = (bf16[1536,384]{1,0:T(8,128)(2,1)S(1)}, bf16[1536,384]{1,0:T(8,128)(2,1)}, u32[]{:S(2)}) copy-start(bf16[1536,384]{1,0:T(8,128)(2,1)} %param.12) | copy-start | bytes 3538948
  7.2 43.2 %all-gather.2.cloned.1.call-start = ((), (), s32[]{:S(2)}) async-start(), calls=%async_computation.2 | async-start | bytes 1966080 | tf_op jit(solution)/shard_map/all_gather | solution.py:75
  10.5 18.8 %copy-start.10 = (s32[1,3,2,16,1]{3,4,2,1,0:T(1,128)S(1)}, s32[1,3,2,16,1]{3,4,2,1,0:T(1,128)}, u32[]{:S(2)}) copy-start(s32[1,3,2,16,1]{3,4,2,1,0:T(1,128)} %param.17) | copy-start | bytes 1156
  10.5 135.9 %reduce-scatter.2.cloned.1.call-start = ((), (), s32[]{:S(2)}) async-start(), calls=%async_computation.3 | async-start | bytes 1966080 | tf_op jit(solution)/shard_map/reduce_scatter | solution.py:126
  36.9 19.3 %copy-start.7 = (f32[512,32]{0,1:T(8,128)S(1)}, f32[512,32]{0,1:T(8,128)}, u32[]{:S(2)}) copy-start(f32[512,32]{0,1:T(8,128)} %get-tuple-element.12) | copy-start | bytes 196612
  36.9 19.3 %copy-start.8 = (f32[512,32]{0,1:T(8,128)S(1)}, f32[512,32]{0,1:T(8,128)}, u32[]{:S(2)}) copy-start(f32[512,32]{0,1:T(8,128)} %get-tuple-element.13) | copy-start | bytes 196612
  36.9 20.2 %copy-start.3 = (bf16[2,2048,128]{1,2,0:T(8,128)(2,1)S(1)}, bf16[2,2048,128]{1,2,0:T(8,128)(2,1)}, u32[]{:S(2)}) copy-start(bf16[2,2048,128]{1,2,0:T(8,128)(2,1)} %pad_select_fusion) | copy-start | bytes 3145732
  36.9 21.7 %copy-start.6 = (pred[512,2048]{0,1:T(8,128)(4,1)S(1)}, pred[512,2048]{0,1:T(8,128)(4,1)}, u32[]{:S(2)}) copy-start(pred[512,2048]{0,1:T(8,128)(4,1)} %iota_compare_fusion) | copy-start | bytes 3145732
  58.5 20.9 %copy-start.4 = (bf16[2,2048,128]{1,2,0:T(8,128)(2,1)}, bf16[2,2048,128]{1,2,0:T(8,128)(2,1)S(1)}, u32[]{:S(2)}) copy-start(bf16[2,2048,128]{1,2,0:T(8,128)(2,1)S(1)} %dynamic_update_slice.3) | copy-start | bytes 3145732
  58.6 8.6 %copy-start.9 = (bf16[512,6,32]{0,2,1:T(8,128)(2,1)S(1)}, bf16[512,6,32]{0,2,1:T(8,128)(2,1)}, u32[]{:S(2)}) copy-start(bf16[512,6,32]{0,2,1:T(8,128)(2,1)} %get-tuple-element.8) | copy-start | bytes 589828
  75.3 4.6 %copy-start.1 = (bf16[3,512,2048]{1,2,0:T(8,128)(2,1)S(1)}, bf16[3,512,2048]{1,2,0:T(8,128)(2,1)}, u32[]{:S(2)}) copy-start(bf16[3,512,2048]{1,2,0:T(8,128)(2,1)} %get-tuple-element.17) | copy-start | bytes 18874372
  81.1 6.9 %copy-start.2 = (bf16[2,32,16384]{2,1,0:T(8,128)(2,1)S(1)}, bf16[2,32,16384]{2,1,0:T(8,128)(2,1)}, u32[]{:S(2)}) copy-start(bf16[2,32,16384]{2,1,0:T(8,128)(2,1)} %broadcast_select_fusion) | copy-start | bytes 6291460
Sparse Core Ops, SparseCore 0:
  10.6 39.7 all-gather.1
  83.5 35.6 reduce-scatter.1
where the time goes:
time: 154 us; the launch traced here: 153 us
  blocking collectives  43.1 us (28%)
  local copies, waits for them, and re-layouts  33.7 us (22%)
  matrix products  31.2 us (20%)
  between operations  16.6 us (11%)
  other arithmetic  15 us (10%)
  waiting for transfers between devices  13.6 us (9%)
    all_to_all x1, blocking collectives, local(): lax.all_to_all(route_blocks(dispatch, all_rows), 'seq', split_axis=0, con...  43.1 us
    sub x2, matrix products, local(): weights = jnp.where(visible, jnp.exp(scores - row_max), 0.0)  16.7 us
    all_gather x1, waiting for transfers between devices, local(): portion = lax.all_gather(normed, 'dec', axis=0, tiled=True)  13.6 us
    unnamed x26, local copies, waits for them, and re-layouts  8.75 us
    reshape x1, local copies, waits for them, and re-layouts, local(): received.reshape(1, 1, layer_count, owner_count, capacity, block_len, kv_...  6.61 us
    dot_general x2, matrix products, local(): jnp.einsum('jtp,pd->tjd', weights.astype(jnp.bfloat16), value_part, prefe...  5.28 us
    dynamic_update_slice x2, local copies, waits for them, and re-layouts, local(): lax.dynamic_update_slice(kept_cache, fresh_rows, (zero_index, req_length,...  3.82 us
    broadcast_in_dim x2, local copies, waits for them, and re-layouts, local(): earlier = jnp.where(live_mask, prior_kv[0], jnp.zeros_like(prior_kv[0]))  3.34 us
  transfers between devices with their start and end apart: 2, of which 1 were waited for; matrix products, arithmetic and copies ran while one was open for 29% of the time, Pallas kernels for 0%

commit v1 on v0

--- a/solution.py
+++ b/solution.py
@@ -26,19 +26,6 @@
     )
 
 
-def route_blocks(dispatch_table, block_data):
-    moved_blocks = jnp.einsum(
-        "locr,lrf->olcf", dispatch_table, block_data, preferred_element_type=jnp.float32
-    ).astype(jnp.bfloat16)
-    return moved_blocks.reshape(
-        moved_blocks.shape[0],
-        moved_blocks.shape[1],
-        1,
-        moved_blocks.shape[2],
-        moved_blocks.shape[3],
-    )
-
-
 def local(tokens, norm_gain, lengths, w_query, w_keyval, w_out, kv_cache, prior_kv, owners):
     query_cols = w_query.shape[1]
     heads_here = kv_cache.shape[1]
@@ -58,14 +45,13 @@
         jnp.int32
     )
     owner_rank = jnp.sum((jnp.cumsum(owner_hits, axis=1) - owner_hits) * owner_hits, axis=-1)
-    slot_index = owner_rows * capacity + owner_rank
-    dispatch = (
-        slot_index[:, None, :] == jnp.arange(owner_count * capacity, dtype=jnp.int32)[None, :, None]
-    ).astype(jnp.bfloat16)
-    dispatch = dispatch.reshape(layer_count, owner_count, capacity, rows_here)
-    live_mask = (slot_ids < req_length + NEW_TOK)[None, None, :, None]
-    earlier = jnp.where(live_mask, prior_kv[0], jnp.zeros_like(prior_kv[0]))
-    earlier_rows = earlier.reshape(layer_count - 1, rows_here, block_len * kv_width)
+    row_ids = jnp.arange(rows_here, dtype=jnp.int32)
+    match = (owner_rows[:, None, None, :] == jnp.arange(owner_count, dtype=jnp.int32)[None, :, None, None]) & (
+        owner_rank[:, None, None, :] == jnp.arange(capacity, dtype=jnp.int32)[None, None, :, None]
+    )
+    pick_row = jnp.sum(jnp.where(match, row_ids, 0), axis=-1)
+    pick_ok = jnp.any(match, axis=-1)
+    me = lax.axis_index("seq")
     widened = tokens.astype(jnp.float32)
     normed = (
         widened
@@ -131,12 +117,35 @@
         scatter_dimension=0,
         tiled=True,
     )
-    current_rows = assembled.reshape(1, rows_here, block_len * kv_width)
-    all_rows = jnp.concatenate([earlier_rows, current_rows], axis=0)
-    received = lax.all_to_all(
-        route_blocks(dispatch, all_rows), "seq", split_axis=0, concat_axis=2, tiled=True
-    )
-    decode_pool = received.reshape(1, 1, layer_count, owner_count, capacity, block_len, kv_width)
+    earlier_blocks = prior_kv[0].reshape(layer_count - 1, rows_here, block_len, kv_width)
+    current_blocks = assembled.reshape(1, rows_here, block_len, kv_width)
+    in_block = jnp.arange(block_len, dtype=jnp.int32)
+
+    def pick(blocks, layers, target):
+        rows = lax.dynamic_index_in_dim(pick_row[layers], target, axis=1, keepdims=False)
+        ok = lax.dynamic_index_in_dim(pick_ok[layers], target, axis=1, keepdims=False)
+        layer_ids = jnp.arange(blocks.shape[0], dtype=jnp.int32)[:, None]
+        taken = blocks[layer_ids, rows]
+        position = (rows % block_count)[:, :, None] * block_len + in_block
+        keep = ok[:, :, None] & (position < req_length + NEW_TOK)
+        return jnp.where(keep[..., None], taken, jnp.zeros_like(taken))
+
+    pool = jnp.zeros((layer_count, owner_count, capacity, block_len, kv_width), jnp.bfloat16)
+    for shift in range(owner_count):
+        target = lax.rem(me + shift, owner_count)
+        source = lax.rem(me - shift + owner_count, owner_count)
+        parts = [
+            pick(earlier_blocks, slice(0, layer_count - 1), target),
+            pick(current_blocks, slice(layer_count - 1, layer_count), target),
+        ]
+        if shift:
+            perm = [(i, (i + shift) % owner_count) for i in range(owner_count)]
+            parts = [lax.ppermute(part, "seq", perm) for part in parts]
+        piece = jnp.concatenate(parts, axis=0)
+        pool = lax.dynamic_update_slice(
+            pool, piece[:, None], (zero_index, source, zero_index, zero_index, zero_index)
+        )
+    decode_pool = pool.reshape(1, 1, layer_count, owner_count, capacity, block_len, kv_width)
     return (summed, decode_pool)
 
 

time: 154 us -> 178 us (1.16)
  blocking collectives: 43.1 us -> 0 us
  other arithmetic: 15 us -> 56.9 us
  starting transfers between devices: 0.08 us -> 28.7 us
  waiting for transfers between devices: 13.6 us -> 5.16 us
  local copies, waits for them, and re-layouts: 33.7 us -> 40.4 us
  matrix products: 31.2 us -> 27.9 us
    all_to_all x1 -> x0, blocking collectives: 43.1 us -> none  [local(): lax.all_to_all(route_blocks(dispatch, all_rows), 'seq', split_axis=0, con...]
    ppermute x0 -> x14, starting transfers between devices: none -> 28.6 us  [local(): parts = [lax.ppermute(part, 'seq', perm) for part in parts]]
    gather x0 -> x16, local copies, waits for them, and re-layouts: none -> 19.4 us  [pick(): taken = blocks[layer_ids, rows]]
    all_gather x1, waiting for transfers between devices: 13.6 us -> 0.01 us  [local(): portion = lax.all_gather(normed, 'dec', axis=0, tiled=True)]
    select_n x1 -> x20, other arithmetic: 2.68 us -> 13.5 us  [the longest x16 13.5 us: pick(): return jnp.where(keep[..., None], taken, jnp.zeros_like(taken))]
    and x0 -> x16, other arithmetic: none -> 10.6 us  [pick(): keep = ok[:, :, None] & (position < req_length + NEW_TOK)]
    dynamic_update_slice x0 -> x8, other arithmetic: none -> 9.53 us  [local(): lax.dynamic_update_slice(pool, piece[:, None], (zero_index, source, zero_...]
    reshape x3 -> x1, local copies, waits for them, and re-layouts: 11.4 us -> 2.44 us  [local(): pool.reshape(1, 1, layer_count, owner_count, capacity, block_len, kv_width)]
  transfers between devices with their start and end apart: 2 -> 16, of which waited for: 1 -> 3; matrix products, arithmetic and copies ran while one was open for 29% -> 69% of each run, Pallas kernels for 0% -> 0%
where the time goes in v1:
time: 178 us; the launch traced here: 176 us
  other arithmetic  56.9 us (32%)
  local copies, waits for them, and re-layouts  40.4 us (23%)
  starting transfers between devices  28.7 us (16%)
  matrix products  27.9 us (16%)
  between operations  17.4 us (10%)
  waiting for transfers between devices  5.16 us (3%)
    ppermute x14, starting transfers between devices, local(): parts = [lax.ppermute(part, 'seq', perm) for part in parts]  28.6 us
    gather x16, local copies, waits for them, and re-layouts, pick(): taken = blocks[layer_ids, rows]  19.4 us
    sub x2, matrix products, local(): weights = jnp.where(visible, jnp.exp(scores - row_max), 0.0)  17.3 us
    select_n x16, other arithmetic, pick(): return jnp.where(keep[..., None], taken, jnp.zeros_like(taken))  13.5 us
    and x16, other arithmetic, pick(): keep = ok[:, :, None] & (position < req_length + NEW_TOK)  10.6 us
    dynamic_update_slice x8, other arithmetic, local(): lax.dynamic_update_slice(pool, piece[:, None], (zero_index, source, zero_...  9.53 us
    concatenate x12, other arithmetic, pick(): taken = blocks[layer_ids, rows]  8.07 us
    dot_general x2, matrix products, local(): jnp.einsum('jtp,pd->tjd', weights.astype(jnp.bfloat16), value_part, prefe...  5.28 us
  transfers between devices with their start and end apart: 16, of which 3 were waited for; matrix products, arithmetic and copies ran while one was open for 69% of the time, Pallas kernels for 0%

profile of v1, /device:TPU:0, one launch (start us, length us, event | category | flops | bytes accessed | tf_op | source)
XLA Modules:
  0.0 176.5 jit_solution(10897212244825306776)
XLA Ops:
  7.2 1.3 fusion.47
  8.5 1.9 %fusion.49 = bf16[128,1,1536]{2,0,1:T(8,128)(2,1)} fusion(bf16[128,1,1536]{2,0,1:T(8,128)(2,1)} %param.9, f32[1536]{0:T(1024)} %param.10, f32[128]{0:T(128)S(1)} %add_rsqrt_fusion), kind=kLoop, calls=%fused_computation.60 | loop fusion | flops 786432 | bytes 793088 | tf_op jit(solution)/shard_map/convert_element_type | solution.py:60
  11.0 1.3 reduce.84
  13.6 1.0 fusion.76
  15.7 1.0 fusion.92
  16.8 1.3 dynamic_slice.103
  21.6 1.3 fusion.141
  22.8 1.3 fusion.119
  25.5 0.9 broadcast_select_fusion.5
  26.4 2.5 %collective-permute-start.2 = (bf16[2,4,128,128]{3,2,1,0:T(8,128)(2,1)}, bf16[2,4,128,128]{3,2,1,0:T(8,128)(2,1)}, u32[]{:S(2)}, u32[]{:S(2)}) collective-permute-start(bf16[2,4,128,128]{3,2,1,0:T(8,128)(2,1)} %broadcast_select_fusion.5), channel_id=1, source_target_pairs={{0,8},{4,12},{8,16},{12,20},{16,24},{20,28},{24,0},{28,4},{1,9},{5... | collective-permute-start | bytes 786440 | tf_op jit(solution)/shard_map/ppermute | solution.py:143
  31.0 0.9 broadcast_select_fusion.4
  31.9 2.4 %collective-permute-start.4 = (bf16[2,4,128,128]{3,2,1,0:T(8,128)(2,1)}, bf16[2,4,128,128]{3,2,1,0:T(8,128)(2,1)}, u32[]{:S(2)}, u32[]{:S(2)}) collective-permute-start(bf16[2,4,128,128]{3,2,1,0:T(8,128)(2,1)} %broadcast_select_fusion.4), channel_id=1, source_target_pairs={{0,12},{4,16},{8,20},{12,24},{16,28},{20,0},{24,4},{28,8},{1,13},{... | collective-permute-start | bytes 786440 | tf_op jit(solution)/shard_map/ppermute | solution.py:143
  38.7 1.2 fusion.153
  53.4 2.3 %copy.49 = bf16[1,2,1536,128]{2,3,1,0:T(8,128)(2,1)} copy(bf16[1,2,1536,128]{3,2,1,0:T(8,128)(2,1)} %param.15) | data formatting | bytes 1572864 | tf_op args[6]
  55.7 2.3 %copy.64 = bf16[256,1536]{1,0:T(8,128)(2,1)} copy(bf16[256,1536]{0,1:T(8,128)(2,1)} %bitcast.310) | data formatting | bytes 1572864 | tf_op jit(solution)/shard_map/dot_general | solution.py:66
  58.6 1.5 copy.51
  65.1 0.9 broadcast_select_fusion.7
  66.0 0.9 broadcast_select_fusion.3
  67.8 0.9 broadcast_select_fusion.1
  68.7 1.3 pad_select_fusion
  70.1 1.9 %iota_compare_fusion = pred[512,2048]{0,1:T(8,128)(4,1)} fusion(s32[512]{0:T(512)S(1)} %get-tuple-element.76), kind=kLoop, calls=%fused_computation.40 | loop fusion | flops 1048576 | bytes 1050624 | tf_op jit(solution)/shard_map/le | solution.py:88
  71.9 2.4 %fusion.23 = f32[512,2,128]{0,2,1:T(8,128)S(1)} fusion(bf16[2,128,1536]{2,1,0:T(8,128)(2,1)} %bitcast.311, bf16[512,1,1536]{2,0,1:T(8,128)(2,1)} %all-gather.2.cloned.1.call-done), kind=kOutput, calls=%fused_computation.45 | convolution fusion | flops 402653184 | bytes 2883584 | tf_op jit(solution)/shard_map/dot_general | solution.py:66
  76.1 3.0 %dynamic_update_slice.35 = bf16[2,2048,128]{1,2,0:T(8,128)(2,1)S(1)} dynamic-update-slice(bf16[2,2048,128]{1,2,0:T(8,128)(2,1)S(1)} %pad_select_fusion, bf16[2,512,128]{1,2,0:T(8,128)(2,1)S(1)} %maximum_bitcast_fusion.8, s32[]{:T(128)} %constant.264.clone.1, s32[]{:T(128)S(6)} %select_n.546, s32[]{:T(128)} %constant.264.clone.1) | dynamic-update-slice | bytes 524292 | tf_op jit(solution)/shard_map/dynamic_update_slice | solution.py:84
  79.1 8.7 %fusion.186 = (f32[3,512]{1,0:T(4,128)S(1)}, bf16[3,512,2048]{1,2,0:T(8,128)(2,1)}) fusion(pred[512,2048]{0,1:T(8,128)(4,1)} %iota_compare_fusion, bf16[2,2048,128]{1,2,0:T(8,128)(2,1)S(1)} %dynamic_update_slice.35, bf16[512,2,3,32]{0,3,2,1:T(8,128)(2,1)} %bitcast.314, bf16[512,2,3,32]{0,3,2,1:T(8,128)(2,1)} %bitcast.312), kind=kOutput, calls=%fused_computation.366 | convolution fusion | flops 828114944 | bytes 9705472 | tf_op jit(solution)/shard_map/sub | solution.py:101
  87.9 8.6 %fusion.191 = (f32[3,512]{1,0:T(4,128)S(1)}, bf16[3,512,2048]{1,2,0:T(8,128)(2,1)}) fusion(pred[512,2048]{0,1:T(8,128)(4,1)} %iota_compare_fusion, bf16[2,2048,128]{1,2,0:T(8,128)(2,1)S(1)} %dynamic_update_slice.35, bf16[512,2,3,32]{0,3,2,1:T(8,128)(2,1)S(1)} %bitcast.313, bf16[512,2,3,32]{0,3,2,1:T(8,128)(2,1)S(1)} %bitcast.315), kind=kOutput, calls=%fused_computation.367 | convolution fusion | flops 828114944 | bytes 9705472 | tf_op jit(solution)/shard_map/sub | solution.py:101
  96.5 4.1 %fusion.44 = bf16[512,3,64]{0,2,1:T(8,128)(2,1)S(1)} fusion(bf16[3,512,2048]{1,2,0:T(8,128)(2,1)} %get-tuple-element.41, bf16[2,2048,128]{1,2,0:T(8,128)(2,1)S(1)} %dynamic_update_slice.35, f32[512,3]{0,1:T(4,128)S(1)} %bitcast.317), kind=kOutput, calls=%fused_computation.54 | convolution fusion | flops 402849792 | bytes 6758400 | tf_op jit(solution)/shard_map/jtp,pd->tjd/dot_general | solution.py:103
  101.1 1.2 fusion.41
  102.4 2.2 %fusion.20 = bf16[512,1,1536]{2,0,1:T(8,128)(2,1)} fusion(bf16[512,384]{0,1:T(8,128)(2,1)S(1)} %bitcast.300, bf16[384,1536]{1,0:T(8,128)(2,1)S(1)} %copy-done.2), kind=kOutput, calls=%fused_computation.42 | convolution fusion | flops 604766208 | bytes 3145728 | tf_op jit(solution)/shard_map/dot_general | solution.py:111
  106.0 0.9 broadcast_select_fusion
  106.9 1.3 copy.54
  108.2 1.8 %gather_fusion.1 = bf16[4,128,128]{2,1,0:T(8,128)(2,1)S(1)} fusion(bf16[1,32,128,128]{3,2,1,0:T(8,128)(2,1)} %bitcast.291, s32[4]{0:T(128)S(1)} %copy-done.12), kind=kCustom, calls=%fused_computation.1 | custom fusion | bytes 262176 | tf_op jit(solution)/shard_map/gather | solution.py:128
  110.0 1.8 %gather_fusion.3 = bf16[4,128,128]{2,1,0:T(8,128)(2,1)S(1)} fusion(bf16[1,32,128,128]{3,2,1,0:T(8,128)(2,1)} %bitcast.292, s32[4]{0:T(128)S(1)} %copy-done.18), kind=kCustom, calls=%fused_computation.3 | custom fusion | bytes 262176 | tf_op jit(solution)/shard_map/gather | solution.py:128
  112.6 1.8 %gather_fusion.5 = bf16[4,128,128]{2,1,0:T(8,128)(2,1)S(1)} fusion(bf16[1,32,128,128]{3,2,1,0:T(8,128)(2,1)} %bitcast.293, s32[4]{0:T(128)S(1)} %copy-done.15), kind=kCustom, calls=%fused_computation.5 | custom fusion | bytes 262176 | tf_op jit(solution)/shard_map/gather | solution.py:128
  115.7 1.8 %gather_fusion.7 = bf16[4,128,128]{2,1,0:T(8,128)(2,1)S(1)} fusion(bf16[1,32,128,128]{3,2,1,0:T(8,128)(2,1)} %bitcast.294, s32[4]{0:T(128)S(1)} %copy-done.13), kind=kCustom, calls=%fused_computation.7 | custom fusion | bytes 262176 | tf_op jit(solution)/shard_map/gather | solution.py:128
  117.5 1.8 %gather_fusion.9 = bf16[4,128,128]{2,1,0:T(8,128)(2,1)S(1)} fusion(bf16[1,32,128,128]{3,2,1,0:T(8,128)(2,1)} %bitcast.295, s32[4]{0:T(128)S(1)} %copy-done.14), kind=kCustom, calls=%fused_computation.9 | custom fusion | bytes 262176 | tf_op jit(solution)/shard_map/gather | solution.py:128
  119.3 1.8 %gather_fusion.11 = bf16[4,128,128]{2,1,0:T(8,128)(2,1)S(1)} fusion(bf16[1,32,128,128]{3,2,1,0:T(8,128)(2,1)} %bitcast.296, s32[4]{0:T(128)S(1)} %copy-done.16), kind=kCustom, calls=%fused_computation.11 | custom fusion | bytes 262176 | tf_op jit(solution)/shard_map/gather | solution.py:128
  121.2 1.8 %gather_fusion.13 = bf16[4,128,128]{2,1,0:T(8,128)(2,1)S(1)} fusion(bf16[1,32,128,128]{3,2,1,0:T(8,128)(2,1)} %bitcast.297, s32[4]{0:T(128)S(1)} %copy-done.17), kind=kCustom, calls=%fused_computation.13 | custom fusion | bytes 262176 | tf_op jit(solution)/shard_map/gather | solution.py:128
  123.0 1.9 %gather_fusion.15 = bf16[4,128,128]{2,1,0:T(8,128)(2,1)S(1)} fusion(bf16[1,32,128,128]{3,2,1,0:T(8,128)(2,1)} %bitcast.298, s32[4]{0:T(128)} %or_bitcast_fusion), kind=kCustom, calls=%fused_computation.15 | custom fusion | bytes 262176 | tf_op jit(solution)/shard_map/gather | solution.py:128
  129.6 2.4 %reshape.1679 = bf16[1,1,3,8,4,128,128]{6,5,4,3,2,1,0:T(8,128)(2,1)} broadcast(bf16[]{:T(256)} %constant.266.clone.1), dimensions={} | broadcast | bytes 3145730 | tf_op jit(solution)/shard_map/reshape | solution.py:148
  133.8 1.8 %collective-permute-start.5 = (bf16[1,4,128,128]{3,2,1,0:T(8,128)(2,1)S(1)}, bf16[1,4,128,128]{3,2,1,0:T(8,128)(2,1)S(1)}, u32[]{:S(2)}, u32[]{:S(2)}) collective-permute-start(bf16[1,4,128,128]{3,2,1,0:T(8,128)(2,1)S(1)} %bitcast_select_fusion.12), channel_id=1, source_target_pairs={{0,12},{4,16},{8,20},{12,24},{16,28},{20,0},{24,4},{28,8},{1,13},{... | collective-permute-start | bytes 393224 | tf_op jit(solution)/shard_map/ppermute | solution.py:143
  135.5 1.8 %fusion.51 = bf16[1,1,3,8,4,128,128]{6,5,4,3,2,1,0:T(8,128)(2,1)} fusion(bf16[1,1,3,8,4,128,128]{6,5,4,3,2,1,0:T(8,128)(2,1)} %fusion.50, s32[]{:T(128)S(6)} %select_n.567, bf16[1,4,128,128]{3,2,1,0:T(8,128)(2,1)} %collective-permute-done.1, bf16[2,4,128,128]{3,2,1,0:T(8,128)(2,1)} %collective-permute-done), kind=kLoop, calls=%fused_computation.67 | loop fusion | flops 786432 | bytes 786436 | tf_op jit(solution)/shard_map/dynamic_update_slice | solution.py:145
  137.5 1.5 collective-permute-start.7
  139.1 1.8 %fusion.52 = bf16[1,1,3,8,4,128,128]{6,5,4,3,2,1,0:T(8,128)(2,1)} fusion(bf16[1,1,3,8,4,128,128]{6,5,4,3,2,1,0:T(8,128)(2,1)} %fusion.51, s32[]{:T(128)S(6)} %select_n.575, bf16[1,4,128,128]{3,2,1,0:T(8,128)(2,1)} %collective-permute-done.3, bf16[2,4,128,128]{3,2,1,0:T(8,128)(2,1)} %collective-permute-done.2), kind=kLoop, calls=%fused_computation.69 | loop fusion | flops 786432 | bytes 786436 | tf_op jit(solution)/shard_map/dynamic_update_slice | solution.py:145
  140.9 2.1 %collective-permute-start.10 = (bf16[2,4,128,128]{3,2,1,0:T(8,128)(2,1)S(1)}, bf16[2,4,128,128]{3,2,1,0:T(8,128)(2,1)S(1)}, u32[]{:S(2)}, u32[]{:S(2)}) collective-permute-start(bf16[2,4,128,128]{3,2,1,0:T(8,128)(2,1)S(1)} %copy-done.6), channel_id=1, source_target_pairs={{0,24},{4,28},{8,0},{12,4},{16,8},{20,12},{24,16},{28,20},{1,25},{... | collective-permute-start | bytes 786440 | tf_op jit(solution)/shard_map/ppermute | solution.py:143
  143.0 3.7 %collective-permute-done.5 = bf16[1,4,128,128]{3,2,1,0:T(8,128)(2,1)S(1)} collective-permute-done((bf16[1,4,128,128]{3,2,1,0:T(8,128)(2,1)S(1)}, bf16[1,4,128,128]{3,2,1,0:T(8,128)(2,1)S(1)}, u32[]{:S(2)}, u32[]{:S(2)}) %collective-permute-start.5) | collective-permute-done | bytes 131104 | tf_op jit(solution)/shard_map/ppermute | solution.py:143
  146.7 1.8 %fusion.53 = bf16[1,1,3,8,4,128,128]{6,5,4,3,2,1,0:T(8,128)(2,1)} fusion(bf16[1,1,3,8,4,128,128]{6,5,4,3,2,1,0:T(8,128)(2,1)} %fusion.52, s32[]{:T(128)S(6)} %select_n.583, bf16[1,4,128,128]{3,2,1,0:T(8,128)(2,1)S(1)} %collective-permute-done.5, bf16[2,4,128,128]{3,2,1,0:T(8,128)(2,1)} %collective-permute-done.4), kind=kLoop, calls=%fused_computation.71 | loop fusion | flops 786432 | bytes 786436 | tf_op jit(solution)/shard_map/dynamic_update_slice | solution.py:145
  148.4 5.4 %collective-permute-start.12 = (bf16[2,4,128,128]{3,2,1,0:T(8,128)(2,1)S(1)}, bf16[2,4,128,128]{3,2,1,0:T(8,128)(2,1)S(1)}, u32[]{:S(2)}, u32[]{:S(2)}) collective-permute-start(bf16[2,4,128,128]{3,2,1,0:T(8,128)(2,1)S(1)} %copy-done.9), channel_id=1, source_target_pairs={{0,28},{4,0},{8,4},{12,8},{16,12},{20,16},{24,20},{28,24},{1,29},{... | collective-permute-start | bytes 786440 | tf_op jit(solution)/shard_map/ppermute | solution.py:143
  153.8 11.1 %collective-permute-start.11 = (bf16[1,4,128,128]{3,2,1,0:T(8,128)(2,1)S(1)}, bf16[1,4,128,128]{3,2,1,0:T(8,128)(2,1)S(1)}, u32[]{:S(2)}, u32[]{:S(2)}) collective-permute-start(bf16[1,4,128,128]{3,2,1,0:T(8,128)(2,1)S(1)} %bitcast_select_fusion.9), channel_id=1, source_target_pairs={{0,24},{4,28},{8,0},{12,4},{16,8},{20,12},{24,16},{28,20},{1,25},{... | collective-permute-start | bytes 393224 | tf_op jit(solution)/shard_map/ppermute | solution.py:143
  (182 shorter events, 48.5 us)
Async XLA Ops:
  7.2 11.6 %copy-start = (bf16[1,2,2,2048,128]{4,3,2,1,0:T(8,128)(2,1)S(1)}, bf16[1,2,2,2048,128]{4,3,2,1,0:T(8,128)(2,1)}, u32[]{:S(2)}) copy-start(bf16[1,2,2,2048,128]{4,3,2,1,0:T(8,128)(2,1)} %param.16) | copy-start | bytes 6291460
  7.2 64.8 %all-gather.2.cloned.1.call-start = ((), (), s32[]{:S(2)}) async-start(), calls=%async_computation.1 | async-start | bytes 1966080 | tf_op jit(solution)/shard_map/all_gather | solution.py:61
  10.5 159.2 %reduce-scatter.2.cloned.1.call-start = ((), (), s32[]{:S(2)}) async-start(), calls=%async_computation.2 | async-start | bytes 1966080 | tf_op jit(solution)/shard_map/reduce_scatter | solution.py:112
  13.5 5.3 %copy-start.19 = (pred[3,8,4]{1,2,0:T(4,128)(4,1)}, pred[3,8,4]{1,2,0:T(4,128)(4,1)S(1)}, u32[]{:S(2)}) copy-start(pred[3,8,4]{1,2,0:T(4,128)(4,1)S(1)} %and_reduce_fusion) | copy-start | bytes 292
  19.4 39.3 %copy-start.3 = (bf16[1536,384]{1,0:T(8,128)(2,1)S(1)}, bf16[1536,384]{1,0:T(8,128)(2,1)}, u32[]{:S(2)}) copy-start(bf16[1536,384]{1,0:T(8,128)(2,1)} %param.12) | copy-start | bytes 3538948
  21.1 111.8 %collective-permute-start = (bf16[2,4,128,128]{3,2,1,0:T(8,128)(2,1)}, bf16[2,4,128,128]{3,2,1,0:T(8,128)(2,1)}, u32[]{:S(2)}, u32[]{:S(2)}) collective-permute-start(bf16[2,4,128,128]{3,2,1,0:T(8,128)(2,1)} %broadcast_select_fusion.6), channel_id=1, source_target_pairs={{0,4},{4,8},{8,12},{12,16},{16,20},{20,24},{24,28},{28,0},{1,5},{5... | collective-permute-start | bytes 786440 | tf_op jit(solution)/shard_map/ppermute | solution.py:143
  26.4 111.0 %collective-permute-start.2 = (bf16[2,4,128,128]{3,2,1,0:T(8,128)(2,1)}, bf16[2,4,128,128]{3,2,1,0:T(8,128)(2,1)}, u32[]{:S(2)}, u32[]{:S(2)}) collective-permute-start(bf16[2,4,128,128]{3,2,1,0:T(8,128)(2,1)} %broadcast_select_fusion.5), channel_id=1, source_target_pairs={{0,8},{4,12},{8,16},{12,20},{16,24},{20,28},{24,0},{28,4},{1,9},{5... | collective-permute-start | bytes 786440 | tf_op jit(solution)/shard_map/ppermute | solution.py:143
  31.9 109.0 %collective-permute-start.4 = (bf16[2,4,128,128]{3,2,1,0:T(8,128)(2,1)}, bf16[2,4,128,128]{3,2,1,0:T(8,128)(2,1)}, u32[]{:S(2)}, u32[]{:S(2)}) collective-permute-start(bf16[2,4,128,128]{3,2,1,0:T(8,128)(2,1)} %broadcast_select_fusion.4), channel_id=1, source_target_pairs={{0,12},{4,16},{8,20},{12,24},{16,28},{20,0},{24,4},{28,8},{1,13},{... | collective-permute-start | bytes 786440 | tf_op jit(solution)/shard_map/ppermute | solution.py:143
  55.7 8.5 %copy-start.22 = (pred[2,4]{1,0:T(4,128)(4,1)S(1)}, pred[2,4]{1,0:T(4,128)(4,1)}, u32[]{:S(2)}) copy-start(pred[2,4]{1,0:T(4,128)(4,1)} %get-tuple-element.18) | copy-start | bytes 28
  71.9 2.4 %copy-start.4 = (bf16[1536,384]{0,1:T(8,128)(2,1)S(1)}, bf16[1536,384]{0,1:T(8,128)(2,1)}, u32[]{:S(2)}) copy-start(bf16[1536,384]{0,1:T(8,128)(2,1)} %copy.51) | copy-start | bytes 3538948
  71.9 2.5 %copy-start.26 = (bf16[512,1,1536]{2,0,1:T(8,128)(2,1)S(1)}, bf16[512,1,1536]{2,0,1:T(8,128)(2,1)}, u32[]{:S(2)}) copy-start(bf16[512,1,1536]{2,0,1:T(8,128)(2,1)} %all-gather.2.cloned.1.call-done) | copy-start | bytes 4718596
  79.1 8.7 %copy-start.10 = (bf16[512,6,32]{0,2,1:T(8,128)(2,1)S(1)}, bf16[512,6,32]{0,2,1:T(8,128)(2,1)}, u32[]{:S(2)}) copy-start(bf16[512,6,32]{0,2,1:T(8,128)(2,1)} %get-tuple-element.34) | copy-start | bytes 589828
  79.1 8.7 %copy-start.11 = (bf16[512,6,32]{0,2,1:T(8,128)(2,1)S(1)}, bf16[512,6,32]{0,2,1:T(8,128)(2,1)}, u32[]{:S(2)}) copy-start(bf16[512,6,32]{0,2,1:T(8,128)(2,1)} %get-tuple-element.35) | copy-start | bytes 589828
  96.5 4.6 %copy-start.1 = (bf16[3,512,2048]{1,2,0:T(8,128)(2,1)S(1)}, bf16[3,512,2048]{1,2,0:T(8,128)(2,1)}, u32[]{:S(2)}) copy-start(bf16[3,512,2048]{1,2,0:T(8,128)(2,1)} %get-tuple-element.43) | copy-start | bytes 18874372
  101.1 1.3 copy-start.2
  102.3 2.3 %copy-start.23 = (pred[4]{0:T(512)(128)(4,1)S(1)}, pred[4]{0:T(512)(128)(4,1)}, u32[]{:S(2)}) copy-start(pred[4]{0:T(512)(128)(4,1)} %get-tuple-element.26) | copy-start | bytes 16
  102.3 2.3 %copy-start.24 = (s32[4]{0:T(128)S(1)}, s32[4]{0:T(128)}, u32[]{:S(2)}) copy-start(s32[4]{0:T(128)} %get-tuple-element.75) | copy-start | bytes 52
  102.3 3.0 %copy-start.25 = (s32[2,4,1]{1,0,2:T(2,128)S(1)}, s32[2,4,1]{1,0,2:T(2,128)}, u32[]{:S(2)}) copy-start(s32[2,4,1]{1,0,2:T(2,128)} %get-tuple-element.67) | copy-start | bytes 100
  102.3 3.7 %copy-start.20 = (pred[2,4,128]{2,1,0:T(4,128)(4,1)S(1)}, pred[2,4,128]{2,1,0:T(4,128)(4,1)}, u32[]{:S(2)}) copy-start(pred[2,4,128]{2,1,0:T(4,128)(4,1)} %fusion.84) | copy-start | bytes 3076
  104.5 3.7 %copy-start.12 = (s32[4]{0:T(128)S(1)}, s32[4]{0:T(128)}, u32[]{:S(2)}) copy-start(s32[4]{0:T(128)} %or_bitcast_fusion.7) | copy-start | bytes 52
  104.5 5.5 %copy-start.18 = (s32[4]{0:T(128)S(1)}, s32[4]{0:T(128)}, u32[]{:S(2)}) copy-start(s32[4]{0:T(128)} %or_bitcast_fusion.6) | copy-start | bytes 52
  104.5 7.3 %copy-start.21 = (pred[4,128]{1,0:T(4,128)(4,1)S(1)}, pred[4,128]{1,0:T(4,128)(4,1)}, u32[]{:S(2)}) copy-start(pred[4,128]{1,0:T(4,128)(4,1)} %fusion.102) | copy-start | bytes 1540
  104.5 8.1 %copy-start.15 = (s32[4]{0:T(128)S(1)}, s32[4]{0:T(128)}, u32[]{:S(2)}) copy-start(s32[4]{0:T(128)} %or_bitcast_fusion.5) | copy-start | bytes 52
  104.5 11.1 %copy-start.13 = (s32[4]{0:T(128)S(1)}, s32[4]{0:T(128)}, u32[]{:S(2)}) copy-start(s32[4]{0:T(128)} %or_bitcast_fusion.4) | copy-start | bytes 52
  104.5 12.9 %copy-start.14 = (s32[4]{0:T(128)S(1)}, s32[4]{0:T(128)}, u32[]{:S(2)}) copy-start(s32[4]{0:T(128)} %or_bitcast_fusion.3) | copy-start | bytes 52
  104.6 14.7 %copy-start.16 = (s32[4]{0:T(128)S(1)}, s32[4]{0:T(128)}, u32[]{:S(2)}) copy-start(s32[4]{0:T(128)} %or_bitcast_fusion.2) | copy-start | bytes 52
  104.6 16.6 %copy-start.17 = (s32[4]{0:T(128)S(1)}, s32[4]{0:T(128)}, u32[]{:S(2)}) copy-start(s32[4]{0:T(128)} %or_bitcast_fusion.1) | copy-start | bytes 52
  112.6 21.1 %collective-permute-start.1 = (bf16[1,4,128,128]{3,2,1,0:T(8,128)(2,1)}, bf16[1,4,128,128]{3,2,1,0:T(8,128)(2,1)}, u32[]{:S(2)}, u32[]{:S(2)}) collective-permute-start(bf16[1,4,128,128]{3,2,1,0:T(8,128)(2,1)} %bitcast_select_fusion.14), channel_id=1, source_target_pairs={{0,4},{4,8},{8,12},{12,16},{16,20},{20,24},{24,28},{28,0},{1,5},{5... | collective-permute-start | bytes 393224 | tf_op jit(solution)/shard_map/ppermute | solution.py:143
  114.4 17.7 %copy-start.5 = (bf16[2,4,128,128]{3,2,1,0:T(8,128)(2,1)S(1)}, bf16[2,4,128,128]{3,2,1,0:T(8,128)(2,1)}, u32[]{:S(2)}) copy-start(bf16[2,4,128,128]{3,2,1,0:T(8,128)(2,1)} %broadcast_select_fusion.7) | copy-start | bytes 786436
  115.2 22.3 %collective-permute-start.3 = (bf16[1,4,128,128]{3,2,1,0:T(8,128)(2,1)S(1)}, bf16[1,4,128,128]{3,2,1,0:T(8,128)(2,1)}, u32[]{:S(2)}, u32[]{:S(2)}) collective-permute-start(bf16[1,4,128,128]{3,2,1,0:T(8,128)(2,1)S(1)} %bitcast_select_fusion.13), channel_id=1, source_target_pairs={{0,8},{4,12},{8,16},{12,20},{16,24},{20,28},{24,0},{28,4},{1,9},{5... | collective-permute-start | bytes 393224 | tf_op jit(solution)/shard_map/ppermute | solution.py:143
  119.3 13.6 %copy-start.8 = (bf16[2,4,128,128]{3,2,1,0:T(8,128)(2,1)S(1)}, bf16[2,4,128,128]{3,2,1,0:T(8,128)(2,1)}, u32[]{:S(2)}) copy-start(bf16[2,4,128,128]{3,2,1,0:T(8,128)(2,1)} %broadcast_select_fusion.3) | copy-start | bytes 786436
  124.9 12.5 %copy-start.7 = (bf16[2,4,128,128]{3,2,1,0:T(8,128)(2,1)S(1)}, bf16[2,4,128,128]{3,2,1,0:T(8,128)(2,1)}, u32[]{:S(2)}) copy-start(bf16[2,4,128,128]{3,2,1,0:T(8,128)(2,1)} %broadcast_select_fusion.2) | copy-start | bytes 786436
  127.2 13.7 %copy-start.6 = (bf16[2,4,128,128]{3,2,1,0:T(8,128)(2,1)S(1)}, bf16[2,4,128,128]{3,2,1,0:T(8,128)(2,1)}, u32[]{:S(2)}) copy-start(bf16[2,4,128,128]{3,2,1,0:T(8,128)(2,1)} %broadcast_select_fusion.1) | copy-start | bytes 786436
  129.6 18.8 %copy-start.9 = (bf16[2,4,128,128]{3,2,1,0:T(8,128)(2,1)S(1)}, bf16[2,4,128,128]{3,2,1,0:T(8,128)(2,1)}, u32[]{:S(2)}) copy-start(bf16[2,4,128,128]{3,2,1,0:T(8,128)(2,1)} %broadcast_select_fusion) | copy-start | bytes 786436
  132.9 15.5 %collective-permute-start.6 = (bf16[2,4,128,128]{3,2,1,0:T(8,128)(2,1)S(1)}, bf16[2,4,128,128]{3,2,1,0:T(8,128)(2,1)S(1)}, u32[]{:S(2)}, u32[]{:S(2)}) collective-permute-start(bf16[2,4,128,128]{3,2,1,0:T(8,128)(2,1)S(1)} %copy-done.8), channel_id=1, source_target_pairs={{0,16},{4,20},{8,24},{12,28},{16,0},{20,4},{24,8},{28,12},{1,17},{... | collective-permute-start | bytes 786440 | tf_op jit(solution)/shard_map/ppermute | solution.py:143
  133.8 12.9 %collective-permute-start.5 = (bf16[1,4,128,128]{3,2,1,0:T(8,128)(2,1)S(1)}, bf16[1,4,128,128]{3,2,1,0:T(8,128)(2,1)S(1)}, u32[]{:S(2)}, u32[]{:S(2)}) collective-permute-start(bf16[1,4,128,128]{3,2,1,0:T(8,128)(2,1)S(1)} %bitcast_select_fusion.12), channel_id=1, source_target_pairs={{0,12},{4,16},{8,20},{12,24},{16,28},{20,0},{24,4},{28,8},{1,13},{... | collective-permute-start | bytes 393224 | tf_op jit(solution)/shard_map/ppermute | solution.py:143
  137.4 28.4 %collective-permute-start.8 = (bf16[2,4,128,128]{3,2,1,0:T(8,128)(2,1)S(1)}, bf16[2,4,128,128]{3,2,1,0:T(8,128)(2,1)S(1)}, u32[]{:S(2)}, u32[]{:S(2)}) collective-permute-start(bf16[2,4,128,128]{3,2,1,0:T(8,128)(2,1)S(1)} %copy-done.7), channel_id=1, source_target_pairs={{0,20},{4,24},{8,28},{12,0},{16,4},{20,8},{24,12},{28,16},{1,21},{... | collective-permute-start | bytes 786440 | tf_op jit(solution)/shard_map/ppermute | solution.py:143
  137.5 16.3 %collective-permute-start.7 = (bf16[1,4,128,128]{3,2,1,0:T(8,128)(2,1)S(1)}, bf16[1,4,128,128]{3,2,1,0:T(8,128)(2,1)S(1)}, u32[]{:S(2)}, u32[]{:S(2)}) collective-permute-start(bf16[1,4,128,128]{3,2,1,0:T(8,128)(2,1)S(1)} %bitcast_select_fusion.11), channel_id=1, source_target_pairs={{0,16},{4,20},{8,24},{12,28},{16,0},{20,4},{24,8},{28,12},{1,17},{... | collective-permute-start | bytes 393224 | tf_op jit(solution)/shard_map/ppermute | solution.py:143
  140.9 25.7 %collective-permute-start.10 = (bf16[2,4,128,128]{3,2,1,0:T(8,128)(2,1)S(1)}, bf16[2,4,128,128]{3,2,1,0:T(8,128)(2,1)S(1)}, u32[]{:S(2)}, u32[]{:S(2)}) collective-permute-start(bf16[2,4,128,128]{3,2,1,0:T(8,128)(2,1)S(1)} %copy-done.6), channel_id=1, source_target_pairs={{0,24},{4,28},{8,0},{12,4},{16,8},{20,12},{24,16},{28,20},{1,25},{... | collective-permute-start | bytes 786440 | tf_op jit(solution)/shard_map/ppermute | solution.py:143
  146.7 19.1 %collective-permute-start.9 = (bf16[1,4,128,128]{3,2,1,0:T(8,128)(2,1)S(1)}, bf16[1,4,128,128]{3,2,1,0:T(8,128)(2,1)S(1)}, u32[]{:S(2)}, u32[]{:S(2)}) collective-permute-start(bf16[1,4,128,128]{3,2,1,0:T(8,128)(2,1)S(1)} %bitcast_select_fusion.10), channel_id=1, source_target_pairs={{0,20},{4,24},{8,28},{12,0},{16,4},{20,8},{24,12},{28,16},{1,21},{... | collective-permute-start | bytes 393224 | tf_op jit(solution)/shard_map/ppermute | solution.py:143
  148.4 19.8 %collective-permute-start.12 = (bf16[2,4,128,128]{3,2,1,0:T(8,128)(2,1)S(1)}, bf16[2,4,128,128]{3,2,1,0:T(8,128)(2,1)S(1)}, u32[]{:S(2)}, u32[]{:S(2)}) collective-permute-start(bf16[2,4,128,128]{3,2,1,0:T(8,128)(2,1)S(1)} %copy-done.9), channel_id=1, source_target_pairs={{0,28},{4,0},{8,4},{12,8},{16,12},{20,16},{24,20},{28,24},{1,29},{... | collective-permute-start | bytes 786440 | tf_op jit(solution)/shard_map/ppermute | solution.py:143
  153.8 13.6 %collective-permute-start.11 = (bf16[1,4,128,128]{3,2,1,0:T(8,128)(2,1)S(1)}, bf16[1,4,128,128]{3,2,1,0:T(8,128)(2,1)S(1)}, u32[]{:S(2)}, u32[]{:S(2)}) collective-permute-start(bf16[1,4,128,128]{3,2,1,0:T(8,128)(2,1)S(1)} %bitcast_select_fusion.9), channel_id=1, source_target_pairs={{0,24},{4,28},{8,0},{12,4},{16,8},{20,12},{24,16},{28,20},{1,25},{... | collective-permute-start | bytes 393224 | tf_op jit(solution)/shard_map/ppermute | solution.py:143
  165.7 3.1 %collective-permute-start.13 = (bf16[1,4,128,128]{3,2,1,0:T(8,128)(2,1)S(1)}, bf16[1,4,128,128]{3,2,1,0:T(8,128)(2,1)S(1)}, u32[]{:S(2)}, u32[]{:S(2)}) collective-permute-start(bf16[1,4,128,128]{3,2,1,0:T(8,128)(2,1)S(1)} %bitcast_select_fusion.8), channel_id=1, source_target_pairs={{0,28},{4,0},{8,4},{12,8},{16,12},{20,16},{24,20},{28,24},{1,29},{... | collective-permute-start | bytes 393224 | tf_op jit(solution)/shard_map/ppermute | solution.py:143
Sparse Core Ops, SparseCore 0:
  10.6 39.8 all-gather.1
  104.7 34.6 reduce-scatter.1

commit v2 on v0

--- a/solution.py
+++ b/solution.py
@@ -27,16 +27,14 @@
 
 
 def route_blocks(dispatch_table, block_data):
+    layers = dispatch_table.shape[0]
+    same_layer = jnp.eye(layers, dtype=dispatch_table.dtype)
+    spread = dispatch_table[:, :, :, None, :] * same_layer[:, None, None, :, None]
     moved_blocks = jnp.einsum(
-        "locr,lrf->olcf", dispatch_table, block_data, preferred_element_type=jnp.float32
+        "locms,msbw->olcbw", spread, block_data, preferred_element_type=jnp.float32
     ).astype(jnp.bfloat16)
-    return moved_blocks.reshape(
-        moved_blocks.shape[0],
-        moved_blocks.shape[1],
-        1,
-        moved_blocks.shape[2],
-        moved_blocks.shape[3],
-    )
+    shape = moved_blocks.shape
+    return moved_blocks.reshape(shape[0], shape[1] * shape[2] * shape[3], shape[4])
 
 
 def local(tokens, norm_gain, lengths, w_query, w_keyval, w_out, kv_cache, prior_kv, owners):
@@ -65,7 +63,10 @@
     dispatch = dispatch.reshape(layer_count, owner_count, capacity, rows_here)
     live_mask = (slot_ids < req_length + NEW_TOK)[None, None, :, None]
     earlier = jnp.where(live_mask, prior_kv[0], jnp.zeros_like(prior_kv[0]))
-    earlier_rows = earlier.reshape(layer_count - 1, rows_here, block_len * kv_width)
+    earlier_rows = earlier.reshape(layer_count - 1, rows_here, block_len, kv_width)
+    received_early = lax.all_to_all(
+        route_blocks(dispatch[: layer_count - 1], earlier_rows), "seq", 0, 0, tiled=True
+    )
     widened = tokens.astype(jnp.float32)
     normed = (
         widened
@@ -73,6 +74,7 @@
         * norm_gain
     ).astype(jnp.bfloat16)
     portion = lax.all_gather(normed, "dec", axis=0, tiled=True)
+    received_early, portion = lax.optimization_barrier((received_early, portion))
     flattened = portion.reshape(-1, portion.shape[-1])
     combined = jnp.concatenate(
         [
@@ -131,12 +133,20 @@
         scatter_dimension=0,
         tiled=True,
     )
-    current_rows = assembled.reshape(1, rows_here, block_len * kv_width)
-    all_rows = jnp.concatenate([earlier_rows, current_rows], axis=0)
-    received = lax.all_to_all(
-        route_blocks(dispatch, all_rows), "seq", split_axis=0, concat_axis=2, tiled=True
+    current_rows = assembled.reshape(1, rows_here, block_len, kv_width)
+    received_last = lax.all_to_all(
+        route_blocks(dispatch[layer_count - 1 :], current_rows), "seq", 0, 0, tiled=True
     )
-    decode_pool = received.reshape(1, 1, layer_count, owner_count, capacity, block_len, kv_width)
+    received = jnp.concatenate(
+        [
+            received_early.reshape(owner_count, layer_count - 1, capacity, block_len, kv_width),
+            received_last.reshape(owner_count, 1, capacity, block_len, kv_width),
+        ],
+        axis=1,
+    )
+    decode_pool = jnp.transpose(received, (1, 0, 2, 3, 4)).reshape(
+        1, 1, layer_count, owner_count, capacity, block_len, kv_width
+    )
     return (summed, decode_pool)
 
 

time: 154 us -> 132 us (0.86)
  blocking collectives: 43.1 us -> 17.8 us
  local copies, waits for them, and re-layouts: 33.7 us -> 20.6 us
  waiting for transfers between devices: 13.6 us -> 21.9 us
  matrix products: 31.2 us -> 37.2 us
  starting transfers between devices: 0.08 us -> 5.43 us
  other arithmetic: 15 us -> 11.9 us
    all_to_all x1, blocking collectives: 43.1 us -> 17.8 us  [local(): lax.all_to_all(route_blocks(dispatch[layer_count - 1:], current_rows), 's...]
    all_gather x1, waiting for transfers between devices: 13.6 us -> 0.01 us  [local(): portion = lax.all_gather(normed, 'dec', axis=0, tiled=True)]
    all_to_all x0 -> x1, waiting for transfers between devices: none -> 11.8 us  [local(): lax.all_to_all(route_blocks(dispatch[:layer_count - 1], earlier_rows), 's...]
    reshape x3 -> x0, local copies, waits for them, and re-layouts: 11.4 us -> none  [the longest x1 6.61 us: local(): received.reshape(1, 1, layer_count, owner_count, capacity, block_len, kv_...]
    reduce_scatter x1, waiting for transfers between devices: 0.01 us -> 10 us  [local(): lax.psum_scatter(product.reshape(NEW_TOK // lax.axis_size('dec') * lax.ax...]
    all_to_all x0 -> x1, starting transfers between devices: none -> 5.17 us  [local(): lax.all_to_all(route_blocks(dispatch[:layer_count - 1], earlier_rows), 's...]
    dot_general x1 -> x2, matrix products: 2.23 us -> 5.53 us  [route_blocks(): jnp.einsum('locms,msbw->olcbw', spread, block_data, preferred_element_typ...]
    broadcast_in_dim x2, local copies, waits for them, and re-layouts: 3.34 us -> 0.13 us  [local(): earlier = jnp.where(live_mask, prior_kv[0], jnp.zeros_like(prior_kv[0]))]
  transfers between devices with their start and end apart: 2 -> 3, of which waited for: 1 -> 2; matrix products, arithmetic and copies ran while one was open for 29% -> 23% of each run, Pallas kernels for 0% -> 0%
where the time goes in v2:
time: 132 us; the launch traced here: 131 us
  matrix products  37.2 us (28%)
  waiting for transfers between devices  21.9 us (17%)
  local copies, waits for them, and re-layouts  20.6 us (16%)
  blocking collectives  17.8 us (13%)
  between operations  16.7 us (13%)
  other arithmetic  11.9 us (9%)
  starting transfers between devices  5.43 us (4%)
    sub x2, matrix products, local(): weights = jnp.where(visible, jnp.exp(scores - row_max), 0.0)  18.4 us
    all_to_all x1, blocking collectives, local(): lax.all_to_all(route_blocks(dispatch[layer_count - 1:], current_rows), 's...  17.8 us
    all_to_all x1, waiting for transfers between devices, local(): lax.all_to_all(route_blocks(dispatch[:layer_count - 1], earlier_rows), 's...  11.8 us
    reduce_scatter x1, waiting for transfers between devices, local(): lax.psum_scatter(product.reshape(NEW_TOK // lax.axis_size('dec') * lax.ax...  10 us
    unnamed x10, local copies, waits for them, and re-layouts  7.78 us
    dot_general x2, matrix products, local(): jnp.einsum('jtp,pd->tjd', weights.astype(jnp.bfloat16), value_part, prefe...  6.31 us
    dynamic_update_slice x2, local copies, waits for them, and re-layouts, local(): lax.dynamic_update_slice(kept_cache, fresh_rows, (zero_index, req_length,...  5.96 us
    dot_general x2, matrix products, route_blocks(): jnp.einsum('locms,msbw->olcbw', spread, block_data, preferred_element_typ...  5.53 us
  transfers between devices with their start and end apart: 3, of which 2 were waited for; matrix products, arithmetic and copies ran while one was open for 23% of the time, Pallas kernels for 0%

profile of v2, /device:TPU:0, one launch (start us, length us, event | category | flops | bytes accessed | tf_op | source)
XLA Modules:
  0.0 131.5 jit_solution(6249389547671661406)
XLA Ops:
  7.2 0.0 copy-start
  7.2 0.0 all-gather.2.cloned.1.call-start
  7.2 1.2 fusion.55
  8.5 1.9 %fusion.57 = bf16[128,1,1536]{2,0,1:T(8,128)(2,1)} fusion(bf16[128,1,1536]{2,0,1:T(8,128)(2,1)} %param.9, f32[1536]{0:T(1024)} %param.10, f32[128]{0:T(128)S(1)} %add_rsqrt_fusion), kind=kLoop, calls=%fused_computation.54 | loop fusion | flops 786432 | bytes 793088 | tf_op jit(solution)/shard_map/convert_element_type | solution.py:75
  10.4 0.0 all-gather.2.cloned.1.call-update
  10.4 0.5 broadcast.110
  10.9 1.3 %reduce.4 = s32[3,2,16]{2,1,0:T(2,128)S(1)} reduce(s32[1,3,2,16,1]{3,4,2,1,0:T(1,128)} %param.17, s32[]{:T(128)} %broadcast.110), dimensions={0,4}, to_apply=%param.17.reduce_sub_computation.3 | reduce | bytes 772 | tf_op args[8]
  12.3 0.1 reshape_squeeze.3
  12.4 0.1 fusion.63
  12.4 0.1 reduce_window_sum.11
  12.5 0.2 select_reduce_fusion
  12.8 1.3 dynamic_slice.3
  14.7 0.1 copy.18
  14.8 3.6 %fusion.23 = bf16[8,2,4,128,128]{4,0,2,1,3:T(8,128)(2,1)S(1)} fusion(bf16[2,32,128,128]{3,2,1,0:T(8,128)(2,1)} %bitcast.189, pred[32,128]{0,1:T(8,128)(4,1)S(1)} %copy.18, bf16[2,2]{1,0:T(2,128)(2,1)S(1)} %compare_convert_fusion, bf16[2,8,4,32]{3,1,2,0:T(8,128)(2,1)S(1)} %copy.20), kind=kOutput, calls=%fused_computation.32 | convolution fusion | flops 136331264 | bytes 4202504 | tf_op jit(solution)/shard_map/locms,msbw->olcbw/dot_general | solution.py:33
  18.4 2.7 %copy.21 = bf16[8,2,4,128,128]{4,3,2,1,0:T(8,128)(2,1)} copy(bf16[8,2,4,128,128]{4,0,2,1,3:T(8,128)(2,1)S(1)} %fusion.23) | data formatting | bytes 4194304 | tf_op jit(solution)/shard_map/convert_element_type | solution.py:35
  21.1 5.2 %all-to-all-start = ((bf16[8,1024,128]{2,1,0:T(8,128)(2,1)}), bf16[8,1024,128]{2,1,0:T(8,128)(2,1)S(1)}, u32[]{:S(2)}, u32[]{:S(2)}) async-start(bf16[8,1024,128]{2,1,0:T(8,128)(2,1)} %bitcast.171), calls=%async_computation | async-start | bytes 4194304 | tf_op jit(solution)/shard_map/all_to_all | solution.py:67
  26.2 0.2 reduce-scatter.2.cloned.1.call-start
  27.1 2.3 %copy.36 = bf16[256,1536]{1,0:T(8,128)(2,1)} copy(bf16[256,1536]{0,1:T(8,128)(2,1)} %bitcast.178) | data formatting | bytes 1572864 | tf_op jit(solution)/shard_map/dot_general | solution.py:82
  30.0 2.3 %copy.17 = bf16[1,2,1536,128]{2,3,1,0:T(8,128)(2,1)} copy(bf16[1,2,1536,128]{3,2,1,0:T(8,128)(2,1)} %param.15) | data formatting | bytes 1572864 | tf_op args[6]
  32.3 2.4 %copy.23 = bf16[1536,384]{0,1:T(8,128)(2,1)} copy(bf16[1536,384]{1,0:T(8,128)(2,1)} %param.12) | data formatting | bytes 2359296 | tf_op args[3]
  35.3 0.6 iota_compare_fusion.3
  35.9 0.6 iota_add_fusion
  36.6 0.3 multiply_cosine_fusion
  36.9 2.3 %pad_select_fusion = bf16[2,2048,128]{1,2,0:T(8,128)(2,1)} fusion(bf16[2,1536,128]{1,2,0:T(8,128)(2,1)} %bitcast.175, pred[2048]{0:T(1024)(128)(4,1)S(1)} %iota_compare_fusion.3), kind=kLoop, calls=%fused_computation.49 | loop fusion | flops 524288 | bytes 1837056 | tf_op jit(solution)/shard_map/jit(_where)/select_n | solution.py:98
  39.2 1.9 %iota_compare_fusion = pred[512,2048]{0,1:T(8,128)(4,1)} fusion(s32[512]{0:T(512)S(1)} %get-tuple-element.18), kind=kLoop, calls=%fused_computation.25 | loop fusion | flops 1048576 | bytes 1050624 | tf_op jit(solution)/shard_map/le | solution.py:104
  41.1 11.8 %all-to-all-done = bf16[8,1024,128]{2,1,0:T(8,128)(2,1)S(1)} async-done(((bf16[8,1024,128]{2,1,0:T(8,128)(2,1)}), bf16[8,1024,128]{2,1,0:T(8,128)(2,1)S(1)}, u32[]{:S(2)}, u32[]{:S(2)}) %all-to-all-start) | async-done | bytes 2097184 | tf_op jit(solution)/shard_map/all_to_all | solution.py:67
  52.9 0.0 all-gather.2.cloned.1.call-done
  52.9 2.2 %fusion.28 = f32[512,2,128]{0,2,1:T(8,128)S(1)} fusion(bf16[2,128,1536]{2,1,0:T(8,128)(2,1)} %bitcast.179, bf16[512,1,1536]{2,0,1:T(8,128)(2,1)} %all-gather.2.cloned.1.call-done), kind=kOutput, calls=%fused_computation.35 | convolution fusion | flops 402653184 | bytes 2883584 | tf_op jit(solution)/shard_map/dot_general | solution.py:82
  55.1 2.5 %fusion.26 = f32[512,6,64]{0,2,1:T(8,128)S(1)} fusion(bf16[6,64,1536]{2,1,0:T(8,128)(2,1)} %bitcast.177, bf16[512,1,1536]{2,0,1:T(8,128)(2,1)} %all-gather.2.cloned.1.call-done), kind=kOutput, calls=%fused_computation.33 | convolution fusion | flops 603979776 | bytes 3538944 | tf_op jit(solution)/shard_map/dot_general | solution.py:81
  57.7 0.9 subtract_convert_fusion
  58.6 3.7 %dynamic_update_slice.3 = bf16[2,2048,128]{1,2,0:T(8,128)(2,1)} dynamic-update-slice(bf16[2,2048,128]{1,2,0:T(8,128)(2,1)} %pad_select_fusion, bf16[2,512,128]{1,2,0:T(8,128)(2,1)S(1)} %maximum_bitcast_fusion.1, s32[]{:T(128)} %constant.10.clone.1, s32[]{:T(128)S(6)} %select_n.31, s32[]{:T(128)} %constant.10.clone.1) | dynamic-update-slice | bytes 524292 | tf_op jit(solution)/shard_map/dynamic_update_slice | solution.py:100
  62.3 0.0 copy-start.2
  62.3 9.2 %fusion.93 = (f32[3,512]{1,0:T(4,128)S(1)}, bf16[3,512,2048]{1,2,0:T(8,128)(2,1)}) fusion(pred[512,2048]{0,1:T(8,128)(4,1)} %iota_compare_fusion, bf16[2,2048,128]{1,2,0:T(8,128)(2,1)} %dynamic_update_slice.3, bf16[512,2,3,32]{0,3,2,1:T(8,128)(2,1)} %bitcast.180, bf16[512,2,3,32]{0,3,2,1:T(8,128)(2,1)} %bitcast.182), kind=kOutput, calls=%fused_computation.103 | convolution fusion | flops 828114944 | bytes 9705472 | tf_op jit(solution)/shard_map/sub | solution.py:117
  71.5 0.0 copy-done.2
  71.5 9.2 %fusion.88 = (f32[3,512]{1,0:T(4,128)S(1)}, bf16[3,512,2048]{1,2,0:T(8,128)(2,1)}) fusion(pred[512,2048]{0,1:T(8,128)(4,1)} %iota_compare_fusion, bf16[2,2048,128]{1,2,0:T(8,128)(2,1)} %dynamic_update_slice.3, bf16[512,2,3,32]{0,3,2,1:T(8,128)(2,1)} %bitcast.183, bf16[512,2,3,32]{0,3,2,1:T(8,128)(2,1)S(1)} %bitcast.181), kind=kOutput, calls=%fused_computation.102 | convolution fusion | flops 828114944 | bytes 9705472 | tf_op jit(solution)/shard_map/sub | solution.py:117
  80.7 4.2 %fusion.47 = bf16[512,3,64]{0,2,1:T(8,128)(2,1)S(1)} fusion(bf16[3,512,2048]{1,2,0:T(8,128)(2,1)} %get-tuple-element.17, bf16[2,2048,128]{1,2,0:T(8,128)(2,1)} %dynamic_update_slice.3, f32[512,3]{0,1:T(4,128)S(1)} %bitcast.185), kind=kOutput, calls=%fused_computation.45 | convolution fusion | flops 402849792 | bytes 6756352 | tf_op jit(solution)/shard_map/jtp,pd->tjd/dot_general | solution.py:119
  84.9 0.5 copy-done.1
  85.4 2.1 %fusion.50 = bf16[512,3,64]{0,2,1:T(8,128)(2,1)S(1)} fusion(bf16[3,512,2048]{1,2,0:T(8,128)(2,1)S(1)} %copy-done.1, bf16[2,2048,128]{1,2,0:T(8,128)(2,1)} %dynamic_update_slice.3, f32[512,3]{0,1:T(4,128)S(1)} %bitcast.184), kind=kOutput, calls=%fused_computation.46 | convolution fusion | flops 402849792 | bytes 6756352 | tf_op jit(solution)/shard_map/jtp,pd->tjd/dot_general | solution.py:119
  87.6 0.0 copy-done
  87.6 2.2 %fusion.20 = bf16[512,1,1536]{2,0,1:T(8,128)(2,1)} fusion(bf16[512,384]{0,1:T(8,128)(2,1)S(1)} %bitcast.176, bf16[384,1536]{1,0:T(8,128)(2,1)S(1)} %copy-done), kind=kOutput, calls=%fused_computation.28 | convolution fusion | flops 604766208 | bytes 3145728 | tf_op jit(solution)/shard_map/dot_general | solution.py:127
  89.8 0.0 reduce-scatter.2.cloned.1.call-update
  89.8 2.3 %copy.26 = bf16[2,2048,128]{2,1,0:T(8,128)(2,1)} copy(bf16[2,2048,128]{1,2,0:T(8,128)(2,1)} %dynamic_update_slice.3) | data formatting | bytes 2097152 | tf_op jit(solution)/shard_map/dynamic_update_slice | solution.py:100
  92.1 2.0 %fusion.34 = bf16[8,1,4,128,128]{4,0,2,3,1:T(8,128)(2,1)S(1)} fusion(bf16[32,128,128,1]{2,1,0,3:T(8,128)(2,1)} %bitcast.172, pred[8,4,32]{2,1,0:T(4,128)(4,1)S(1)} %bitcast.187), kind=kOutput, calls=%fused_computation.40 | convolution fusion | flops 34078720 | bytes 2098176 | tf_op jit(solution)/shard_map/locms,msbw->olcbw/dot_general | solution.py:33
  94.0 0.4 copy.29
  94.5 17.8 %all_to_all.10 = bf16[8,512,128]{2,1,0:T(8,128)(2,1)S(1)} all-to-all(bf16[8,512,128]{2,1,0:T(8,128)(2,1)S(1)} %bitcast.173), channel_id=1, replica_groups=mesh['seq'=8,'dec'=4] {'seq'}, dimensions={0} | all-to-all | bytes 2097152 | tf_op jit(solution)/shard_map/all_to_all | solution.py:137
  112.3 0.3 maximum_bitcast_fusion
  112.5 2.1 %copy.30 = bf16[1,1,3,8,4,128,128]{6,5,4,3,2,1,0:T(8,128)(2,1)} copy(bf16[1,1,3,8,4,128,128]{6,5,4,2,3,1,0:T(8,128)(2,1)S(1)} %maximum_bitcast_fusion) | data formatting | bytes 6291456
  114.6 10.0 %reduce-scatter.2.cloned.1.call-done = bf16[128,1,1536]{2,0,1:T(8,128)(2,1)} async-done(((bf16[512,1,1536]{2,0,1:T(8,128)(2,1)}), bf16[128,1,1536]{2,0,1:T(8,128)(2,1)}) %reduce-scatter.2.cloned.1.call-update) | async-done | bytes 393232 | tf_op jit(solution)/shard_map/reduce_scatter | solution.py:128
  (15 shorter events, 0.2 us)
Async XLA Ops:
  7.2 80.4 %copy-start = (bf16[384,1536]{1,0:T(8,128)(2,1)S(1)}, bf16[384,1536]{1,0:T(8,128)(2,1)}, u32[]{:S(2)}) copy-start(bf16[384,1536]{1,0:T(8,128)(2,1)} %param.14) | copy-start | bytes 3538948
  7.2 45.7 %all-gather.2.cloned.1.call-start = ((), (), s32[]{:S(2)}) async-start(), calls=%async_computation.3 | async-start | bytes 1966080 | tf_op jit(solution)/shard_map/all_gather | solution.py:76
  21.1 31.8 %all-to-all-start = ((bf16[8,1024,128]{2,1,0:T(8,128)(2,1)}), bf16[8,1024,128]{2,1,0:T(8,128)(2,1)S(1)}, u32[]{:S(2)}, u32[]{:S(2)}) async-start(bf16[8,1024,128]{2,1,0:T(8,128)(2,1)} %bitcast.171), calls=%async_computation | async-start | bytes 4194304 | tf_op jit(solution)/shard_map/all_to_all | solution.py:67
  26.2 98.4 %reduce-scatter.2.cloned.1.call-start = ((), (), s32[]{:S(2)}) async-start(), calls=%async_computation.4 | async-start | bytes 1966080 | tf_op jit(solution)/shard_map/reduce_scatter | solution.py:128
  62.3 9.2 %copy-start.2 = (bf16[512,6,32]{0,2,1:T(8,128)(2,1)S(1)}, bf16[512,6,32]{0,2,1:T(8,128)(2,1)}, u32[]{:S(2)}) copy-start(bf16[512,6,32]{0,2,1:T(8,128)(2,1)} %get-tuple-element.8) | copy-start | bytes 589828
  80.7 4.7 %copy-start.1 = (bf16[3,512,2048]{1,2,0:T(8,128)(2,1)S(1)}, bf16[3,512,2048]{1,2,0:T(8,128)(2,1)}, u32[]{:S(2)}) copy-start(bf16[3,512,2048]{1,2,0:T(8,128)(2,1)} %get-tuple-element.15) | copy-start | bytes 18874372
Sparse Core Ops, SparseCore 0:
  10.5 39.7 all-gather.1
  89.9 34.6 reduce-scatter.1

commit v3 on v2

--- a/solution.py
+++ b/solution.py
@@ -101,38 +101,51 @@
         kept_cache, fresh_rows, (zero_index, req_length, zero_index)
     )
     grouped = queries.reshape(NEW_TOK, heads_here, query_cols // HD // heads_here, HD)
-    visible = slot_ids[None, :] <= (req_length + jnp.arange(NEW_TOK, dtype=jnp.int32))[:, None]
+    dec_count = lax.axis_size("dec")
+    chunk_len = NEW_TOK // dec_count
+    half_len = chunk_len // 2
     score_scale = HD ** (-0.5)
-    contexts = []
-    for head_index in range(heads_here):
-        key_part = assembled[head_index, :, :HD]
-        value_part = assembled[head_index, :, HD:]
-        scores = (
-            jnp.einsum(
-                "tjd,pd->jtp", grouped[:, head_index], key_part, preferred_element_type=jnp.float32
+
+    def attend(half):
+        row_ids = (
+            jnp.arange(dec_count, dtype=jnp.int32)[:, None] * chunk_len
+            + half * half_len
+            + jnp.arange(half_len, dtype=jnp.int32)[None, :]
+        ).reshape(-1)
+        rows = grouped.reshape(dec_count, 2, half_len, *grouped.shape[1:])[:, half].reshape(
+            dec_count * half_len, *grouped.shape[1:]
+        )
+        visible = slot_ids[None, :] <= (req_length + row_ids)[:, None]
+        contexts = []
+        for head_index in range(heads_here):
+            key_part = assembled[head_index, :, :HD]
+            value_part = assembled[head_index, :, HD:]
+            scores = (
+                jnp.einsum(
+                    "tjd,pd->jtp", rows[:, head_index], key_part, preferred_element_type=jnp.float32
+                )
+                * score_scale
             )
-            * score_scale
+            row_max = jnp.max(jnp.where(visible, scores, -jnp.inf), axis=-1, keepdims=True)
+            weights = jnp.where(visible, jnp.exp(scores - row_max), 0.0)
+            row_total = jnp.sum(weights, axis=-1, keepdims=True)
+            mixed_rows = jnp.einsum(
+                "jtp,pd->tjd",
+                weights.astype(jnp.bfloat16),
+                value_part,
+                preferred_element_type=jnp.float32,
+            )
+            contexts.append((mixed_rows / jnp.transpose(row_total, (1, 0, 2))).astype(jnp.bfloat16))
+        context = jnp.concatenate(contexts, axis=1).reshape(dec_count * half_len, query_cols)
+        product = jnp.dot(context, w_out, preferred_element_type=jnp.float32)
+        return lax.psum_scatter(
+            product.reshape(dec_count * half_len, 1, product.shape[-1]).astype(jnp.bfloat16),
+            "dec",
+            scatter_dimension=0,
+            tiled=True,
         )
-        row_max = jnp.max(jnp.where(visible, scores, -jnp.inf), axis=-1, keepdims=True)
-        weights = jnp.where(visible, jnp.exp(scores - row_max), 0.0)
-        row_total = jnp.sum(weights, axis=-1, keepdims=True)
-        mixed_rows = jnp.einsum(
-            "jtp,pd->tjd",
-            weights.astype(jnp.bfloat16),
-            value_part,
-            preferred_element_type=jnp.float32,
-        )
-        contexts.append((mixed_rows / jnp.transpose(row_total, (1, 0, 2))).astype(jnp.bfloat16))
-    context = jnp.concatenate(contexts, axis=1).reshape(NEW_TOK, query_cols)
-    product = jnp.dot(context, w_out, preferred_element_type=jnp.float32)
-    summed = lax.psum_scatter(
-        product.reshape(
-            NEW_TOK // lax.axis_size("dec") * lax.axis_size("dec"), 1, product.shape[-1]
-        ).astype(jnp.bfloat16),
-        "dec",
-        scatter_dimension=0,
-        tiled=True,
-    )
+
+    summed = jnp.concatenate([attend(0), attend(1)], axis=0)
     current_rows = assembled.reshape(1, rows_here, block_len, kv_width)
     received_last = lax.all_to_all(
         route_blocks(dispatch[layer_count - 1 :], current_rows), "seq", 0, 0, tiled=True

time: 132 us -> 151 us (1.14)
  waiting for transfers between devices: 21.9 us -> 35.7 us
  matrix products: 37.2 us -> 39.1 us
  other arithmetic: 11.9 us -> 13.6 us
    all_gather x1, waiting for transfers between devices: 0.01 us -> 15.6 us  [local(): portion = lax.all_gather(normed, 'dec', axis=0, tiled=True)]
    reduce_scatter x1 -> x2, waiting for transfers between devices: 10 us -> 6.56 us  [attend(): lax.psum_scatter(product.reshape(dec_count * half_len, 1, product.shape[-...]
    dot_general x3 -> x6, matrix products: 8.49 us -> 11.4 us  [the longest x4 8.4 us: attend(): jnp.einsum('jtp,pd->tjd', weights.astype(jnp.bfloat16), value_part, prefe...]
    dynamic_update_slice x2, local copies, waits for them, and re-layouts: 5.96 us -> 3.67 us  [local(): lax.dynamic_update_slice(kept_cache, fresh_rows, (zero_index, req_length,...]
    select_n x1, other arithmetic: 2.31 us -> 0.18 us  [local(): jnp.where((slot_ids < req_length)[None, :, None], padded, jnp.zeros_like(...]
    concatenate x1 -> x3, other arithmetic: 0.04 us -> 1.83 us  [the longest x1 1.79 us: local(): summed = jnp.concatenate([attend(0), attend(1)], axis=0)]
    all_to_all x1, waiting for transfers between devices: 11.8 us -> 13.5 us  [local(): lax.all_to_all(route_blocks(dispatch[:layer_count - 1], earlier_rows), 's...]
    reshape x1, other arithmetic: 0.27 us -> 1.88 us  [local(): jnp.transpose(received, (1, 0, 2, 3, 4))]
  transfers between devices with their start and end apart: 3 -> 4, of which waited for: 2 -> 3; matrix products, arithmetic and copies ran while one was open for 23% -> 22% of each run, Pallas kernels for 0% -> 0%
where the time goes in v3:
time: 151 us; the launch traced here: 150 us
  matrix products  39.1 us (26%)
  waiting for transfers between devices  35.7 us (24%)
  local copies, waits for them, and re-layouts  20.7 us (14%)
  blocking collectives  18.5 us (12%)
  between operations  16.5 us (11%)
  other arithmetic  13.6 us (9%)
  starting transfers between devices  5.82 us (4%)
    sub x4, matrix products, attend(): weights = jnp.where(visible, jnp.exp(scores - row_max), 0.0)  19 us
    all_to_all x1, blocking collectives, local(): lax.all_to_all(route_blocks(dispatch[layer_count - 1:], current_rows), 's...  18.5 us
    all_gather x1, waiting for transfers between devices, local(): portion = lax.all_gather(normed, 'dec', axis=0, tiled=True)  15.6 us
    all_to_all x1, waiting for transfers between devices, local(): lax.all_to_all(route_blocks(dispatch[:layer_count - 1], earlier_rows), 's...  13.5 us
    dot_general x4, matrix products, attend(): jnp.einsum('jtp,pd->tjd', weights.astype(jnp.bfloat16), value_part, prefe...  8.4 us
    unnamed x21, local copies, waits for them, and re-layouts  6.81 us
    reduce_scatter x2, waiting for transfers between devices, attend(): lax.psum_scatter(product.reshape(dec_count * half_len, 1, product.shape[-...  6.56 us
    all_to_all x1, starting transfers between devices, local(): lax.all_to_all(route_blocks(dispatch[:layer_count - 1], earlier_rows), 's...  5.3 us
  transfers between devices with their start and end apart: 4, of which 3 were waited for; matrix products, arithmetic and copies ran while one was open for 22% of the time, Pallas kernels for 0%

profile of v3, /device:TPU:0, one launch (start us, length us, event | category | flops | bytes accessed | tf_op | source)
XLA Modules:
  0.0 150.1 jit_solution(2101283514140152700)
XLA Ops:
  7.2 1.3 dynamic_slice.3
  9.3 0.5 broadcast.160
  9.8 1.3 reduce.4
  11.7 3.6 %fusion.44 = bf16[8,2,4,128,128]{4,0,2,1,3:T(8,128)(2,1)S(1)} fusion(bf16[2,32,128,128]{3,2,1,0:T(8,128)(2,1)} %bitcast.291, pred[32,128]{0,1:T(8,128)(4,1)S(1)} %copy.20, bf16[2,2]{1,0:T(2,128)(2,1)S(1)} %compare_convert_fusion, bf16[2,8,4,32]{3,1,2,0:T(8,128)(2,1)S(1)} %copy.22), kind=kOutput, calls=%fused_computation.59 | convolution fusion | flops 136331264 | bytes 4202504 | tf_op jit(solution)/shard_map/locms,msbw->olcbw/dot_general | solution.py:33
  15.3 2.7 %copy.23 = bf16[8,2,4,128,128]{4,3,2,1,0:T(8,128)(2,1)} copy(bf16[8,2,4,128,128]{4,0,2,1,3:T(8,128)(2,1)S(1)} %fusion.44) | data formatting | bytes 4194304 | tf_op jit(solution)/shard_map/convert_element_type | solution.py:35
  17.9 5.3 %all-to-all-start = ((bf16[8,1024,128]{2,1,0:T(8,128)(2,1)}), bf16[8,1024,128]{2,1,0:T(8,128)(2,1)}, u32[]{:S(2)}, u32[]{:S(2)}) async-start(bf16[8,1024,128]{2,1,0:T(8,128)(2,1)} %bitcast.11), calls=%async_computation | async-start | bytes 4194304 | tf_op jit(solution)/shard_map/all_to_all | solution.py:67
  23.5 0.9 fusion.100
  24.4 0.2 reduce-scatter.3.cloned.1.call-start
  25.3 1.2 copy.44
  27.1 1.4 copy.19
  28.5 2.5 %copy.25 = bf16[1536,384]{0,1:T(8,128)(2,1)} copy(bf16[1536,384]{1,0:T(8,128)(2,1)} %param.12) | data formatting | bytes 2359296 | tf_op args[3]
  30.9 0.7 add_add_fusion
  32.4 0.6 add_convert_fusion.2
  33.1 0.6 iota_compare_fusion.4
  33.7 0.3 multiply_cosine_fusion
  34.0 1.2 iota_compare_fusion.1
  35.2 1.1 iota_compare_fusion
  36.5 13.5 %all-to-all-done = bf16[8,1024,128]{2,1,0:T(8,128)(2,1)} async-done(((bf16[8,1024,128]{2,1,0:T(8,128)(2,1)}), bf16[8,1024,128]{2,1,0:T(8,128)(2,1)}, u32[]{:S(2)}, u32[]{:S(2)}) %all-to-all-start) | async-done | bytes 2097184 | tf_op jit(solution)/shard_map/all_to_all | solution.py:67
  50.0 15.6 %all-gather.2.cloned.1.call-done = bf16[512,1,1536]{2,0,1:T(8,128)(2,1)} async-done(((bf16[128,1,1536]{2,0,1:T(8,128)(2,1)}), bf16[512,1,1536]{2,0,1:T(8,128)(2,1)}) %all-gather.2.cloned.1.call-update) | async-done | bytes 1572880 | tf_op jit(solution)/shard_map/all_gather | solution.py:76
  65.6 2.3 %fusion.49 = f32[512,2,128]{0,2,1:T(8,128)S(1)} fusion(bf16[2,128,1536]{2,1,0:T(8,128)(2,1)} %bitcast.283, bf16[512,1,1536]{2,0,1:T(8,128)(2,1)} %all-gather.2.cloned.1.call-done), kind=kOutput, calls=%fused_computation.62 | convolution fusion | flops 402653184 | bytes 2883584 | tf_op jit(solution)/shard_map/dot_general | solution.py:82
  68.0 2.1 %fusion.47 = f32[512,6,64]{0,2,1:T(8,128)S(1)} fusion(bf16[6,64,1536]{2,1,0:T(8,128)(2,1)} %bitcast.279, bf16[512,1,1536]{2,0,1:T(8,128)(2,1)S(1)} %copy-done.7), kind=kOutput, calls=%fused_computation.60 | convolution fusion | flops 603979776 | bytes 3538944 | tf_op jit(solution)/shard_map/dot_general | solution.py:81
  70.1 0.7 subtract_convert_fusion.1
  70.8 0.8 add_convert_fusion
  71.9 1.2 concatenate.27
  73.3 1.1 fusion.121
  74.4 1.3 reshape_squeeze.10
  75.7 0.9 maximum_bitcast_fusion.1
  76.6 3.0 %dynamic_update_slice.3 = bf16[2,2048,128]{1,2,0:T(8,128)(2,1)S(1)} dynamic-update-slice(bf16[2,2048,128]{1,2,0:T(8,128)(2,1)S(1)} %pad_select_fusion, bf16[2,512,128]{1,2,0:T(8,128)(2,1)S(1)} %maximum_bitcast_fusion.1, s32[]{:T(128)} %constant.19.clone.1, s32[]{:T(128)S(6)} %select_n.43, s32[]{:T(128)} %constant.19.clone.1) | dynamic-update-slice | bytes 524292 | tf_op jit(solution)/shard_map/dynamic_update_slice | solution.py:100
  79.6 5.8 %fusion.125 = (f32[3,256]{1,0:T(4,128)S(1)}, bf16[3,256,2048]{1,2,0:T(8,128)(2,1)}) fusion(pred[256,2048]{0,1:T(8,128)(4,1)} %iota_compare_fusion.1, bf16[2,2048,128]{1,2,0:T(8,128)(2,1)S(1)} %dynamic_update_slice.3, bf16[256,2,3,64]{0,3,2,1:T(8,128)(2,1)S(1)} %reshape_squeeze.10), kind=kOutput, calls=%fused_computation.150 | convolution fusion | flops 413665280 | bytes 4918272 | tf_op jit(solution)/shard_map/sub | solution.py:130
  85.4 4.4 %fusion.124 = (f32[3,256]{1,0:T(4,128)S(1)}, bf16[3,256,2048]{1,2,0:T(8,128)(2,1)}) fusion(pred[256,2048]{0,1:T(8,128)(4,1)S(1)} %copy-done.5, bf16[2,2048,128]{1,2,0:T(8,128)(2,1)S(1)} %dynamic_update_slice.3, bf16[256,2,3,64]{0,3,2,1:T(8,128)(2,1)S(1)} %reshape_squeeze.10), kind=kOutput, calls=%fused_computation.149 | convolution fusion | flops 413665280 | bytes 4918272 | tf_op jit(solution)/shard_map/sub | solution.py:130
  89.8 2.7 %fusion.85 = bf16[256,3,64]{0,2,1:T(8,128)(2,1)S(1)} fusion(bf16[3,256,2048]{1,2,0:T(8,128)(2,1)} %get-tuple-element.23, bf16[2,2048,128]{1,2,0:T(8,128)(2,1)S(1)} %dynamic_update_slice.3, f32[256,3]{0,1:T(4,128)S(1)} %bitcast.288), kind=kOutput, calls=%fused_computation.77 | convolution fusion | flops 201424896 | bytes 3510272 | tf_op jit(solution)/shard_map/jtp,pd->tjd/dot_general | solution.py:132
  92.7 0.6 fusion.82
  93.3 1.5 %fusion.40 = bf16[256,1,1536]{2,0,1:T(8,128)(2,1)} fusion(bf16[256,384]{0,1:T(8,128)(2,1)S(1)} %bitcast.280, bf16[384,1536]{1,0:T(8,128)(2,1)S(1)} %copy-done), kind=kOutput, calls=%fused_computation.52 | convolution fusion | flops 302383104 | bytes 2162688 | tf_op jit(solution)/shard_map/dot_general | solution.py:140
  94.9 0.3 reduce-scatter.5.cloned.1.call-start
  95.1 0.3 reshape_squeeze.11
  95.4 4.4 %fusion.123 = (f32[3,256]{1,0:T(4,128)S(1)}, bf16[3,256,2048]{1,2,0:T(8,128)(2,1)}) fusion(pred[256,2048]{0,1:T(8,128)(4,1)S(1)} %copy-done.4, bf16[2,2048,128]{1,2,0:T(8,128)(2,1)S(1)} %dynamic_update_slice.3, bf16[256,2,3,64]{0,3,2,1:T(8,128)(2,1)S(1)} %reshape_squeeze.11), kind=kOutput, calls=%fused_computation.148 | convolution fusion | flops 413665280 | bytes 4918272 | tf_op jit(solution)/shard_map/sub | solution.py:130
  99.8 2.5 %fusion.79 = bf16[256,3,64]{0,2,1:T(8,128)(2,1)S(1)} fusion(bf16[3,256,2048]{1,2,0:T(8,128)(2,1)} %get-tuple-element.19, bf16[2,2048,128]{1,2,0:T(8,128)(2,1)S(1)} %dynamic_update_slice.3, f32[256,3]{0,1:T(4,128)S(1)} %bitcast.290), kind=kOutput, calls=%fused_computation.75 | convolution fusion | flops 201424896 | bytes 3510272 | tf_op jit(solution)/shard_map/jtp,pd->tjd/dot_general | solution.py:132
  102.4 4.4 %fusion.122 = (f32[3,256]{1,0:T(4,128)S(1)}, bf16[3,256,2048]{1,2,0:T(8,128)(2,1)}) fusion(pred[256,2048]{0,1:T(8,128)(4,1)S(1)} %copy-done.4, bf16[2,2048,128]{1,2,0:T(8,128)(2,1)S(1)} %dynamic_update_slice.3, bf16[256,2,3,64]{0,3,2,1:T(8,128)(2,1)S(1)} %reshape_squeeze.11), kind=kOutput, calls=%fused_computation.147 | convolution fusion | flops 413665280 | bytes 4918272 | tf_op jit(solution)/shard_map/sub | solution.py:130
  106.8 2.5 %fusion.76 = bf16[256,3,64]{0,2,1:T(8,128)(2,1)S(1)} fusion(bf16[3,256,2048]{1,2,0:T(8,128)(2,1)} %get-tuple-element.17, bf16[2,2048,128]{1,2,0:T(8,128)(2,1)S(1)} %dynamic_update_slice.3, f32[256,3]{0,1:T(4,128)S(1)} %bitcast.289), kind=kOutput, calls=%fused_computation.74 | convolution fusion | flops 201424896 | bytes 3510272 | tf_op jit(solution)/shard_map/jtp,pd->tjd/dot_general | solution.py:132
  109.4 1.5 fusion.41
  110.9 0.7 copy.32
  111.6 0.8 fusion.51
  112.3 0.4 copy.35
  112.7 18.5 %all_to_all.10 = bf16[8,512,128]{2,1,0:T(8,128)(2,1)S(1)} all-to-all(bf16[8,512,128]{2,1,0:T(8,128)(2,1)S(1)} %bitcast.276), channel_id=1, replica_groups=mesh['seq'=8,'dec'=4] {'seq'}, dimensions={0} | all-to-all | bytes 2097152 | tf_op jit(solution)/shard_map/all_to_all | solution.py:150
  131.2 1.9 %maximum_bitcast_fusion = bf16[1,1,3,8,4,128,128]{6,5,4,2,3,1,0:T(8,128)(2,1)S(1)} fusion(bf16[8,1,4,128,128]{4,3,2,1,0:T(8,128)(2,1)S(1)} %bitcast.277, bf16[8,2,4,128,128]{4,3,2,1,0:T(8,128)(2,1)} %bitcast.55), kind=kLoop, calls=%fused_computation.29 | loop fusion | flops 1572864 | bytes 6291456 | tf_op jit(solution)/shard_map/reshape | solution.py:160
  133.1 2.1 %copy.36 = bf16[1,1,3,8,4,128,128]{6,5,4,3,2,1,0:T(8,128)(2,1)} copy(bf16[1,1,3,8,4,128,128]{6,5,4,2,3,1,0:T(8,128)(2,1)S(1)} %maximum_bitcast_fusion) | data formatting | bytes 6291456
  135.2 6.6 %reduce-scatter.5.cloned.1.call-done = bf16[64,1,1536]{2,0,1:T(8,128)(2,1)} async-done(((bf16[256,1,1536]{2,0,1:T(8,128)(2,1)}), bf16[64,1,1536]{2,0,1:T(8,128)(2,1)}) %reduce-scatter.5.cloned.1.call-update) | async-done | bytes 196624 | tf_op jit(solution)/shard_map/reduce_scatter | solution.py:141
  141.8 1.8 %pad_maximum_fusion = bf16[128,1,1536]{2,0,1:T(8,128)(2,1)} fusion(bf16[64,1,1536]{2,0,1:T(8,128)(2,1)} %reduce-scatter.5.cloned.1.call-done, bf16[64,1,1536]{2,0,1:T(8,128)(2,1)} %reduce-scatter.3.cloned.1.call-done), kind=kLoop, calls=%fused_computation.90 | loop fusion | flops 786432 | bytes 786432 | tf_op jit(solution)/shard_map/concatenate | solution.py:148
  (48 shorter events, 2.0 us)
Async XLA Ops:
  7.2 86.2 %copy-start = (bf16[384,1536]{1,0:T(8,128)(2,1)S(1)}, bf16[384,1536]{1,0:T(8,128)(2,1)}, u32[]{:S(2)}) copy-start(bf16[384,1536]{1,0:T(8,128)(2,1)} %param.14) | copy-start | bytes 3538948
  17.9 5.4 %copy-start.2 = (bf16[128,1,1536]{2,0,1:T(8,128)(2,1)S(1)}, bf16[128,1,1536]{2,0,1:T(8,128)(2,1)}, u32[]{:S(2)}) copy-start(bf16[128,1,1536]{2,0,1:T(8,128)(2,1)} %param.9) | copy-start | bytes 1179652
  17.9 5.5 %copy-start.6 = (f32[1536]{0:T(1024)S(1)}, f32[1536]{0:T(1024)}, u32[]{:S(2)}) copy-start(f32[1536]{0:T(1024)} %param.10) | copy-start | bytes 18436
  17.9 7.3 %copy-start.3 = (bf16[1536,256]{1,0:T(8,128)(2,1)S(1)}, bf16[1536,256]{1,0:T(8,128)(2,1)}, u32[]{:S(2)}) copy-start(bf16[1536,256]{1,0:T(8,128)(2,1)} %param.13) | copy-start | bytes 2359300
  17.9 32.1 %all-to-all-start = ((bf16[8,1024,128]{2,1,0:T(8,128)(2,1)}), bf16[8,1024,128]{2,1,0:T(8,128)(2,1)}, u32[]{:S(2)}, u32[]{:S(2)}) async-start(bf16[8,1024,128]{2,1,0:T(8,128)(2,1)} %bitcast.11), calls=%async_computation | async-start | bytes 4194304 | tf_op jit(solution)/shard_map/all_to_all | solution.py:67
  23.2 42.4 %all-gather.2.cloned.1.call-start = ((), (), s32[]{:S(2)}) async-start(), calls=%async_computation.4 | async-start | bytes 1966080 | tf_op jit(solution)/shard_map/all_gather | solution.py:76
  24.4 110.8 %reduce-scatter.3.cloned.1.call-start = ((), (), s32[]{:S(2)}) async-start(), calls=%async_computation.5 | async-start | bytes 983040 | tf_op jit(solution)/shard_map/reduce_scatter | solution.py:141
  65.6 2.4 %copy-start.7 = (bf16[512,1,1536]{2,0,1:T(8,128)(2,1)S(1)}, bf16[512,1,1536]{2,0,1:T(8,128)(2,1)}, u32[]{:S(2)}) copy-start(bf16[512,1,1536]{2,0,1:T(8,128)(2,1)} %all-gather.2.cloned.1.call-done) | copy-start | bytes 4718596
  79.6 5.8 %copy-start.5 = (pred[256,2048]{0,1:T(8,128)(4,1)S(1)}, pred[256,2048]{0,1:T(8,128)(4,1)}, u32[]{:S(2)}) copy-start(pred[256,2048]{0,1:T(8,128)(4,1)} %iota_compare_fusion.1) | copy-start | bytes 1572868
  89.8 2.8 %copy-start.1 = (bf16[3,256,2048]{1,2,0:T(8,128)(2,1)S(1)}, bf16[3,256,2048]{1,2,0:T(8,128)(2,1)}, u32[]{:S(2)}) copy-start(bf16[3,256,2048]{1,2,0:T(8,128)(2,1)} %get-tuple-element.21) | copy-start | bytes 9437188
  92.7 2.8 %copy-start.4 = (pred[256,2048]{0,1:T(8,128)(4,1)S(1)}, pred[256,2048]{0,1:T(8,128)(4,1)}, u32[]{:S(2)}) copy-start(pred[256,2048]{0,1:T(8,128)(4,1)} %iota_compare_fusion) | copy-start | bytes 1572868
  94.9 46.9 %reduce-scatter.5.cloned.1.call-start = ((), (), s32[]{:S(2)}) async-start(), calls=%async_computation.6 | async-start | bytes 983040 | tf_op jit(solution)/shard_map/reduce_scatter | solution.py:141
Sparse Core Ops, SparseCore 0:
  26.2 39.3 all-gather.1
  95.0 21.8 reduce-scatter.2
  119.2 22.5 reduce-scatter.4

commit v4 on v2

--- a/solution.py
+++ b/solution.py
@@ -1,6 +1,10 @@
+import functools
+
 import jax
 import jax.numpy as jnp
 from jax import lax
+from jax.experimental import pallas as pl
+from jax.experimental.pallas import tpu as pltpu
 from jax.sharding import PartitionSpec as P
 
 HD = 64
@@ -35,6 +39,59 @@
     ).astype(jnp.bfloat16)
     shape = moved_blocks.shape
     return moved_blocks.reshape(shape[0], shape[1] * shape[2] * shape[3], shape[4])
+
+
+def attention_kernel(length_ref, q_ref, k_ref, v_ref, out_ref, *, tile, scale):
+    tile_index = pl.program_id(1)
+    span = k_ref.shape[1]
+    keys = k_ref[0]
+    values = v_ref[0]
+    token = lax.broadcasted_iota(jnp.int32, (tile, span), 0) + tile_index * tile
+    slot = lax.broadcasted_iota(jnp.int32, (tile, span), 1)
+    visible = slot <= length_ref[0] + token
+    for group_index in range(q_ref.shape[1]):
+        scores = (
+            lax.dot_general(
+                q_ref[0, group_index],
+                keys,
+                (((1,), (1,)), ((), ())),
+                preferred_element_type=jnp.float32,
+            )
+            * scale
+        )
+        row_max = jnp.max(jnp.where(visible, scores, -jnp.inf), axis=-1, keepdims=True)
+        weights = jnp.where(visible, jnp.exp(scores - row_max), 0.0)
+        row_total = jnp.sum(weights, axis=-1, keepdims=True)
+        mixed = jnp.dot(
+            weights.astype(jnp.bfloat16), values, preferred_element_type=jnp.float32
+        )
+        out_ref[0, group_index] = (mixed / row_total).astype(out_ref.dtype)
+
+
+def attend(length, queries, keys, values, tile=128):
+    heads, group, tokens, width = queries.shape
+    span = keys.shape[1]
+    kernel = functools.partial(attention_kernel, tile=tile, scale=HD ** (-0.5))
+    flops = 4 * heads * group * tokens * span * width
+    return pl.pallas_call(
+        kernel,
+        out_shape=jax.ShapeDtypeStruct(queries.shape, jnp.bfloat16),
+        grid_spec=pltpu.PrefetchScalarGridSpec(
+            num_scalar_prefetch=1,
+            grid=(heads, tokens // tile),
+            in_specs=[
+                pl.BlockSpec((1, group, tile, width), lambda h, i, n: (h, 0, i, 0)),
+                pl.BlockSpec((1, span, width), lambda h, i, n: (h, 0, 0)),
+                pl.BlockSpec((1, span, width), lambda h, i, n: (h, 0, 0)),
+            ],
+            out_specs=pl.BlockSpec((1, group, tile, width), lambda h, i, n: (h, 0, i, 0)),
+        ),
+        cost_estimate=pl.CostEstimate(
+            flops=flops,
+            transcendentals=heads * group * tokens * span,
+            bytes_accessed=2 * (2 * queries.size + keys.size + values.size),
+        ),
+    )(length, queries, keys, values)
 
 
 def local(tokens, norm_gain, lengths, w_query, w_keyval, w_out, kv_cache, prior_kv, owners):
@@ -100,30 +157,14 @@
     assembled = lax.dynamic_update_slice(
         kept_cache, fresh_rows, (zero_index, req_length, zero_index)
     )
-    grouped = queries.reshape(NEW_TOK, heads_here, query_cols // HD // heads_here, HD)
-    visible = slot_ids[None, :] <= (req_length + jnp.arange(NEW_TOK, dtype=jnp.int32))[:, None]
-    score_scale = HD ** (-0.5)
-    contexts = []
-    for head_index in range(heads_here):
-        key_part = assembled[head_index, :, :HD]
-        value_part = assembled[head_index, :, HD:]
-        scores = (
-            jnp.einsum(
-                "tjd,pd->jtp", grouped[:, head_index], key_part, preferred_element_type=jnp.float32
-            )
-            * score_scale
-        )
-        row_max = jnp.max(jnp.where(visible, scores, -jnp.inf), axis=-1, keepdims=True)
-        weights = jnp.where(visible, jnp.exp(scores - row_max), 0.0)
-        row_total = jnp.sum(weights, axis=-1, keepdims=True)
-        mixed_rows = jnp.einsum(
-            "jtp,pd->tjd",
-            weights.astype(jnp.bfloat16),
-            value_part,
-            preferred_element_type=jnp.float32,
-        )
-        contexts.append((mixed_rows / jnp.transpose(row_total, (1, 0, 2))).astype(jnp.bfloat16))
-    context = jnp.concatenate(contexts, axis=1).reshape(NEW_TOK, query_cols)
+    group_size = query_cols // HD // heads_here
+    grouped = jnp.transpose(
+        queries.reshape(NEW_TOK, heads_here, group_size, HD), (1, 2, 0, 3)
+    )
+    attended = attend(
+        req_length.reshape(1), grouped, assembled[:, :, :HD], assembled[:, :, HD:]
+    )
+    context = jnp.transpose(attended, (2, 0, 1, 3)).reshape(NEW_TOK, query_cols)
     product = jnp.dot(context, w_out, preferred_element_type=jnp.float32)
     summed = lax.psum_scatter(
         product.reshape(

time: 132 us -> 129 us (0.977)
  matrix products: 37.2 us -> 10.9 us
  Pallas kernels: 0 us -> 20 us
  waiting for transfers between devices: 21.9 us -> 29.4 us
  local copies, waits for them, and re-layouts: 20.6 us -> 17.2 us
    pallas_call x0 -> x1, Pallas kernels: none -> 20 us  [attend(): pl.pallas_call(kernel, out_shape=jax.ShapeDtypeStruct(queries.shape, jnp....]
    sub x2 -> x0, matrix products: 18.4 us -> none  [local(): weights = jnp.where(visible, jnp.exp(scores - row_max), 0.0)]
    dot_general x2 -> x0, matrix products: 6.31 us -> none  [local(): jnp.einsum('jtp,pd->tjd', weights.astype(jnp.bfloat16), value_part, prefe...]
    all_to_all x1, waiting for transfers between devices: 11.8 us -> 16.9 us  [local(): lax.all_to_all(route_blocks(dispatch[:layer_count - 1], earlier_rows), 's...]
    dynamic_update_slice x2 -> x1, local copies, waits for them, and re-layouts: 5.96 us -> 1.35 us  [local(): lax.dynamic_update_slice(kept_cache, fresh_rows, (zero_index, req_length,...]
    unnamed x10 -> x17, local copies, waits for them, and re-layouts: 7.78 us -> 3.27 us
    reduce_scatter x1, waiting for transfers between devices: 10 us -> 12.4 us  [local(): lax.psum_scatter(product.reshape(NEW_TOK // lax.axis_size('dec') * lax.ax...]
    le x1 -> x0, other arithmetic: 1.87 us -> none  [local(): slot_ids[None, :]]
  transfers between devices with their start and end apart: 3 -> 3, of which waited for: 2 -> 2; matrix products, arithmetic and copies ran while one was open for 23% -> 17% of each run, Pallas kernels for 0% -> 0%
where the time goes in v4:
time: 129 us
  waiting for transfers between devices  29.4 us (23%)
  Pallas kernels  20 us (16%)
  blocking collectives  17.8 us (14%)
  local copies, waits for them, and re-layouts  17.2 us (13%)
  between operations  16.9 us (13%)
  other arithmetic  11 us (9%)
  matrix products  10.9 us (8%)
  starting transfers between devices  5.56 us (4%)
    pallas_call x1, Pallas kernels, attend(): pl.pallas_call(kernel, out_shape=jax.ShapeDtypeStruct(queries.shape, jnp....  20 us
    all_to_all x1, blocking collectives, local(): lax.all_to_all(route_blocks(dispatch[layer_count - 1:], current_rows), 's...  17.8 us
    all_to_all x1, waiting for transfers between devices, local(): lax.all_to_all(route_blocks(dispatch[:layer_count - 1], earlier_rows), 's...  16.9 us
    reduce_scatter x1, waiting for transfers between devices, local(): lax.psum_scatter(product.reshape(NEW_TOK // lax.axis_size('dec') * lax.ax...  12.4 us
    all_to_all x1, starting transfers between devices, local(): lax.all_to_all(route_blocks(dispatch[:layer_count - 1], earlier_rows), 's...  5.3 us
    dot_general x2, matrix products, route_blocks(): jnp.einsum('locms,msbw->olcbw', spread, block_data, preferred_element_typ...  4.31 us
    unnamed x17, local copies, waits for them, and re-layouts  3.27 us
    convert_element_type x2, local copies, waits for them, and re-layouts, route_blocks(): moved_blocks = jnp.einsum('locms,msbw->olcbw', spread, block_data, prefer...  3.08 us
  transfers between devices with their start and end apart: 3, of which 2 were waited for; matrix products, arithmetic and copies ran while one was open for 17% of the time, Pallas kernels for 0%

profile of v4, /device:TPU:0, one launch (start us, length us, event | category | flops | bytes accessed | tf_op | source)
XLA Modules:
  0.0 128.8 jit_solution(7325122932169750171)
XLA Ops:
  7.2 0.0 copy-start
  7.2 0.0 all-gather.2.cloned.1.call-start
  7.2 1.2 fusion.13
  8.5 1.9 %fusion.15 = bf16[128,1,1536]{2,0,1:T(8,128)(2,1)} fusion(bf16[128,1,1536]{2,0,1:T(8,128)(2,1)} %param.9, f32[1536]{0:T(1024)} %param.10, f32[128]{0:T(128)S(1)} %add_rsqrt_fusion), kind=kLoop, calls=%fused_computation.21 | loop fusion | flops 786432 | bytes 793088 | tf_op jit(solution)/shard_map/convert_element_type | solution.py:132
  10.4 0.0 all-gather.2.cloned.1.call-update
  10.4 0.5 broadcast.87
  10.9 0.0 copy-done.5
  10.9 0.7 reduce.4
  11.6 0.1 reshape_squeeze.3
  11.7 0.1 fusion.16
  11.8 0.1 reduce_window_sum.11
  11.9 0.2 select_reduce_fusion
  12.1 0.6 dynamic_slice.3.length_ref
  13.4 0.1 copy.40
  13.6 3.6 %fusion.3 = bf16[8,2,4,128,128]{4,0,2,1,3:T(8,128)(2,1)S(1)} fusion(bf16[2,32,128,128]{3,2,1,0:T(8,128)(2,1)} %bitcast.81, pred[32,128]{0,1:T(8,128)(4,1)S(1)} %copy.40, bf16[2,2]{1,0:T(2,128)(2,1)S(1)} %compare_convert_fusion, bf16[2,8,4,32]{3,1,2,0:T(8,128)(2,1)S(1)} %copy.42), kind=kOutput, calls=%fused_computation.7 | convolution fusion | flops 136331264 | bytes 4202504 | tf_op jit(solution)/shard_map/locms,msbw->olcbw/dot_general | solution.py:37
  17.1 2.7 %copy.43 = bf16[8,2,4,128,128]{4,3,2,1,0:T(8,128)(2,1)} copy(bf16[8,2,4,128,128]{4,0,2,1,3:T(8,128)(2,1)S(1)} %fusion.3) | data formatting | bytes 4194304 | tf_op jit(solution)/shard_map/convert_element_type | solution.py:39
  19.8 5.3 %all-to-all-start = ((bf16[8,1024,128]{2,1,0:T(8,128)(2,1)}), bf16[8,1024,128]{2,1,0:T(8,128)(2,1)}, u32[]{:S(2)}, u32[]{:S(2)}) async-start(bf16[8,1024,128]{2,1,0:T(8,128)(2,1)} %bitcast.10), calls=%async_computation | async-start | bytes 4194304 | tf_op jit(solution)/shard_map/all_to_all | solution.py:124
  25.1 0.2 reduce-scatter.2.cloned.1.call-start
  26.0 0.6 copy.44
  26.6 2.3 %copy.62 = bf16[256,1536]{1,0:T(8,128)(2,1)} copy(bf16[256,1536]{0,1:T(8,128)(2,1)} %bitcast.74) | data formatting | bytes 1572864 | tf_op jit(solution)/shard_map/dot_general | solution.py:139
  28.9 0.6 add_convert_fusion.2
  29.6 0.3 multiply_cosine_fusion
  29.9 0.8 copy.51
  30.7 0.8 copy.49
  32.8 0.6 iota_compare_fusion.2
  33.5 1.4 %pad_select_fusion = bf16[2,2048,128]{2,1,0:T(8,128)(2,1)S(1)} fusion(bf16[2,1536,128]{2,1,0:T(8,128)(2,1)} %bitcast.75, pred[2048]{0:T(1024)(128)(4,1)S(1)} %iota_compare_fusion.2), kind=kLoop, calls=%fused_computation.15 | loop fusion | flops 524288 | bytes 1837056 | tf_op jit(solution)/shard_map/jit(_where)/select_n | solution.py:155
  34.9 16.9 %all-to-all-done = bf16[8,1024,128]{2,1,0:T(8,128)(2,1)} async-done(((bf16[8,1024,128]{2,1,0:T(8,128)(2,1)}), bf16[8,1024,128]{2,1,0:T(8,128)(2,1)}, u32[]{:S(2)}, u32[]{:S(2)}) %all-to-all-start) | async-done | bytes 2097184 | tf_op jit(solution)/shard_map/all_to_all | solution.py:124
  51.8 2.2 %fusion.8 = f32[512,6,64]{0,2,1:T(8,128)S(1)} fusion(bf16[6,64,1536]{2,1,0:T(8,128)(2,1)S(1)} %bitcast.73, bf16[512,1,1536]{2,0,1:T(8,128)(2,1)} %all-gather.2.cloned.1.call-done), kind=kOutput, calls=%fused_computation.10 | convolution fusion | flops 603979776 | bytes 3538944 | tf_op jit(solution)/shard_map/dot_general | solution.py:138
  54.1 0.1 subtract_convert_fusion.1
  54.2 0.4 copy.46
  54.6 1.2 copy.45
  55.7 2.3 %fusion.6 = f32[512,2,128]{2,0,1:T(8,128)S(1)} fusion(bf16[2,128,1536]{2,1,0:T(8,128)(2,1)} %bitcast.76, bf16[512,1,1536]{2,0,1:T(8,128)(2,1)} %all-gather.2.cloned.1.call-done), kind=kOutput, calls=%fused_computation.8 | convolution fusion | flops 402653184 | bytes 2883584 | tf_op jit(solution)/shard_map/dot_general | solution.py:139
  58.0 0.1 slice.62
  58.2 0.2 subtract_convert_fusion
  58.4 0.3 maximum_bitcast_fusion.2
  58.7 1.3 %dynamic_update_slice.3 = bf16[2,2048,128]{2,1,0:T(8,128)(2,1)S(1)} dynamic-update-slice(bf16[2,2048,128]{2,1,0:T(8,128)(2,1)S(1)} %pad_select_fusion, bf16[2,512,128]{2,1,0:T(8,128)(2,1)S(1)} %maximum_bitcast_fusion.2, s32[]{:T(128)} %constant.10.clone.1, s32[]{:T(128)S(6)} %select_n.18, s32[]{:T(128)} %constant.10.clone.1) | dynamic-update-slice | bytes 524292 | tf_op jit(solution)/shard_map/dynamic_update_slice | solution.py:157
  60.0 1.7 %fusion.24 = (bf16[2,2048,64]{2,1,0:T(8,128)(2,1)}, bf16[2,2048,64]{2,1,0:T(8,128)(2,1)}) fusion(bf16[2,2048,128]{2,1,0:T(8,128)(2,1)S(1)} %dynamic_update_slice.3), kind=kLoop, calls=%fused_computation.50 | loop fusion | bytes 2097152 | tf_op jit(solution)/shard_map/slice | solution.py:165
  61.7 1.3 %maximum_bitcast_fusion.1.q_ref = bf16[2,3,512,64]{3,2,1,0:T(8,128)(2,1)} fusion(bf16[512,2,3,32]{3,0,2,1:T(8,128)(2,1)S(1)} %bitcast.70, bf16[512,2,3,32]{3,0,2,1:T(8,128)(2,1)S(1)} %bitcast.71), kind=kLoop, calls=%fused_computation.22 | loop fusion | flops 786432 | bytes 786432 | tf_op jit(solution)/shard_map/transpose | solution.py:161
  63.0 20.0 %shard_map.104 = bf16[2,3,512,64]{3,2,1,0:T(8,128)(2,1)} custom-call(s32[1]{0:T(128)} %dynamic_slice.3.length_ref, bf16[2,3,512,64]{3,2,1,0:T(8,128)(2,1)} %maximum_bitcast_fusion.1.q_ref, bf16[2,2048,64]{2,1,0:T(8,128)(2,1)} %get-tuple-element.11.k_ref, bf16[2,2048,64]{2,1,0:T(8,128)(2,1)} %get-tuple-element.10.v_ref), custom_call_target="tpu_custom_call" | custom-call | flops 1610612736 | bytes 1835008 | tf_op jit(solution)/shard_map/pallas_call | solution.py:76
  83.0 1.4 %copy.53 = bf16[512,2,3,64]{0,3,2,1:T(8,128)(2,1)S(1)} copy(bf16[512,2,3,64]{3,0,2,1:T(8,128)(2,1)} %bitcast.77) | data formatting | bytes 786432 | tf_op jit(solution)/shard_map/transpose | solution.py:167
  84.4 2.2 %fusion = bf16[512,1,1536]{2,0,1:T(8,128)(2,1)} fusion(bf16[512,384]{0,1:T(8,128)(2,1)S(1)} %bitcast.72, bf16[384,1536]{1,0:T(8,128)(2,1)S(1)} %copy-done), kind=kOutput, calls=%fused_computation.3 | convolution fusion | flops 604766208 | bytes 3145728 | tf_op jit(solution)/shard_map/dot_general | solution.py:168
  86.6 0.0 reduce-scatter.2.cloned.1.call-update
  86.6 0.8 fusion.10
  87.4 0.4 copy.56
  87.8 17.8 %all_to_all.10 = bf16[8,512,128]{2,1,0:T(8,128)(2,1)S(1)} all-to-all(bf16[8,512,128]{2,1,0:T(8,128)(2,1)S(1)} %bitcast.68), channel_id=1, replica_groups=mesh['seq'=8,'dec'=4] {'seq'}, dimensions={0} | all-to-all | bytes 2097152 | tf_op jit(solution)/shard_map/all_to_all | solution.py:178
  105.6 1.9 %maximum_bitcast_fusion = bf16[1,1,3,8,4,128,128]{6,5,4,2,3,1,0:T(8,128)(2,1)S(1)} fusion(bf16[8,1,4,128,128]{4,3,2,1,0:T(8,128)(2,1)S(1)} %bitcast.69, bf16[8,2,4,128,128]{4,3,2,1,0:T(8,128)(2,1)} %bitcast.25), kind=kLoop, calls=%fused_computation.1 | loop fusion | flops 1572864 | bytes 6291456 | tf_op jit(solution)/shard_map/reshape | solution.py:188
  107.5 2.1 %copy.57 = bf16[1,1,3,8,4,128,128]{6,5,4,3,2,1,0:T(8,128)(2,1)} copy(bf16[1,1,3,8,4,128,128]{6,5,4,2,3,1,0:T(8,128)(2,1)S(1)} %maximum_bitcast_fusion) | data formatting | bytes 6291456
  109.5 12.4 %reduce-scatter.2.cloned.1.call-done = bf16[128,1,1536]{2,0,1:T(8,128)(2,1)} async-done(((bf16[512,1,1536]{2,0,1:T(8,128)(2,1)}), bf16[128,1,1536]{2,0,1:T(8,128)(2,1)}) %reduce-scatter.2.cloned.1.call-update) | async-done | bytes 393232 | tf_op jit(solution)/shard_map/reduce_scatter | solution.py:169
  (23 shorter events, 0.1 us)
Async XLA Ops:
  7.2 77.3 %copy-start = (bf16[384,1536]{1,0:T(8,128)(2,1)S(1)}, bf16[384,1536]{1,0:T(8,128)(2,1)}, u32[]{:S(2)}) copy-start(bf16[384,1536]{1,0:T(8,128)(2,1)} %param.14) | copy-start | bytes 3538948
  7.2 3.8 %copy-start.5 = (s32[1,3,2,16,1]{3,4,2,1,0:T(1,128)S(1)}, s32[1,3,2,16,1]{3,4,2,1,0:T(1,128)}, u32[]{:S(2)}) copy-start(s32[1,3,2,16,1]{3,4,2,1,0:T(1,128)} %param.17) | copy-start | bytes 1156
  7.2 4.9 %copy-start.6 = (s32[8]{0:T(128)S(1)}, s32[8]{0:T(128)}, u32[]{:S(2)}) copy-start(s32[8]{0:T(128)} %param.11) | copy-start | bytes 100
  7.2 44.6 %all-gather.2.cloned.1.call-start = ((), (), s32[]{:S(2)}) async-start(), calls=%async_computation.3 | async-start | bytes 1966080 | tf_op jit(solution)/shard_map/all_gather | solution.py:133
  19.8 6.2 %copy-start.2 = (bf16[1536,384]{1,0:T(8,128)(2,1)S(1)}, bf16[1536,384]{1,0:T(8,128)(2,1)}, u32[]{:S(2)}) copy-start(bf16[1536,384]{1,0:T(8,128)(2,1)} %param.12) | copy-start | bytes 3538948
  19.8 32.1 %all-to-all-start = ((bf16[8,1024,128]{2,1,0:T(8,128)(2,1)}), bf16[8,1024,128]{2,1,0:T(8,128)(2,1)}, u32[]{:S(2)}, u32[]{:S(2)}) async-start(bf16[8,1024,128]{2,1,0:T(8,128)(2,1)} %bitcast.10), calls=%async_computation | async-start | bytes 4194304 | tf_op jit(solution)/shard_map/all_to_all | solution.py:124
  25.1 96.9 %reduce-scatter.2.cloned.1.call-start = ((), (), s32[]{:S(2)}) async-start(), calls=%async_computation.4 | async-start | bytes 1966080 | tf_op jit(solution)/shard_map/reduce_scatter | solution.py:169
  55.7 2.4 %copy-start.3 = (f32[512,32]{1,0:T(8,128)S(1)}, f32[512,32]{1,0:T(8,128)}, u32[]{:S(2)}) copy-start(f32[512,32]{1,0:T(8,128)} %copy.51) | copy-start | bytes 196612
  55.7 2.4 %copy-start.4 = (f32[512,32]{1,0:T(8,128)S(1)}, f32[512,32]{1,0:T(8,128)}, u32[]{:S(2)}) copy-start(f32[512,32]{1,0:T(8,128)} %copy.49) | copy-start | bytes 196612
  60.0 1.7 %copy-start.1 = (bf16[512,6,32]{2,0,1:T(8,128)(2,1)S(1)}, bf16[512,6,32]{2,0,1:T(8,128)(2,1)}, u32[]{:S(2)}) copy-start(bf16[512,6,32]{2,0,1:T(8,128)(2,1)} %copy.45) | copy-start | bytes 589828
Sparse Core Ops, SparseCore 0:
  10.5 39.7 all-gather.1
  86.7 35.1 reduce-scatter.1

commit v5 on v4

--- a/solution.py
+++ b/solution.py
@@ -94,6 +94,54 @@
     )(length, queries, keys, values)
 
 
+def line_all_gather(chunk, axis):
+    count = lax.axis_size(axis)
+    here = lax.axis_index(axis)
+    upward = [(i, i + 1) for i in range(count - 1)]
+    downward = [(i + 1, i) for i in range(count - 1)]
+    from_below, from_above = [], []
+    carry_up = chunk
+    carry_down = chunk
+    for step in range(1, count):
+        carry_up = lax.ppermute(carry_up, axis, upward)
+        carry_down = lax.ppermute(carry_down, axis, downward)
+        from_below.append(carry_up)
+        from_above.append(carry_down)
+    below = jnp.stack(from_below)
+    above = jnp.stack(from_above)
+    pieces = []
+    for index in range(count):
+        gap = here - index
+        near = jnp.where(
+            gap > 0,
+            lax.dynamic_index_in_dim(below, jnp.clip(gap - 1, 0, count - 2), keepdims=False),
+            lax.dynamic_index_in_dim(above, jnp.clip(-gap - 1, 0, count - 2), keepdims=False),
+        )
+        pieces.append(jnp.where(gap == 0, chunk, near))
+    return jnp.concatenate(pieces, axis=0)
+
+
+def line_reduce_scatter(parts, axis):
+    count = lax.axis_size(axis)
+    here = lax.axis_index(axis)
+    upward = [(i, i + 1) for i in range(count - 1)]
+    downward = [(i + 1, i) for i in range(count - 1)]
+    chunk = parts.shape[0] // count
+
+    def part_of(index):
+        index = jnp.clip(index, 0, count - 1)
+        return lax.dynamic_slice_in_dim(parts, index * chunk, chunk, axis=0)
+
+    got_up = jnp.zeros((chunk,) + parts.shape[1:], jnp.float32)
+    got_down = jnp.zeros((chunk,) + parts.shape[1:], jnp.float32)
+    for step in range(1, count):
+        send_up = (part_of(here + count - step) + got_up).astype(jnp.bfloat16)
+        send_down = (part_of(here - count + step) + got_down).astype(jnp.bfloat16)
+        got_up = lax.ppermute(send_up, axis, upward).astype(jnp.float32)
+        got_down = lax.ppermute(send_down, axis, downward).astype(jnp.float32)
+    return (part_of(here) + got_up + got_down).astype(jnp.bfloat16)
+
+
 def local(tokens, norm_gain, lengths, w_query, w_keyval, w_out, kv_cache, prior_kv, owners):
     query_cols = w_query.shape[1]
     heads_here = kv_cache.shape[1]
@@ -130,7 +178,7 @@
         * lax.rsqrt(jnp.mean(widened * widened, axis=-1, keepdims=True) + EPSILON)
         * norm_gain
     ).astype(jnp.bfloat16)
-    portion = lax.all_gather(normed, "dec", axis=0, tiled=True)
+    portion = line_all_gather(normed, "dec")
     received_early, portion = lax.optimization_barrier((received_early, portion))
     flattened = portion.reshape(-1, portion.shape[-1])
     combined = jnp.concatenate(
@@ -166,14 +214,7 @@
     )
     context = jnp.transpose(attended, (2, 0, 1, 3)).reshape(NEW_TOK, query_cols)
     product = jnp.dot(context, w_out, preferred_element_type=jnp.float32)
-    summed = lax.psum_scatter(
-        product.reshape(
-            NEW_TOK // lax.axis_size("dec") * lax.axis_size("dec"), 1, product.shape[-1]
-        ).astype(jnp.bfloat16),
-        "dec",
-        scatter_dimension=0,
-        tiled=True,
-    )
+    summed = line_reduce_scatter(product.reshape(NEW_TOK, 1, product.shape[-1]), "dec")
     current_rows = assembled.reshape(1, rows_here, block_len, kv_width)
     received_last = lax.all_to_all(
         route_blocks(dispatch[layer_count - 1 :], current_rows), "seq", 0, 0, tiled=True

time: 129 us -> 155 us (1.20)
  starting transfers between devices: 5.56 us -> 48.6 us
  blocking collectives: 17.8 us -> 0 us
  between operations: 16.9 us -> 3.65 us
  other arithmetic: 11 us -> 22.8 us
  local copies, waits for them, and re-layouts: 17.2 us -> 22.8 us
  waiting for transfers between devices: 29.4 us -> 27.3 us
    ppermute x0 -> x12, starting transfers between devices: none -> 37.9 us  [the longest x3 16.4 us: line_all_gather(): carry_up = lax.ppermute(carry_up, axis, upward)]
    ppermute x0 -> x12, waiting for transfers between devices: none -> 19.5 us  [the longest x3 9.98 us: line_reduce_scatter(): got_up = lax.ppermute(send_up, axis, upward).astype(jnp.float32)]
    all_to_all x1 -> x0, blocking collectives: 17.8 us -> none  [local(): lax.all_to_all(route_blocks(dispatch[layer_count - 1:], current_rows), 's...]
    all_to_all x1, waiting for transfers between devices: 16.9 us -> 0.01 us  [local(): lax.all_to_all(route_blocks(dispatch[:layer_count - 1], earlier_rows), 's...]
    reduce_scatter x1 -> x0, waiting for transfers between devices: 12.4 us -> none  [local(): lax.psum_scatter(product.reshape(NEW_TOK // lax.axis_size('dec') * lax.ax...]
    all_to_all x0 -> x1, waiting for transfers between devices: none -> 7.86 us  [local(): lax.all_to_all(route_blocks(dispatch[layer_count - 1:], current_rows), 's...]
    convert_element_type x0 -> x4, other arithmetic: none -> 6.95 us  [the longest x2 3.74 us: line_reduce_scatter(): send_up = (part_of(here + count - step) + got_up).astype(jnp.bfloat16)]
    all_to_all x0 -> x1, starting transfers between devices: none -> 6.38 us  [local(): lax.all_to_all(route_blocks(dispatch[layer_count - 1:], current_rows), 's...]
  transfers between devices with their start and end apart: 3 -> 14, of which waited for: 2 -> 6; matrix products, arithmetic and copies ran while one was open for 17% -> 21% of each run, Pallas kernels for 0% -> 0%
where the time goes in v5:
time: 155 us
  starting transfers between devices  48.6 us (31%)
  waiting for transfers between devices  27.3 us (18%)
  local copies, waits for them, and re-layouts  22.8 us (15%)
  other arithmetic  22.8 us (15%)
  Pallas kernels  20 us (13%)
  matrix products  9.78 us (6%)
  between operations  3.65 us (2%)
    pallas_call x1, Pallas kernels, attend(): pl.pallas_call(kernel, out_shape=jax.ShapeDtypeStruct(queries.shape, jnp....  20 us
    ppermute x3, starting transfers between devices, line_all_gather(): carry_up = lax.ppermute(carry_up, axis, upward)  16.4 us
    ppermute x3, starting transfers between devices, line_reduce_scatter(): got_up = lax.ppermute(send_up, axis, upward).astype(jnp.float32)  13.7 us
    ppermute x3, waiting for transfers between devices, line_reduce_scatter(): got_up = lax.ppermute(send_up, axis, upward).astype(jnp.float32)  9.98 us
    all_to_all x1, waiting for transfers between devices, local(): lax.all_to_all(route_blocks(dispatch[layer_count - 1:], current_rows), 's...  7.86 us
    all_to_all x1, starting transfers between devices, local(): lax.all_to_all(route_blocks(dispatch[layer_count - 1:], current_rows), 's...  6.38 us
    unnamed x25, local copies, waits for them, and re-layouts  6.31 us
    ppermute x3, waiting for transfers between devices, line_all_gather(): carry_down = lax.ppermute(carry_down, axis, downward)  5.56 us
  transfers between devices with their start and end apart: 14, of which 6 were waited for; matrix products, arithmetic and copies ran while one was open for 21% of the time, Pallas kernels for 0%

profile of v5, /device:TPU:0, one launch (start us, length us, event | category | flops | bytes accessed | tf_op | source)
XLA Modules:
  0.0 154.8 jit_solution(7186231501523412407)
XLA Ops:
  0.6 1.3 fusion.12
  1.9 1.2 fusion.14
  3.1 1.3 collective-permute-start.3
  4.4 6.3 %collective-permute-start = (bf16[128,1,1536]{2,0,1:T(8,128)(2,1)S(1)}, bf16[128,1,1536]{2,0,1:T(8,128)(2,1)}, u32[]{:S(2)}, u32[]{:S(2)}) collective-permute-start(bf16[128,1,1536]{2,0,1:T(8,128)(2,1)S(1)} %fusion.14), channel_id=1, source_target_pairs={{0,1},{1,2},{2,3},{4,5},{5,6},{6,7},{8,9},{9,10},{10,11},{12,13},{... | collective-permute-start | bytes 1179656 | tf_op jit(solution)/shard_map/ppermute | solution.py:106
  10.7 1.3 dynamic_slice.45.length_ref
  13.3 1.3 reduce.4
  15.2 3.6 %fusion.2 = bf16[8,2,4,128,128]{4,0,2,1,3:T(8,128)(2,1)S(1)} fusion(bf16[2,32,128,128]{3,2,1,0:T(8,128)(2,1)} %bitcast.119, pred[32,128]{0,1:T(8,128)(4,1)S(1)} %copy.40, bf16[2,2]{1,0:T(2,128)(2,1)S(1)} %compare_convert_fusion, bf16[2,8,4,32]{3,1,2,0:T(8,128)(2,1)S(1)} %copy.42), kind=kOutput, calls=%fused_computation.5 | convolution fusion | flops 136331264 | bytes 4202504 | tf_op jit(solution)/shard_map/locms,msbw->olcbw/dot_general | solution.py:37
  18.7 2.7 %copy.43 = bf16[8,2,4,128,128]{4,3,2,1,0:T(8,128)(2,1)} copy(bf16[8,2,4,128,128]{4,0,2,1,3:T(8,128)(2,1)S(1)} %fusion.2) | data formatting | bytes 4194304 | tf_op jit(solution)/shard_map/convert_element_type | solution.py:39
  21.4 4.4 %all-to-all-start = ((bf16[8,1024,128]{2,1,0:T(8,128)(2,1)}), bf16[8,1024,128]{2,1,0:T(8,128)(2,1)}, u32[]{:S(2)}, u32[]{:S(2)}) async-start(bf16[8,1024,128]{2,1,0:T(8,128)(2,1)} %bitcast.10), calls=%async_computation | async-start | bytes 4194304 | tf_op jit(solution)/shard_map/all_to_all | solution.py:172
  26.5 1.3 collective-permute-start.4
  27.8 5.3 %collective-permute-start.1 = (bf16[128,1,1536]{2,0,1:T(8,128)(2,1)}, bf16[128,1,1536]{2,0,1:T(8,128)(2,1)}, u32[]{:S(2)}, u32[]{:S(2)}) collective-permute-start(bf16[128,1,1536]{2,0,1:T(8,128)(2,1)} %collective-permute-done), channel_id=1, source_target_pairs={{0,1},{1,2},{2,3},{4,5},{5,6},{6,7},{8,9},{9,10},{10,11},{12,13},{... | collective-permute-start | bytes 1179656 | tf_op jit(solution)/shard_map/ppermute | solution.py:106
  33.1 1.4 pad_select_fusion
  34.6 5.6 %collective-permute-done.4 = bf16[128,1,1536]{2,0,1:T(8,128)(2,1)} collective-permute-done((bf16[128,1,1536]{2,0,1:T(8,128)(2,1)}, bf16[128,1,1536]{2,0,1:T(8,128)(2,1)}, u32[]{:S(2)}, u32[]{:S(2)}) %collective-permute-start.4) | collective-permute-done | bytes 393248 | tf_op jit(solution)/shard_map/ppermute | solution.py:107
  40.1 1.3 collective-permute-start.5
  42.6 1.5 copy.44
  44.0 2.3 %copy.62 = bf16[256,1536]{1,0:T(8,128)(2,1)} copy(bf16[256,1536]{0,1:T(8,128)(2,1)} %bitcast.112) | data formatting | bytes 1572864 | tf_op jit(solution)/shard_map/dot_general | solution.py:187
  47.0 4.8 %collective-permute-start.2 = (bf16[128,1,1536]{2,0,1:T(8,128)(2,1)}, bf16[128,1,1536]{2,0,1:T(8,128)(2,1)S(1)}, u32[]{:S(2)}, u32[]{:S(2)}) collective-permute-start(bf16[128,1,1536]{2,0,1:T(8,128)(2,1)} %collective-permute-done.1), channel_id=1, source_target_pairs={{0,1},{1,2},{2,3},{4,5},{5,6},{6,7},{8,9},{9,10},{10,11},{12,13},{... | collective-permute-start | bytes 1179656 | tf_op jit(solution)/shard_map/ppermute | solution.py:106
  55.0 1.4 pad_maximum_fusion.2
  56.4 3.6 %collective-permute-done.2 = bf16[128,1,1536]{2,0,1:T(8,128)(2,1)S(1)} collective-permute-done((bf16[128,1,1536]{2,0,1:T(8,128)(2,1)}, bf16[128,1,1536]{2,0,1:T(8,128)(2,1)S(1)}, u32[]{:S(2)}, u32[]{:S(2)}) %collective-permute-start.2) | collective-permute-done | bytes 393248 | tf_op jit(solution)/shard_map/ppermute | solution.py:106
  60.0 1.2 pad_maximum_fusion.1
  61.7 1.3 pad_maximum_fusion
  63.5 2.2 %fusion.7 = f32[512,6,64]{0,2,1:T(8,128)S(1)} fusion(bf16[6,64,1536]{2,1,0:T(8,128)(2,1)S(1)} %bitcast.110, bf16[512,1,1536]{2,0,1:T(8,128)(2,1)} %pad_maximum_fusion), kind=kOutput, calls=%fused_computation.9 | convolution fusion | flops 603979776 | bytes 3538944 | tf_op jit(solution)/shard_map/dot_general | solution.py:186
  66.2 1.2 copy.45
  67.4 2.3 %fusion.5 = f32[512,2,128]{2,0,1:T(8,128)S(1)} fusion(bf16[2,128,1536]{2,1,0:T(8,128)(2,1)} %bitcast.113, bf16[512,1,1536]{2,0,1:T(8,128)(2,1)} %pad_maximum_fusion), kind=kOutput, calls=%fused_computation.7 | convolution fusion | flops 402653184 | bytes 2883584 | tf_op jit(solution)/shard_map/dot_general | solution.py:187
  70.3 2.1 %dynamic_update_slice.3 = bf16[2,2048,128]{2,1,0:T(8,128)(2,1)S(1)} dynamic-update-slice(bf16[2,2048,128]{2,1,0:T(8,128)(2,1)S(1)} %pad_select_fusion, bf16[2,512,128]{2,1,0:T(8,128)(2,1)S(1)} %maximum_bitcast_fusion.2, s32[]{:T(128)} %constant.84.clone.1, s32[]{:T(128)S(6)} %select_n.162, s32[]{:T(128)} %constant.84.clone.1) | dynamic-update-slice | bytes 524292 | tf_op jit(solution)/shard_map/dynamic_update_slice | solution.py:205
  72.4 1.7 %fusion.31 = (bf16[2,2048,64]{2,1,0:T(8,128)(2,1)}, bf16[2,2048,64]{2,1,0:T(8,128)(2,1)}) fusion(bf16[2,2048,128]{2,1,0:T(8,128)(2,1)S(1)} %dynamic_update_slice.3), kind=kLoop, calls=%fused_computation.70 | loop fusion | bytes 2097152 | tf_op jit(solution)/shard_map/slice | solution.py:213
  74.1 1.3 maximum_bitcast_fusion.1.q_ref
  75.5 20.0 %shard_map.104 = bf16[2,3,512,64]{3,2,1,0:T(8,128)(2,1)} custom-call(s32[1]{0:T(128)} %dynamic_slice.45.length_ref, bf16[2,3,512,64]{3,2,1,0:T(8,128)(2,1)} %maximum_bitcast_fusion.1.q_ref, bf16[2,2048,64]{2,1,0:T(8,128)(2,1)} %get-tuple-element.19.k_ref, bf16[2,2048,64]{2,1,0:T(8,128)(2,1)} %get-tuple-element.18.v_ref), custom_call_target="tpu_custom_call" | custom-call | flops 1610612736 | bytes 1835008 | tf_op jit(solution)/shard_map/pallas_call | solution.py:76
  95.4 1.4 copy.53
  96.8 1.0 fusion.32
  97.8 1.6 %copy-done.1 = f32[512,1536]{1,0:T(8,128)} copy-done((f32[512,1536]{1,0:T(8,128)}, f32[512,1536]{1,0:T(8,128)S(1)}, u32[]{:S(2)}) %copy-start.1) | copy-done | bytes 3145752
  99.6 4.3 %collective-permute-start.6 = (bf16[128,1,1536]{2,0,1:T(8,128)(2,1)S(1)}, bf16[128,1,1536]{2,0,1:T(8,128)(2,1)S(1)}, u32[]{:S(2)}, u32[]{:S(2)}) collective-permute-start(bf16[128,1,1536]{2,0,1:T(8,128)(2,1)S(1)} %get-tuple-element.12), channel_id=1, source_target_pairs={{0,1},{1,2},{2,3},{4,5},{5,6},{6,7},{8,9},{9,10},{10,11},{12,13},{... | collective-permute-start | bytes 1179656 | tf_op jit(solution)/shard_map/ppermute | solution.py:140
  103.9 1.3 collective-permute-start.9
  105.2 4.8 %collective-permute-done.6 = bf16[128,1,1536]{2,0,1:T(8,128)(2,1)S(1)} collective-permute-done((bf16[128,1,1536]{2,0,1:T(8,128)(2,1)S(1)}, bf16[128,1,1536]{2,0,1:T(8,128)(2,1)S(1)}, u32[]{:S(2)}, u32[]{:S(2)}) %collective-permute-start.6) | collective-permute-done | bytes 393248 | tf_op jit(solution)/shard_map/ppermute | solution.py:140
  109.9 1.2 fusion.17
  111.1 4.4 %collective-permute-start.7 = (bf16[128,1,1536]{2,0,1:T(8,128)(2,1)S(1)}, bf16[128,1,1536]{2,0,1:T(8,128)(2,1)S(1)}, u32[]{:S(2)}, u32[]{:S(2)}) collective-permute-start(bf16[128,1,1536]{2,0,1:T(8,128)(2,1)S(1)} %fusion.17), channel_id=1, source_target_pairs={{0,1},{1,2},{2,3},{4,5},{5,6},{6,7},{8,9},{9,10},{10,11},{12,13},{... | collective-permute-start | bytes 1179656 | tf_op jit(solution)/shard_map/ppermute | solution.py:140
  115.6 5.2 %collective-permute-done.7 = bf16[128,1,1536]{2,0,1:T(8,128)(2,1)S(1)} collective-permute-done((bf16[128,1,1536]{2,0,1:T(8,128)(2,1)S(1)}, bf16[128,1,1536]{2,0,1:T(8,128)(2,1)S(1)}, u32[]{:S(2)}, u32[]{:S(2)}) %collective-permute-start.7) | collective-permute-done | bytes 393248 | tf_op jit(solution)/shard_map/ppermute | solution.py:140
  120.8 2.5 %fusion.18 = (bf16[128,1,1536]{2,0,1:T(8,128)(2,1)}, bf16[128,1,1536]{2,0,1:T(8,128)(2,1)}) fusion(bf16[128,1,1536]{2,0,1:T(8,128)(2,1)S(1)} %collective-permute-done.7, f32[512,1536]{1,0:T(8,128)} %copy-done.1, s32[]{:T(128)S(6)} %select_n.164, bf16[128,1,1536]{2,0,1:T(8,128)(2,1)} %collective-permute-done.9, s32[]{:T(128)S(6)} %select_n.168), kind=kLoop, calls=%fused_computation.31 | loop fusion | flops 1179648 | bytes 3145736 | tf_op jit(solution)/shard_map/convert_element_type | solution.py:138
  123.4 1.3 collective-permute-start.10
  125.4 1.4 copy.56
  126.8 6.4 %all-to-all-start.1 = ((bf16[8,512,128]{2,1,0:T(8,128)(2,1)}), bf16[8,512,128]{2,1,0:T(8,128)(2,1)S(1)}, u32[]{:S(2)}, u32[]{:S(2)}) async-start(bf16[8,512,128]{2,1,0:T(8,128)(2,1)} %bitcast.48), calls=%async_computation.1 | async-start | bytes 2097152 | tf_op jit(solution)/shard_map/all_to_all | solution.py:219
  133.2 5.0 %collective-permute-start.8 = (bf16[128,1,1536]{2,0,1:T(8,128)(2,1)}, bf16[128,1,1536]{2,0,1:T(8,128)(2,1)S(1)}, u32[]{:S(2)}, u32[]{:S(2)}) collective-permute-start(bf16[128,1,1536]{2,0,1:T(8,128)(2,1)} %get-tuple-element.10), channel_id=1, source_target_pairs={{0,1},{1,2},{2,3},{4,5},{5,6},{6,7},{8,9},{9,10},{10,11},{12,13},{... | collective-permute-start | bytes 1179656 | tf_op jit(solution)/shard_map/ppermute | solution.py:140
  138.2 1.2 fusion.16
  139.4 1.3 collective-permute-start.11
  140.7 7.9 %all-to-all-done.1 = bf16[8,512,128]{2,1,0:T(8,128)(2,1)S(1)} async-done(((bf16[8,512,128]{2,1,0:T(8,128)(2,1)}), bf16[8,512,128]{2,1,0:T(8,128)(2,1)S(1)}, u32[]{:S(2)}, u32[]{:S(2)}) %all-to-all-start.1) | async-done | bytes 1048608 | tf_op jit(solution)/shard_map/all_to_all | solution.py:219
  148.6 1.9 %maximum_bitcast_fusion = bf16[1,1,3,8,4,128,128]{6,5,4,2,3,1,0:T(8,128)(2,1)S(1)} fusion(bf16[8,1,4,128,128]{4,3,2,1,0:T(8,128)(2,1)S(1)} %bitcast.106, bf16[8,2,4,128,128]{4,3,2,1,0:T(8,128)(2,1)} %bitcast.41), kind=kLoop, calls=%fused_computation.1 | loop fusion | flops 1572864 | bytes 6291456 | tf_op jit(solution)/shard_map/reshape | solution.py:229
  150.4 2.1 %copy.57 = bf16[1,1,3,8,4,128,128]{6,5,4,3,2,1,0:T(8,128)(2,1)} copy(bf16[1,1,3,8,4,128,128]{6,5,4,2,3,1,0:T(8,128)(2,1)S(1)} %maximum_bitcast_fusion) | data formatting | bytes 6291456
  152.8 2.0 %fusion.20 = bf16[128,1,1536]{2,0,1:T(8,128)(2,1)} fusion(bf16[128,1,1536]{2,0,1:T(8,128)(2,1)S(1)} %collective-permute-done.11, bf16[128,1,1536]{2,0,1:T(8,128)(2,1)S(1)} %collective-permute-done.8, f32[512,1536]{1,0:T(8,128)} %copy-done.1, s32[]{:T(128)S(6)} %select_n.163), kind=kLoop, calls=%fused_computation.34 | loop fusion | flops 983040 | bytes 1966084 | tf_op jit(solution)/shard_map/convert_element_type | solution.py:142
  (60 shorter events, 8.2 us)
Async XLA Ops:
  0.6 96.2 %copy-start = (bf16[384,1536]{1,0:T(8,128)(2,1)S(1)}, bf16[384,1536]{1,0:T(8,128)(2,1)}, u32[]{:S(2)}) copy-start(bf16[384,1536]{1,0:T(8,128)(2,1)} %param.14) | copy-start | bytes 3538948
  3.1 23.4 %collective-permute-start.3 = (bf16[128,1,1536]{2,0,1:T(8,128)(2,1)S(1)}, bf16[128,1,1536]{2,0,1:T(8,128)(2,1)}, u32[]{:S(2)}, u32[]{:S(2)}) collective-permute-start(bf16[128,1,1536]{2,0,1:T(8,128)(2,1)S(1)} %fusion.14), channel_id=1, source_target_pairs={{1,0},{2,1},{3,2},{5,4},{6,5},{7,6},{9,8},{10,9},{11,10},{13,12},{... | collective-permute-start | bytes 1179656 | tf_op jit(solution)/shard_map/ppermute | solution.py:107
  4.4 23.4 %collective-permute-start = (bf16[128,1,1536]{2,0,1:T(8,128)(2,1)S(1)}, bf16[128,1,1536]{2,0,1:T(8,128)(2,1)}, u32[]{:S(2)}, u32[]{:S(2)}) collective-permute-start(bf16[128,1,1536]{2,0,1:T(8,128)(2,1)S(1)} %fusion.14), channel_id=1, source_target_pairs={{0,1},{1,2},{2,3},{4,5},{5,6},{6,7},{8,9},{9,10},{10,11},{12,13},{... | collective-permute-start | bytes 1179656 | tf_op jit(solution)/shard_map/ppermute | solution.py:106
  15.1 100.5 %copy-start.8 = (pred[3,32,32]{2,1,0:T(8,128)(4,1)}, pred[3,32,32]{2,1,0:T(8,128)(4,1)S(1)}, u32[]{:S(2)}) copy-start(pred[3,32,32]{2,1,0:T(8,128)(4,1)S(1)} %iota_compare_fusion) | copy-start | bytes 9220
  21.4 41.5 %all-to-all-start = ((bf16[8,1024,128]{2,1,0:T(8,128)(2,1)}), bf16[8,1024,128]{2,1,0:T(8,128)(2,1)}, u32[]{:S(2)}, u32[]{:S(2)}) async-start(bf16[8,1024,128]{2,1,0:T(8,128)(2,1)} %bitcast.10), calls=%async_computation | async-start | bytes 4194304 | tf_op jit(solution)/shard_map/all_to_all | solution.py:172
  25.8 16.8 %copy-start.4 = (bf16[1536,384]{1,0:T(8,128)(2,1)S(1)}, bf16[1536,384]{1,0:T(8,128)(2,1)}, u32[]{:S(2)}) copy-start(bf16[1536,384]{1,0:T(8,128)(2,1)} %param.12) | copy-start | bytes 3538948
  26.5 13.6 %collective-permute-start.4 = (bf16[128,1,1536]{2,0,1:T(8,128)(2,1)}, bf16[128,1,1536]{2,0,1:T(8,128)(2,1)}, u32[]{:S(2)}, u32[]{:S(2)}) collective-permute-start(bf16[128,1,1536]{2,0,1:T(8,128)(2,1)} %collective-permute-done.3), channel_id=1, source_target_pairs={{1,0},{2,1},{3,2},{5,4},{6,5},{7,6},{9,8},{10,9},{11,10},{13,12},{... | collective-permute-start | bytes 1179656 | tf_op jit(solution)/shard_map/ppermute | solution.py:107
  27.8 19.2 %collective-permute-start.1 = (bf16[128,1,1536]{2,0,1:T(8,128)(2,1)}, bf16[128,1,1536]{2,0,1:T(8,128)(2,1)}, u32[]{:S(2)}, u32[]{:S(2)}) collective-permute-start(bf16[128,1,1536]{2,0,1:T(8,128)(2,1)} %collective-permute-done), channel_id=1, source_target_pairs={{0,1},{1,2},{2,3},{4,5},{5,6},{6,7},{8,9},{9,10},{10,11},{12,13},{... | collective-permute-start | bytes 1179656 | tf_op jit(solution)/shard_map/ppermute | solution.py:106
  40.1 14.9 %collective-permute-start.5 = (bf16[128,1,1536]{2,0,1:T(8,128)(2,1)}, bf16[128,1,1536]{2,0,1:T(8,128)(2,1)}, u32[]{:S(2)}, u32[]{:S(2)}) collective-permute-start(bf16[128,1,1536]{2,0,1:T(8,128)(2,1)} %collective-permute-done.4), channel_id=1, source_target_pairs={{1,0},{2,1},{3,2},{5,4},{6,5},{7,6},{9,8},{10,9},{11,10},{13,12},{... | collective-permute-start | bytes 1179656 | tf_op jit(solution)/shard_map/ppermute | solution.py:107
  44.0 7.7 %copy-start.10 = (f32[32]{0:T(128)S(1)}, f32[32]{0:T(128)}, u32[]{:S(2)}) copy-start(f32[32]{0:T(128)} %negate_power_fusion) | copy-start | bytes 388
  47.0 13.0 %collective-permute-start.2 = (bf16[128,1,1536]{2,0,1:T(8,128)(2,1)}, bf16[128,1,1536]{2,0,1:T(8,128)(2,1)S(1)}, u32[]{:S(2)}, u32[]{:S(2)}) collective-permute-start(bf16[128,1,1536]{2,0,1:T(8,128)(2,1)} %collective-permute-done.1), channel_id=1, source_target_pairs={{0,1},{1,2},{2,3},{4,5},{5,6},{6,7},{8,9},{9,10},{10,11},{12,13},{... | collective-permute-start | bytes 1179656 | tf_op jit(solution)/shard_map/ppermute | solution.py:106
  56.4 4.9 %copy-start.2 = (bf16[128,1,1536]{2,0,1:T(8,128)(2,1)S(1)}, bf16[128,1,1536]{2,0,1:T(8,128)(2,1)}, u32[]{:S(2)}) copy-start(bf16[128,1,1536]{2,0,1:T(8,128)(2,1)} %param.9) | copy-start | bytes 1179652
  56.4 4.9 %copy-start.9 = (f32[1536]{0:T(1024)S(1)}, f32[1536]{0:T(1024)}, u32[]{:S(2)}) copy-start(f32[1536]{0:T(1024)} %param.10) | copy-start | bytes 18436
  61.6 1.8 %copy-start.5 = (bf16[1536,384]{0,1:T(8,128)(2,1)S(1)}, bf16[1536,384]{0,1:T(8,128)(2,1)}, u32[]{:S(2)}) copy-start(bf16[1536,384]{0,1:T(8,128)(2,1)} %copy.44) | copy-start | bytes 3538948
  67.4 2.4 %copy-start.6 = (f32[512,32]{1,0:T(8,128)S(1)}, f32[512,32]{1,0:T(8,128)}, u32[]{:S(2)}) copy-start(f32[512,32]{1,0:T(8,128)} %copy.51) | copy-start | bytes 196612
  67.4 2.4 %copy-start.7 = (f32[512,32]{1,0:T(8,128)S(1)}, f32[512,32]{1,0:T(8,128)}, u32[]{:S(2)}) copy-start(f32[512,32]{1,0:T(8,128)} %copy.49) | copy-start | bytes 196612
  72.4 1.7 %copy-start.3 = (bf16[512,6,32]{2,0,1:T(8,128)(2,1)S(1)}, bf16[512,6,32]{2,0,1:T(8,128)(2,1)}, u32[]{:S(2)}) copy-start(bf16[512,6,32]{2,0,1:T(8,128)(2,1)} %copy.45) | copy-start | bytes 589828
  97.8 1.6 %copy-start.1 = (f32[512,1536]{1,0:T(8,128)}, f32[512,1536]{1,0:T(8,128)S(1)}, u32[]{:S(2)}) copy-start(f32[512,1536]{1,0:T(8,128)S(1)} %fusion.32) | copy-start | bytes 9437188
  99.6 10.4 %collective-permute-start.6 = (bf16[128,1,1536]{2,0,1:T(8,128)(2,1)S(1)}, bf16[128,1,1536]{2,0,1:T(8,128)(2,1)S(1)}, u32[]{:S(2)}, u32[]{:S(2)}) collective-permute-start(bf16[128,1,1536]{2,0,1:T(8,128)(2,1)S(1)} %get-tuple-element.12), channel_id=1, source_target_pairs={{0,1},{1,2},{2,3},{4,5},{5,6},{6,7},{8,9},{9,10},{10,11},{12,13},{... | collective-permute-start | bytes 1179656 | tf_op jit(solution)/shard_map/ppermute | solution.py:140
  103.9 11.7 %collective-permute-start.9 = (bf16[128,1,1536]{2,0,1:T(8,128)(2,1)S(1)}, bf16[128,1,1536]{2,0,1:T(8,128)(2,1)}, u32[]{:S(2)}, u32[]{:S(2)}) collective-permute-start(bf16[128,1,1536]{2,0,1:T(8,128)(2,1)S(1)} %get-tuple-element.13), channel_id=1, source_target_pairs={{1,0},{2,1},{3,2},{5,4},{6,5},{7,6},{9,8},{10,9},{11,10},{13,12},{... | collective-permute-start | bytes 1179656 | tf_op jit(solution)/shard_map/ppermute | solution.py:141
  111.1 9.7 %collective-permute-start.7 = (bf16[128,1,1536]{2,0,1:T(8,128)(2,1)S(1)}, bf16[128,1,1536]{2,0,1:T(8,128)(2,1)S(1)}, u32[]{:S(2)}, u32[]{:S(2)}) collective-permute-start(bf16[128,1,1536]{2,0,1:T(8,128)(2,1)S(1)} %fusion.17), channel_id=1, source_target_pairs={{0,1},{1,2},{2,3},{4,5},{5,6},{6,7},{8,9},{9,10},{10,11},{12,13},{... | collective-permute-start | bytes 1179656 | tf_op jit(solution)/shard_map/ppermute | solution.py:140
  115.6 9.1 %slice-start = ((pred[3,32,32]{2,1,0:T(8,128)(4,1)}), pred[1,32,32]{2,1,0:T(8,128)(4,1)S(1)}, s32[]{:S(2)}) async-start(pred[3,32,32]{2,1,0:T(8,128)(4,1)} %copy-done.8), calls=%async_computation.2 | async-start | bytes 8192 | tf_op jit(solution)/shard_map/slice | solution.py:220
  123.4 14.8 %collective-permute-start.10 = (bf16[128,1,1536]{2,0,1:T(8,128)(2,1)}, bf16[128,1,1536]{2,0,1:T(8,128)(2,1)S(1)}, u32[]{:S(2)}, u32[]{:S(2)}) collective-permute-start(bf16[128,1,1536]{2,0,1:T(8,128)(2,1)} %get-tuple-element.11), channel_id=1, source_target_pairs={{1,0},{2,1},{3,2},{5,4},{6,5},{7,6},{9,8},{10,9},{11,10},{13,12},{... | collective-permute-start | bytes 1179656 | tf_op jit(solution)/shard_map/ppermute | solution.py:141
  126.8 21.8 %all-to-all-start.1 = ((bf16[8,512,128]{2,1,0:T(8,128)(2,1)}), bf16[8,512,128]{2,1,0:T(8,128)(2,1)S(1)}, u32[]{:S(2)}, u32[]{:S(2)}) async-start(bf16[8,512,128]{2,1,0:T(8,128)(2,1)} %bitcast.48), calls=%async_computation.1 | async-start | bytes 2097152 | tf_op jit(solution)/shard_map/all_to_all | solution.py:219
  133.2 19.4 %collective-permute-start.8 = (bf16[128,1,1536]{2,0,1:T(8,128)(2,1)}, bf16[128,1,1536]{2,0,1:T(8,128)(2,1)S(1)}, u32[]{:S(2)}, u32[]{:S(2)}) collective-permute-start(bf16[128,1,1536]{2,0,1:T(8,128)(2,1)} %get-tuple-element.10), channel_id=1, source_target_pairs={{0,1},{1,2},{2,3},{4,5},{5,6},{6,7},{8,9},{9,10},{10,11},{12,13},{... | collective-permute-start | bytes 1179656 | tf_op jit(solution)/shard_map/ppermute | solution.py:140
  139.4 13.4 %collective-permute-start.11 = (bf16[128,1,1536]{2,0,1:T(8,128)(2,1)S(1)}, bf16[128,1,1536]{2,0,1:T(8,128)(2,1)S(1)}, u32[]{:S(2)}, u32[]{:S(2)}) collective-permute-start(bf16[128,1,1536]{2,0,1:T(8,128)(2,1)S(1)} %fusion.16), channel_id=1, source_target_pairs={{1,0},{2,1},{3,2},{5,4},{6,5},{7,6},{9,8},{10,9},{11,10},{13,12},{... | collective-permute-start | bytes 1179656 | tf_op jit(solution)/shard_map/ppermute | solution.py:141

commit v6 on v4

--- a/solution.py
+++ b/solution.py
@@ -41,37 +41,31 @@
     return moved_blocks.reshape(shape[0], shape[1] * shape[2] * shape[3], shape[4])
 
 
-def attention_kernel(length_ref, q_ref, k_ref, v_ref, out_ref, *, tile, scale):
+def attention_kernel(length_ref, q_ref, k_ref, v_ref, out_ref, score_ref, weight_ref, total_ref, *, tile, scale, rows_per_pass):
     tile_index = pl.program_id(1)
-    span = k_ref.shape[1]
-    keys = k_ref[0]
-    values = v_ref[0]
-    token = lax.broadcasted_iota(jnp.int32, (tile, span), 0) + tile_index * tile
-    slot = lax.broadcasted_iota(jnp.int32, (tile, span), 1)
-    visible = slot <= length_ref[0] + token
-    for group_index in range(q_ref.shape[1]):
-        scores = (
-            lax.dot_general(
-                q_ref[0, group_index],
-                keys,
-                (((1,), (1,)), ((), ())),
-                preferred_element_type=jnp.float32,
-            )
-            * scale
-        )
+    group, span = q_ref.shape[1], k_ref.shape[2]
+    queries = q_ref[0].reshape(group * tile, q_ref.shape[3])
+    score_ref[...] = jnp.dot(queries, k_ref[0], preferred_element_type=jnp.float32)
+    slot = lax.broadcasted_iota(jnp.int32, (rows_per_pass, span), 1)
+    row = lax.broadcasted_iota(jnp.int32, (rows_per_pass, span), 0)
+    for first in range(0, group * tile, rows_per_pass):
+        limit = length_ref[0] + tile_index * tile + (first % tile)
+        visible = slot <= row + limit
+        scores = score_ref[first : first + rows_per_pass, :] * scale
         row_max = jnp.max(jnp.where(visible, scores, -jnp.inf), axis=-1, keepdims=True)
         weights = jnp.where(visible, jnp.exp(scores - row_max), 0.0)
-        row_total = jnp.sum(weights, axis=-1, keepdims=True)
-        mixed = jnp.dot(
-            weights.astype(jnp.bfloat16), values, preferred_element_type=jnp.float32
-        )
-        out_ref[0, group_index] = (mixed / row_total).astype(out_ref.dtype)
-
-
-def attend(length, queries, keys, values, tile=128):
+        total_ref[first : first + rows_per_pass, :] = jnp.sum(weights, axis=-1, keepdims=True)
+        weight_ref[first : first + rows_per_pass, :] = weights.astype(jnp.bfloat16)
+    mixed = jnp.dot(weight_ref[...], v_ref[0], preferred_element_type=jnp.float32)
+    out_ref[0] = (mixed / total_ref[...]).astype(out_ref.dtype).reshape(out_ref.shape[1:])
+
+
+def attend(length, queries, keys_t, values, tile=128, rows_per_pass=16):
     heads, group, tokens, width = queries.shape
-    span = keys.shape[1]
-    kernel = functools.partial(attention_kernel, tile=tile, scale=HD ** (-0.5))
+    span = keys_t.shape[2]
+    kernel = functools.partial(
+        attention_kernel, tile=tile, scale=HD ** (-0.5), rows_per_pass=rows_per_pass
+    )
     flops = 4 * heads * group * tokens * span * width
     return pl.pallas_call(
         kernel,
@@ -81,17 +75,22 @@
             grid=(heads, tokens // tile),
             in_specs=[
                 pl.BlockSpec((1, group, tile, width), lambda h, i, n: (h, 0, i, 0)),
-                pl.BlockSpec((1, span, width), lambda h, i, n: (h, 0, 0)),
+                pl.BlockSpec((1, width, span), lambda h, i, n: (h, 0, 0)),
                 pl.BlockSpec((1, span, width), lambda h, i, n: (h, 0, 0)),
             ],
             out_specs=pl.BlockSpec((1, group, tile, width), lambda h, i, n: (h, 0, i, 0)),
+            scratch_shapes=[
+                pltpu.VMEM((group * tile, span), jnp.float32),
+                pltpu.VMEM((group * tile, span), jnp.bfloat16),
+                pltpu.VMEM((group * tile, 1), jnp.float32),
+            ],
         ),
         cost_estimate=pl.CostEstimate(
             flops=flops,
             transcendentals=heads * group * tokens * span,
-            bytes_accessed=2 * (2 * queries.size + keys.size + values.size),
+            bytes_accessed=2 * (2 * queries.size + keys_t.size + values.size),
         ),
-    )(length, queries, keys, values)
+    )(length, queries, keys_t, values)
 
 
 def local(tokens, norm_gain, lengths, w_query, w_keyval, w_out, kv_cache, prior_kv, owners):
@@ -162,7 +161,10 @@
         queries.reshape(NEW_TOK, heads_here, group_size, HD), (1, 2, 0, 3)
     )
     attended = attend(
-        req_length.reshape(1), grouped, assembled[:, :, :HD], assembled[:, :, HD:]
+        req_length.reshape(1),
+        grouped,
+        jnp.transpose(assembled[:, :, :HD], (0, 2, 1)),
+        assembled[:, :, HD:],
     )
     context = jnp.transpose(attended, (2, 0, 1, 3)).reshape(NEW_TOK, query_cols)
     product = jnp.dot(context, w_out, preferred_element_type=jnp.float32)

time: 129 us -> 135 us (1.047)
  Pallas kernels: 20 us -> 22.6 us
  other arithmetic: 11 us -> 12.4 us
    pallas_call x1, Pallas kernels: 20 us -> 22.6 us  [attend(): pl.pallas_call(kernel, out_shape=jax.ShapeDtypeStruct(queries.shape, jnp....]
    transpose x1, other arithmetic: 1.31 us -> 2.68 us  [local(): jnp.transpose(queries.reshape(NEW_TOK, heads_here, group_size, HD), (1, 2...]
    unnamed x17 -> x25, local copies, waits for them, and re-layouts: 3.27 us -> 3.29 us
  transfers between devices with their start and end apart: 3 -> 3, of which waited for: 2 -> 2; matrix products, arithmetic and copies ran while one was open for 17% -> 16% of each run, Pallas kernels for 0% -> 0%
where the time goes in v6:
time: 135 us; the launch traced here: 134 us
  waiting for transfers between devices  29.4 us (22%)
  Pallas kernels  22.6 us (17%)
  local copies, waits for them, and re-layouts  18.4 us (14%)
  blocking collectives  17.8 us (13%)
  between operations  16.9 us (13%)
  other arithmetic  12.4 us (9%)
  matrix products  10.8 us (8%)
  starting transfers between devices  5.56 us (4%)
    pallas_call x1, Pallas kernels, attend(): pl.pallas_call(kernel, out_shape=jax.ShapeDtypeStruct(queries.shape, jnp....  22.6 us
    all_to_all x1, blocking collectives, local(): lax.all_to_all(route_blocks(dispatch[layer_count - 1:], current_rows), 's...  17.8 us
    all_to_all x1, waiting for transfers between devices, local(): lax.all_to_all(route_blocks(dispatch[:layer_count - 1], earlier_rows), 's...  16.9 us
    reduce_scatter x1, waiting for transfers between devices, local(): lax.psum_scatter(product.reshape(NEW_TOK // lax.axis_size('dec') * lax.ax...  12.5 us
    all_to_all x1, starting transfers between devices, local(): lax.all_to_all(route_blocks(dispatch[:layer_count - 1], earlier_rows), 's...  5.3 us
    dot_general x2, matrix products, route_blocks(): jnp.einsum('locms,msbw->olcbw', spread, block_data, preferred_element_typ...  4.31 us
    unnamed x25, local copies, waits for them, and re-layouts  3.29 us
    convert_element_type x2, local copies, waits for them, and re-layouts, route_blocks(): moved_blocks = jnp.einsum('locms,msbw->olcbw', spread, block_data, prefer...  3.08 us
  transfers between devices with their start and end apart: 3, of which 2 were waited for; matrix products, arithmetic and copies ran while one was open for 16% of the time, Pallas kernels for 0%

profile of v6, /device:TPU:0, one launch (start us, length us, event | category | flops | bytes accessed | tf_op | source)
XLA Modules:
  0.0 133.9 jit_solution(2790381826805074195)
XLA Ops:
  7.2 0.0 copy-start
  7.2 0.0 all-gather.2.cloned.1.call-start
  7.2 1.2 fusion.13
  8.5 1.9 %fusion.15 = bf16[128,1,1536]{2,0,1:T(8,128)(2,1)} fusion(bf16[128,1,1536]{2,0,1:T(8,128)(2,1)} %param.9, f32[1536]{0:T(1024)} %param.10, f32[128]{0:T(128)S(1)} %add_rsqrt_fusion), kind=kLoop, calls=%fused_computation.22 | loop fusion | flops 786432 | bytes 793088 | tf_op jit(solution)/shard_map/convert_element_type | solution.py:131
  10.4 0.0 all-gather.2.cloned.1.call-update
  10.4 0.5 broadcast.87
  10.9 0.7 reduce.4
  11.6 0.1 reshape_squeeze.3
  11.7 0.1 fusion.16
  11.8 0.1 reduce_window_sum.11
  11.9 0.2 select_reduce_fusion
  12.1 0.6 dynamic_slice.3.length_ref
  13.4 0.1 copy.42
  13.6 3.6 %fusion.3 = bf16[8,2,4,128,128]{4,0,2,1,3:T(8,128)(2,1)S(1)} fusion(bf16[2,32,128,128]{3,2,1,0:T(8,128)(2,1)} %bitcast.83, pred[32,128]{0,1:T(8,128)(4,1)S(1)} %copy.42, bf16[2,2]{1,0:T(2,128)(2,1)S(1)} %compare_convert_fusion, bf16[2,8,4,32]{3,1,2,0:T(8,128)(2,1)S(1)} %copy.44), kind=kOutput, calls=%fused_computation.7 | convolution fusion | flops 136331264 | bytes 4202504 | tf_op jit(solution)/shard_map/locms,msbw->olcbw/dot_general | solution.py:37
  17.1 2.7 %copy.45 = bf16[8,2,4,128,128]{4,3,2,1,0:T(8,128)(2,1)} copy(bf16[8,2,4,128,128]{4,0,2,1,3:T(8,128)(2,1)S(1)} %fusion.3) | data formatting | bytes 4194304 | tf_op jit(solution)/shard_map/convert_element_type | solution.py:39
  19.8 5.3 %all-to-all-start = ((bf16[8,1024,128]{2,1,0:T(8,128)(2,1)}), bf16[8,1024,128]{2,1,0:T(8,128)(2,1)}, u32[]{:S(2)}, u32[]{:S(2)}) async-start(bf16[8,1024,128]{2,1,0:T(8,128)(2,1)} %bitcast.10), calls=%async_computation | async-start | bytes 4194304 | tf_op jit(solution)/shard_map/all_to_all | solution.py:123
  25.1 0.2 reduce-scatter.2.cloned.1.call-start
  26.0 0.6 copy.46
  26.6 2.3 %copy.65 = bf16[256,1536]{1,0:T(8,128)(2,1)} copy(bf16[256,1536]{0,1:T(8,128)(2,1)} %bitcast.76) | data formatting | bytes 1572864 | tf_op jit(solution)/shard_map/dot_general | solution.py:138
  28.9 0.6 add_convert_fusion.2
  29.6 0.3 multiply_cosine_fusion
  29.9 0.8 copy.53
  30.7 0.8 copy.51
  32.8 0.6 iota_compare_fusion.2
  33.5 1.4 %pad_select_fusion = bf16[2,2048,128]{2,1,0:T(8,128)(2,1)S(1)} fusion(bf16[2,1536,128]{2,1,0:T(8,128)(2,1)} %bitcast.77, pred[2048]{0:T(1024)(128)(4,1)S(1)} %iota_compare_fusion.2), kind=kLoop, calls=%fused_computation.16 | loop fusion | flops 524288 | bytes 1837056 | tf_op jit(solution)/shard_map/jit(_where)/select_n | solution.py:154
  34.9 16.9 %all-to-all-done = bf16[8,1024,128]{2,1,0:T(8,128)(2,1)} async-done(((bf16[8,1024,128]{2,1,0:T(8,128)(2,1)}), bf16[8,1024,128]{2,1,0:T(8,128)(2,1)}, u32[]{:S(2)}, u32[]{:S(2)}) %all-to-all-start) | async-done | bytes 2097184 | tf_op jit(solution)/shard_map/all_to_all | solution.py:123
  51.9 2.2 %fusion.8 = f32[512,6,64]{0,2,1:T(8,128)S(1)} fusion(bf16[6,64,1536]{2,1,0:T(8,128)(2,1)S(1)} %bitcast.75, bf16[512,1,1536]{2,0,1:T(8,128)(2,1)} %all-gather.2.cloned.1.call-done), kind=kOutput, calls=%fused_computation.10 | convolution fusion | flops 603979776 | bytes 3538944 | tf_op jit(solution)/shard_map/dot_general | solution.py:137
  54.1 0.1 subtract_convert_fusion.1
  54.3 1.2 copy.48
  55.4 1.2 copy.47
  56.6 2.1 %fusion.6 = f32[512,2,128]{2,0,1:T(8,128)S(1)} fusion(bf16[2,128,1536]{2,1,0:T(8,128)(2,1)S(1)} %bitcast.78, bf16[512,1,1536]{2,0,1:T(8,128)(2,1)} %all-gather.2.cloned.1.call-done), kind=kOutput, calls=%fused_computation.8 | convolution fusion | flops 402653184 | bytes 2883584 | tf_op jit(solution)/shard_map/dot_general | solution.py:138
  58.7 0.1 slice.63
  58.8 0.2 subtract_convert_fusion
  59.1 0.3 maximum_bitcast_fusion.2
  59.4 0.9 dynamic_update_slice.3
  60.3 1.4 %fusion.24 = (bf16[2,2048,64]{2,1,0:T(8,128)(2,1)}, bf16[2,64,2048]{1,2,0:T(8,128)(2,1)S(1)}) fusion(bf16[2,2048,128]{2,1,0:T(8,128)(2,1)S(1)} %dynamic_update_slice.3), kind=kLoop, calls=%fused_computation.51 | loop fusion | bytes 2097152 | tf_op jit(solution)/shard_map/slice | solution.py:167
  61.6 1.1 copy.55.k_ref
  62.8 2.7 %maximum_bitcast_fusion.1.q_ref = bf16[2,3,512,64]{3,2,1,0:T(8,128)(2,1)} fusion(bf16[512,2,3,32]{3,0,2,1:T(8,128)(2,1)} %bitcast.72, bf16[512,2,3,32]{3,0,2,1:T(8,128)(2,1)} %bitcast.73), kind=kLoop, calls=%fused_computation.23 | loop fusion | flops 786432 | bytes 786432 | tf_op jit(solution)/shard_map/transpose | solution.py:160
  65.5 22.6 %shard_map.104 = bf16[2,3,512,64]{3,2,1,0:T(8,128)(2,1)} custom-call(s32[1]{0:T(128)} %dynamic_slice.3.length_ref, bf16[2,3,512,64]{3,2,1,0:T(8,128)(2,1)} %maximum_bitcast_fusion.1.q_ref, bf16[2,64,2048]{2,1,0:T(8,128)(2,1)} %copy.55.k_ref, bf16[2,2048,64]{2,1,0:T(8,128)(2,1)} %get-tuple-element.10.v_ref), custom_call_target="tpu_custom_call" | custom-call | flops 1610612736 | bytes 1835008 | tf_op jit(solution)/shard_map/pallas_call | solution.py:70
  88.1 1.4 %copy.56 = bf16[512,2,3,64]{0,3,2,1:T(8,128)(2,1)S(1)} copy(bf16[512,2,3,64]{3,0,2,1:T(8,128)(2,1)} %bitcast.79) | data formatting | bytes 786432 | tf_op jit(solution)/shard_map/transpose | solution.py:169
  89.5 2.1 %fusion = bf16[512,1,1536]{2,0,1:T(8,128)(2,1)} fusion(bf16[512,384]{0,1:T(8,128)(2,1)S(1)} %bitcast.74, bf16[384,1536]{1,0:T(8,128)(2,1)S(1)} %copy-done), kind=kOutput, calls=%fused_computation.3 | convolution fusion | flops 604766208 | bytes 3145728 | tf_op jit(solution)/shard_map/dot_general | solution.py:170
  91.6 0.0 reduce-scatter.2.cloned.1.call-update
  91.7 0.8 fusion.10
  92.4 0.4 copy.59
  92.8 17.8 %all_to_all.10 = bf16[8,512,128]{2,1,0:T(8,128)(2,1)S(1)} all-to-all(bf16[8,512,128]{2,1,0:T(8,128)(2,1)S(1)} %bitcast.70), channel_id=1, replica_groups=mesh['seq'=8,'dec'=4] {'seq'}, dimensions={0} | all-to-all | bytes 2097152 | tf_op jit(solution)/shard_map/all_to_all | solution.py:180
  110.6 1.9 %maximum_bitcast_fusion = bf16[1,1,3,8,4,128,128]{6,5,4,2,3,1,0:T(8,128)(2,1)S(1)} fusion(bf16[8,1,4,128,128]{4,3,2,1,0:T(8,128)(2,1)S(1)} %bitcast.71, bf16[8,2,4,128,128]{4,3,2,1,0:T(8,128)(2,1)} %bitcast.26), kind=kLoop, calls=%fused_computation.1 | loop fusion | flops 1572864 | bytes 6291456 | tf_op jit(solution)/shard_map/reshape | solution.py:190
  112.5 2.1 %copy.60 = bf16[1,1,3,8,4,128,128]{6,5,4,3,2,1,0:T(8,128)(2,1)} copy(bf16[1,1,3,8,4,128,128]{6,5,4,2,3,1,0:T(8,128)(2,1)S(1)} %maximum_bitcast_fusion) | data formatting | bytes 6291456
  114.6 12.5 %reduce-scatter.2.cloned.1.call-done = bf16[128,1,1536]{2,0,1:T(8,128)(2,1)} async-done(((bf16[512,1,1536]{2,0,1:T(8,128)(2,1)}), bf16[128,1,1536]{2,0,1:T(8,128)(2,1)}) %reduce-scatter.2.cloned.1.call-update) | async-done | bytes 393232 | tf_op jit(solution)/shard_map/reduce_scatter | solution.py:171
  (32 shorter events, 0.1 us)
Async XLA Ops:
  7.2 82.3 %copy-start = (bf16[384,1536]{1,0:T(8,128)(2,1)S(1)}, bf16[384,1536]{1,0:T(8,128)(2,1)}, u32[]{:S(2)}) copy-start(bf16[384,1536]{1,0:T(8,128)(2,1)} %param.14) | copy-start | bytes 3538948
  7.2 3.8 %copy-start.9 = (s32[1,3,2,16,1]{3,4,2,1,0:T(1,128)S(1)}, s32[1,3,2,16,1]{3,4,2,1,0:T(1,128)}, u32[]{:S(2)}) copy-start(s32[1,3,2,16,1]{3,4,2,1,0:T(1,128)} %param.17) | copy-start | bytes 1156
  7.2 4.9 %copy-start.10 = (s32[8]{0:T(128)S(1)}, s32[8]{0:T(128)}, u32[]{:S(2)}) copy-start(s32[8]{0:T(128)} %param.11) | copy-start | bytes 100
  7.2 44.6 %all-gather.2.cloned.1.call-start = ((), (), s32[]{:S(2)}) async-start(), calls=%async_computation.3 | async-start | bytes 1966080 | tf_op jit(solution)/shard_map/all_gather | solution.py:132
  19.8 6.2 %copy-start.1 = (bf16[1536,384]{1,0:T(8,128)(2,1)S(1)}, bf16[1536,384]{1,0:T(8,128)(2,1)}, u32[]{:S(2)}) copy-start(bf16[1536,384]{1,0:T(8,128)(2,1)} %param.12) | copy-start | bytes 3538948
  19.8 32.1 %all-to-all-start = ((bf16[8,1024,128]{2,1,0:T(8,128)(2,1)}), bf16[8,1024,128]{2,1,0:T(8,128)(2,1)}, u32[]{:S(2)}, u32[]{:S(2)}) async-start(bf16[8,1024,128]{2,1,0:T(8,128)(2,1)} %bitcast.10), calls=%async_computation | async-start | bytes 4194304 | tf_op jit(solution)/shard_map/all_to_all | solution.py:123
  25.1 101.9 %reduce-scatter.2.cloned.1.call-start = ((), (), s32[]{:S(2)}) async-start(), calls=%async_computation.4 | async-start | bytes 1966080 | tf_op jit(solution)/shard_map/reduce_scatter | solution.py:171
  29.9 3.6 %copy-start.5 = (f32[512,32]{0,1:T(8,128)}, f32[512,32]{0,1:T(8,128)S(1)}, u32[]{:S(2)}) copy-start(f32[512,32]{0,1:T(8,128)S(1)} %get-tuple-element.16) | copy-start | bytes 196612
  29.9 3.6 %copy-start.7 = (f32[512,32]{0,1:T(8,128)}, f32[512,32]{0,1:T(8,128)S(1)}, u32[]{:S(2)}) copy-start(f32[512,32]{0,1:T(8,128)S(1)} %get-tuple-element.17) | copy-start | bytes 196612
  51.8 2.3 %copy-start.6 = (f32[512,32]{0,1:T(8,128)S(1)}, f32[512,32]{0,1:T(8,128)}, u32[]{:S(2)}) copy-start(f32[512,32]{0,1:T(8,128)} %copy-done.5) | copy-start | bytes 196612
  51.8 2.3 %copy-start.8 = (f32[512,32]{0,1:T(8,128)S(1)}, f32[512,32]{0,1:T(8,128)}, u32[]{:S(2)}) copy-start(f32[512,32]{0,1:T(8,128)} %copy-done.7) | copy-start | bytes 196612
  54.1 2.5 %copy-start.4 = (bf16[256,1536]{1,0:T(8,128)(2,1)S(1)}, bf16[256,1536]{1,0:T(8,128)(2,1)}, u32[]{:S(2)}) copy-start(bf16[256,1536]{1,0:T(8,128)(2,1)} %copy.65) | copy-start | bytes 2359300
  56.6 2.2 %copy-start.2 = (f32[512,32]{1,0:T(8,128)S(1)}, f32[512,32]{1,0:T(8,128)}, u32[]{:S(2)}) copy-start(f32[512,32]{1,0:T(8,128)} %copy.53) | copy-start | bytes 196612
  56.6 2.2 %copy-start.3 = (f32[512,32]{1,0:T(8,128)S(1)}, f32[512,32]{1,0:T(8,128)}, u32[]{:S(2)}) copy-start(f32[512,32]{1,0:T(8,128)} %copy.51) | copy-start | bytes 196612
Sparse Core Ops, SparseCore 0:
  10.5 39.7 all-gather.1
  91.8 35.2 reduce-scatter.1

commit v7 on v4

--- a/solution.py
+++ b/solution.py
@@ -43,7 +43,7 @@
 
 def attention_kernel(length_ref, q_ref, k_ref, v_ref, out_ref, *, tile, scale):
     tile_index = pl.program_id(1)
-    span = k_ref.shape[1]
+    span = k_ref.shape[2]
     keys = k_ref[0]
     values = v_ref[0]
     token = lax.broadcasted_iota(jnp.int32, (tile, span), 0) + tile_index * tile
@@ -51,12 +51,7 @@
     visible = slot <= length_ref[0] + token
     for group_index in range(q_ref.shape[1]):
         scores = (
-            lax.dot_general(
-                q_ref[0, group_index],
-                keys,
-                (((1,), (1,)), ((), ())),
-                preferred_element_type=jnp.float32,
-            )
+            jnp.dot(q_ref[0, group_index], keys, preferred_element_type=jnp.float32)
             * scale
         )
         row_max = jnp.max(jnp.where(visible, scores, -jnp.inf), axis=-1, keepdims=True)
@@ -68,9 +63,9 @@
         out_ref[0, group_index] = (mixed / row_total).astype(out_ref.dtype)
 
 
-def attend(length, queries, keys, values, tile=128):
+def attend(length, queries, keys_t, values, tile=256):
     heads, group, tokens, width = queries.shape
-    span = keys.shape[1]
+    span = keys_t.shape[2]
     kernel = functools.partial(attention_kernel, tile=tile, scale=HD ** (-0.5))
     flops = 4 * heads * group * tokens * span * width
     return pl.pallas_call(
@@ -81,7 +76,7 @@
             grid=(heads, tokens // tile),
             in_specs=[
                 pl.BlockSpec((1, group, tile, width), lambda h, i, n: (h, 0, i, 0)),
-                pl.BlockSpec((1, span, width), lambda h, i, n: (h, 0, 0)),
+                pl.BlockSpec((1, width, span), lambda h, i, n: (h, 0, 0)),
                 pl.BlockSpec((1, span, width), lambda h, i, n: (h, 0, 0)),
             ],
             out_specs=pl.BlockSpec((1, group, tile, width), lambda h, i, n: (h, 0, i, 0)),
@@ -89,9 +84,9 @@
         cost_estimate=pl.CostEstimate(
             flops=flops,
             transcendentals=heads * group * tokens * span,
-            bytes_accessed=2 * (2 * queries.size + keys.size + values.size),
+            bytes_accessed=2 * (2 * queries.size + keys_t.size + values.size),
         ),
-    )(length, queries, keys, values)
+    )(length, queries, keys_t, values)
 
 
 def local(tokens, norm_gain, lengths, w_query, w_keyval, w_out, kv_cache, prior_kv, owners):
@@ -162,7 +157,10 @@
         queries.reshape(NEW_TOK, heads_here, group_size, HD), (1, 2, 0, 3)
     )
     attended = attend(
-        req_length.reshape(1), grouped, assembled[:, :, :HD], assembled[:, :, HD:]
+        req_length.reshape(1),
+        grouped,
+        jnp.transpose(assembled[:, :, :HD], (0, 2, 1)),
+        assembled[:, :, HD:],
     )
     context = jnp.transpose(attended, (2, 0, 1, 3)).reshape(NEW_TOK, query_cols)
     product = jnp.dot(context, w_out, preferred_element_type=jnp.float32)

time: 129 us -> 130 us (level)
  Pallas kernels: 20 us -> 16.9 us
  local copies, waits for them, and re-layouts: 17.2 us -> 18.6 us
  other arithmetic: 11 us -> 12.4 us
    pallas_call x1, Pallas kernels: 20 us -> 16.9 us  [attend(): pl.pallas_call(kernel, out_shape=jax.ShapeDtypeStruct(queries.shape, jnp....]
    transpose x1, other arithmetic: 1.31 us -> 2.68 us  [local(): jnp.transpose(queries.reshape(NEW_TOK, heads_here, group_size, HD), (1, 2...]
    unnamed x17 -> x25, local copies, waits for them, and re-layouts: 3.27 us -> 3.29 us
where the time goes in v7:
time: 130 us; the launch traced here: 129 us
  waiting for transfers between devices  29.8 us (23%)
  local copies, waits for them, and re-layouts  18.6 us (14%)
  blocking collectives  18 us (14%)
  Pallas kernels  16.9 us (13%)
  between operations  16.9 us (13%)
  other arithmetic  12.4 us (10%)
  matrix products  10.8 us (8%)
  starting transfers between devices  5.56 us (4%)
    all_to_all x1, blocking collectives, local(): lax.all_to_all(route_blocks(dispatch[layer_count - 1:], current_rows), 's...  18 us
    all_to_all x1, waiting for transfers between devices, local(): lax.all_to_all(route_blocks(dispatch[:layer_count - 1], earlier_rows), 's...  16.9 us
    pallas_call x1, Pallas kernels, attend(): pl.pallas_call(kernel, out_shape=jax.ShapeDtypeStruct(queries.shape, jnp....  16.9 us
    reduce_scatter x1, waiting for transfers between devices, local(): lax.psum_scatter(product.reshape(NEW_TOK // lax.axis_size('dec') * lax.ax...  12.8 us
    all_to_all x1, starting transfers between devices, local(): lax.all_to_all(route_blocks(dispatch[:layer_count - 1], earlier_rows), 's...  5.3 us
    dot_general x2, matrix products, route_blocks(): jnp.einsum('locms,msbw->olcbw', spread, block_data, preferred_element_typ...  4.31 us
    unnamed x25, local copies, waits for them, and re-layouts  3.29 us
    convert_element_type x2, local copies, waits for them, and re-layouts, route_blocks(): moved_blocks = jnp.einsum('locms,msbw->olcbw', spread, block_data, prefer...  3.08 us
  transfers between devices with their start and end apart: 3, of which 2 were waited for; matrix products, arithmetic and copies ran while one was open for 17% of the time, Pallas kernels for 0%

profile of v7, /device:TPU:0, one launch (start us, length us, event | category | flops | bytes accessed | tf_op | source)
XLA Modules:
  0.0 129.0 jit_solution(4758265421699709036)
XLA Ops:
  7.2 0.0 copy-start
  7.2 0.0 all-gather.2.cloned.1.call-start
  7.2 1.2 fusion.13
  8.5 1.9 %fusion.15 = bf16[128,1,1536]{2,0,1:T(8,128)(2,1)} fusion(bf16[128,1,1536]{2,0,1:T(8,128)(2,1)} %param.9, f32[1536]{0:T(1024)} %param.10, f32[128]{0:T(128)S(1)} %add_rsqrt_fusion), kind=kLoop, calls=%fused_computation.22 | loop fusion | flops 786432 | bytes 793088 | tf_op jit(solution)/shard_map/convert_element_type | solution.py:127
  10.4 0.0 all-gather.2.cloned.1.call-update
  10.4 0.5 broadcast.87
  10.9 0.7 reduce.4
  11.6 0.1 reshape_squeeze.3
  11.7 0.1 fusion.16
  11.8 0.1 reduce_window_sum.11
  11.9 0.2 select_reduce_fusion
  12.1 0.6 dynamic_slice.3.length_ref
  13.4 0.1 copy.42
  13.6 3.6 %fusion.3 = bf16[8,2,4,128,128]{4,0,2,1,3:T(8,128)(2,1)S(1)} fusion(bf16[2,32,128,128]{3,2,1,0:T(8,128)(2,1)} %bitcast.83, pred[32,128]{0,1:T(8,128)(4,1)S(1)} %copy.42, bf16[2,2]{1,0:T(2,128)(2,1)S(1)} %compare_convert_fusion, bf16[2,8,4,32]{3,1,2,0:T(8,128)(2,1)S(1)} %copy.44), kind=kOutput, calls=%fused_computation.7 | convolution fusion | flops 136331264 | bytes 4202504 | tf_op jit(solution)/shard_map/locms,msbw->olcbw/dot_general | solution.py:37
  17.1 2.7 %copy.45 = bf16[8,2,4,128,128]{4,3,2,1,0:T(8,128)(2,1)} copy(bf16[8,2,4,128,128]{4,0,2,1,3:T(8,128)(2,1)S(1)} %fusion.3) | data formatting | bytes 4194304 | tf_op jit(solution)/shard_map/convert_element_type | solution.py:39
  19.8 5.3 %all-to-all-start = ((bf16[8,1024,128]{2,1,0:T(8,128)(2,1)}), bf16[8,1024,128]{2,1,0:T(8,128)(2,1)}, u32[]{:S(2)}, u32[]{:S(2)}) async-start(bf16[8,1024,128]{2,1,0:T(8,128)(2,1)} %bitcast.10), calls=%async_computation | async-start | bytes 4194304 | tf_op jit(solution)/shard_map/all_to_all | solution.py:119
  25.1 0.2 reduce-scatter.2.cloned.1.call-start
  26.0 0.6 copy.46
  26.6 2.3 %copy.65 = bf16[256,1536]{1,0:T(8,128)(2,1)} copy(bf16[256,1536]{0,1:T(8,128)(2,1)} %bitcast.76) | data formatting | bytes 1572864 | tf_op jit(solution)/shard_map/dot_general | solution.py:134
  28.9 0.6 add_convert_fusion.2
  29.6 0.3 multiply_cosine_fusion
  29.9 0.8 copy.53
  30.7 0.8 copy.51
  32.8 0.6 iota_compare_fusion.2
  33.5 1.4 %pad_select_fusion = bf16[2,2048,128]{2,1,0:T(8,128)(2,1)S(1)} fusion(bf16[2,1536,128]{2,1,0:T(8,128)(2,1)} %bitcast.77, pred[2048]{0:T(1024)(128)(4,1)S(1)} %iota_compare_fusion.2), kind=kLoop, calls=%fused_computation.16 | loop fusion | flops 524288 | bytes 1837056 | tf_op jit(solution)/shard_map/jit(_where)/select_n | solution.py:150
  34.9 16.9 %all-to-all-done = bf16[8,1024,128]{2,1,0:T(8,128)(2,1)} async-done(((bf16[8,1024,128]{2,1,0:T(8,128)(2,1)}), bf16[8,1024,128]{2,1,0:T(8,128)(2,1)}, u32[]{:S(2)}, u32[]{:S(2)}) %all-to-all-start) | async-done | bytes 2097184 | tf_op jit(solution)/shard_map/all_to_all | solution.py:119
  51.9 2.2 %fusion.8 = f32[512,6,64]{0,2,1:T(8,128)S(1)} fusion(bf16[6,64,1536]{2,1,0:T(8,128)(2,1)S(1)} %bitcast.75, bf16[512,1,1536]{2,0,1:T(8,128)(2,1)} %all-gather.2.cloned.1.call-done), kind=kOutput, calls=%fused_computation.10 | convolution fusion | flops 603979776 | bytes 3538944 | tf_op jit(solution)/shard_map/dot_general | solution.py:133
  54.1 0.1 subtract_convert_fusion.1
  54.3 1.2 copy.48
  55.4 1.2 copy.47
  56.6 2.1 %fusion.6 = f32[512,2,128]{2,0,1:T(8,128)S(1)} fusion(bf16[2,128,1536]{2,1,0:T(8,128)(2,1)S(1)} %bitcast.78, bf16[512,1,1536]{2,0,1:T(8,128)(2,1)} %all-gather.2.cloned.1.call-done), kind=kOutput, calls=%fused_computation.8 | convolution fusion | flops 402653184 | bytes 2883584 | tf_op jit(solution)/shard_map/dot_general | solution.py:134
  58.7 0.1 slice.63
  58.8 0.2 subtract_convert_fusion
  59.1 0.3 maximum_bitcast_fusion.2
  59.4 1.2 dynamic_update_slice.3
  60.5 1.4 %fusion.24 = (bf16[2,2048,64]{2,1,0:T(8,128)(2,1)}, bf16[2,64,2048]{1,2,0:T(8,128)(2,1)S(1)}) fusion(bf16[2,2048,128]{2,1,0:T(8,128)(2,1)S(1)} %dynamic_update_slice.3), kind=kLoop, calls=%fused_computation.51 | loop fusion | bytes 2097152 | tf_op jit(solution)/shard_map/slice | solution.py:163
  61.9 1.1 copy.55.k_ref
  63.0 2.7 %maximum_bitcast_fusion.1.q_ref = bf16[2,3,512,64]{3,2,1,0:T(8,128)(2,1)} fusion(bf16[512,2,3,32]{3,0,2,1:T(8,128)(2,1)} %bitcast.72, bf16[512,2,3,32]{3,0,2,1:T(8,128)(2,1)} %bitcast.73), kind=kLoop, calls=%fused_computation.23 | loop fusion | flops 786432 | bytes 786432 | tf_op jit(solution)/shard_map/transpose | solution.py:156
  65.7 16.9 %shard_map.104 = bf16[2,3,512,64]{3,2,1,0:T(8,128)(2,1)} custom-call(s32[1]{0:T(128)} %dynamic_slice.3.length_ref, bf16[2,3,512,64]{3,2,1,0:T(8,128)(2,1)} %maximum_bitcast_fusion.1.q_ref, bf16[2,64,2048]{2,1,0:T(8,128)(2,1)} %copy.55.k_ref, bf16[2,2048,64]{2,1,0:T(8,128)(2,1)} %get-tuple-element.10.v_ref), custom_call_target="tpu_custom_call" | custom-call | flops 1610612736 | bytes 1835008 | tf_op jit(solution)/shard_map/pallas_call | solution.py:71
  82.6 1.4 %copy.56 = bf16[512,2,3,64]{0,3,2,1:T(8,128)(2,1)S(1)} copy(bf16[512,2,3,64]{3,0,2,1:T(8,128)(2,1)} %bitcast.79) | data formatting | bytes 786432 | tf_op jit(solution)/shard_map/transpose | solution.py:165
  84.0 2.1 %fusion = bf16[512,1,1536]{2,0,1:T(8,128)(2,1)} fusion(bf16[512,384]{0,1:T(8,128)(2,1)S(1)} %bitcast.74, bf16[384,1536]{1,0:T(8,128)(2,1)S(1)} %copy-done), kind=kOutput, calls=%fused_computation.3 | convolution fusion | flops 604766208 | bytes 3145728 | tf_op jit(solution)/shard_map/dot_general | solution.py:166
  86.1 0.0 reduce-scatter.2.cloned.1.call-update
  86.2 0.8 fusion.10
  86.9 0.4 copy.59
  87.3 18.0 %all_to_all.10 = bf16[8,512,128]{2,1,0:T(8,128)(2,1)S(1)} all-to-all(bf16[8,512,128]{2,1,0:T(8,128)(2,1)S(1)} %bitcast.70), channel_id=1, replica_groups=mesh['seq'=8,'dec'=4] {'seq'}, dimensions={0} | all-to-all | bytes 2097152 | tf_op jit(solution)/shard_map/all_to_all | solution.py:176
  105.3 1.9 %maximum_bitcast_fusion = bf16[1,1,3,8,4,128,128]{6,5,4,2,3,1,0:T(8,128)(2,1)S(1)} fusion(bf16[8,1,4,128,128]{4,3,2,1,0:T(8,128)(2,1)S(1)} %bitcast.71, bf16[8,2,4,128,128]{4,3,2,1,0:T(8,128)(2,1)} %bitcast.26), kind=kLoop, calls=%fused_computation.1 | loop fusion | flops 1572864 | bytes 6291456 | tf_op jit(solution)/shard_map/reshape | solution.py:186
  107.2 2.1 %copy.60 = bf16[1,1,3,8,4,128,128]{6,5,4,3,2,1,0:T(8,128)(2,1)} copy(bf16[1,1,3,8,4,128,128]{6,5,4,2,3,1,0:T(8,128)(2,1)S(1)} %maximum_bitcast_fusion) | data formatting | bytes 6291456
  109.3 12.8 %reduce-scatter.2.cloned.1.call-done = bf16[128,1,1536]{2,0,1:T(8,128)(2,1)} async-done(((bf16[512,1,1536]{2,0,1:T(8,128)(2,1)}), bf16[128,1,1536]{2,0,1:T(8,128)(2,1)}) %reduce-scatter.2.cloned.1.call-update) | async-done | bytes 393232 | tf_op jit(solution)/shard_map/reduce_scatter | solution.py:167
  (32 shorter events, 0.1 us)
Async XLA Ops:
  7.2 76.8 %copy-start = (bf16[384,1536]{1,0:T(8,128)(2,1)S(1)}, bf16[384,1536]{1,0:T(8,128)(2,1)}, u32[]{:S(2)}) copy-start(bf16[384,1536]{1,0:T(8,128)(2,1)} %param.14) | copy-start | bytes 3538948
  7.2 3.8 %copy-start.9 = (s32[1,3,2,16,1]{3,4,2,1,0:T(1,128)S(1)}, s32[1,3,2,16,1]{3,4,2,1,0:T(1,128)}, u32[]{:S(2)}) copy-start(s32[1,3,2,16,1]{3,4,2,1,0:T(1,128)} %param.17) | copy-start | bytes 1156
  7.2 4.9 %copy-start.10 = (s32[8]{0:T(128)S(1)}, s32[8]{0:T(128)}, u32[]{:S(2)}) copy-start(s32[8]{0:T(128)} %param.11) | copy-start | bytes 100
  7.2 44.6 %all-gather.2.cloned.1.call-start = ((), (), s32[]{:S(2)}) async-start(), calls=%async_computation.3 | async-start | bytes 1966080 | tf_op jit(solution)/shard_map/all_gather | solution.py:128
  19.8 6.2 %copy-start.1 = (bf16[1536,384]{1,0:T(8,128)(2,1)S(1)}, bf16[1536,384]{1,0:T(8,128)(2,1)}, u32[]{:S(2)}) copy-start(bf16[1536,384]{1,0:T(8,128)(2,1)} %param.12) | copy-start | bytes 3538948
  19.8 32.1 %all-to-all-start = ((bf16[8,1024,128]{2,1,0:T(8,128)(2,1)}), bf16[8,1024,128]{2,1,0:T(8,128)(2,1)}, u32[]{:S(2)}, u32[]{:S(2)}) async-start(bf16[8,1024,128]{2,1,0:T(8,128)(2,1)} %bitcast.10), calls=%async_computation | async-start | bytes 4194304 | tf_op jit(solution)/shard_map/all_to_all | solution.py:119
  25.1 97.0 %reduce-scatter.2.cloned.1.call-start = ((), (), s32[]{:S(2)}) async-start(), calls=%async_computation.4 | async-start | bytes 1966080 | tf_op jit(solution)/shard_map/reduce_scatter | solution.py:167
  29.9 3.6 %copy-start.5 = (f32[512,32]{0,1:T(8,128)}, f32[512,32]{0,1:T(8,128)S(1)}, u32[]{:S(2)}) copy-start(f32[512,32]{0,1:T(8,128)S(1)} %get-tuple-element.16) | copy-start | bytes 196612
  29.9 3.6 %copy-start.7 = (f32[512,32]{0,1:T(8,128)}, f32[512,32]{0,1:T(8,128)S(1)}, u32[]{:S(2)}) copy-start(f32[512,32]{0,1:T(8,128)S(1)} %get-tuple-element.17) | copy-start | bytes 196612
  51.8 2.3 %copy-start.6 = (f32[512,32]{0,1:T(8,128)S(1)}, f32[512,32]{0,1:T(8,128)}, u32[]{:S(2)}) copy-start(f32[512,32]{0,1:T(8,128)} %copy-done.5) | copy-start | bytes 196612
  51.8 2.3 %copy-start.8 = (f32[512,32]{0,1:T(8,128)S(1)}, f32[512,32]{0,1:T(8,128)}, u32[]{:S(2)}) copy-start(f32[512,32]{0,1:T(8,128)} %copy-done.7) | copy-start | bytes 196612
  54.1 2.5 %copy-start.4 = (bf16[256,1536]{1,0:T(8,128)(2,1)S(1)}, bf16[256,1536]{1,0:T(8,128)(2,1)}, u32[]{:S(2)}) copy-start(bf16[256,1536]{1,0:T(8,128)(2,1)} %copy.65) | copy-start | bytes 2359300
  56.6 2.2 %copy-start.2 = (f32[512,32]{1,0:T(8,128)S(1)}, f32[512,32]{1,0:T(8,128)}, u32[]{:S(2)}) copy-start(f32[512,32]{1,0:T(8,128)} %copy.53) | copy-start | bytes 196612
  56.6 2.2 %copy-start.3 = (f32[512,32]{1,0:T(8,128)S(1)}, f32[512,32]{1,0:T(8,128)}, u32[]{:S(2)}) copy-start(f32[512,32]{1,0:T(8,128)} %copy.51) | copy-start | bytes 196612
Sparse Core Ops, SparseCore 0:
  10.5 39.7 all-gather.1
  86.3 35.8 reduce-scatter.1

commit v8 on v7

--- a/solution.py
+++ b/solution.py
@@ -41,52 +41,118 @@
     return moved_blocks.reshape(shape[0], shape[1] * shape[2] * shape[3], shape[4])
 
 
-def attention_kernel(length_ref, q_ref, k_ref, v_ref, out_ref, *, tile, scale):
-    tile_index = pl.program_id(1)
-    span = k_ref.shape[2]
-    keys = k_ref[0]
-    values = v_ref[0]
+def swap_halves(values, half):
+    lane = lax.broadcasted_iota(jnp.int32, values.shape, 1)
+    width = values.shape[1]
+    wanted = jnp.where((lane % (2 * half)) < half, lane + half, lane - half)
+    ahead = pltpu.roll(values, half, 1)
+    behind = pltpu.roll(values, width - half, 1)
+    ahead_lane = pltpu.roll(lane, half, 1)
+    return jnp.where(ahead_lane == wanted, ahead, behind)
+
+
+def project_kernel(x_ref, wq_ref, wkv_ref, cq_ref, sq_ref, ckv_ref, skv_ref, q_out, kv_out):
+    x = x_ref[...]
+    query = jnp.dot(x, wq_ref[...], preferred_element_type=jnp.float32)
+    q_out[...] = (query * cq_ref[...] + swap_halves(query, HD // 2) * sq_ref[...]).astype(
+        q_out.dtype
+    )
+    key_value = jnp.dot(x, wkv_ref[...], preferred_element_type=jnp.float32)
+    rotated = (
+        key_value * ckv_ref[...] + swap_halves(key_value, HD // 2) * skv_ref[...]
+    ).astype(kv_out.dtype)
+    width = kv_out.shape[2]
+    for head_index in range(kv_out.shape[0]):
+        kv_out[head_index] = rotated[:, head_index * width : (head_index + 1) * width]
+
+
+def project(x, w_query, w_keyval, cos_q, sin_q, cos_kv, sin_kv, tile=256):
+    tokens, depth = x.shape
+    q_cols, kv_cols = w_query.shape[1], w_keyval.shape[1]
+    heads = kv_cols // (2 * HD)
+    row_spec = lambda cols: pl.BlockSpec((tile, cols), lambda i: (i, 0))
+    return pl.pallas_call(
+        project_kernel,
+        out_shape=(
+            jax.ShapeDtypeStruct((tokens, q_cols), jnp.bfloat16),
+            jax.ShapeDtypeStruct((heads, tokens, 2 * HD), jnp.bfloat16),
+        ),
+        grid=(tokens // tile,),
+        in_specs=[
+            row_spec(depth),
+            pl.BlockSpec((depth, q_cols), lambda i: (0, 0)),
+            pl.BlockSpec((depth, kv_cols), lambda i: (0, 0)),
+            row_spec(q_cols),
+            row_spec(q_cols),
+            row_spec(kv_cols),
+            row_spec(kv_cols),
+        ],
+        out_specs=(
+            row_spec(q_cols),
+            pl.BlockSpec((heads, tile, 2 * HD), lambda i: (0, i, 0)),
+        ),
+        cost_estimate=pl.CostEstimate(
+            flops=2 * tokens * depth * (q_cols + kv_cols),
+            transcendentals=0,
+            bytes_accessed=2 * (x.size + w_query.size + w_keyval.size)
+            + 8 * tokens * (q_cols + kv_cols),
+        ),
+    )(x, w_query, w_keyval, cos_q, sin_q, cos_kv, sin_kv)
+
+
+def attention_kernel(length_ref, q_ref, kt_ref, kv_ref, out_ref, *, tile, scale, group):
+    tile_index = pl.program_id(0)
+    span = kt_ref.shape[2]
+    pair = 2 * HD
     token = lax.broadcasted_iota(jnp.int32, (tile, span), 0) + tile_index * tile
     slot = lax.broadcasted_iota(jnp.int32, (tile, span), 1)
     visible = slot <= length_ref[0] + token
-    for group_index in range(q_ref.shape[1]):
-        scores = (
-            jnp.dot(q_ref[0, group_index], keys, preferred_element_type=jnp.float32)
-            * scale
-        )
-        row_max = jnp.max(jnp.where(visible, scores, -jnp.inf), axis=-1, keepdims=True)
-        weights = jnp.where(visible, jnp.exp(scores - row_max), 0.0)
-        row_total = jnp.sum(weights, axis=-1, keepdims=True)
-        mixed = jnp.dot(
-            weights.astype(jnp.bfloat16), values, preferred_element_type=jnp.float32
-        )
-        out_ref[0, group_index] = (mixed / row_total).astype(out_ref.dtype)
-
-
-def attend(length, queries, keys_t, values, tile=256):
-    heads, group, tokens, width = queries.shape
-    span = keys_t.shape[2]
-    kernel = functools.partial(attention_kernel, tile=tile, scale=HD ** (-0.5))
-    flops = 4 * heads * group * tokens * span * width
+    lane = lax.broadcasted_iota(jnp.int32, (tile, pair), 1)
+    for pair_index in range(q_ref.shape[1] // pair):
+        both = q_ref[:, pair_index * pair : (pair_index + 1) * pair]
+        halves = []
+        for parity in range(2):
+            head = (2 * pair_index + parity) // group
+            lined = both if parity == 0 else pltpu.roll(both, HD, 1)
+            scores = (
+                jnp.dot(lined[:, :HD], kt_ref[head], preferred_element_type=jnp.float32) * scale
+            )
+            row_max = jnp.max(jnp.where(visible, scores, -jnp.inf), axis=-1, keepdims=True)
+            weights = jnp.where(visible, jnp.exp(scores - row_max), 0.0)
+            row_total = jnp.sum(weights, axis=-1, keepdims=True)
+            mixed = jnp.dot(
+                weights.astype(jnp.bfloat16), kv_ref[head], preferred_element_type=jnp.float32
+            )
+            halves.append((mixed, row_total))
+        (even, even_total), (odd, odd_total) = halves
+        joined = jnp.where(lane < HD, pltpu.roll(even, HD, 1) / even_total, odd / odd_total)
+        out_ref[:, pair_index * pair : (pair_index + 1) * pair] = joined.astype(out_ref.dtype)
+
+
+def attend(length, queries, keys_t, assembled, group, tile=256):
+    tokens, q_cols = queries.shape
+    heads, span = assembled.shape[0], assembled.shape[1]
+    kernel = functools.partial(attention_kernel, tile=tile, scale=HD ** (-0.5), group=group)
+    flops = 4 * tokens * q_cols * span
     return pl.pallas_call(
         kernel,
         out_shape=jax.ShapeDtypeStruct(queries.shape, jnp.bfloat16),
         grid_spec=pltpu.PrefetchScalarGridSpec(
             num_scalar_prefetch=1,
-            grid=(heads, tokens // tile),
+            grid=(tokens // tile,),
             in_specs=[
-                pl.BlockSpec((1, group, tile, width), lambda h, i, n: (h, 0, i, 0)),
-                pl.BlockSpec((1, width, span), lambda h, i, n: (h, 0, 0)),
-                pl.BlockSpec((1, span, width), lambda h, i, n: (h, 0, 0)),
+                pl.BlockSpec((tile, q_cols), lambda i, n: (i, 0)),
+                pl.BlockSpec(keys_t.shape, lambda i, n: (0, 0, 0)),
+                pl.BlockSpec(assembled.shape, lambda i, n: (0, 0, 0)),
             ],
-            out_specs=pl.BlockSpec((1, group, tile, width), lambda h, i, n: (h, 0, i, 0)),
+            out_specs=pl.BlockSpec((tile, q_cols), lambda i, n: (i, 0)),
         ),
         cost_estimate=pl.CostEstimate(
             flops=flops,
-            transcendentals=heads * group * tokens * span,
-            bytes_accessed=2 * (2 * queries.size + keys_t.size + values.size),
-        ),
-    )(length, queries, keys_t, values)
+            transcendentals=tokens * (q_cols // HD) * span,
+            bytes_accessed=2 * (2 * queries.size + keys_t.size + assembled.size),
+        ),
+    )(length, queries, keys_t, assembled)
 
 
 def local(tokens, norm_gain, lengths, w_query, w_keyval, w_out, kv_cache, prior_kv, owners):
@@ -128,41 +194,33 @@
     portion = lax.all_gather(normed, "dec", axis=0, tiled=True)
     received_early, portion = lax.optimization_barrier((received_early, portion))
     flattened = portion.reshape(-1, portion.shape[-1])
-    combined = jnp.concatenate(
-        [
-            jnp.dot(flattened, w_query, preferred_element_type=jnp.float32),
-            jnp.dot(flattened, w_keyval, preferred_element_type=jnp.float32),
-        ],
-        axis=-1,
-    )
     positions = (jnp.arange(NEW_TOK, dtype=jnp.int32) + req_length).astype(jnp.float32)
     inverse_freq = ROPE_BASE ** (-(jnp.arange(0, HD, 2, dtype=jnp.float32) / HD))
-    angles = positions[:, None, None] * inverse_freq
-    queries = rotate(
-        combined[:, :query_cols].reshape(NEW_TOK, query_cols // HD, HD), angles
-    ).astype(jnp.bfloat16)
-    key_value = combined[:, query_cols:].reshape(NEW_TOK, heads_here, kv_width)
-    key_value = jnp.concatenate(
-        [rotate(key_value[..., :HD], angles), key_value[..., HD:]], axis=-1
-    ).astype(jnp.bfloat16)
+    angles = positions[:, None] * inverse_freq
+    cosine, sine = jnp.cos(angles), jnp.sin(angles)
+    signed_sine = jnp.concatenate([-sine, sine], axis=-1)
+    head_cos = jnp.concatenate([cosine, cosine], axis=-1)
+    cos_q = jnp.tile(head_cos, (1, query_cols // HD))
+    sin_q = jnp.tile(signed_sine, (1, query_cols // HD))
+    cos_kv = jnp.tile(jnp.concatenate([head_cos, jnp.ones_like(head_cos)], axis=-1), (1, heads_here))
+    sin_kv = jnp.tile(
+        jnp.concatenate([signed_sine, jnp.zeros_like(signed_sine)], axis=-1), (1, heads_here)
+    )
+    queries, fresh_rows = project(flattened, w_query, w_keyval, cos_q, sin_q, cos_kv, sin_kv)
     cached = kv_cache[0]
     padded = jnp.pad(cached, ((0, 0), (0, span_len - cached.shape[1]), (0, 0)))
     kept_cache = jnp.where((slot_ids < req_length)[None, :, None], padded, jnp.zeros_like(padded))
-    fresh_rows = jnp.transpose(key_value, (1, 0, 2))
     assembled = lax.dynamic_update_slice(
         kept_cache, fresh_rows, (zero_index, req_length, zero_index)
     )
     group_size = query_cols // HD // heads_here
-    grouped = jnp.transpose(
-        queries.reshape(NEW_TOK, heads_here, group_size, HD), (1, 2, 0, 3)
-    )
-    attended = attend(
+    context = attend(
         req_length.reshape(1),
-        grouped,
+        queries,
         jnp.transpose(assembled[:, :, :HD], (0, 2, 1)),
-        assembled[:, :, HD:],
-    )
-    context = jnp.transpose(attended, (2, 0, 1, 3)).reshape(NEW_TOK, query_cols)
+        assembled,
+        group_size,
+    )
     product = jnp.dot(context, w_out, preferred_element_type=jnp.float32)
     summed = lax.psum_scatter(
         product.reshape(

time: 130 us -> 124 us (0.954)
  Pallas kernels: 16.9 us -> 20.9 us
  local copies, waits for them, and re-layouts: 18.6 us -> 15.3 us
  matrix products: 10.8 us -> 7.52 us
  other arithmetic: 12.4 us -> 9.34 us
    pallas_call x0 -> x1, Pallas kernels: none -> 5.01 us  [project(): pl.pallas_call(project_kernel, out_shape=(jax.ShapeDtypeStruct((tokens, q...]
    dot_general x2 -> x0, matrix products: 4.3 us -> none  [the longest x1 2.24 us: local(): jnp.dot(flattened, w_query, preferred_element_type=jnp.float32)]
    transpose x2 -> x0, other arithmetic: 2.94 us -> none  [the longest x1 2.68 us: local(): jnp.transpose(queries.reshape(NEW_TOK, heads_here, group_size, HD), (1, 2...]
    dot_general x1 -> x0, local copies, waits for them, and re-layouts: 2.29 us -> none  [local(): jnp.dot(flattened, w_keyval, preferred_element_type=jnp.float32)]
    another operation x2 -> x7, local copies, waits for them, and re-layouts: 2.35 us -> 3.93 us  [the longest x2 1.26 us: local(): jnp.tile(jnp.concatenate([signed_sine, jnp.zeros_like(signed_sine)], axis...]
    slice x2 -> x0, local copies, waits for them, and re-layouts: 1.49 us -> none  [the longest x1 1.35 us: local(): assembled[:, :, HD:]]
    transpose x1 -> x0, local copies, waits for them, and re-layouts: 1.39 us -> none  [local(): context = jnp.transpose(attended, (2, 0, 1, 3)).reshape(NEW_TOK, query_cols)]
    unnamed x25 -> x10, local copies, waits for them, and re-layouts: 3.29 us -> 2.62 us
  transfers between devices with their start and end apart: 3 -> 3, of which waited for: 2 -> 2; matrix products, arithmetic and copies ran while one was open for 17% -> 18% of each run, Pallas kernels for 0% -> 0%
where the time goes in v8:
time: 124 us; the launch traced here: 123 us
  waiting for transfers between devices  30.1 us (24%)
  Pallas kernels  20.9 us (17%)
  blocking collectives  17.8 us (14%)
  between operations  16.8 us (14%)
  local copies, waits for them, and re-layouts  15.3 us (12%)
  other arithmetic  9.34 us (8%)
  matrix products  7.52 us (6%)
  starting transfers between devices  5.24 us (4%)
    all_to_all x1, blocking collectives, local(): lax.all_to_all(route_blocks(dispatch[layer_count - 1:], current_rows), 's...  17.8 us
    all_to_all x1, waiting for transfers between devices, local(): lax.all_to_all(route_blocks(dispatch[:layer_count - 1], earlier_rows), 's...  17.6 us
    pallas_call x1, Pallas kernels, attend(): pl.pallas_call(kernel, out_shape=jax.ShapeDtypeStruct(queries.shape, jnp....  15.9 us
    reduce_scatter x1, waiting for transfers between devices, local(): lax.psum_scatter(product.reshape(NEW_TOK // lax.axis_size('dec') * lax.ax...  12.4 us
    all_to_all x1, starting transfers between devices, local(): lax.all_to_all(route_blocks(dispatch[:layer_count - 1], earlier_rows), 's...  5.17 us
    pallas_call x1, Pallas kernels, project(): pl.pallas_call(project_kernel, out_shape=(jax.ShapeDtypeStruct((tokens, q...  5.01 us
    dot_general x2, matrix products, route_blocks(): jnp.einsum('locms,msbw->olcbw', spread, block_data, preferred_element_typ...  4.31 us
    dot_general x1, matrix products, local(): product = jnp.dot(context, w_out, preferred_element_type=jnp.float32)  3.21 us
  transfers between devices with their start and end apart: 3, of which 2 were waited for; matrix products, arithmetic and copies ran while one was open for 18% of the time, Pallas kernels for 0%

profile of v8, /device:TPU:0, one launch (start us, length us, event | category | flops | bytes accessed | tf_op | source)
XLA Modules:
  0.0 123.0 jit_solution(4002116291497204560)
XLA Ops:
  7.2 0.0 all-gather.2.cloned.1.call-start
  7.2 1.2 %fusion.9 = f32[128]{0:T(128)S(1)} fusion(bf16[128,1,1536]{2,0,1:T(8,128)(2,1)} %param.9), kind=kLoop, calls=%fused_computation.16 | loop fusion | flops 589696 | bytes 393728 | tf_op jit(solution)/shard_map/reduce_sum | solution.py:191
  8.5 1.9 %fusion.11 = bf16[128,1,1536]{2,0,1:T(8,128)(2,1)} fusion(bf16[128,1,1536]{2,0,1:T(8,128)(2,1)} %param.9, f32[1536]{0:T(1024)} %param.10, f32[128]{0:T(128)S(1)} %add_rsqrt_fusion), kind=kLoop, calls=%fused_computation.18 | loop fusion | flops 786432 | bytes 793088 | tf_op jit(solution)/shard_map/convert_element_type | solution.py:193
  10.4 0.0 all-gather.2.cloned.1.call-update
  10.4 0.5 broadcast.73
  10.9 1.3 %reduce.4 = s32[3,2,16]{2,1,0:T(2,128)S(1)} reduce(s32[1,3,2,16,1]{3,4,2,1,0:T(1,128)} %param.17, s32[]{:T(128)} %broadcast.73), dimensions={0,4}, to_apply=%param.17.reduce_sub_computation.3 | reduce | bytes 772 | tf_op args[8]
  12.3 0.1 reshape_squeeze.3
  12.4 0.1 fusion.12
  12.4 0.1 reduce_window_sum.11
  12.5 0.2 select_reduce_fusion
  12.8 1.3 %dynamic_slice.3.length_ref = s32[1]{0:T(128)} dynamic-slice(s32[8]{0:T(128)} %param.11, s32[]{:T(128)S(6)} %select_n.15), dynamic_slice_sizes={1} | dynamic-slice | bytes 12 | tf_op jit(solution)/shard_map/dynamic_slice | solution.py:169
  14.8 0.1 copy.14
  14.9 3.6 %fusion.3 = bf16[8,2,4,128,128]{4,0,2,1,3:T(8,128)(2,1)S(1)} fusion(bf16[2,32,128,128]{3,2,1,0:T(8,128)(2,1)} %bitcast.69, pred[32,128]{0,1:T(8,128)(4,1)S(1)} %copy.14, bf16[2,2]{1,0:T(2,128)(2,1)S(1)} %compare_convert_fusion, bf16[2,8,4,32]{3,1,2,0:T(8,128)(2,1)S(1)} %copy.16), kind=kOutput, calls=%fused_computation.7 | convolution fusion | flops 136331264 | bytes 4202504 | tf_op jit(solution)/shard_map/locms,msbw->olcbw/dot_general | solution.py:37
  18.5 2.7 %copy.17 = bf16[8,2,4,128,128]{4,3,2,1,0:T(8,128)(2,1)} copy(bf16[8,2,4,128,128]{4,0,2,1,3:T(8,128)(2,1)S(1)} %fusion.3) | data formatting | bytes 4194304 | tf_op jit(solution)/shard_map/convert_element_type | solution.py:39
  21.1 5.2 %all-to-all-start = ((bf16[8,1024,128]{2,1,0:T(8,128)(2,1)}), bf16[8,1024,128]{2,1,0:T(8,128)(2,1)}, u32[]{:S(2)}, u32[]{:S(2)}) async-start(bf16[8,1024,128]{2,1,0:T(8,128)(2,1)} %bitcast.10), calls=%async_computation | async-start | bytes 4194304 | tf_op jit(solution)/shard_map/all_to_all | solution.py:185
  26.3 0.0 reduce-scatter.2.cloned.1.call-start
  27.0 0.6 add_convert_fusion
  27.6 0.3 fusion.15
  28.0 0.1 copy.21
  28.1 0.1 copy.20
  28.2 0.1 copy.18
  28.4 0.1 tile.16
  28.5 1.2 copy.22.cq_ref
  29.6 0.1 tile.18
  29.7 1.2 copy.23.sq_ref
  30.9 0.1 pad.9.clone
  31.0 0.1 pad.12.clone
  32.3 0.6 iota_compare_fusion.2
  33.0 0.1 maximum_maximum_fusion
  33.1 0.1 maximum_maximum_fusion.1
  33.3 0.2 tile.42
  33.5 0.2 tile.40
  33.6 1.1 copy_bitcast_fusion
  34.7 0.7 pad_select_fusion
  35.4 17.6 %all-to-all-done = bf16[8,1024,128]{2,1,0:T(8,128)(2,1)} async-done(((bf16[8,1024,128]{2,1,0:T(8,128)(2,1)}), bf16[8,1024,128]{2,1,0:T(8,128)(2,1)}, u32[]{:S(2)}, u32[]{:S(2)}) %all-to-all-start) | async-done | bytes 2097184 | tf_op jit(solution)/shard_map/all_to_all | solution.py:185
  53.1 5.0 %shard_map.104 = (bf16[512,384]{1,0:T(8,128)(2,1)}, bf16[2,512,128]{2,1,0:T(8,128)(2,1)}) custom-call(bf16[512,1536]{1,0:T(8,128)(2,1)} %bitcast.64, bf16[1536,384]{1,0:T(8,128)(2,1)} %wq_ref.1, bf16[1536,256]{1,0:T(8,128)(2,1)} %wkv_ref.1, f32[512,384]{1,0:T(8,128)} %copy.22.cq_ref, f32[512,384]{1,0:T(8,128)} %copy.23.sq_ref, ...), custom_call_target="tpu_custom_call" | custom-call | flops 1006632960 | bytes 6160384 | tf_op jit(solution)/shard_map/pallas_call | solution.py:74
  58.1 2.4 %dynamic_update_slice.3.kv_ref = bf16[2,2048,128]{2,1,0:T(8,128)(2,1)S(1)} dynamic-update-slice(bf16[2,2048,128]{2,1,0:T(8,128)(2,1)S(1)} %pad_select_fusion, bf16[2,512,128]{2,1,0:T(8,128)(2,1)} %get-tuple-element.8, s32[]{:T(128)} %constant.17.clone.1, s32[]{:T(128)S(6)} %select_n.18, s32[]{:T(128)} %constant.17.clone.1) | dynamic-update-slice | bytes 524292 | tf_op jit(solution)/shard_map/dynamic_update_slice | solution.py:213
  60.5 0.1 slice_bitcast_fusion
  60.5 1.2 copy.24.kt_ref
  61.7 15.9 %shard_map.105 = bf16[512,384]{1,0:T(8,128)(2,1)} custom-call(s32[1]{0:T(128)} %dynamic_slice.3.length_ref, bf16[512,384]{1,0:T(8,128)(2,1)} %get-tuple-element.7.q_ref, bf16[2,64,2048]{2,1,0:T(8,128)(2,1)} %copy.24.kt_ref, bf16[2,2048,128]{2,1,0:T(8,128)(2,1)} %copy-done.1), custom_call_target="tpu_custom_call" | custom-call | flops 1610612736 | bytes 2359296 | tf_op jit(solution)/shard_map/pallas_call | solution.py:137
  77.6 3.2 %fusion = bf16[512,1,1536]{2,0,1:T(8,128)(2,1)} fusion(bf16[512,384]{1,0:T(8,128)(2,1)} %shard_map.105, bf16[384,1536]{1,0:T(8,128)(2,1)S(1)} %copy-done), kind=kOutput, calls=%fused_computation.3 | convolution fusion | flops 604766208 | bytes 3145728 | tf_op jit(solution)/shard_map/dot_general | solution.py:224
  80.8 0.0 reduce-scatter.2.cloned.1.call-update
  80.8 0.8 fusion.6
  81.6 0.4 copy.27
  82.0 17.8 %all_to_all.10 = bf16[8,512,128]{2,1,0:T(8,128)(2,1)S(1)} all-to-all(bf16[8,512,128]{2,1,0:T(8,128)(2,1)S(1)} %bitcast.58), channel_id=1, replica_groups=mesh['seq'=8,'dec'=4] {'seq'}, dimensions={0} | all-to-all | bytes 2097152 | tf_op jit(solution)/shard_map/all_to_all | solution.py:234
  99.8 1.9 %maximum_bitcast_fusion = bf16[1,1,3,8,4,128,128]{6,5,4,2,3,1,0:T(8,128)(2,1)S(1)} fusion(bf16[8,1,4,128,128]{4,3,2,1,0:T(8,128)(2,1)S(1)} %bitcast.59, bf16[8,2,4,128,128]{4,3,2,1,0:T(8,128)(2,1)} %bitcast.17), kind=kLoop, calls=%fused_computation.1 | loop fusion | flops 1572864 | bytes 6291456 | tf_op jit(solution)/shard_map/reshape | solution.py:244
  101.7 2.1 %copy.28 = bf16[1,1,3,8,4,128,128]{6,5,4,3,2,1,0:T(8,128)(2,1)} copy(bf16[1,1,3,8,4,128,128]{6,5,4,2,3,1,0:T(8,128)(2,1)S(1)} %maximum_bitcast_fusion) | data formatting | bytes 6291456
  103.7 12.4 %reduce-scatter.2.cloned.1.call-done = bf16[128,1,1536]{2,0,1:T(8,128)(2,1)} async-done(((bf16[512,1,1536]{2,0,1:T(8,128)(2,1)}), bf16[128,1,1536]{2,0,1:T(8,128)(2,1)}) %reduce-scatter.2.cloned.1.call-update) | async-done | bytes 393232 | tf_op jit(solution)/shard_map/reduce_scatter | solution.py:225
  (22 shorter events, 0.1 us)
Async XLA Ops:
  7.2 70.4 %copy-start = (bf16[384,1536]{1,0:T(8,128)(2,1)S(1)}, bf16[384,1536]{1,0:T(8,128)(2,1)}, u32[]{:S(2)}) copy-start(bf16[384,1536]{1,0:T(8,128)(2,1)} %param.14) | copy-start | bytes 3538948
  7.2 45.9 %all-gather.2.cloned.1.call-start = ((), (), s32[]{:S(2)}) async-start(), calls=%async_computation.3 | async-start | bytes 1966080 | tf_op jit(solution)/shard_map/all_gather | solution.py:194
  21.1 31.9 %all-to-all-start = ((bf16[8,1024,128]{2,1,0:T(8,128)(2,1)}), bf16[8,1024,128]{2,1,0:T(8,128)(2,1)}, u32[]{:S(2)}, u32[]{:S(2)}) async-start(bf16[8,1024,128]{2,1,0:T(8,128)(2,1)} %bitcast.10), calls=%async_computation | async-start | bytes 4194304 | tf_op jit(solution)/shard_map/all_to_all | solution.py:185
  26.3 89.9 %reduce-scatter.2.cloned.1.call-start = ((), (), s32[]{:S(2)}) async-start(), calls=%async_computation.4 | async-start | bytes 1966080 | tf_op jit(solution)/shard_map/reduce_scatter | solution.py:225
  33.1 1.6 %copy-start.3 = (bf16[1,2,1536,128]{3,2,1,0:T(8,128)(2,1)S(1)}, bf16[1,2,1536,128]{3,2,1,0:T(8,128)(2,1)}, u32[]{:S(2)}) copy-start(bf16[1,2,1536,128]{3,2,1,0:T(8,128)(2,1)} %param.15) | copy-start | bytes 2359300
  60.4 1.2 %copy-start.1 = (bf16[2,2048,128]{2,1,0:T(8,128)(2,1)}, bf16[2,2048,128]{2,1,0:T(8,128)(2,1)S(1)}, u32[]{:S(2)}) copy-start(bf16[2,2048,128]{2,1,0:T(8,128)(2,1)S(1)} %dynamic_update_slice.3.kv_ref) | copy-start | bytes 3145732
  77.6 3.2 %copy-start.2 = (bf16[2,2048,128]{2,1,0:T(8,128)(2,1)S(1)}, bf16[2,2048,128]{2,1,0:T(8,128)(2,1)}, u32[]{:S(2)}) copy-start(bf16[2,2048,128]{2,1,0:T(8,128)(2,1)} %copy-done.1) | copy-start | bytes 3145732
Sparse Core Ops, SparseCore 0:
  10.5 39.7 all-gather.1
  80.9 35.1 reduce-scatter.1

commit v9 on v8

--- a/solution.py
+++ b/solution.py
@@ -100,7 +100,7 @@
     )(x, w_query, w_keyval, cos_q, sin_q, cos_kv, sin_kv)
 
 
-def attention_kernel(length_ref, q_ref, kt_ref, kv_ref, out_ref, *, tile, scale, group):
+def attention_kernel(length_ref, q_ref, kt_ref, kv_ref, wo_ref, out_ref, ctx_ref, *, tile, scale, group):
     tile_index = pl.program_id(0)
     span = kt_ref.shape[2]
     pair = 2 * HD
@@ -126,17 +126,21 @@
             halves.append((mixed, row_total))
         (even, even_total), (odd, odd_total) = halves
         joined = jnp.where(lane < HD, pltpu.roll(even, HD, 1) / even_total, odd / odd_total)
-        out_ref[:, pair_index * pair : (pair_index + 1) * pair] = joined.astype(out_ref.dtype)
-
-
-def attend(length, queries, keys_t, assembled, group, tile=256):
+        ctx_ref[:, pair_index * pair : (pair_index + 1) * pair] = joined.astype(ctx_ref.dtype)
+    out_ref[...] = jnp.dot(ctx_ref[...], wo_ref[...], preferred_element_type=jnp.float32).astype(
+        out_ref.dtype
+    )
+
+
+def attend(length, queries, keys_t, assembled, w_out, group, tile=256):
     tokens, q_cols = queries.shape
     heads, span = assembled.shape[0], assembled.shape[1]
+    model = w_out.shape[1]
     kernel = functools.partial(attention_kernel, tile=tile, scale=HD ** (-0.5), group=group)
-    flops = 4 * tokens * q_cols * span
+    flops = 4 * tokens * q_cols * span + 2 * tokens * q_cols * model
     return pl.pallas_call(
         kernel,
-        out_shape=jax.ShapeDtypeStruct(queries.shape, jnp.bfloat16),
+        out_shape=jax.ShapeDtypeStruct((tokens, model), jnp.bfloat16),
         grid_spec=pltpu.PrefetchScalarGridSpec(
             num_scalar_prefetch=1,
             grid=(tokens // tile,),
@@ -144,15 +148,34 @@
                 pl.BlockSpec((tile, q_cols), lambda i, n: (i, 0)),
                 pl.BlockSpec(keys_t.shape, lambda i, n: (0, 0, 0)),
                 pl.BlockSpec(assembled.shape, lambda i, n: (0, 0, 0)),
+                pl.BlockSpec(w_out.shape, lambda i, n: (0, 0)),
             ],
-            out_specs=pl.BlockSpec((tile, q_cols), lambda i, n: (i, 0)),
+            out_specs=pl.BlockSpec((tile, model), lambda i, n: (i, 0)),
+            scratch_shapes=[pltpu.VMEM((tile, q_cols), jnp.bfloat16)],
         ),
         cost_estimate=pl.CostEstimate(
             flops=flops,
             transcendentals=tokens * (q_cols // HD) * span,
-            bytes_accessed=2 * (2 * queries.size + keys_t.size + assembled.size),
-        ),
-    )(length, queries, keys_t, assembled)
+            bytes_accessed=2 * (queries.size + keys_t.size + assembled.size + w_out.size)
+            + 2 * tokens * model,
+        ),
+    )(length, queries, keys_t, assembled, w_out)
+
+
+def norm_kernel(x_ref, gain_ref, out_ref):
+    widened = x_ref[...].astype(jnp.float32)
+    scale = lax.rsqrt(jnp.mean(widened * widened, axis=-1, keepdims=True) + EPSILON)
+    out_ref[...] = (widened * scale * gain_ref[...]).astype(out_ref.dtype)
+
+
+def rms_norm(x, gain):
+    return pl.pallas_call(
+        norm_kernel,
+        out_shape=jax.ShapeDtypeStruct(x.shape, jnp.bfloat16),
+        cost_estimate=pl.CostEstimate(
+            flops=4 * x.size, transcendentals=x.shape[0], bytes_accessed=4 * x.size
+        ),
+    )(x, gain.reshape(1, -1))
 
 
 def local(tokens, norm_gain, lengths, w_query, w_keyval, w_out, kv_cache, prior_kv, owners):
@@ -185,12 +208,7 @@
     received_early = lax.all_to_all(
         route_blocks(dispatch[: layer_count - 1], earlier_rows), "seq", 0, 0, tiled=True
     )
-    widened = tokens.astype(jnp.float32)
-    normed = (
-        widened
-        * lax.rsqrt(jnp.mean(widened * widened, axis=-1, keepdims=True) + EPSILON)
-        * norm_gain
-    ).astype(jnp.bfloat16)
+    normed = rms_norm(tokens.reshape(-1, tokens.shape[-1]), norm_gain).reshape(tokens.shape)
     portion = lax.all_gather(normed, "dec", axis=0, tiled=True)
     received_early, portion = lax.optimization_barrier((received_early, portion))
     flattened = portion.reshape(-1, portion.shape[-1])
@@ -214,18 +232,16 @@
         kept_cache, fresh_rows, (zero_index, req_length, zero_index)
     )
     group_size = query_cols // HD // heads_here
-    context = attend(
+    product = attend(
         req_length.reshape(1),
         queries,
         jnp.transpose(assembled[:, :, :HD], (0, 2, 1)),
         assembled,
+        w_out,
         group_size,
     )
-    product = jnp.dot(context, w_out, preferred_element_type=jnp.float32)
     summed = lax.psum_scatter(
-        product.reshape(
-            NEW_TOK // lax.axis_size("dec") * lax.axis_size("dec"), 1, product.shape[-1]
-        ).astype(jnp.bfloat16),
+        product.reshape(NEW_TOK, 1, product.shape[-1]),
         "dec",
         scatter_dimension=0,
         tiled=True,

time: 124 us -> 123 us (level)
  local copies, waits for them, and re-layouts: 15.3 us -> 20.6 us
  other arithmetic: 9.34 us -> 5.46 us
  matrix products: 7.52 us -> 4.31 us
  Pallas kernels: 20.9 us -> 24 us
  waiting for transfers between devices: 30.1 us -> 28.6 us
    dot_general x1 -> x0, matrix products: 3.21 us -> none  [local(): product = jnp.dot(context, w_out, preferred_element_type=jnp.float32)]
    pallas_call x1 -> x2, Pallas kernels: 15.9 us -> 19 us  [the longest x1 17 us: attend(): pl.pallas_call(kernel, out_shape=jax.ShapeDtypeStruct((tokens, model), jn...]
    transpose x2, local copies, waits for them, and re-layouts: 1.22 us -> 3.5 us  [local(): jnp.transpose(assembled[:, :, :HD], (0, 2, 1))]
    convert_element_type x1 -> x0, other arithmetic: 1.91 us -> none  [local(): normed = (widened * lax.rsqrt(jnp.mean(widened * widened, axis=-1, keepdi...]
    all_to_all x1, waiting for transfers between devices: 17.6 us -> 16 us  [local(): lax.all_to_all(route_blocks(dispatch[:layer_count - 1], earlier_rows), 's...]
    reshape x1, other arithmetic: 1.86 us -> 0.27 us  [local(): jnp.transpose(received, (1, 0, 2, 3, 4))]
    reshape x0 -> x1, local copies, waits for them, and re-layouts: none -> 1.3 us  [rms_norm(): gain.reshape(1, -1)]
    reduce_sum x1 -> x0, other arithmetic: 1.24 us -> none  [local(): jnp.mean(widened * widened, axis=-1, keepdims=True) + EPSILON]
where the time goes in v9:
time: 123 us
  waiting for transfers between devices  28.6 us (23%)
  Pallas kernels  24 us (20%)
  local copies, waits for them, and re-layouts  20.6 us (17%)
  blocking collectives  17.8 us (14%)
  between operations  16.5 us (13%)
  other arithmetic  5.46 us (4%)
  starting transfers between devices  5.43 us (4%)
  matrix products  4.31 us (4%)
    all_to_all x1, blocking collectives, local(): lax.all_to_all(route_blocks(dispatch[layer_count - 1:], current_rows), 's...  17.8 us
    pallas_call x1, Pallas kernels, attend(): pl.pallas_call(kernel, out_shape=jax.ShapeDtypeStruct((tokens, model), jn...  17 us
    all_to_all x1, waiting for transfers between devices, local(): lax.all_to_all(route_blocks(dispatch[:layer_count - 1], earlier_rows), 's...  16 us
    reduce_scatter x1, waiting for transfers between devices, local(): lax.psum_scatter(product.reshape(NEW_TOK, 1, product.shape[-1]), 'dec', s...  12.5 us
    all_to_all x1, starting transfers between devices, local(): lax.all_to_all(route_blocks(dispatch[:layer_count - 1], earlier_rows), 's...  5.17 us
    pallas_call x1, Pallas kernels, project(): pl.pallas_call(project_kernel, out_shape=(jax.ShapeDtypeStruct((tokens, q...  5.01 us
    dot_general x2, matrix products, route_blocks(): jnp.einsum('locms,msbw->olcbw', spread, block_data, preferred_element_typ...  4.31 us
    unnamed x8, local copies, waits for them, and re-layouts  3.79 us
  transfers between devices with their start and end apart: 3, of which 2 were waited for; matrix products, arithmetic and copies ran while one was open for 18% of the time, Pallas kernels for 0%

profile of v9, /device:TPU:0, one launch (start us, length us, event | category | flops | bytes accessed | tf_op | source)
XLA Modules:
  0.0 122.7 jit_solution(2140681512055872866)
XLA Ops:
  7.2 0.0 all-gather.3.cloned.1.call-start
  7.2 1.3 %reshape.111.gain_ref = f32[1,1536]{1,0:T(1,128)} reshape(f32[1536]{0:T(1024)} %param.10) | data formatting | bytes 12288 | tf_op jit(solution)/shard_map/reshape | solution.py:178
  8.5 1.9 %shard_map.104 = bf16[128,1536]{1,0:T(8,128)(2,1)} custom-call(bf16[128,1536]{1,0:T(8,128)(2,1)} %bitcast.67, f32[1,1536]{1,0:T(1,128)} %reshape.111.gain_ref), custom_call_target="tpu_custom_call" | custom-call | flops 786432 | bytes 786432 | tf_op jit(solution)/shard_map/pallas_call | solution.py:172
  10.4 0.0 all-gather.3.cloned.1.call-update
  10.5 0.5 broadcast.59
  11.0 1.3 %reduce.3 = s32[3,2,16]{2,1,0:T(2,128)S(1)} reduce(s32[1,3,2,16,1]{3,4,2,1,0:T(1,128)} %param.17, s32[]{:T(128)} %broadcast.59), dimensions={0,4}, to_apply=%param.17.reduce_sub_computation.3 | reduce | bytes 772 | tf_op args[8]
  12.3 0.1 reshape_squeeze.3
  12.4 0.1 fusion.8
  12.5 0.1 reduce_window_sum.11
  12.6 0.2 select_reduce_fusion
  12.8 1.2 %dynamic_slice.3.length_ref = s32[1]{0:T(128)} dynamic-slice(s32[8]{0:T(128)} %param.11, s32[]{:T(128)S(6)} %select_n.15), dynamic_slice_sizes={1} | dynamic-slice | bytes 12 | tf_op jit(solution)/shard_map/dynamic_slice | solution.py:192
  14.7 0.1 copy.14
  14.8 3.6 %fusion.2 = bf16[8,2,4,128,128]{4,0,2,1,3:T(8,128)(2,1)S(1)} fusion(bf16[2,32,128,128]{3,2,1,0:T(8,128)(2,1)} %bitcast.71, pred[32,128]{0,1:T(8,128)(4,1)S(1)} %copy.14, bf16[2,2]{1,0:T(2,128)(2,1)S(1)} %compare_convert_fusion, bf16[2,8,4,32]{3,1,2,0:T(8,128)(2,1)S(1)} %copy.16), kind=kOutput, calls=%fused_computation.5 | convolution fusion | flops 136331264 | bytes 4202504 | tf_op jit(solution)/shard_map/locms,msbw->olcbw/dot_general | solution.py:37
  18.4 2.7 %copy.17 = bf16[8,2,4,128,128]{4,3,2,1,0:T(8,128)(2,1)} copy(bf16[8,2,4,128,128]{4,0,2,1,3:T(8,128)(2,1)S(1)} %fusion.2) | data formatting | bytes 4194304 | tf_op jit(solution)/shard_map/convert_element_type | solution.py:39
  21.0 5.2 %all-to-all-start = ((bf16[8,1024,128]{2,1,0:T(8,128)(2,1)}), bf16[8,1024,128]{2,1,0:T(8,128)(2,1)S(1)}, u32[]{:S(2)}, u32[]{:S(2)}) async-start(bf16[8,1024,128]{2,1,0:T(8,128)(2,1)} %bitcast.58), calls=%async_computation | async-start | bytes 4194304 | tf_op jit(solution)/shard_map/all_to_all | solution.py:208
  26.2 0.2 reduce-scatter.2.cloned.1.call-start
  27.0 0.6 add_convert_fusion
  27.6 0.3 fusion.11
  27.9 0.1 copy.21
  28.0 0.8 copy.20
  28.9 0.1 copy.18
  29.0 0.1 tile.16
  29.1 1.2 copy.22.cq_ref
  30.3 0.1 tile.18
  30.4 1.2 copy.23.sq_ref
  31.5 0.1 pad.9.clone
  31.6 0.1 pad.12.clone
  32.8 0.6 iota_compare_fusion.2
  33.4 0.1 maximum_maximum_fusion
  33.5 1.2 maximum_maximum_fusion.1
  34.7 0.2 tile.42
  34.9 0.2 tile.40
  35.1 1.1 copy_bitcast_fusion
  36.2 0.7 pad_select_fusion
  36.8 16.0 %all-to-all-done = bf16[8,1024,128]{2,1,0:T(8,128)(2,1)S(1)} async-done(((bf16[8,1024,128]{2,1,0:T(8,128)(2,1)}), bf16[8,1024,128]{2,1,0:T(8,128)(2,1)S(1)}, u32[]{:S(2)}, u32[]{:S(2)}) %all-to-all-start) | async-done | bytes 2097184 | tf_op jit(solution)/shard_map/all_to_all | solution.py:208
  52.9 5.0 %shard_map.105 = (bf16[512,384]{1,0:T(8,128)(2,1)}, bf16[2,512,128]{2,1,0:T(8,128)(2,1)}) custom-call(bf16[512,1536]{1,0:T(8,128)(2,1)} %all-gather.3.cloned.1.call-done, bf16[1536,384]{1,0:T(8,128)(2,1)} %wq_ref.1, bf16[1536,256]{1,0:T(8,128)(2,1)} %wkv_ref.1, f32[512,384]{1,0:T(8,128)} %copy.22.cq_ref, f32[512,384]{1,0:T(8,128)} %copy.23.sq_ref, ...), custom_call_target="tpu_custom_call" | custom-call | flops 1006632960 | bytes 6160384 | tf_op jit(solution)/shard_map/pallas_call | solution.py:74
  57.9 2.4 %dynamic_update_slice.3.kv_ref = bf16[2,2048,128]{2,1,0:T(8,128)(2,1)S(1)} dynamic-update-slice(bf16[2,2048,128]{2,1,0:T(8,128)(2,1)S(1)} %pad_select_fusion, bf16[2,512,128]{2,1,0:T(8,128)(2,1)} %get-tuple-element.8, s32[]{:T(128)} %constant.9.clone.1, s32[]{:T(128)S(6)} %select_n.18, s32[]{:T(128)} %constant.9.clone.1) | dynamic-update-slice | bytes 524292 | tf_op jit(solution)/shard_map/dynamic_update_slice | solution.py:231
  60.2 1.1 slice_bitcast_fusion
  61.4 2.4 %copy.24.kt_ref = bf16[2,64,2048]{2,1,0:T(8,128)(2,1)} copy(bf16[2,64,2048]{1,2,0:T(8,128)(2,1)} %slice_bitcast_fusion) | data formatting | bytes 1048576 | tf_op jit(solution)/shard_map/transpose | solution.py:238
  63.8 17.0 %shard_map.106 = bf16[512,1536]{1,0:T(8,128)(2,1)} custom-call(s32[1]{0:T(128)} %dynamic_slice.3.length_ref, bf16[512,384]{1,0:T(8,128)(2,1)} %get-tuple-element.7.q_ref, bf16[2,64,2048]{2,1,0:T(8,128)(2,1)} %copy.24.kt_ref, bf16[2,2048,128]{2,1,0:T(8,128)(2,1)} %copy-done, bf16[384,1536]{1,0:T(8,128)(2,1)} %wo_ref.1), custom_call_target="tpu_custom_call" | custom-call | flops 2214592512 | bytes 4718592 | tf_op jit(solution)/shard_map/pallas_call | solution.py:141
  80.8 0.0 reduce-scatter.2.cloned.1.call-update
  80.8 1.2 copy-done.1
  82.0 0.7 fusion.5
  82.8 0.4 copy.27
  83.2 17.8 %all_to_all.10 = bf16[8,512,128]{2,1,0:T(8,128)(2,1)S(1)} all-to-all(bf16[8,512,128]{2,1,0:T(8,128)(2,1)S(1)} %bitcast.59), channel_id=1, replica_groups=mesh['seq'=8,'dec'=4] {'seq'}, dimensions={0} | all-to-all | bytes 2097152 | tf_op jit(solution)/shard_map/all_to_all | solution.py:250
  101.0 0.3 maximum_bitcast_fusion
  101.3 2.1 %copy.28 = bf16[1,1,3,8,4,128,128]{6,5,4,3,2,1,0:T(8,128)(2,1)} copy(bf16[1,1,3,8,4,128,128]{6,5,4,2,3,1,0:T(8,128)(2,1)S(1)} %maximum_bitcast_fusion) | data formatting | bytes 6291456
  103.3 12.5 %reduce-scatter.2.cloned.1.call-done = bf16[128,1,1536]{2,0,1:T(8,128)(2,1)} async-done(((bf16[512,1,1536]{2,0,1:T(8,128)(2,1)}), bf16[128,1,1536]{2,0,1:T(8,128)(2,1)}) %reduce-scatter.2.cloned.1.call-update) | async-done | bytes 393232 | tf_op jit(solution)/shard_map/reduce_scatter | solution.py:243
  (18 shorter events, 0.1 us)
Async XLA Ops:
  7.2 45.7 %all-gather.3.cloned.1.call-start = ((), (), s32[]{:S(2)}) async-start(), calls=%async_computation.4 | async-start | bytes 1966080 | tf_op jit(solution)/shard_map/all_gather | solution.py:212
  21.0 31.8 %all-to-all-start = ((bf16[8,1024,128]{2,1,0:T(8,128)(2,1)}), bf16[8,1024,128]{2,1,0:T(8,128)(2,1)S(1)}, u32[]{:S(2)}, u32[]{:S(2)}) async-start(bf16[8,1024,128]{2,1,0:T(8,128)(2,1)} %bitcast.58), calls=%async_computation | async-start | bytes 4194304 | tf_op jit(solution)/shard_map/all_to_all | solution.py:208
  26.2 89.6 %reduce-scatter.2.cloned.1.call-start = ((), (), s32[]{:S(2)}) async-start(), calls=%async_computation.3 | async-start | bytes 1966080 | tf_op jit(solution)/shard_map/reduce_scatter | solution.py:243
  33.5 2.6 %copy-start.2 = (bf16[1,2,1536,128]{3,2,1,0:T(8,128)(2,1)S(1)}, bf16[1,2,1536,128]{3,2,1,0:T(8,128)(2,1)}, u32[]{:S(2)}) copy-start(bf16[1,2,1536,128]{3,2,1,0:T(8,128)(2,1)} %param.15) | copy-start | bytes 2359300
  60.2 3.5 %copy-start = (bf16[2,2048,128]{2,1,0:T(8,128)(2,1)}, bf16[2,2048,128]{2,1,0:T(8,128)(2,1)S(1)}, u32[]{:S(2)}) copy-start(bf16[2,2048,128]{2,1,0:T(8,128)(2,1)S(1)} %dynamic_update_slice.3.kv_ref) | copy-start | bytes 3145732
  80.8 1.2 copy-start.1
Sparse Core Ops, SparseCore 0:
  10.6 39.7 all-gather.2
  80.9 34.8 reduce-scatter.1

commit v10 on v9

--- a/solution.py
+++ b/solution.py
@@ -51,19 +51,19 @@
     return jnp.where(ahead_lane == wanted, ahead, behind)
 
 
-def project_kernel(x_ref, wq_ref, wkv_ref, cq_ref, sq_ref, ckv_ref, skv_ref, q_out, kv_out):
+def project_kernel(x_ref, wq_ref, wkv_ref, cq_ref, sq_ref, ckv_ref, skv_ref, q_out, kv_out, kt_out):
     x = x_ref[...]
     query = jnp.dot(x, wq_ref[...], preferred_element_type=jnp.float32)
     q_out[...] = (query * cq_ref[...] + swap_halves(query, HD // 2) * sq_ref[...]).astype(
         q_out.dtype
     )
     key_value = jnp.dot(x, wkv_ref[...], preferred_element_type=jnp.float32)
-    rotated = (
-        key_value * ckv_ref[...] + swap_halves(key_value, HD // 2) * skv_ref[...]
-    ).astype(kv_out.dtype)
+    rotated = key_value * ckv_ref[...] + swap_halves(key_value, HD // 2) * skv_ref[...]
     width = kv_out.shape[2]
     for head_index in range(kv_out.shape[0]):
-        kv_out[head_index] = rotated[:, head_index * width : (head_index + 1) * width]
+        block = rotated[:, head_index * width : (head_index + 1) * width].astype(kv_out.dtype)
+        kv_out[head_index] = block
+        kt_out[head_index] = block[:, :HD].astype(jnp.float32).T.astype(kt_out.dtype)
 
 
 def project(x, w_query, w_keyval, cos_q, sin_q, cos_kv, sin_kv, tile=256):
@@ -76,6 +76,7 @@
         out_shape=(
             jax.ShapeDtypeStruct((tokens, q_cols), jnp.bfloat16),
             jax.ShapeDtypeStruct((heads, tokens, 2 * HD), jnp.bfloat16),
+            jax.ShapeDtypeStruct((heads, HD, tokens), jnp.bfloat16),
         ),
         grid=(tokens // tile,),
         in_specs=[
@@ -90,6 +91,7 @@
         out_specs=(
             row_spec(q_cols),
             pl.BlockSpec((heads, tile, 2 * HD), lambda i: (0, i, 0)),
+            pl.BlockSpec((heads, HD, tile), lambda i: (0, 0, i)),
         ),
         cost_estimate=pl.CostEstimate(
             flops=2 * tokens * depth * (q_cols + kv_cols),
@@ -100,29 +102,38 @@
     )(x, w_query, w_keyval, cos_q, sin_q, cos_kv, sin_kv)
 
 
-def attention_kernel(length_ref, q_ref, kt_ref, kv_ref, wo_ref, out_ref, ctx_ref, *, tile, scale, group):
+def attention_kernel(
+    length_ref, q_ref, kt_ref, kv_ref, ktf_ref, kvf_ref, wo_ref, out_ref, ctx_ref, *, tile, scale, group
+):
     tile_index = pl.program_id(0)
-    span = kt_ref.shape[2]
+    span, fresh = kt_ref.shape[2], ktf_ref.shape[2]
     pair = 2 * HD
-    token = lax.broadcasted_iota(jnp.int32, (tile, span), 0) + tile_index * tile
     slot = lax.broadcasted_iota(jnp.int32, (tile, span), 1)
-    visible = slot <= length_ref[0] + token
+    cached_visible = slot < length_ref[0]
+    token = lax.broadcasted_iota(jnp.int32, (tile, fresh), 0) + tile_index * tile
+    new_slot = lax.broadcasted_iota(jnp.int32, (tile, fresh), 1)
+    fresh_visible = new_slot <= token
     lane = lax.broadcasted_iota(jnp.int32, (tile, pair), 1)
     for pair_index in range(q_ref.shape[1] // pair):
         both = q_ref[:, pair_index * pair : (pair_index + 1) * pair]
         halves = []
         for parity in range(2):
             head = (2 * pair_index + parity) // group
-            lined = both if parity == 0 else pltpu.roll(both, HD, 1)
-            scores = (
-                jnp.dot(lined[:, :HD], kt_ref[head], preferred_element_type=jnp.float32) * scale
+            lined = (both if parity == 0 else pltpu.roll(both, HD, 1))[:, :HD]
+            old = jnp.dot(lined, kt_ref[head], preferred_element_type=jnp.float32) * scale
+            new = jnp.dot(lined, ktf_ref[head], preferred_element_type=jnp.float32) * scale
+            row_max = jnp.maximum(
+                jnp.max(jnp.where(cached_visible, old, -jnp.inf), axis=-1, keepdims=True),
+                jnp.max(jnp.where(fresh_visible, new, -jnp.inf), axis=-1, keepdims=True),
             )
-            row_max = jnp.max(jnp.where(visible, scores, -jnp.inf), axis=-1, keepdims=True)
-            weights = jnp.where(visible, jnp.exp(scores - row_max), 0.0)
-            row_total = jnp.sum(weights, axis=-1, keepdims=True)
+            old_w = jnp.where(cached_visible, jnp.exp(old - row_max), 0.0)
+            new_w = jnp.where(fresh_visible, jnp.exp(new - row_max), 0.0)
+            row_total = jnp.sum(old_w, axis=-1, keepdims=True) + jnp.sum(
+                new_w, axis=-1, keepdims=True
+            )
             mixed = jnp.dot(
-                weights.astype(jnp.bfloat16), kv_ref[head], preferred_element_type=jnp.float32
-            )
+                old_w.astype(jnp.bfloat16), kv_ref[head], preferred_element_type=jnp.float32
+            ) + jnp.dot(new_w.astype(jnp.bfloat16), kvf_ref[head], preferred_element_type=jnp.float32)
             halves.append((mixed, row_total))
         (even, even_total), (odd, odd_total) = halves
         joined = jnp.where(lane < HD, pltpu.roll(even, HD, 1) / even_total, odd / odd_total)
@@ -132,12 +143,13 @@
     )
 
 
-def attend(length, queries, keys_t, assembled, w_out, group, tile=256):
+def attend(length, queries, keys_t, cache, fresh_keys_t, fresh, w_out, group, tile=256):
     tokens, q_cols = queries.shape
-    heads, span = assembled.shape[0], assembled.shape[1]
+    span = cache.shape[1] + fresh.shape[1]
     model = w_out.shape[1]
     kernel = functools.partial(attention_kernel, tile=tile, scale=HD ** (-0.5), group=group)
     flops = 4 * tokens * q_cols * span + 2 * tokens * q_cols * model
+    whole = lambda shape: pl.BlockSpec(shape, lambda i, n: (0,) * len(shape))
     return pl.pallas_call(
         kernel,
         out_shape=jax.ShapeDtypeStruct((tokens, model), jnp.bfloat16),
@@ -146,9 +158,11 @@
             grid=(tokens // tile,),
             in_specs=[
                 pl.BlockSpec((tile, q_cols), lambda i, n: (i, 0)),
-                pl.BlockSpec(keys_t.shape, lambda i, n: (0, 0, 0)),
-                pl.BlockSpec(assembled.shape, lambda i, n: (0, 0, 0)),
-                pl.BlockSpec(w_out.shape, lambda i, n: (0, 0)),
+                whole(keys_t.shape),
+                whole(cache.shape),
+                whole(fresh_keys_t.shape),
+                whole(fresh.shape),
+                whole(w_out.shape),
             ],
             out_specs=pl.BlockSpec((tile, model), lambda i, n: (i, 0)),
             scratch_shapes=[pltpu.VMEM((tile, q_cols), jnp.bfloat16)],
@@ -156,10 +170,11 @@
         cost_estimate=pl.CostEstimate(
             flops=flops,
             transcendentals=tokens * (q_cols // HD) * span,
-            bytes_accessed=2 * (queries.size + keys_t.size + assembled.size + w_out.size)
+            bytes_accessed=2
+            * (queries.size + keys_t.size + cache.size + fresh_keys_t.size + fresh.size + w_out.size)
             + 2 * tokens * model,
         ),
-    )(length, queries, keys_t, assembled, w_out)
+    )(length, queries, keys_t, cache, fresh_keys_t, fresh, w_out)
 
 
 def norm_kernel(x_ref, gain_ref, out_ref):
@@ -224,7 +239,9 @@
     sin_kv = jnp.tile(
         jnp.concatenate([signed_sine, jnp.zeros_like(signed_sine)], axis=-1), (1, heads_here)
     )
-    queries, fresh_rows = project(flattened, w_query, w_keyval, cos_q, sin_q, cos_kv, sin_kv)
+    queries, fresh_rows, fresh_keys_t = project(
+        flattened, w_query, w_keyval, cos_q, sin_q, cos_kv, sin_kv
+    )
     cached = kv_cache[0]
     padded = jnp.pad(cached, ((0, 0), (0, span_len - cached.shape[1]), (0, 0)))
     kept_cache = jnp.where((slot_ids < req_length)[None, :, None], padded, jnp.zeros_like(padded))
@@ -235,8 +252,10 @@
     product = attend(
         req_length.reshape(1),
         queries,
-        jnp.transpose(assembled[:, :, :HD], (0, 2, 1)),
-        assembled,
+        jnp.transpose(cached[:, :, :HD], (0, 2, 1)),
+        cached,
+        fresh_keys_t,
+        fresh_rows,
         w_out,
         group_size,
     )

time: 123 us -> 116 us (0.943)
  waiting for transfers between devices: 28.6 us -> 19.6 us
  local copies, waits for them, and re-layouts: 20.6 us -> 22.3 us
    all_to_all x1, waiting for transfers between devices: 16 us -> 11.2 us  [local(): lax.all_to_all(route_blocks(dispatch[:layer_count - 1], earlier_rows), 's...]
    reduce_scatter x1, waiting for transfers between devices: 12.5 us -> 8.36 us  [local(): lax.psum_scatter(product.reshape(NEW_TOK, 1, product.shape[-1]), 'dec', s...]
    another operation x2, local copies, waits for them, and re-layouts: 1.26 us -> 3.36 us  [local(): cos_q = jnp.tile(head_cos, (1, query_cols // HD))]
    another operation x2, local copies, waits for them, and re-layouts: 1.25 us -> 3.27 us  [local(): sin_q = jnp.tile(signed_sine, (1, query_cols // HD))]
    dynamic_update_slice x1, local copies, waits for them, and re-layouts: 2.36 us -> 0.93 us  [local(): lax.dynamic_update_slice(kept_cache, fresh_rows, (zero_index, req_length,...]
    pallas_call x1, Pallas kernels: 17 us -> 15.8 us  [attend(): pl.pallas_call(kernel, out_shape=jax.ShapeDtypeStruct((tokens, model), jn...]
    unnamed x8 -> x10, local copies, waits for them, and re-layouts: 3.79 us -> 2.61 us
  transfers between devices with their start and end apart: 3 -> 3, of which waited for: 2 -> 2; matrix products, arithmetic and copies ran while one was open for 18% -> 27% of each run, Pallas kernels for 0% -> 0%
where the time goes in v10:
time: 116 us
  Pallas kernels  22.9 us (20%)
  local copies, waits for them, and re-layouts  22.3 us (19%)
  waiting for transfers between devices  19.6 us (17%)
  blocking collectives  17.8 us (15%)
  between operations  17 us (15%)
  other arithmetic  6.37 us (5%)
  starting transfers between devices  5.43 us (5%)
  matrix products  4.31 us (4%)
    all_to_all x1, blocking collectives, local(): lax.all_to_all(route_blocks(dispatch[layer_count - 1:], current_rows), 's...  17.8 us
    pallas_call x1, Pallas kernels, attend(): pl.pallas_call(kernel, out_shape=jax.ShapeDtypeStruct((tokens, model), jn...  15.8 us
    all_to_all x1, waiting for transfers between devices, local(): lax.all_to_all(route_blocks(dispatch[:layer_count - 1], earlier_rows), 's...  11.2 us
    reduce_scatter x1, waiting for transfers between devices, local(): lax.psum_scatter(product.reshape(NEW_TOK, 1, product.shape[-1]), 'dec', s...  8.36 us
    all_to_all x1, starting transfers between devices, local(): lax.all_to_all(route_blocks(dispatch[:layer_count - 1], earlier_rows), 's...  5.17 us
    pallas_call x1, Pallas kernels, project(): pl.pallas_call(project_kernel, out_shape=(jax.ShapeDtypeStruct((tokens, q...  5.16 us
    dot_general x2, matrix products, route_blocks(): jnp.einsum('locms,msbw->olcbw', spread, block_data, preferred_element_typ...  4.31 us
    another operation x2, local copies, waits for them, and re-layouts, local(): cos_q = jnp.tile(head_cos, (1, query_cols // HD))  3.36 us
  transfers between devices with their start and end apart: 3, of which 2 were waited for; matrix products, arithmetic and copies ran while one was open for 27% of the time, Pallas kernels for 0%

profile of v10, /device:TPU:0, one launch (start us, length us, event | category | flops | bytes accessed | tf_op | source)
XLA Modules:
  0.0 115.8 jit_solution(1686810586245433575)
XLA Ops:
  7.2 0.0 all-gather.3.cloned.1.call-start
  7.2 1.3 %reshape.111.gain_ref = f32[1,1536]{1,0:T(1,128)} reshape(f32[1536]{0:T(1024)} %param.10) | data formatting | bytes 12288 | tf_op jit(solution)/shard_map/reshape | solution.py:193
  8.5 1.9 %shard_map.104 = bf16[128,1536]{1,0:T(8,128)(2,1)} custom-call(bf16[128,1536]{1,0:T(8,128)(2,1)} %bitcast.69, f32[1,1536]{1,0:T(1,128)} %reshape.111.gain_ref), custom_call_target="tpu_custom_call" | custom-call | flops 786432 | bytes 786432 | tf_op jit(solution)/shard_map/pallas_call | solution.py:187
  10.4 0.0 all-gather.3.cloned.1.call-update
  10.5 0.5 broadcast.59
  11.0 1.3 %reduce.3 = s32[3,2,16]{2,1,0:T(2,128)S(1)} reduce(s32[1,3,2,16,1]{3,4,2,1,0:T(1,128)} %param.17, s32[]{:T(128)} %broadcast.59), dimensions={0,4}, to_apply=%param.17.reduce_sub_computation.3 | reduce | bytes 772 | tf_op args[8]
  12.3 0.1 reshape_squeeze.3
  12.4 0.1 fusion.8
  12.5 0.1 reduce_window_sum.11
  12.6 0.2 select_reduce_fusion
  12.8 1.3 %dynamic_slice.3.length_ref = s32[1]{0:T(128)} dynamic-slice(s32[8]{0:T(128)} %param.11, s32[]{:T(128)S(6)} %select_n.15), dynamic_slice_sizes={1} | dynamic-slice | bytes 12 | tf_op jit(solution)/shard_map/dynamic_slice | solution.py:207
  14.9 0.1 copy.14
  15.0 3.6 %fusion.2 = bf16[8,2,4,128,128]{4,0,2,1,3:T(8,128)(2,1)S(1)} fusion(bf16[2,32,128,128]{3,2,1,0:T(8,128)(2,1)} %bitcast.73, pred[32,128]{0,1:T(8,128)(4,1)S(1)} %copy.14, bf16[2,2]{1,0:T(2,128)(2,1)S(1)} %compare_convert_fusion, bf16[2,8,4,32]{3,1,2,0:T(8,128)(2,1)S(1)} %copy.16), kind=kOutput, calls=%fused_computation.5 | convolution fusion | flops 136331264 | bytes 4202504 | tf_op jit(solution)/shard_map/locms,msbw->olcbw/dot_general | solution.py:37
  18.6 2.7 %copy.17 = bf16[8,2,4,128,128]{4,3,2,1,0:T(8,128)(2,1)} copy(bf16[8,2,4,128,128]{4,0,2,1,3:T(8,128)(2,1)S(1)} %fusion.2) | data formatting | bytes 4194304 | tf_op jit(solution)/shard_map/convert_element_type | solution.py:39
  21.2 5.2 %all-to-all-start = ((bf16[8,1024,128]{2,1,0:T(8,128)(2,1)}), bf16[8,1024,128]{2,1,0:T(8,128)(2,1)S(1)}, u32[]{:S(2)}, u32[]{:S(2)}) async-start(bf16[8,1024,128]{2,1,0:T(8,128)(2,1)} %bitcast.57), calls=%async_computation | async-start | bytes 4194304 | tf_op jit(solution)/shard_map/all_to_all | solution.py:223
  26.4 0.2 reduce-scatter.2.cloned.1.call-start
  26.7 0.7 add_convert_fusion
  27.3 0.3 fusion.11
  27.7 0.1 copy.20
  27.8 0.8 copy.21
  28.6 0.1 copy.18
  28.8 0.6 pad.9.clone
  29.3 0.1 pad.12.clone
  29.4 1.0 tile.16
  30.4 2.4 %copy.22.cq_ref = f32[512,384]{1,0:T(8,128)} copy(f32[512,384]{0,1:T(8,128)} %bitcast.64) | data formatting | bytes 1572864 | tf_op jit(solution)/shard_map/tile | solution.py:236
  32.8 1.0 tile.18
  33.8 2.3 %copy.23.sq_ref = f32[512,384]{1,0:T(8,128)} copy(f32[512,384]{0,1:T(8,128)} %bitcast.65) | data formatting | bytes 1572864 | tf_op jit(solution)/shard_map/tile | solution.py:237
  36.1 0.9 slice_bitcast_fusion
  37.0 2.1 %copy.24.kt_ref = bf16[2,64,1536]{2,1,0:T(8,128)(2,1)} copy(bf16[2,64,1536]{1,2,0:T(8,128)(2,1)} %slice_bitcast_fusion) | data formatting | bytes 786432 | tf_op jit(solution)/shard_map/transpose | solution.py:255
  39.2 0.1 maximum_maximum_fusion
  39.3 1.1 maximum_maximum_fusion.1
  40.4 0.2 tile.42
  40.6 0.2 tile.40
  40.8 1.1 copy_bitcast_fusion
  41.8 11.2 %all-to-all-done = bf16[8,1024,128]{2,1,0:T(8,128)(2,1)S(1)} async-done(((bf16[8,1024,128]{2,1,0:T(8,128)(2,1)}), bf16[8,1024,128]{2,1,0:T(8,128)(2,1)S(1)}, u32[]{:S(2)}, u32[]{:S(2)}) %all-to-all-start) | async-done | bytes 2097184 | tf_op jit(solution)/shard_map/all_to_all | solution.py:223
  53.1 5.2 %shard_map.105 = (bf16[512,384]{1,0:T(8,128)(2,1)}, bf16[2,512,128]{2,1,0:T(8,128)(2,1)}, bf16[2,64,512]{2,1,0:T(8,128)(2,1)}) custom-call(bf16[512,1536]{1,0:T(8,128)(2,1)} %all-gather.3.cloned.1.call-done, bf16[1536,384]{1,0:T(8,128)(2,1)} %wq_ref.1, bf16[1536,256]{1,0:T(8,128)(2,1)} %wkv_ref.1, f32[512,384]{1,0:T(8,128)} %copy.22.cq_ref, ...), custom_call_target="tpu_custom_call" | custom-call | flops 1006632960 | bytes 6160384 | tf_op jit(solution)/shard_map/pallas_call | solution.py:74
  58.2 15.8 %shard_map.106 = bf16[512,1536]{1,0:T(8,128)(2,1)} custom-call(s32[1]{0:T(128)} %dynamic_slice.3.length_ref, bf16[512,384]{1,0:T(8,128)(2,1)} %get-tuple-element.8.q_ref, bf16[2,64,1536]{2,1,0:T(8,128)(2,1)} %copy.24.kt_ref, bf16[2,1536,128]{2,1,0:T(8,128)(2,1)} %bitcast.61, bf16[2,64,512]{2,1,0:T(8,128)(2,1)} %get-tuple-element.9.ktf_ref, ...), custom_call_target="tpu_custom_call" | custom-call | flops 2214592512 | bytes 4718592 | tf_op jit(solution)/shard_map/pallas_call | solution.py:153
  74.0 0.0 reduce-scatter.2.cloned.1.call-update
  74.8 0.0 slice-start
  76.2 0.7 iota_compare_fusion.2
  76.9 1.4 %pad_select_fusion = bf16[2,2048,128]{2,1,0:T(8,128)(2,1)S(1)} fusion(bf16[2,1536,128]{2,1,0:T(8,128)(2,1)} %bitcast.62, pred[2048]{0:T(1024)(128)(4,1)S(1)} %iota_compare_fusion.2), kind=kLoop, calls=%fused_computation.9 | loop fusion | flops 524288 | bytes 1837056 | tf_op jit(solution)/shard_map/jit(_where)/select_n | solution.py:247
  78.3 0.9 dynamic_update_slice.3
  79.3 0.8 fusion.5
  80.0 0.4 copy.27
  80.4 17.8 %all_to_all.10 = bf16[8,512,128]{2,1,0:T(8,128)(2,1)S(1)} all-to-all(bf16[8,512,128]{2,1,0:T(8,128)(2,1)S(1)} %bitcast.59), channel_id=1, replica_groups=mesh['seq'=8,'dec'=4] {'seq'}, dimensions={0} | all-to-all | bytes 2097152 | tf_op jit(solution)/shard_map/all_to_all | solution.py:269
  98.2 0.3 maximum_bitcast_fusion
  98.5 2.1 %copy.28 = bf16[1,1,3,8,4,128,128]{6,5,4,3,2,1,0:T(8,128)(2,1)} copy(bf16[1,1,3,8,4,128,128]{6,5,4,2,3,1,0:T(8,128)(2,1)S(1)} %maximum_bitcast_fusion) | data formatting | bytes 6291456
  100.6 8.4 %reduce-scatter.2.cloned.1.call-done = bf16[128,1,1536]{2,0,1:T(8,128)(2,1)} async-done(((bf16[512,1,1536]{2,0,1:T(8,128)(2,1)}), bf16[128,1,1536]{2,0,1:T(8,128)(2,1)}) %reduce-scatter.2.cloned.1.call-update) | async-done | bytes 393232 | tf_op jit(solution)/shard_map/reduce_scatter | solution.py:262
  (21 shorter events, 0.1 us)
Async XLA Ops:
  7.2 45.9 %all-gather.3.cloned.1.call-start = ((), (), s32[]{:S(2)}) async-start(), calls=%async_computation.4 | async-start | bytes 1966080 | tf_op jit(solution)/shard_map/all_gather | solution.py:227
  12.8 62.0 %copy-start.2 = (pred[3,32,32]{2,1,0:T(8,128)(4,1)}, pred[3,32,32]{2,1,0:T(8,128)(4,1)S(1)}, u32[]{:S(2)}) copy-start(pred[3,32,32]{2,1,0:T(8,128)(4,1)S(1)} %iota_compare_fusion) | copy-start | bytes 9220
  21.2 31.8 %all-to-all-start = ((bf16[8,1024,128]{2,1,0:T(8,128)(2,1)}), bf16[8,1024,128]{2,1,0:T(8,128)(2,1)S(1)}, u32[]{:S(2)}, u32[]{:S(2)}) async-start(bf16[8,1024,128]{2,1,0:T(8,128)(2,1)} %bitcast.57), calls=%async_computation | async-start | bytes 4194304 | tf_op jit(solution)/shard_map/all_to_all | solution.py:223
  26.4 82.5 %reduce-scatter.2.cloned.1.call-start = ((), (), s32[]{:S(2)}) async-start(), calls=%async_computation.3 | async-start | bytes 1966080 | tf_op jit(solution)/shard_map/reduce_scatter | solution.py:262
  30.4 5.7 %copy-start = (bf16[1,2,1536,128]{3,2,1,0:T(8,128)(2,1)S(1)}, bf16[1,2,1536,128]{3,2,1,0:T(8,128)(2,1)}, u32[]{:S(2)}) copy-start(bf16[1,2,1536,128]{3,2,1,0:T(8,128)(2,1)} %param.15) | copy-start | bytes 2359300
  33.8 5.5 %copy-start.3 = (f32[128]{0:T(128)S(1)}, f32[128]{0:T(128)}, u32[]{:S(2)}) copy-start(f32[128]{0:T(128)} %pad.9.clone) | copy-start | bytes 1540
  74.0 4.3 %copy-start.1 = (bf16[2,512,128]{2,1,0:T(8,128)(2,1)S(1)}, bf16[2,512,128]{2,1,0:T(8,128)(2,1)}, u32[]{:S(2)}) copy-start(bf16[2,512,128]{2,1,0:T(8,128)(2,1)} %get-tuple-element.10.kvf_ref) | copy-start | bytes 786436
  74.8 4.4 %slice-start = ((pred[3,32,32]{2,1,0:T(8,128)(4,1)}), pred[1,32,32]{2,1,0:T(8,128)(4,1)S(1)}, s32[]{:S(2)}) async-start(pred[3,32,32]{2,1,0:T(8,128)(4,1)} %copy-done.2), calls=%async_computation.5 | async-start | bytes 8192 | tf_op jit(solution)/shard_map/slice | solution.py:270
Sparse Core Ops, SparseCore 0:
  10.6 39.7 all-gather.2
  74.2 34.6 reduce-scatter.1

commit v11 on v10

--- a/solution.py
+++ b/solution.py
@@ -190,7 +190,7 @@
         cost_estimate=pl.CostEstimate(
             flops=4 * x.size, transcendentals=x.shape[0], bytes_accessed=4 * x.size
         ),
-    )(x, gain.reshape(1, -1))
+    )(x, gain)
 
 
 def local(tokens, norm_gain, lengths, w_query, w_keyval, w_out, kv_cache, prior_kv, owners):
@@ -225,7 +225,6 @@
     )
     normed = rms_norm(tokens.reshape(-1, tokens.shape[-1]), norm_gain).reshape(tokens.shape)
     portion = lax.all_gather(normed, "dec", axis=0, tiled=True)
-    received_early, portion = lax.optimization_barrier((received_early, portion))
     flattened = portion.reshape(-1, portion.shape[-1])
     positions = (jnp.arange(NEW_TOK, dtype=jnp.int32) + req_length).astype(jnp.float32)
     inverse_freq = ROPE_BASE ** (-(jnp.arange(0, HD, 2, dtype=jnp.float32) / HD))
@@ -242,6 +241,7 @@
     queries, fresh_rows, fresh_keys_t = project(
         flattened, w_query, w_keyval, cos_q, sin_q, cos_kv, sin_kv
     )
+    received_early, queries = lax.optimization_barrier((received_early, queries))
     cached = kv_cache[0]
     padded = jnp.pad(cached, ((0, 0), (0, span_len - cached.shape[1]), (0, 0)))
     kept_cache = jnp.where((slot_ids < req_length)[None, :, None], padded, jnp.zeros_like(padded))

time: 116 us -> 113 us (0.974)
  waiting for transfers between devices: 19.6 us -> 16.6 us
  local copies, waits for them, and re-layouts: 22.3 us -> 21 us
    all_to_all x1, waiting for transfers between devices: 11.2 us -> 0.01 us  [local(): lax.all_to_all(route_blocks(dispatch[:layer_count - 1], earlier_rows), 's...]
    all_gather x1, waiting for transfers between devices: 0.01 us -> 9.55 us  [local(): portion = lax.all_gather(normed, 'dec', axis=0, tiled=True)]
    reduce_scatter x1, waiting for transfers between devices: 8.36 us -> 6.97 us  [local(): lax.psum_scatter(product.reshape(NEW_TOK, 1, product.shape[-1]), 'dec', s...]
    reshape x1 -> x0, local copies, waits for them, and re-layouts: 1.3 us -> none  [rms_norm(): gain.reshape(1, -1)]
  transfers between devices with their start and end apart: 3 -> 3, of which waited for: 2 -> 2; matrix products, arithmetic and copies ran while one was open for 27% -> 28% of each run, Pallas kernels for 0% -> 5%
where the time goes in v11:
time: 113 us; the launch traced here: 112 us
  Pallas kernels  22.8 us (20%)
  local copies, waits for them, and re-layouts  21 us (19%)
  blocking collectives  18.8 us (17%)
  between operations  16.9 us (15%)
  waiting for transfers between devices  16.6 us (15%)
  other arithmetic  6.28 us (6%)
  starting transfers between devices  5.43 us (5%)
  matrix products  4.31 us (4%)
    all_to_all x1, blocking collectives, local(): lax.all_to_all(route_blocks(dispatch[layer_count - 1:], current_rows), 's...  18.8 us
    pallas_call x1, Pallas kernels, attend(): pl.pallas_call(kernel, out_shape=jax.ShapeDtypeStruct((tokens, model), jn...  15.8 us
    all_gather x1, waiting for transfers between devices, local(): portion = lax.all_gather(normed, 'dec', axis=0, tiled=True)  9.55 us
    reduce_scatter x1, waiting for transfers between devices, local(): lax.psum_scatter(product.reshape(NEW_TOK, 1, product.shape[-1]), 'dec', s...  6.97 us
    all_to_all x1, starting transfers between devices, local(): lax.all_to_all(route_blocks(dispatch[:layer_count - 1], earlier_rows), 's...  5.17 us
    pallas_call x1, Pallas kernels, project(): pl.pallas_call(project_kernel, out_shape=(jax.ShapeDtypeStruct((tokens, q...  5.15 us
    dot_general x2, matrix products, route_blocks(): jnp.einsum('locms,msbw->olcbw', spread, block_data, preferred_element_typ...  4.31 us
    another operation x2, local copies, waits for them, and re-layouts, local(): cos_q = jnp.tile(head_cos, (1, query_cols // HD))  3.35 us
  transfers between devices with their start and end apart: 3, of which 2 were waited for; matrix products, arithmetic and copies ran while one was open for 28% of the time, Pallas kernels for 5%

profile of v11, /device:TPU:0, one launch (start us, length us, event | category | flops | bytes accessed | tf_op | source)
XLA Modules:
  0.0 112.1 jit_solution(12731507893268499064)
XLA Ops:
  7.2 0.0 all-gather.3.cloned.1.call-start
  7.2 1.9 %shard_map.104 = bf16[128,1536]{1,0:T(8,128)(2,1)} custom-call(bf16[128,1536]{1,0:T(8,128)(2,1)} %bitcast.67, f32[1536]{0:T(1024)} %gain_ref.1), custom_call_target="tpu_custom_call" | custom-call | flops 786432 | bytes 786432 | tf_op jit(solution)/shard_map/pallas_call | solution.py:187
  9.1 0.0 all-gather.3.cloned.1.call-update
  9.2 0.5 broadcast.59
  9.7 1.3 %reduce.3 = s32[3,2,16]{2,1,0:T(2,128)S(1)} reduce(s32[1,3,2,16,1]{3,4,2,1,0:T(1,128)} %param.17, s32[]{:T(128)} %broadcast.59), dimensions={0,4}, to_apply=%param.17.reduce_sub_computation.3 | reduce | bytes 772 | tf_op args[8]
  11.0 0.1 reshape_squeeze.3
  11.1 0.1 fusion.8
  11.2 0.1 reduce_window_sum.11
  11.3 0.2 select_reduce_fusion
  11.5 1.3 %dynamic_slice.3.length_ref = s32[1]{0:T(128)} dynamic-slice(s32[8]{0:T(128)} %param.11, s32[]{:T(128)S(6)} %select_n.15), dynamic_slice_sizes={1} | dynamic-slice | bytes 12 | tf_op jit(solution)/shard_map/dynamic_slice | solution.py:207
  13.5 0.1 copy.14
  13.6 3.6 %fusion.2 = bf16[8,2,4,128,128]{4,0,2,1,3:T(8,128)(2,1)S(1)} fusion(bf16[2,32,128,128]{3,2,1,0:T(8,128)(2,1)} %bitcast.71, pred[32,128]{0,1:T(8,128)(4,1)S(1)} %copy.14, bf16[2,2]{1,0:T(2,128)(2,1)S(1)} %compare_convert_fusion, bf16[2,8,4,32]{3,1,2,0:T(8,128)(2,1)S(1)} %copy.16), kind=kOutput, calls=%fused_computation.5 | convolution fusion | flops 136331264 | bytes 4202504 | tf_op jit(solution)/shard_map/locms,msbw->olcbw/dot_general | solution.py:37
  17.2 2.7 %copy.17 = bf16[8,2,4,128,128]{4,3,2,1,0:T(8,128)(2,1)} copy(bf16[8,2,4,128,128]{4,0,2,1,3:T(8,128)(2,1)S(1)} %fusion.2) | data formatting | bytes 4194304 | tf_op jit(solution)/shard_map/convert_element_type | solution.py:39
  19.9 5.2 %all-to-all-start = ((bf16[8,1024,128]{2,1,0:T(8,128)(2,1)}), bf16[8,1024,128]{2,1,0:T(8,128)(2,1)S(1)}, u32[]{:S(2)}, u32[]{:S(2)}) async-start(bf16[8,1024,128]{2,1,0:T(8,128)(2,1)} %bitcast.55), calls=%async_computation | async-start | bytes 4194304 | tf_op jit(solution)/shard_map/all_to_all | solution.py:223
  25.0 0.2 reduce-scatter.2.cloned.1.call-start
  25.3 0.6 add_convert_fusion
  25.9 0.3 fusion.11
  26.2 0.1 copy.20
  26.4 0.8 copy.21
  27.2 0.1 copy.18
  27.3 0.6 pad.9.clone
  27.9 0.1 pad.12.clone
  28.0 1.0 tile.16
  29.0 2.4 %copy.22.cq_ref = f32[512,384]{1,0:T(8,128)} copy(f32[512,384]{0,1:T(8,128)} %bitcast.62) | data formatting | bytes 1572864 | tf_op jit(solution)/shard_map/tile | solution.py:235
  31.4 1.0 tile.18
  32.4 2.3 %copy.23.sq_ref = f32[512,384]{1,0:T(8,128)} copy(f32[512,384]{0,1:T(8,128)} %bitcast.63) | data formatting | bytes 1572864 | tf_op jit(solution)/shard_map/tile | solution.py:236
  34.6 0.9 slice_bitcast_fusion
  35.6 2.2 %copy.24.kt_ref = bf16[2,64,1536]{2,1,0:T(8,128)(2,1)} copy(bf16[2,64,1536]{1,2,0:T(8,128)(2,1)} %slice_bitcast_fusion) | data formatting | bytes 786432 | tf_op jit(solution)/shard_map/transpose | solution.py:255
  37.7 0.1 maximum_maximum_fusion
  37.9 1.1 maximum_maximum_fusion.1
  39.0 0.2 tile.42
  39.2 0.2 tile.40
  39.4 1.1 copy_bitcast_fusion
  40.4 9.5 %all-gather.3.cloned.1.call-done.x_ref = bf16[512,1536]{1,0:T(8,128)(2,1)} async-done(((bf16[128,1536]{1,0:T(8,128)(2,1)}), bf16[512,1536]{1,0:T(8,128)(2,1)}) %all-gather.3.cloned.1.call-update) | async-done | bytes 1572880 | tf_op jit(solution)/shard_map/all_gather | solution.py:227
  50.0 5.1 %shard_map.105 = (bf16[512,384]{1,0:T(8,128)(2,1)}, bf16[2,512,128]{2,1,0:T(8,128)(2,1)}, bf16[2,64,512]{2,1,0:T(8,128)(2,1)}) custom-call(bf16[512,1536]{1,0:T(8,128)(2,1)} %all-gather.3.cloned.1.call-done.x_ref, bf16[1536,384]{1,0:T(8,128)(2,1)} %wq_ref.1, bf16[1536,256]{1,0:T(8,128)(2,1)} %wkv_ref.1, f32[512,384]{1,0:T(8,128)} %copy.22.cq_ref, ...), custom_call_target="tpu_custom_call" | custom-call | flops 1006632960 | bytes 6160384 | tf_op jit(solution)/shard_map/pallas_call | solution.py:74
  55.1 0.0 all-to-all-done
  55.1 15.8 %shard_map.106 = bf16[512,1536]{1,0:T(8,128)(2,1)} custom-call(s32[1]{0:T(128)} %dynamic_slice.3.length_ref, bf16[512,384]{1,0:T(8,128)(2,1)} %get-tuple-element.8.q_ref, bf16[2,64,1536]{2,1,0:T(8,128)(2,1)} %copy.24.kt_ref, bf16[2,1536,128]{2,1,0:T(8,128)(2,1)} %bitcast.59, bf16[2,64,512]{2,1,0:T(8,128)(2,1)} %get-tuple-element.9.ktf_ref, ...), custom_call_target="tpu_custom_call" | custom-call | flops 2214592512 | bytes 4718592 | tf_op jit(solution)/shard_map/pallas_call | solution.py:153
  70.9 0.0 reduce-scatter.2.cloned.1.call-update
  71.6 0.0 slice-start
  72.9 0.6 iota_compare_fusion.2
  73.5 1.4 %pad_select_fusion = bf16[2,2048,128]{2,1,0:T(8,128)(2,1)S(1)} fusion(bf16[2,1536,128]{2,1,0:T(8,128)(2,1)} %bitcast.60, pred[2048]{0:T(1024)(128)(4,1)S(1)} %iota_compare_fusion.2), kind=kLoop, calls=%fused_computation.9 | loop fusion | flops 524288 | bytes 1837056 | tf_op jit(solution)/shard_map/jit(_where)/select_n | solution.py:247
  75.0 0.9 dynamic_update_slice.3
  75.9 0.8 fusion.5
  76.7 0.4 copy.27
  77.1 18.8 %all_to_all.10 = bf16[8,512,128]{2,1,0:T(8,128)(2,1)S(1)} all-to-all(bf16[8,512,128]{2,1,0:T(8,128)(2,1)S(1)} %bitcast.57), channel_id=1, replica_groups=mesh['seq'=8,'dec'=4] {'seq'}, dimensions={0} | all-to-all | bytes 2097152 | tf_op jit(solution)/shard_map/all_to_all | solution.py:269
  95.9 0.3 maximum_bitcast_fusion
  96.2 2.1 %copy.28 = bf16[1,1,3,8,4,128,128]{6,5,4,3,2,1,0:T(8,128)(2,1)} copy(bf16[1,1,3,8,4,128,128]{6,5,4,2,3,1,0:T(8,128)(2,1)S(1)} %maximum_bitcast_fusion) | data formatting | bytes 6291456
  98.3 7.0 %reduce-scatter.2.cloned.1.call-done = bf16[128,1,1536]{2,0,1:T(8,128)(2,1)} async-done(((bf16[512,1,1536]{2,0,1:T(8,128)(2,1)}), bf16[128,1,1536]{2,0,1:T(8,128)(2,1)}) %reduce-scatter.2.cloned.1.call-update) | async-done | bytes 393232 | tf_op jit(solution)/shard_map/reduce_scatter | solution.py:262
  (20 shorter events, 0.1 us)
Async XLA Ops:
  7.2 42.8 %all-gather.3.cloned.1.call-start = ((), (), s32[]{:S(2)}) async-start(), calls=%async_computation.4 | async-start | bytes 1966080 | tf_op jit(solution)/shard_map/all_gather | solution.py:227
  11.5 60.1 %copy-start.2 = (pred[3,32,32]{2,1,0:T(8,128)(4,1)}, pred[3,32,32]{2,1,0:T(8,128)(4,1)S(1)}, u32[]{:S(2)}) copy-start(pred[3,32,32]{2,1,0:T(8,128)(4,1)S(1)} %iota_compare_fusion) | copy-start | bytes 9220
  19.9 35.3 %all-to-all-start = ((bf16[8,1024,128]{2,1,0:T(8,128)(2,1)}), bf16[8,1024,128]{2,1,0:T(8,128)(2,1)S(1)}, u32[]{:S(2)}, u32[]{:S(2)}) async-start(bf16[8,1024,128]{2,1,0:T(8,128)(2,1)} %bitcast.55), calls=%async_computation | async-start | bytes 4194304 | tf_op jit(solution)/shard_map/all_to_all | solution.py:223
  25.0 80.2 %reduce-scatter.2.cloned.1.call-start = ((), (), s32[]{:S(2)}) async-start(), calls=%async_computation.3 | async-start | bytes 1966080 | tf_op jit(solution)/shard_map/reduce_scatter | solution.py:262
  29.0 5.6 %copy-start = (bf16[1,2,1536,128]{3,2,1,0:T(8,128)(2,1)S(1)}, bf16[1,2,1536,128]{3,2,1,0:T(8,128)(2,1)}, u32[]{:S(2)}) copy-start(bf16[1,2,1536,128]{3,2,1,0:T(8,128)(2,1)} %param.15) | copy-start | bytes 2359300
  32.4 5.5 %copy-start.3 = (f32[128]{0:T(128)S(1)}, f32[128]{0:T(128)}, u32[]{:S(2)}) copy-start(f32[128]{0:T(128)} %pad.9.clone) | copy-start | bytes 1540
  70.9 4.1 %copy-start.1 = (bf16[2,512,128]{2,1,0:T(8,128)(2,1)S(1)}, bf16[2,512,128]{2,1,0:T(8,128)(2,1)}, u32[]{:S(2)}) copy-start(bf16[2,512,128]{2,1,0:T(8,128)(2,1)} %get-tuple-element.10.kvf_ref) | copy-start | bytes 786436
  71.6 4.3 %slice-start = ((pred[3,32,32]{2,1,0:T(8,128)(4,1)}), pred[1,32,32]{2,1,0:T(8,128)(4,1)S(1)}, s32[]{:S(2)}) async-start(pred[3,32,32]{2,1,0:T(8,128)(4,1)} %copy-done.2), calls=%async_computation.5 | async-start | bytes 8192 | tf_op jit(solution)/shard_map/slice | solution.py:270
Sparse Core Ops, SparseCore 0:
  10.1 39.7 all-gather.2
  71.0 34.1 reduce-scatter.1

commit v12 on v11

--- a/solution.py
+++ b/solution.py
@@ -108,11 +108,11 @@
     tile_index = pl.program_id(0)
     span, fresh = kt_ref.shape[2], ktf_ref.shape[2]
     pair = 2 * HD
-    slot = lax.broadcasted_iota(jnp.int32, (tile, span), 1)
-    cached_visible = slot < length_ref[0]
+    slot = lax.broadcasted_iota(jnp.int32, (1, span), 1)
+    cached_bias = jnp.where(slot < length_ref[0], 0.0, -jnp.inf).astype(jnp.float32)
     token = lax.broadcasted_iota(jnp.int32, (tile, fresh), 0) + tile_index * tile
     new_slot = lax.broadcasted_iota(jnp.int32, (tile, fresh), 1)
-    fresh_visible = new_slot <= token
+    fresh_bias = jnp.where(new_slot <= token, 0.0, -jnp.inf).astype(jnp.float32)
     lane = lax.broadcasted_iota(jnp.int32, (tile, pair), 1)
     for pair_index in range(q_ref.shape[1] // pair):
         both = q_ref[:, pair_index * pair : (pair_index + 1) * pair]
@@ -120,14 +120,14 @@
         for parity in range(2):
             head = (2 * pair_index + parity) // group
             lined = (both if parity == 0 else pltpu.roll(both, HD, 1))[:, :HD]
-            old = jnp.dot(lined, kt_ref[head], preferred_element_type=jnp.float32) * scale
-            new = jnp.dot(lined, ktf_ref[head], preferred_element_type=jnp.float32) * scale
+            lined = lined * jnp.asarray(scale, lined.dtype)
+            old = jnp.dot(lined, kt_ref[head], preferred_element_type=jnp.float32) + cached_bias
+            new = jnp.dot(lined, ktf_ref[head], preferred_element_type=jnp.float32) + fresh_bias
             row_max = jnp.maximum(
-                jnp.max(jnp.where(cached_visible, old, -jnp.inf), axis=-1, keepdims=True),
-                jnp.max(jnp.where(fresh_visible, new, -jnp.inf), axis=-1, keepdims=True),
+                jnp.max(old, axis=-1, keepdims=True), jnp.max(new, axis=-1, keepdims=True)
             )
-            old_w = jnp.where(cached_visible, jnp.exp(old - row_max), 0.0)
-            new_w = jnp.where(fresh_visible, jnp.exp(new - row_max), 0.0)
+            old_w = jnp.exp(old - row_max)
+            new_w = jnp.exp(new - row_max)
             row_total = jnp.sum(old_w, axis=-1, keepdims=True) + jnp.sum(
                 new_w, axis=-1, keepdims=True
             )

time: 113 us -> 111 us (0.982)
  Pallas kernels: 22.8 us -> 21.5 us
    pallas_call x1, Pallas kernels: 15.8 us -> 14.5 us  [attend(): pl.pallas_call(kernel, out_shape=jax.ShapeDtypeStruct((tokens, model), jn...]
  transfers between devices with their start and end apart: 3 -> 3, of which waited for: 2 -> 2; matrix products, arithmetic and copies ran while one was open for 28% -> 29% of each run, Pallas kernels for 5% -> 5%
where the time goes in v12:
time: 111 us
  local copies, waits for them, and re-layouts  21.8 us (20%)
  Pallas kernels  21.5 us (19%)
  blocking collectives  18.2 us (16%)
  between operations  16.9 us (15%)
  waiting for transfers between devices  16.4 us (15%)
  other arithmetic  6.28 us (6%)
  starting transfers between devices  5.43 us (5%)
  matrix products  4.31 us (4%)
    all_to_all x1, blocking collectives, local(): lax.all_to_all(route_blocks(dispatch[layer_count - 1:], current_rows), 's...  18.2 us
    pallas_call x1, Pallas kernels, attend(): pl.pallas_call(kernel, out_shape=jax.ShapeDtypeStruct((tokens, model), jn...  14.5 us
    all_gather x1, waiting for transfers between devices, local(): portion = lax.all_gather(normed, 'dec', axis=0, tiled=True)  9.55 us
    reduce_scatter x1, waiting for transfers between devices, local(): lax.psum_scatter(product.reshape(NEW_TOK, 1, product.shape[-1]), 'dec', s...  6.8 us
    all_to_all x1, starting transfers between devices, local(): lax.all_to_all(route_blocks(dispatch[:layer_count - 1], earlier_rows), 's...  5.17 us
    pallas_call x1, Pallas kernels, project(): pl.pallas_call(project_kernel, out_shape=(jax.ShapeDtypeStruct((tokens, q...  5.15 us
    dot_general x2, matrix products, route_blocks(): jnp.einsum('locms,msbw->olcbw', spread, block_data, preferred_element_typ...  4.31 us
    another operation x2, local copies, waits for them, and re-layouts, local(): cos_q = jnp.tile(head_cos, (1, query_cols // HD))  3.35 us
  transfers between devices with their start and end apart: 3, of which 2 were waited for; matrix products, arithmetic and copies ran while one was open for 29% of the time, Pallas kernels for 5%

profile of v12, /device:TPU:0, one launch (start us, length us, event | category | flops | bytes accessed | tf_op | source)
XLA Modules:
  0.0 110.8 jit_solution(17139216164321448868)
XLA Ops:
  7.2 0.0 all-gather.3.cloned.1.call-start
  7.2 1.9 %shard_map.104 = bf16[128,1536]{1,0:T(8,128)(2,1)} custom-call(bf16[128,1536]{1,0:T(8,128)(2,1)} %bitcast.67, f32[1536]{0:T(1024)} %gain_ref.1), custom_call_target="tpu_custom_call" | custom-call | flops 786432 | bytes 786432 | tf_op jit(solution)/shard_map/pallas_call | solution.py:187
  9.1 0.0 all-gather.3.cloned.1.call-update
  9.2 0.5 broadcast.59
  9.7 1.3 %reduce.3 = s32[3,2,16]{2,1,0:T(2,128)S(1)} reduce(s32[1,3,2,16,1]{3,4,2,1,0:T(1,128)} %param.17, s32[]{:T(128)} %broadcast.59), dimensions={0,4}, to_apply=%param.17.reduce_sub_computation.3 | reduce | bytes 772 | tf_op args[8]
  11.0 0.1 reshape_squeeze.3
  11.1 0.1 fusion.8
  11.2 0.1 reduce_window_sum.11
  11.3 0.2 select_reduce_fusion
  11.5 1.3 %dynamic_slice.3.length_ref = s32[1]{0:T(128)} dynamic-slice(s32[8]{0:T(128)} %param.11, s32[]{:T(128)S(6)} %select_n.15), dynamic_slice_sizes={1} | dynamic-slice | bytes 12 | tf_op jit(solution)/shard_map/dynamic_slice | solution.py:207
  13.5 0.1 copy.14
  13.6 3.6 %fusion.2 = bf16[8,2,4,128,128]{4,0,2,1,3:T(8,128)(2,1)S(1)} fusion(bf16[2,32,128,128]{3,2,1,0:T(8,128)(2,1)} %bitcast.71, pred[32,128]{0,1:T(8,128)(4,1)S(1)} %copy.14, bf16[2,2]{1,0:T(2,128)(2,1)S(1)} %compare_convert_fusion, bf16[2,8,4,32]{3,1,2,0:T(8,128)(2,1)S(1)} %copy.16), kind=kOutput, calls=%fused_computation.5 | convolution fusion | flops 136331264 | bytes 4202504 | tf_op jit(solution)/shard_map/locms,msbw->olcbw/dot_general | solution.py:37
  17.2 2.7 %copy.17 = bf16[8,2,4,128,128]{4,3,2,1,0:T(8,128)(2,1)} copy(bf16[8,2,4,128,128]{4,0,2,1,3:T(8,128)(2,1)S(1)} %fusion.2) | data formatting | bytes 4194304 | tf_op jit(solution)/shard_map/convert_element_type | solution.py:39
  19.9 5.2 %all-to-all-start = ((bf16[8,1024,128]{2,1,0:T(8,128)(2,1)}), bf16[8,1024,128]{2,1,0:T(8,128)(2,1)S(1)}, u32[]{:S(2)}, u32[]{:S(2)}) async-start(bf16[8,1024,128]{2,1,0:T(8,128)(2,1)} %bitcast.55), calls=%async_computation | async-start | bytes 4194304 | tf_op jit(solution)/shard_map/all_to_all | solution.py:223
  25.0 0.2 reduce-scatter.2.cloned.1.call-start
  25.3 0.6 add_convert_fusion
  25.9 0.3 fusion.11
  26.2 0.1 copy.20
  26.4 0.8 copy.21
  27.2 0.1 copy.18
  27.3 0.6 pad.9.clone
  27.9 0.1 pad.12.clone
  28.0 1.0 tile.16
  29.0 2.4 %copy.22.cq_ref = f32[512,384]{1,0:T(8,128)} copy(f32[512,384]{0,1:T(8,128)} %bitcast.62) | data formatting | bytes 1572864 | tf_op jit(solution)/shard_map/tile | solution.py:235
  31.4 1.0 tile.18
  32.4 2.3 %copy.23.sq_ref = f32[512,384]{1,0:T(8,128)} copy(f32[512,384]{0,1:T(8,128)} %bitcast.63) | data formatting | bytes 1572864 | tf_op jit(solution)/shard_map/tile | solution.py:236
  34.6 0.9 slice_bitcast_fusion
  35.6 2.2 %copy.24.kt_ref = bf16[2,64,1536]{2,1,0:T(8,128)(2,1)} copy(bf16[2,64,1536]{1,2,0:T(8,128)(2,1)} %slice_bitcast_fusion) | data formatting | bytes 786432 | tf_op jit(solution)/shard_map/transpose | solution.py:255
  37.7 0.1 maximum_maximum_fusion
  37.9 1.1 maximum_maximum_fusion.1
  39.0 0.2 tile.42
  39.2 0.2 tile.40
  39.4 1.1 copy_bitcast_fusion
  40.4 9.5 %all-gather.3.cloned.1.call-done.x_ref = bf16[512,1536]{1,0:T(8,128)(2,1)} async-done(((bf16[128,1536]{1,0:T(8,128)(2,1)}), bf16[512,1536]{1,0:T(8,128)(2,1)}) %all-gather.3.cloned.1.call-update) | async-done | bytes 1572880 | tf_op jit(solution)/shard_map/all_gather | solution.py:227
  50.0 5.1 %shard_map.105 = (bf16[512,384]{1,0:T(8,128)(2,1)}, bf16[2,512,128]{2,1,0:T(8,128)(2,1)}, bf16[2,64,512]{2,1,0:T(8,128)(2,1)}) custom-call(bf16[512,1536]{1,0:T(8,128)(2,1)} %all-gather.3.cloned.1.call-done.x_ref, bf16[1536,384]{1,0:T(8,128)(2,1)} %wq_ref.1, bf16[1536,256]{1,0:T(8,128)(2,1)} %wkv_ref.1, f32[512,384]{1,0:T(8,128)} %copy.22.cq_ref, ...), custom_call_target="tpu_custom_call" | custom-call | flops 1006632960 | bytes 6160384 | tf_op jit(solution)/shard_map/pallas_call | solution.py:74
  55.1 0.0 all-to-all-done
  55.1 14.5 %shard_map.106 = bf16[512,1536]{1,0:T(8,128)(2,1)} custom-call(s32[1]{0:T(128)} %dynamic_slice.3.length_ref, bf16[512,384]{1,0:T(8,128)(2,1)} %get-tuple-element.8.q_ref, bf16[2,64,1536]{2,1,0:T(8,128)(2,1)} %copy.24.kt_ref, bf16[2,1536,128]{2,1,0:T(8,128)(2,1)} %bitcast.59, bf16[2,64,512]{2,1,0:T(8,128)(2,1)} %get-tuple-element.9.ktf_ref, ...), custom_call_target="tpu_custom_call" | custom-call | flops 2214592512 | bytes 4718592 | tf_op jit(solution)/shard_map/pallas_call | solution.py:153
  69.6 0.0 reduce-scatter.2.cloned.1.call-update
  70.3 0.0 slice-start
  71.6 0.6 iota_compare_fusion.2
  72.2 1.4 %pad_select_fusion = bf16[2,2048,128]{2,1,0:T(8,128)(2,1)S(1)} fusion(bf16[2,1536,128]{2,1,0:T(8,128)(2,1)} %bitcast.60, pred[2048]{0:T(1024)(128)(4,1)S(1)} %iota_compare_fusion.2), kind=kLoop, calls=%fused_computation.9 | loop fusion | flops 524288 | bytes 1837056 | tf_op jit(solution)/shard_map/jit(_where)/select_n | solution.py:247
  73.7 1.7 %dynamic_update_slice.3 = bf16[2,2048,128]{2,1,0:T(8,128)(2,1)S(1)} dynamic-update-slice(bf16[2,2048,128]{2,1,0:T(8,128)(2,1)S(1)} %pad_select_fusion, bf16[2,512,128]{2,1,0:T(8,128)(2,1)S(1)} %copy-done.1, s32[]{:T(128)} %constant.9.clone.1, s32[]{:T(128)S(6)} %select_n.18, s32[]{:T(128)} %constant.9.clone.1) | dynamic-update-slice | bytes 524292 | tf_op jit(solution)/shard_map/dynamic_update_slice | solution.py:248
  75.4 0.8 fusion.5
  76.2 0.4 copy.27
  76.6 18.2 %all_to_all.10 = bf16[8,512,128]{2,1,0:T(8,128)(2,1)S(1)} all-to-all(bf16[8,512,128]{2,1,0:T(8,128)(2,1)S(1)} %bitcast.57), channel_id=1, replica_groups=mesh['seq'=8,'dec'=4] {'seq'}, dimensions={0} | all-to-all | bytes 2097152 | tf_op jit(solution)/shard_map/all_to_all | solution.py:269
  94.8 0.3 maximum_bitcast_fusion
  95.0 2.1 %copy.28 = bf16[1,1,3,8,4,128,128]{6,5,4,3,2,1,0:T(8,128)(2,1)} copy(bf16[1,1,3,8,4,128,128]{6,5,4,2,3,1,0:T(8,128)(2,1)S(1)} %maximum_bitcast_fusion) | data formatting | bytes 6291456
  97.1 6.8 %reduce-scatter.2.cloned.1.call-done = bf16[128,1,1536]{2,0,1:T(8,128)(2,1)} async-done(((bf16[512,1,1536]{2,0,1:T(8,128)(2,1)}), bf16[128,1,1536]{2,0,1:T(8,128)(2,1)}) %reduce-scatter.2.cloned.1.call-update) | async-done | bytes 393232 | tf_op jit(solution)/shard_map/reduce_scatter | solution.py:262
  (20 shorter events, 0.1 us)
Async XLA Ops:
  7.2 42.8 %all-gather.3.cloned.1.call-start = ((), (), s32[]{:S(2)}) async-start(), calls=%async_computation.4 | async-start | bytes 1966080 | tf_op jit(solution)/shard_map/all_gather | solution.py:227
  11.5 58.8 %copy-start.2 = (pred[3,32,32]{2,1,0:T(8,128)(4,1)}, pred[3,32,32]{2,1,0:T(8,128)(4,1)S(1)}, u32[]{:S(2)}) copy-start(pred[3,32,32]{2,1,0:T(8,128)(4,1)S(1)} %iota_compare_fusion) | copy-start | bytes 9220
  19.9 35.3 %all-to-all-start = ((bf16[8,1024,128]{2,1,0:T(8,128)(2,1)}), bf16[8,1024,128]{2,1,0:T(8,128)(2,1)S(1)}, u32[]{:S(2)}, u32[]{:S(2)}) async-start(bf16[8,1024,128]{2,1,0:T(8,128)(2,1)} %bitcast.55), calls=%async_computation | async-start | bytes 4194304 | tf_op jit(solution)/shard_map/all_to_all | solution.py:223
  25.0 78.9 %reduce-scatter.2.cloned.1.call-start = ((), (), s32[]{:S(2)}) async-start(), calls=%async_computation.3 | async-start | bytes 1966080 | tf_op jit(solution)/shard_map/reduce_scatter | solution.py:262
  29.0 5.6 %copy-start = (bf16[1,2,1536,128]{3,2,1,0:T(8,128)(2,1)S(1)}, bf16[1,2,1536,128]{3,2,1,0:T(8,128)(2,1)}, u32[]{:S(2)}) copy-start(bf16[1,2,1536,128]{3,2,1,0:T(8,128)(2,1)} %param.15) | copy-start | bytes 2359300
  32.4 5.5 %copy-start.3 = (f32[128]{0:T(128)S(1)}, f32[128]{0:T(128)}, u32[]{:S(2)}) copy-start(f32[128]{0:T(128)} %pad.9.clone) | copy-start | bytes 1540
  69.6 4.1 %copy-start.1 = (bf16[2,512,128]{2,1,0:T(8,128)(2,1)S(1)}, bf16[2,512,128]{2,1,0:T(8,128)(2,1)}, u32[]{:S(2)}) copy-start(bf16[2,512,128]{2,1,0:T(8,128)(2,1)} %get-tuple-element.10.kvf_ref) | copy-start | bytes 786436
  70.3 5.1 %slice-start = ((pred[3,32,32]{2,1,0:T(8,128)(4,1)}), pred[1,32,32]{2,1,0:T(8,128)(4,1)S(1)}, s32[]{:S(2)}) async-start(pred[3,32,32]{2,1,0:T(8,128)(4,1)} %copy-done.2), calls=%async_computation.5 | async-start | bytes 8192 | tf_op jit(solution)/shard_map/slice | solution.py:270
Sparse Core Ops, SparseCore 0:
  10.1 39.7 all-gather.2
  69.7 34.1 reduce-scatter.1

commit v13 on v12

--- a/solution.py
+++ b/solution.py
@@ -51,8 +51,12 @@
     return jnp.where(ahead_lane == wanted, ahead, behind)
 
 
-def project_kernel(x_ref, wq_ref, wkv_ref, cq_ref, sq_ref, ckv_ref, skv_ref, q_out, kv_out, kt_out):
-    x = x_ref[...]
+def project_kernel(
+    x_ref, gain_ref, wq_ref, wkv_ref, cq_ref, sq_ref, ckv_ref, skv_ref, q_out, kv_out, kt_out
+):
+    widened = x_ref[...].astype(jnp.float32)
+    scale = lax.rsqrt(jnp.mean(widened * widened, axis=-1, keepdims=True) + EPSILON)
+    x = (widened * scale * gain_ref[...]).astype(jnp.bfloat16)
     query = jnp.dot(x, wq_ref[...], preferred_element_type=jnp.float32)
     q_out[...] = (query * cq_ref[...] + swap_halves(query, HD // 2) * sq_ref[...]).astype(
         q_out.dtype
@@ -66,7 +70,7 @@
         kt_out[head_index] = block[:, :HD].astype(jnp.float32).T.astype(kt_out.dtype)
 
 
-def project(x, w_query, w_keyval, cos_q, sin_q, cos_kv, sin_kv, tile=256):
+def project(x, gain, w_query, w_keyval, cos_q, sin_q, cos_kv, sin_kv, tile=256):
     tokens, depth = x.shape
     q_cols, kv_cols = w_query.shape[1], w_keyval.shape[1]
     heads = kv_cols // (2 * HD)
@@ -81,6 +85,7 @@
         grid=(tokens // tile,),
         in_specs=[
             row_spec(depth),
+            pl.BlockSpec((depth,), lambda i: (0,)),
             pl.BlockSpec((depth, q_cols), lambda i: (0, 0)),
             pl.BlockSpec((depth, kv_cols), lambda i: (0, 0)),
             row_spec(q_cols),
@@ -99,7 +104,7 @@
             bytes_accessed=2 * (x.size + w_query.size + w_keyval.size)
             + 8 * tokens * (q_cols + kv_cols),
         ),
-    )(x, w_query, w_keyval, cos_q, sin_q, cos_kv, sin_kv)
+    )(x, gain, w_query, w_keyval, cos_q, sin_q, cos_kv, sin_kv)
 
 
 def attention_kernel(
@@ -223,8 +228,7 @@
     received_early = lax.all_to_all(
         route_blocks(dispatch[: layer_count - 1], earlier_rows), "seq", 0, 0, tiled=True
     )
-    normed = rms_norm(tokens.reshape(-1, tokens.shape[-1]), norm_gain).reshape(tokens.shape)
-    portion = lax.all_gather(normed, "dec", axis=0, tiled=True)
+    portion = lax.all_gather(tokens, "dec", axis=0, tiled=True)
     flattened = portion.reshape(-1, portion.shape[-1])
     positions = (jnp.arange(NEW_TOK, dtype=jnp.int32) + req_length).astype(jnp.float32)
     inverse_freq = ROPE_BASE ** (-(jnp.arange(0, HD, 2, dtype=jnp.float32) / HD))
@@ -239,7 +243,7 @@
         jnp.concatenate([signed_sine, jnp.zeros_like(signed_sine)], axis=-1), (1, heads_here)
     )
     queries, fresh_rows, fresh_keys_t = project(
-        flattened, w_query, w_keyval, cos_q, sin_q, cos_kv, sin_kv
+        flattened, norm_gain, w_query, w_keyval, cos_q, sin_q, cos_kv, sin_kv
     )
     received_early, queries = lax.optimization_barrier((received_early, queries))
     cached = kv_cache[0]

time: 111 us -> 111 us (level)
  Pallas kernels: 21.5 us -> 19.9 us
  waiting for transfers between devices: 16.4 us -> 17.9 us
    pallas_call x1 -> x0, Pallas kernels: 1.93 us -> none  [rms_norm(): pl.pallas_call(norm_kernel, out_shape=jax.ShapeDtypeStruct(x.shape, jnp.b...]
where the time goes in v13:
time: 111 us; the launch traced here: 110 us
  local copies, waits for them, and re-layouts  21 us (19%)
  Pallas kernels  19.9 us (18%)
  blocking collectives  18.8 us (17%)
  waiting for transfers between devices  17.9 us (16%)
  between operations  16.9 us (15%)
  other arithmetic  6.28 us (6%)
  starting transfers between devices  5.42 us (5%)
  matrix products  4.31 us (4%)
    all_to_all x1, blocking collectives, local(): lax.all_to_all(route_blocks(dispatch[layer_count - 1:], current_rows), 's...  18.8 us
    pallas_call x1, Pallas kernels, attend(): pl.pallas_call(kernel, out_shape=jax.ShapeDtypeStruct((tokens, model), jn...  14.5 us
    all_gather x1, waiting for transfers between devices, local(): portion = lax.all_gather(tokens, 'dec', axis=0, tiled=True)  10.2 us
    reduce_scatter x1, waiting for transfers between devices, local(): lax.psum_scatter(product.reshape(NEW_TOK, 1, product.shape[-1]), 'dec', s...  6.98 us
    pallas_call x1, Pallas kernels, project(): pl.pallas_call(project_kernel, out_shape=(jax.ShapeDtypeStruct((tokens, q...  5.43 us
    all_to_all x1, starting transfers between devices, local(): lax.all_to_all(route_blocks(dispatch[:layer_count - 1], earlier_rows), 's...  5.17 us
    dot_general x2, matrix products, route_blocks(): jnp.einsum('locms,msbw->olcbw', spread, block_data, preferred_element_typ...  4.31 us
    another operation x2, local copies, waits for them, and re-layouts, local(): cos_q = jnp.tile(head_cos, (1, query_cols // HD))  3.35 us
  transfers between devices with their start and end apart: 3, of which 2 were waited for; matrix products, arithmetic and copies ran while one was open for 29% of the time, Pallas kernels for 5%

profile of v13, /device:TPU:0, one launch (start us, length us, event | category | flops | bytes accessed | tf_op | source)
XLA Modules:
  0.0 110.4 jit_solution(15093582736413336611)
XLA Ops:
  7.2 0.0 all-gather.2.cloned.1.call-start
  7.2 0.7 all-gather.2.cloned.1.call-update
  7.9 0.5 broadcast.59
  8.4 1.3 %reduce.3 = s32[3,2,16]{2,1,0:T(2,128)S(1)} reduce(s32[1,3,2,16,1]{3,4,2,1,0:T(1,128)} %param.17, s32[]{:T(128)} %broadcast.59), dimensions={0,4}, to_apply=%param.17.reduce_sub_computation.3 | reduce | bytes 772 | tf_op args[8]
  9.8 0.1 reshape_squeeze.3
  9.8 0.1 fusion.8
  9.9 0.1 reduce_window_sum.11
  10.0 0.2 select_reduce_fusion
  10.3 1.3 %dynamic_slice.3.length_ref = s32[1]{0:T(128)} dynamic-slice(s32[8]{0:T(128)} %param.11, s32[]{:T(128)S(6)} %select_n.15), dynamic_slice_sizes={1} | dynamic-slice | bytes 12 | tf_op jit(solution)/shard_map/dynamic_slice | solution.py:212
  12.2 0.1 copy.14
  12.4 3.6 %fusion.2 = bf16[8,2,4,128,128]{4,0,2,1,3:T(8,128)(2,1)S(1)} fusion(bf16[2,32,128,128]{3,2,1,0:T(8,128)(2,1)} %bitcast.71, pred[32,128]{0,1:T(8,128)(4,1)S(1)} %copy.14, bf16[2,2]{1,0:T(2,128)(2,1)S(1)} %compare_convert_fusion, bf16[2,8,4,32]{3,1,2,0:T(8,128)(2,1)S(1)} %copy.16), kind=kOutput, calls=%fused_computation.5 | convolution fusion | flops 136331264 | bytes 4202504 | tf_op jit(solution)/shard_map/locms,msbw->olcbw/dot_general | solution.py:37
  15.9 2.7 %copy.17 = bf16[8,2,4,128,128]{4,3,2,1,0:T(8,128)(2,1)} copy(bf16[8,2,4,128,128]{4,0,2,1,3:T(8,128)(2,1)S(1)} %fusion.2) | data formatting | bytes 4194304 | tf_op jit(solution)/shard_map/convert_element_type | solution.py:39
  18.6 5.2 %all-to-all-start = ((bf16[8,1024,128]{2,1,0:T(8,128)(2,1)}), bf16[8,1024,128]{2,1,0:T(8,128)(2,1)S(1)}, u32[]{:S(2)}, u32[]{:S(2)}) async-start(bf16[8,1024,128]{2,1,0:T(8,128)(2,1)} %bitcast.55), calls=%async_computation | async-start | bytes 4194304 | tf_op jit(solution)/shard_map/all_to_all | solution.py:228
  23.8 0.2 reduce-scatter.2.cloned.1.call-start
  24.0 0.6 add_convert_fusion
  24.6 0.3 fusion.11
  25.0 0.1 copy.20
  25.1 0.8 copy.21
  25.9 0.1 copy.18
  26.1 0.6 pad.9.clone
  26.7 0.1 pad.12.clone
  26.8 1.0 tile.16
  27.8 2.4 %copy.22.cq_ref = f32[512,384]{1,0:T(8,128)} copy(f32[512,384]{0,1:T(8,128)} %bitcast.62) | data formatting | bytes 1572864 | tf_op jit(solution)/shard_map/tile | solution.py:239
  30.2 1.0 tile.18
  31.2 2.3 %copy.23.sq_ref = f32[512,384]{1,0:T(8,128)} copy(f32[512,384]{0,1:T(8,128)} %bitcast.63) | data formatting | bytes 1572864 | tf_op jit(solution)/shard_map/tile | solution.py:240
  33.5 0.9 slice_bitcast_fusion
  34.4 2.1 %copy.24.kt_ref = bf16[2,64,1536]{2,1,0:T(8,128)(2,1)} copy(bf16[2,64,1536]{1,2,0:T(8,128)(2,1)} %slice_bitcast_fusion) | data formatting | bytes 786432 | tf_op jit(solution)/shard_map/transpose | solution.py:259
  36.5 0.1 maximum_maximum_fusion
  36.7 0.0 copy-done.3
  36.7 1.1 maximum_maximum_fusion.1
  37.8 0.2 tile.42
  38.0 0.2 tile.40
  38.2 1.1 copy_bitcast_fusion
  39.2 10.2 %all-gather.2.cloned.1.call-done = bf16[512,1,1536]{2,0,1:T(8,128)(2,1)} async-done(((bf16[128,1,1536]{2,0,1:T(8,128)(2,1)}), bf16[512,1,1536]{2,0,1:T(8,128)(2,1)}) %all-gather.2.cloned.1.call-update) | async-done | bytes 1572880 | tf_op jit(solution)/shard_map/all_gather | solution.py:231
  49.4 5.4 %shard_map.104 = (bf16[512,384]{1,0:T(8,128)(2,1)}, bf16[2,512,128]{2,1,0:T(8,128)(2,1)}, bf16[2,64,512]{2,1,0:T(8,128)(2,1)}) custom-call(bf16[512,1536]{1,0:T(8,128)(2,1)} %bitcast.67, f32[1536]{0:T(1024)} %gain_ref.1, bf16[1536,384]{1,0:T(8,128)(2,1)} %wq_ref.1, bf16[1536,256]{1,0:T(8,128)(2,1)} %wkv_ref.1, f32[512,384]{1,0:T(8,128)} %copy.22.cq_ref, ...), custom_call_target="tpu_custom_call" | custom-call | flops 1006632960 | bytes 6160384 | tf_op jit(solution)/shard_map/pallas_call | solution.py:78
  54.8 0.0 all-to-all-done
  54.8 14.5 %shard_map.105 = bf16[512,1536]{1,0:T(8,128)(2,1)} custom-call(s32[1]{0:T(128)} %dynamic_slice.3.length_ref, bf16[512,384]{1,0:T(8,128)(2,1)} %get-tuple-element.8.q_ref, bf16[2,64,1536]{2,1,0:T(8,128)(2,1)} %copy.24.kt_ref, bf16[2,1536,128]{2,1,0:T(8,128)(2,1)} %bitcast.59, bf16[2,64,512]{2,1,0:T(8,128)(2,1)} %get-tuple-element.9.ktf_ref, ...), custom_call_target="tpu_custom_call" | custom-call | flops 2214592512 | bytes 4718592 | tf_op jit(solution)/shard_map/pallas_call | solution.py:158
  69.3 0.0 reduce-scatter.2.cloned.1.call-update
  70.0 0.0 slice-start
  71.3 0.6 iota_compare_fusion.2
  71.9 1.4 %pad_select_fusion = bf16[2,2048,128]{2,1,0:T(8,128)(2,1)S(1)} fusion(bf16[2,1536,128]{2,1,0:T(8,128)(2,1)} %bitcast.60, pred[2048]{0:T(1024)(128)(4,1)S(1)} %iota_compare_fusion.2), kind=kLoop, calls=%fused_computation.9 | loop fusion | flops 524288 | bytes 1837056 | tf_op jit(solution)/shard_map/jit(_where)/select_n | solution.py:251
  73.4 0.9 dynamic_update_slice.3
  74.3 0.8 fusion.5
  75.1 0.4 copy.27
  75.5 18.8 %all_to_all.10 = bf16[8,512,128]{2,1,0:T(8,128)(2,1)S(1)} all-to-all(bf16[8,512,128]{2,1,0:T(8,128)(2,1)S(1)} %bitcast.57), channel_id=1, replica_groups=mesh['seq'=8,'dec'=4] {'seq'}, dimensions={0} | all-to-all | bytes 2097152 | tf_op jit(solution)/shard_map/all_to_all | solution.py:273
  94.3 0.3 maximum_bitcast_fusion
  94.5 2.1 %copy.28 = bf16[1,1,3,8,4,128,128]{6,5,4,3,2,1,0:T(8,128)(2,1)} copy(bf16[1,1,3,8,4,128,128]{6,5,4,2,3,1,0:T(8,128)(2,1)S(1)} %maximum_bitcast_fusion) | data formatting | bytes 6291456
  96.6 7.0 %reduce-scatter.2.cloned.1.call-done = bf16[128,1,1536]{2,0,1:T(8,128)(2,1)} async-done(((bf16[512,1,1536]{2,0,1:T(8,128)(2,1)}), bf16[128,1,1536]{2,0,1:T(8,128)(2,1)}) %reduce-scatter.2.cloned.1.call-update) | async-done | bytes 393232 | tf_op jit(solution)/shard_map/reduce_scatter | solution.py:266
  (19 shorter events, 0.1 us)
Async XLA Ops:
  7.2 42.2 %all-gather.2.cloned.1.call-start = ((), (), s32[]{:S(2)}) async-start(), calls=%async_computation.3 | async-start | bytes 1966080 | tf_op jit(solution)/shard_map/all_gather | solution.py:231
  10.2 59.7 %copy-start.2 = (pred[3,32,32]{2,1,0:T(8,128)(4,1)}, pred[3,32,32]{2,1,0:T(8,128)(4,1)S(1)}, u32[]{:S(2)}) copy-start(pred[3,32,32]{2,1,0:T(8,128)(4,1)S(1)} %iota_compare_fusion) | copy-start | bytes 9220
  18.6 36.2 %all-to-all-start = ((bf16[8,1024,128]{2,1,0:T(8,128)(2,1)}), bf16[8,1024,128]{2,1,0:T(8,128)(2,1)S(1)}, u32[]{:S(2)}, u32[]{:S(2)}) async-start(bf16[8,1024,128]{2,1,0:T(8,128)(2,1)} %bitcast.55), calls=%async_computation | async-start | bytes 4194304 | tf_op jit(solution)/shard_map/all_to_all | solution.py:228
  23.8 79.8 %reduce-scatter.2.cloned.1.call-start = ((), (), s32[]{:S(2)}) async-start(), calls=%async_computation.4 | async-start | bytes 1966080 | tf_op jit(solution)/shard_map/reduce_scatter | solution.py:266
  27.8 5.7 %copy-start = (bf16[1,2,1536,128]{3,2,1,0:T(8,128)(2,1)S(1)}, bf16[1,2,1536,128]{3,2,1,0:T(8,128)(2,1)}, u32[]{:S(2)}) copy-start(bf16[1,2,1536,128]{3,2,1,0:T(8,128)(2,1)} %param.15) | copy-start | bytes 2359300
  31.1 5.5 %copy-start.3 = (f32[128]{0:T(128)S(1)}, f32[128]{0:T(128)}, u32[]{:S(2)}) copy-start(f32[128]{0:T(128)} %pad.9.clone) | copy-start | bytes 1540
  69.3 4.1 %copy-start.1 = (bf16[2,512,128]{2,1,0:T(8,128)(2,1)S(1)}, bf16[2,512,128]{2,1,0:T(8,128)(2,1)}, u32[]{:S(2)}) copy-start(bf16[2,512,128]{2,1,0:T(8,128)(2,1)} %get-tuple-element.10.kvf_ref) | copy-start | bytes 786436
  70.0 4.3 %slice-start = ((pred[3,32,32]{2,1,0:T(8,128)(4,1)}), pred[1,32,32]{2,1,0:T(8,128)(4,1)S(1)}, s32[]{:S(2)}) async-start(pred[3,32,32]{2,1,0:T(8,128)(4,1)} %copy-done.2), calls=%async_computation.5 | async-start | bytes 8192 | tf_op jit(solution)/shard_map/slice | solution.py:274
Sparse Core Ops, SparseCore 0:
  9.6 39.7 all-gather.1
  69.4 34.1 reduce-scatter.1

commit v14 on v13

--- a/solution.py
+++ b/solution.py
@@ -70,7 +70,7 @@
         kt_out[head_index] = block[:, :HD].astype(jnp.float32).T.astype(kt_out.dtype)
 
 
-def project(x, gain, w_query, w_keyval, cos_q, sin_q, cos_kv, sin_kv, tile=256):
+def project(x, gain, w_query, w_keyval, cos_q, sin_q, cos_kv, sin_kv, tile=128):
     tokens, depth = x.shape
     q_cols, kv_cols = w_query.shape[1], w_keyval.shape[1]
     heads = kv_cols // (2 * HD)

time: 111 us -> 112 us (level)
  transfers between devices with their start and end apart: 3 -> 3, of which waited for: 2 -> 2; matrix products, arithmetic and copies ran while one was open for 29% -> 28% of each run, Pallas kernels for 5% -> 6%
where the time goes in v14:
time: 112 us; the launch traced here: 111 us
  local copies, waits for them, and re-layouts  20.9 us (19%)
  Pallas kernels  20.7 us (18%)
  blocking collectives  19.2 us (17%)
  waiting for transfers between devices  17.6 us (16%)
  between operations  16.9 us (15%)
  other arithmetic  6.28 us (6%)
  starting transfers between devices  5.42 us (5%)
  matrix products  4.31 us (4%)
    all_to_all x1, blocking collectives, local(): lax.all_to_all(route_blocks(dispatch[layer_count - 1:], current_rows), 's...  19.2 us
    pallas_call x1, Pallas kernels, attend(): pl.pallas_call(kernel, out_shape=jax.ShapeDtypeStruct((tokens, model), jn...  14.5 us
    all_gather x1, waiting for transfers between devices, local(): portion = lax.all_gather(tokens, 'dec', axis=0, tiled=True)  10.2 us
    reduce_scatter x1, waiting for transfers between devices, local(): lax.psum_scatter(product.reshape(NEW_TOK, 1, product.shape[-1]), 'dec', s...  6.69 us
    pallas_call x1, Pallas kernels, project(): pl.pallas_call(project_kernel, out_shape=(jax.ShapeDtypeStruct((tokens, q...  6.26 us
    all_to_all x1, starting transfers between devices, local(): lax.all_to_all(route_blocks(dispatch[:layer_count - 1], earlier_rows), 's...  5.17 us
    dot_general x2, matrix products, route_blocks(): jnp.einsum('locms,msbw->olcbw', spread, block_data, preferred_element_typ...  4.31 us
    another operation x2, local copies, waits for them, and re-layouts, local(): cos_q = jnp.tile(head_cos, (1, query_cols // HD))  3.35 us
  transfers between devices with their start and end apart: 3, of which 2 were waited for; matrix products, arithmetic and copies ran while one was open for 28% of the time, Pallas kernels for 6%

profile of v14, /device:TPU:0, one launch (start us, length us, event | category | flops | bytes accessed | tf_op | source)
XLA Modules:
  0.0 111.3 jit_solution(3220968456290288992)
XLA Ops:
  7.2 0.0 all-gather.2.cloned.1.call-start
  7.2 0.7 all-gather.2.cloned.1.call-update
  7.9 0.5 broadcast.59
  8.4 1.3 %reduce.3 = s32[3,2,16]{2,1,0:T(2,128)S(1)} reduce(s32[1,3,2,16,1]{3,4,2,1,0:T(1,128)} %param.17, s32[]{:T(128)} %broadcast.59), dimensions={0,4}, to_apply=%param.17.reduce_sub_computation.3 | reduce | bytes 772 | tf_op args[8]
  9.8 0.1 reshape_squeeze.3
  9.8 0.1 fusion.8
  9.9 0.1 reduce_window_sum.11
  10.0 0.2 select_reduce_fusion
  10.2 0.0 copy-start.2
  10.3 1.3 %dynamic_slice.3.length_ref = s32[1]{0:T(128)} dynamic-slice(s32[8]{0:T(128)} %param.11, s32[]{:T(128)S(6)} %select_n.15), dynamic_slice_sizes={1} | dynamic-slice | bytes 12 | tf_op jit(solution)/shard_map/dynamic_slice | solution.py:212
  12.2 0.1 copy.14
  12.4 3.6 %fusion.2 = bf16[8,2,4,128,128]{4,0,2,1,3:T(8,128)(2,1)S(1)} fusion(bf16[2,32,128,128]{3,2,1,0:T(8,128)(2,1)} %bitcast.71, pred[32,128]{0,1:T(8,128)(4,1)S(1)} %copy.14, bf16[2,2]{1,0:T(2,128)(2,1)S(1)} %compare_convert_fusion, bf16[2,8,4,32]{3,1,2,0:T(8,128)(2,1)S(1)} %copy.16), kind=kOutput, calls=%fused_computation.5 | convolution fusion | flops 136331264 | bytes 4202504 | tf_op jit(solution)/shard_map/locms,msbw->olcbw/dot_general | solution.py:37
  15.9 2.7 %copy.17 = bf16[8,2,4,128,128]{4,3,2,1,0:T(8,128)(2,1)} copy(bf16[8,2,4,128,128]{4,0,2,1,3:T(8,128)(2,1)S(1)} %fusion.2) | data formatting | bytes 4194304 | tf_op jit(solution)/shard_map/convert_element_type | solution.py:39
  18.6 5.2 %all-to-all-start = ((bf16[8,1024,128]{2,1,0:T(8,128)(2,1)}), bf16[8,1024,128]{2,1,0:T(8,128)(2,1)S(1)}, u32[]{:S(2)}, u32[]{:S(2)}) async-start(bf16[8,1024,128]{2,1,0:T(8,128)(2,1)} %bitcast.55), calls=%async_computation | async-start | bytes 4194304 | tf_op jit(solution)/shard_map/all_to_all | solution.py:228
  23.8 0.2 reduce-scatter.2.cloned.1.call-start
  24.0 0.6 add_convert_fusion
  24.6 0.3 fusion.11
  25.0 0.1 copy.20
  25.1 0.8 copy.21
  25.9 0.1 copy.18
  26.1 0.6 pad.9.clone
  26.7 0.1 pad.12.clone
  26.8 1.0 tile.16
  27.8 2.4 %copy.22.cq_ref = f32[512,384]{1,0:T(8,128)} copy(f32[512,384]{0,1:T(8,128)} %bitcast.62) | data formatting | bytes 1572864 | tf_op jit(solution)/shard_map/tile | solution.py:239
  30.2 1.0 tile.18
  31.2 2.3 %copy.23.sq_ref = f32[512,384]{1,0:T(8,128)} copy(f32[512,384]{0,1:T(8,128)} %bitcast.63) | data formatting | bytes 1572864 | tf_op jit(solution)/shard_map/tile | solution.py:240
  33.5 0.9 slice_bitcast_fusion
  34.4 2.1 %copy.24.kt_ref = bf16[2,64,1536]{2,1,0:T(8,128)(2,1)} copy(bf16[2,64,1536]{1,2,0:T(8,128)(2,1)} %slice_bitcast_fusion) | data formatting | bytes 786432 | tf_op jit(solution)/shard_map/transpose | solution.py:259
  36.5 0.1 maximum_maximum_fusion
  36.7 1.1 maximum_maximum_fusion.1
  37.8 0.2 tile.42
  38.0 0.2 tile.40
  38.2 1.1 copy_bitcast_fusion
  39.2 10.2 %all-gather.2.cloned.1.call-done = bf16[512,1,1536]{2,0,1:T(8,128)(2,1)} async-done(((bf16[128,1,1536]{2,0,1:T(8,128)(2,1)}), bf16[512,1,1536]{2,0,1:T(8,128)(2,1)}) %all-gather.2.cloned.1.call-update) | async-done | bytes 1572880 | tf_op jit(solution)/shard_map/all_gather | solution.py:231
  49.4 6.3 %shard_map.104 = (bf16[512,384]{1,0:T(8,128)(2,1)}, bf16[2,512,128]{2,1,0:T(8,128)(2,1)}, bf16[2,64,512]{2,1,0:T(8,128)(2,1)}) custom-call(bf16[512,1536]{1,0:T(8,128)(2,1)} %bitcast.67, f32[1536]{0:T(1024)} %gain_ref.1, bf16[1536,384]{1,0:T(8,128)(2,1)} %wq_ref.1, bf16[1536,256]{1,0:T(8,128)(2,1)} %wkv_ref.1, f32[512,384]{1,0:T(8,128)} %copy.22.cq_ref, ...), custom_call_target="tpu_custom_call" | custom-call | flops 1006632960 | bytes 6160384 | tf_op jit(solution)/shard_map/pallas_call | solution.py:78
  55.7 0.0 all-to-all-done
  55.7 14.5 %shard_map.105 = bf16[512,1536]{1,0:T(8,128)(2,1)} custom-call(s32[1]{0:T(128)} %dynamic_slice.3.length_ref, bf16[512,384]{1,0:T(8,128)(2,1)} %get-tuple-element.8.q_ref, bf16[2,64,1536]{2,1,0:T(8,128)(2,1)} %copy.24.kt_ref, bf16[2,1536,128]{2,1,0:T(8,128)(2,1)} %bitcast.59, bf16[2,64,512]{2,1,0:T(8,128)(2,1)} %get-tuple-element.9.ktf_ref, ...), custom_call_target="tpu_custom_call" | custom-call | flops 2214592512 | bytes 4718592 | tf_op jit(solution)/shard_map/pallas_call | solution.py:158
  70.1 0.0 reduce-scatter.2.cloned.1.call-update
  70.8 0.0 slice-start
  72.1 0.6 iota_compare_fusion.2
  72.7 1.4 %pad_select_fusion = bf16[2,2048,128]{2,1,0:T(8,128)(2,1)S(1)} fusion(bf16[2,1536,128]{2,1,0:T(8,128)(2,1)} %bitcast.60, pred[2048]{0:T(1024)(128)(4,1)S(1)} %iota_compare_fusion.2), kind=kLoop, calls=%fused_computation.9 | loop fusion | flops 524288 | bytes 1837056 | tf_op jit(solution)/shard_map/jit(_where)/select_n | solution.py:251
  74.2 0.8 dynamic_update_slice.3
  75.0 0.8 fusion.5
  75.8 0.4 copy.27
  76.2 19.2 %all_to_all.10 = bf16[8,512,128]{2,1,0:T(8,128)(2,1)S(1)} all-to-all(bf16[8,512,128]{2,1,0:T(8,128)(2,1)S(1)} %bitcast.57), channel_id=1, replica_groups=mesh['seq'=8,'dec'=4] {'seq'}, dimensions={0} | all-to-all | bytes 2097152 | tf_op jit(solution)/shard_map/all_to_all | solution.py:273
  95.4 0.3 maximum_bitcast_fusion
  95.7 2.1 %copy.28 = bf16[1,1,3,8,4,128,128]{6,5,4,3,2,1,0:T(8,128)(2,1)} copy(bf16[1,1,3,8,4,128,128]{6,5,4,2,3,1,0:T(8,128)(2,1)S(1)} %maximum_bitcast_fusion) | data formatting | bytes 6291456
  97.8 6.7 %reduce-scatter.2.cloned.1.call-done = bf16[128,1,1536]{2,0,1:T(8,128)(2,1)} async-done(((bf16[512,1,1536]{2,0,1:T(8,128)(2,1)}), bf16[128,1,1536]{2,0,1:T(8,128)(2,1)}) %reduce-scatter.2.cloned.1.call-update) | async-done | bytes 393232 | tf_op jit(solution)/shard_map/reduce_scatter | solution.py:266
  (19 shorter events, 0.1 us)
Async XLA Ops:
  7.2 42.2 %all-gather.2.cloned.1.call-start = ((), (), s32[]{:S(2)}) async-start(), calls=%async_computation.3 | async-start | bytes 1966080 | tf_op jit(solution)/shard_map/all_gather | solution.py:231
  10.2 60.6 %copy-start.2 = (pred[3,32,32]{2,1,0:T(8,128)(4,1)}, pred[3,32,32]{2,1,0:T(8,128)(4,1)S(1)}, u32[]{:S(2)}) copy-start(pred[3,32,32]{2,1,0:T(8,128)(4,1)S(1)} %iota_compare_fusion) | copy-start | bytes 9220
  18.6 37.1 %all-to-all-start = ((bf16[8,1024,128]{2,1,0:T(8,128)(2,1)}), bf16[8,1024,128]{2,1,0:T(8,128)(2,1)S(1)}, u32[]{:S(2)}, u32[]{:S(2)}) async-start(bf16[8,1024,128]{2,1,0:T(8,128)(2,1)} %bitcast.55), calls=%async_computation | async-start | bytes 4194304 | tf_op jit(solution)/shard_map/all_to_all | solution.py:228
  23.8 80.7 %reduce-scatter.2.cloned.1.call-start = ((), (), s32[]{:S(2)}) async-start(), calls=%async_computation.4 | async-start | bytes 1966080 | tf_op jit(solution)/shard_map/reduce_scatter | solution.py:266
  27.8 5.7 %copy-start = (bf16[1,2,1536,128]{3,2,1,0:T(8,128)(2,1)S(1)}, bf16[1,2,1536,128]{3,2,1,0:T(8,128)(2,1)}, u32[]{:S(2)}) copy-start(bf16[1,2,1536,128]{3,2,1,0:T(8,128)(2,1)} %param.15) | copy-start | bytes 2359300
  31.1 5.5 %copy-start.3 = (f32[128]{0:T(128)S(1)}, f32[128]{0:T(128)}, u32[]{:S(2)}) copy-start(f32[128]{0:T(128)} %pad.9.clone) | copy-start | bytes 1540
  70.1 4.1 %copy-start.1 = (bf16[2,512,128]{2,1,0:T(8,128)(2,1)S(1)}, bf16[2,512,128]{2,1,0:T(8,128)(2,1)}, u32[]{:S(2)}) copy-start(bf16[2,512,128]{2,1,0:T(8,128)(2,1)} %get-tuple-element.10.kvf_ref) | copy-start | bytes 786436
  70.8 4.2 %slice-start = ((pred[3,32,32]{2,1,0:T(8,128)(4,1)}), pred[1,32,32]{2,1,0:T(8,128)(4,1)S(1)}, s32[]{:S(2)}) async-start(pred[3,32,32]{2,1,0:T(8,128)(4,1)} %copy-done.2), calls=%async_computation.5 | async-start | bytes 8192 | tf_op jit(solution)/shard_map/slice | solution.py:274
Sparse Core Ops, SparseCore 0:
  9.6 39.7 all-gather.1
  70.3 34.1 reduce-scatter.1

commit v15 on v13

--- a/solution.py
+++ b/solution.py
@@ -107,11 +107,9 @@
     )(x, gain, w_query, w_keyval, cos_q, sin_q, cos_kv, sin_kv)
 
 
-def attention_kernel(
-    length_ref, q_ref, kt_ref, kv_ref, ktf_ref, kvf_ref, wo_ref, out_ref, ctx_ref, *, tile, scale, group
-):
-    tile_index = pl.program_id(0)
-    span, fresh = kt_ref.shape[2], ktf_ref.shape[2]
+def attend_tile(length_ref, q_ref, kt_ref, kv_ref, ktf_ref, kvf_ref, ctx_ref, *, tile, scale, group, tile_index):
+    span = kt_ref.shape[2]
+    fresh = min(ktf_ref.shape[2], (tile_index + 1) * tile)
     pair = 2 * HD
     slot = lax.broadcasted_iota(jnp.int32, (1, span), 1)
     cached_bias = jnp.where(slot < length_ref[0], 0.0, -jnp.inf).astype(jnp.float32)
@@ -127,7 +125,7 @@
             lined = (both if parity == 0 else pltpu.roll(both, HD, 1))[:, :HD]
             lined = lined * jnp.asarray(scale, lined.dtype)
             old = jnp.dot(lined, kt_ref[head], preferred_element_type=jnp.float32) + cached_bias
-            new = jnp.dot(lined, ktf_ref[head], preferred_element_type=jnp.float32) + fresh_bias
+            new = jnp.dot(lined, ktf_ref[head][:, :fresh], preferred_element_type=jnp.float32) + fresh_bias
             row_max = jnp.maximum(
                 jnp.max(old, axis=-1, keepdims=True), jnp.max(new, axis=-1, keepdims=True)
             )
@@ -138,11 +136,26 @@
             )
             mixed = jnp.dot(
                 old_w.astype(jnp.bfloat16), kv_ref[head], preferred_element_type=jnp.float32
-            ) + jnp.dot(new_w.astype(jnp.bfloat16), kvf_ref[head], preferred_element_type=jnp.float32)
+            ) + jnp.dot(new_w.astype(jnp.bfloat16), kvf_ref[head][:fresh], preferred_element_type=jnp.float32)
             halves.append((mixed, row_total))
         (even, even_total), (odd, odd_total) = halves
         joined = jnp.where(lane < HD, pltpu.roll(even, HD, 1) / even_total, odd / odd_total)
         ctx_ref[:, pair_index * pair : (pair_index + 1) * pair] = joined.astype(ctx_ref.dtype)
+
+
+def attention_kernel(
+    length_ref, q_ref, kt_ref, kv_ref, ktf_ref, kvf_ref, wo_ref, out_ref, ctx_ref, *, tile, scale, group, q_tiles
+):
+    tile_index = pl.program_id(0)
+    for static_tile in range(q_tiles):
+
+        @pl.when(tile_index == static_tile)
+        def _():
+            attend_tile(
+                length_ref, q_ref, kt_ref, kv_ref, ktf_ref, kvf_ref, ctx_ref,
+                tile=tile, scale=scale, group=group, tile_index=static_tile,
+            )
+
     out_ref[...] = jnp.dot(ctx_ref[...], wo_ref[...], preferred_element_type=jnp.float32).astype(
         out_ref.dtype
     )
@@ -152,7 +165,9 @@
     tokens, q_cols = queries.shape
     span = cache.shape[1] + fresh.shape[1]
     model = w_out.shape[1]
-    kernel = functools.partial(attention_kernel, tile=tile, scale=HD ** (-0.5), group=group)
+    kernel = functools.partial(
+        attention_kernel, tile=tile, scale=HD ** (-0.5), group=group, q_tiles=tokens // tile
+    )
     flops = 4 * tokens * q_cols * span + 2 * tokens * q_cols * model
     whole = lambda shape: pl.BlockSpec(shape, lambda i, n: (0,) * len(shape))
     return pl.pallas_call(

time: 111 us -> 111 us (level)
  no operation moved by 1% of the time
where the time goes in v15:
time: 111 us; the launch traced here: 110 us
  local copies, waits for them, and re-layouts  21.2 us (19%)
  Pallas kernels  19.7 us (18%)
  blocking collectives  18.7 us (17%)
  waiting for transfers between devices  18 us (16%)
  between operations  16.9 us (15%)
  other arithmetic  6.28 us (6%)
  starting transfers between devices  5.24 us (5%)
  matrix products  4.31 us (4%)
    all_to_all x1, blocking collectives, local(): lax.all_to_all(route_blocks(dispatch[layer_count - 1:], current_rows), 's...  18.7 us
    pallas_call x1, Pallas kernels, attend(): pl.pallas_call(kernel, out_shape=jax.ShapeDtypeStruct((tokens, model), jn...  14.3 us
    all_gather x1, waiting for transfers between devices, local(): portion = lax.all_gather(tokens, 'dec', axis=0, tiled=True)  10.4 us
    reduce_scatter x1, waiting for transfers between devices, local(): lax.psum_scatter(product.reshape(NEW_TOK, 1, product.shape[-1]), 'dec', s...  6.97 us
    pallas_call x1, Pallas kernels, project(): pl.pallas_call(project_kernel, out_shape=(jax.ShapeDtypeStruct((tokens, q...  5.42 us
    all_to_all x1, starting transfers between devices, local(): lax.all_to_all(route_blocks(dispatch[:layer_count - 1], earlier_rows), 's...  5.17 us
    dot_general x2, matrix products, route_blocks(): jnp.einsum('locms,msbw->olcbw', spread, block_data, preferred_element_typ...  4.31 us
    another operation x2, local copies, waits for them, and re-layouts, local(): cos_q = jnp.tile(head_cos, (1, query_cols // HD))  3.35 us
  transfers between devices with their start and end apart: 3, of which 2 were waited for; matrix products, arithmetic and copies ran while one was open for 29% of the time, Pallas kernels for 5%

profile of v15, /device:TPU:0, one launch (start us, length us, event | category | flops | bytes accessed | tf_op | source)
XLA Modules:
  0.0 110.3 jit_solution(10202974183574051830)
XLA Ops:
  7.2 0.0 all-gather.2.cloned.1.call-start
  7.2 0.7 all-gather.2.cloned.1.call-update
  7.9 0.5 broadcast.59
  8.4 1.3 %reduce.3 = s32[3,2,16]{2,1,0:T(2,128)S(1)} reduce(s32[1,3,2,16,1]{3,4,2,1,0:T(1,128)} %param.17, s32[]{:T(128)} %broadcast.59), dimensions={0,4}, to_apply=%param.17.reduce_sub_computation.3 | reduce | bytes 772 | tf_op args[8]
  9.8 0.1 reshape_squeeze.3
  9.8 0.1 fusion.8
  9.9 0.1 reduce_window_sum.11
  10.0 0.2 select_reduce_fusion
  10.3 1.3 %dynamic_slice.3.length_ref = s32[1]{0:T(128)} dynamic-slice(s32[8]{0:T(128)} %param.11, s32[]{:T(128)S(6)} %select_n.15), dynamic_slice_sizes={1} | dynamic-slice | bytes 12 | tf_op jit(solution)/shard_map/dynamic_slice | solution.py:227
  12.2 0.1 copy.14
  12.4 3.6 %fusion.2 = bf16[8,2,4,128,128]{4,0,2,1,3:T(8,128)(2,1)S(1)} fusion(bf16[2,32,128,128]{3,2,1,0:T(8,128)(2,1)} %bitcast.71, pred[32,128]{0,1:T(8,128)(4,1)S(1)} %copy.14, bf16[2,2]{1,0:T(2,128)(2,1)S(1)} %compare_convert_fusion, bf16[2,8,4,32]{3,1,2,0:T(8,128)(2,1)S(1)} %copy.16), kind=kOutput, calls=%fused_computation.5 | convolution fusion | flops 136331264 | bytes 4202504 | tf_op jit(solution)/shard_map/locms,msbw->olcbw/dot_general | solution.py:37
  15.9 2.7 %copy.17 = bf16[8,2,4,128,128]{4,3,2,1,0:T(8,128)(2,1)} copy(bf16[8,2,4,128,128]{4,0,2,1,3:T(8,128)(2,1)S(1)} %fusion.2) | data formatting | bytes 4194304 | tf_op jit(solution)/shard_map/convert_element_type | solution.py:39
  18.6 5.2 %all-to-all-start = ((bf16[8,1024,128]{2,1,0:T(8,128)(2,1)}), bf16[8,1024,128]{2,1,0:T(8,128)(2,1)S(1)}, u32[]{:S(2)}, u32[]{:S(2)}) async-start(bf16[8,1024,128]{2,1,0:T(8,128)(2,1)} %bitcast.55), calls=%async_computation | async-start | bytes 4194304 | tf_op jit(solution)/shard_map/all_to_all | solution.py:243
  23.8 0.0 reduce-scatter.2.cloned.1.call-start
  23.8 0.6 add_convert_fusion
  24.5 0.3 fusion.11
  24.8 0.1 copy.20
  24.9 0.8 copy.21
  25.8 0.1 copy.18
  25.9 0.6 pad.9.clone
  26.5 0.1 pad.12.clone
  26.6 1.0 tile.16
  27.6 2.4 %copy.22.cq_ref = f32[512,384]{1,0:T(8,128)} copy(f32[512,384]{0,1:T(8,128)} %bitcast.62) | data formatting | bytes 1572864 | tf_op jit(solution)/shard_map/tile | solution.py:254
  30.0 1.0 tile.18
  31.0 2.3 %copy.23.sq_ref = f32[512,384]{1,0:T(8,128)} copy(f32[512,384]{0,1:T(8,128)} %bitcast.63) | data formatting | bytes 1572864 | tf_op jit(solution)/shard_map/tile | solution.py:255
  33.3 0.9 slice_bitcast_fusion
  34.2 2.1 %copy.24.kt_ref = bf16[2,64,1536]{2,1,0:T(8,128)(2,1)} copy(bf16[2,64,1536]{1,2,0:T(8,128)(2,1)} %slice_bitcast_fusion) | data formatting | bytes 786432 | tf_op jit(solution)/shard_map/transpose | solution.py:274
  36.4 0.1 maximum_maximum_fusion
  36.5 1.1 maximum_maximum_fusion.1
  37.6 0.2 tile.42
  37.8 0.2 tile.40
  38.0 1.1 copy_bitcast_fusion
  39.0 10.4 %all-gather.2.cloned.1.call-done = bf16[512,1,1536]{2,0,1:T(8,128)(2,1)} async-done(((bf16[128,1,1536]{2,0,1:T(8,128)(2,1)}), bf16[512,1,1536]{2,0,1:T(8,128)(2,1)}) %all-gather.2.cloned.1.call-update) | async-done | bytes 1572880 | tf_op jit(solution)/shard_map/all_gather | solution.py:246
  49.4 5.4 %shard_map.104 = (bf16[512,384]{1,0:T(8,128)(2,1)}, bf16[2,512,128]{2,1,0:T(8,128)(2,1)}, bf16[2,64,512]{2,1,0:T(8,128)(2,1)}) custom-call(bf16[512,1536]{1,0:T(8,128)(2,1)} %bitcast.67, f32[1536]{0:T(1024)} %gain_ref.1, bf16[1536,384]{1,0:T(8,128)(2,1)} %wq_ref.1, bf16[1536,256]{1,0:T(8,128)(2,1)} %wkv_ref.1, f32[512,384]{1,0:T(8,128)} %copy.22.cq_ref, ...), custom_call_target="tpu_custom_call" | custom-call | flops 1006632960 | bytes 6160384 | tf_op jit(solution)/shard_map/pallas_call | solution.py:78
  54.8 0.0 all-to-all-done
  54.8 14.3 %shard_map.105 = bf16[512,1536]{1,0:T(8,128)(2,1)} custom-call(s32[1]{0:T(128)} %dynamic_slice.3.length_ref, bf16[512,384]{1,0:T(8,128)(2,1)} %get-tuple-element.8.q_ref, bf16[2,64,1536]{2,1,0:T(8,128)(2,1)} %copy.24.kt_ref, bf16[2,1536,128]{2,1,0:T(8,128)(2,1)} %bitcast.59, bf16[2,64,512]{2,1,0:T(8,128)(2,1)} %get-tuple-element.9.ktf_ref, ...), custom_call_target="tpu_custom_call" | custom-call | flops 2214592512 | bytes 4718592 | tf_op jit(solution)/shard_map/pallas_call | solution.py:173
  69.1 0.0 reduce-scatter.2.cloned.1.call-update
  69.8 0.0 slice-start
  71.1 0.6 iota_compare_fusion.2
  71.7 1.4 %pad_select_fusion = bf16[2,2048,128]{2,1,0:T(8,128)(2,1)S(1)} fusion(bf16[2,1536,128]{2,1,0:T(8,128)(2,1)} %bitcast.60, pred[2048]{0:T(1024)(128)(4,1)S(1)} %iota_compare_fusion.2), kind=kLoop, calls=%fused_computation.9 | loop fusion | flops 524288 | bytes 1837056 | tf_op jit(solution)/shard_map/jit(_where)/select_n | solution.py:266
  73.2 1.1 dynamic_update_slice.3
  74.2 0.0 slice-done
  74.3 0.8 fusion.5
  75.0 0.4 copy.27
  75.4 18.7 %all_to_all.10 = bf16[8,512,128]{2,1,0:T(8,128)(2,1)S(1)} all-to-all(bf16[8,512,128]{2,1,0:T(8,128)(2,1)S(1)} %bitcast.57), channel_id=1, replica_groups=mesh['seq'=8,'dec'=4] {'seq'}, dimensions={0} | all-to-all | bytes 2097152 | tf_op jit(solution)/shard_map/all_to_all | solution.py:288
  94.1 0.3 maximum_bitcast_fusion
  94.4 2.1 %copy.28 = bf16[1,1,3,8,4,128,128]{6,5,4,3,2,1,0:T(8,128)(2,1)} copy(bf16[1,1,3,8,4,128,128]{6,5,4,2,3,1,0:T(8,128)(2,1)S(1)} %maximum_bitcast_fusion) | data formatting | bytes 6291456
  96.5 7.0 %reduce-scatter.2.cloned.1.call-done = bf16[128,1,1536]{2,0,1:T(8,128)(2,1)} async-done(((bf16[512,1,1536]{2,0,1:T(8,128)(2,1)}), bf16[128,1,1536]{2,0,1:T(8,128)(2,1)}) %reduce-scatter.2.cloned.1.call-update) | async-done | bytes 393232 | tf_op jit(solution)/shard_map/reduce_scatter | solution.py:281
  (19 shorter events, 0.1 us)
Async XLA Ops:
  7.2 42.2 %all-gather.2.cloned.1.call-start = ((), (), s32[]{:S(2)}) async-start(), calls=%async_computation.3 | async-start | bytes 1966080 | tf_op jit(solution)/shard_map/all_gather | solution.py:246
  10.2 59.6 %copy-start.2 = (pred[3,32,32]{2,1,0:T(8,128)(4,1)}, pred[3,32,32]{2,1,0:T(8,128)(4,1)S(1)}, u32[]{:S(2)}) copy-start(pred[3,32,32]{2,1,0:T(8,128)(4,1)S(1)} %iota_compare_fusion) | copy-start | bytes 9220
  18.6 36.2 %all-to-all-start = ((bf16[8,1024,128]{2,1,0:T(8,128)(2,1)}), bf16[8,1024,128]{2,1,0:T(8,128)(2,1)S(1)}, u32[]{:S(2)}, u32[]{:S(2)}) async-start(bf16[8,1024,128]{2,1,0:T(8,128)(2,1)} %bitcast.55), calls=%async_computation | async-start | bytes 4194304 | tf_op jit(solution)/shard_map/all_to_all | solution.py:243
  23.8 79.7 %reduce-scatter.2.cloned.1.call-start = ((), (), s32[]{:S(2)}) async-start(), calls=%async_computation.4 | async-start | bytes 1966080 | tf_op jit(solution)/shard_map/reduce_scatter | solution.py:281
  27.6 5.6 %copy-start = (bf16[1,2,1536,128]{3,2,1,0:T(8,128)(2,1)S(1)}, bf16[1,2,1536,128]{3,2,1,0:T(8,128)(2,1)}, u32[]{:S(2)}) copy-start(bf16[1,2,1536,128]{3,2,1,0:T(8,128)(2,1)} %param.15) | copy-start | bytes 2359300
  31.0 5.5 %copy-start.3 = (f32[128]{0:T(128)S(1)}, f32[128]{0:T(128)}, u32[]{:S(2)}) copy-start(f32[128]{0:T(128)} %pad.9.clone) | copy-start | bytes 1540
  69.1 4.1 %copy-start.1 = (bf16[2,512,128]{2,1,0:T(8,128)(2,1)S(1)}, bf16[2,512,128]{2,1,0:T(8,128)(2,1)}, u32[]{:S(2)}) copy-start(bf16[2,512,128]{2,1,0:T(8,128)(2,1)} %get-tuple-element.10.kvf_ref) | copy-start | bytes 786436
  69.8 4.4 %slice-start = ((pred[3,32,32]{2,1,0:T(8,128)(4,1)}), pred[1,32,32]{2,1,0:T(8,128)(4,1)S(1)}, s32[]{:S(2)}) async-start(pred[3,32,32]{2,1,0:T(8,128)(4,1)} %copy-done.2), calls=%async_computation.5 | async-start | bytes 8192 | tf_op jit(solution)/shard_map/slice | solution.py:289
Sparse Core Ops, SparseCore 0:
  9.6 39.7 all-gather.1
  69.3 34.1 reduce-scatter.1

commit v16 on v15

--- a/solution.py
+++ b/solution.py
@@ -70,7 +70,7 @@
         kt_out[head_index] = block[:, :HD].astype(jnp.float32).T.astype(kt_out.dtype)
 
 
-def project(x, gain, w_query, w_keyval, cos_q, sin_q, cos_kv, sin_kv, tile=256):
+def project(x, gain, w_query, w_keyval, cos_q, sin_q, cos_kv, sin_kv, tile=512):
     tokens, depth = x.shape
     q_cols, kv_cols = w_query.shape[1], w_keyval.shape[1]
     heads = kv_cols // (2 * HD)

time: 111 us -> 111 us (level)
  no operation moved by 1% of the time
where the time goes in v16:
time: 111 us
  local copies, waits for them, and re-layouts  21 us (19%)
  Pallas kernels  20.2 us (18%)
  blocking collectives  18.8 us (17%)
  waiting for transfers between devices  18 us (16%)
  between operations  16.9 us (15%)
  other arithmetic  6.28 us (6%)
  starting transfers between devices  5.24 us (5%)
  matrix products  4.31 us (4%)
    all_to_all x1, blocking collectives, local(): lax.all_to_all(route_blocks(dispatch[layer_count - 1:], current_rows), 's...  18.8 us
    pallas_call x1, Pallas kernels, attend(): pl.pallas_call(kernel, out_shape=jax.ShapeDtypeStruct((tokens, model), jn...  14.5 us
    all_gather x1, waiting for transfers between devices, local(): portion = lax.all_gather(tokens, 'dec', axis=0, tiled=True)  10.4 us
    reduce_scatter x1, waiting for transfers between devices, local(): lax.psum_scatter(product.reshape(NEW_TOK, 1, product.shape[-1]), 'dec', s...  6.96 us
    pallas_call x1, Pallas kernels, project(): pl.pallas_call(project_kernel, out_shape=(jax.ShapeDtypeStruct((tokens, q...  5.7 us
    all_to_all x1, starting transfers between devices, local(): lax.all_to_all(route_blocks(dispatch[:layer_count - 1], earlier_rows), 's...  5.17 us
    dot_general x2, matrix products, route_blocks(): jnp.einsum('locms,msbw->olcbw', spread, block_data, preferred_element_typ...  4.31 us
    another operation x2, local copies, waits for them, and re-layouts, local(): cos_q = jnp.tile(head_cos, (1, query_cols // HD))  3.35 us
  transfers between devices with their start and end apart: 3, of which 2 were waited for; matrix products, arithmetic and copies ran while one was open for 29% of the time, Pallas kernels for 5%

profile of v16, /device:TPU:0, one launch (start us, length us, event | category | flops | bytes accessed | tf_op | source)
XLA Modules:
  0.0 110.7 jit_solution(10692455945613938764)
XLA Ops:
  7.2 0.0 all-gather.2.cloned.1.call-start
  7.2 0.7 all-gather.2.cloned.1.call-update
  7.9 0.5 broadcast.59
  8.4 1.3 %reduce.3 = s32[3,2,16]{2,1,0:T(2,128)S(1)} reduce(s32[1,3,2,16,1]{3,4,2,1,0:T(1,128)} %param.17, s32[]{:T(128)} %broadcast.59), dimensions={0,4}, to_apply=%param.17.reduce_sub_computation.3 | reduce | bytes 772 | tf_op args[8]
  9.8 0.1 reshape_squeeze.3
  9.8 0.1 fusion.8
  9.9 0.1 reduce_window_sum.11
  10.0 0.2 select_reduce_fusion
  10.3 1.3 %dynamic_slice.3.length_ref = s32[1]{0:T(128)} dynamic-slice(s32[8]{0:T(128)} %param.11, s32[]{:T(128)S(6)} %select_n.15), dynamic_slice_sizes={1} | dynamic-slice | bytes 12 | tf_op jit(solution)/shard_map/dynamic_slice | solution.py:227
  12.2 0.1 copy.14
  12.4 3.6 %fusion.2 = bf16[8,2,4,128,128]{4,0,2,1,3:T(8,128)(2,1)S(1)} fusion(bf16[2,32,128,128]{3,2,1,0:T(8,128)(2,1)} %bitcast.71, pred[32,128]{0,1:T(8,128)(4,1)S(1)} %copy.14, bf16[2,2]{1,0:T(2,128)(2,1)S(1)} %compare_convert_fusion, bf16[2,8,4,32]{3,1,2,0:T(8,128)(2,1)S(1)} %copy.16), kind=kOutput, calls=%fused_computation.5 | convolution fusion | flops 136331264 | bytes 4202504 | tf_op jit(solution)/shard_map/locms,msbw->olcbw/dot_general | solution.py:37
  15.9 2.7 %copy.17 = bf16[8,2,4,128,128]{4,3,2,1,0:T(8,128)(2,1)} copy(bf16[8,2,4,128,128]{4,0,2,1,3:T(8,128)(2,1)S(1)} %fusion.2) | data formatting | bytes 4194304 | tf_op jit(solution)/shard_map/convert_element_type | solution.py:39
  18.6 5.2 %all-to-all-start = ((bf16[8,1024,128]{2,1,0:T(8,128)(2,1)}), bf16[8,1024,128]{2,1,0:T(8,128)(2,1)S(1)}, u32[]{:S(2)}, u32[]{:S(2)}) async-start(bf16[8,1024,128]{2,1,0:T(8,128)(2,1)} %bitcast.55), calls=%async_computation | async-start | bytes 4194304 | tf_op jit(solution)/shard_map/all_to_all | solution.py:243
  23.8 0.0 reduce-scatter.2.cloned.1.call-start
  23.8 0.6 add_convert_fusion
  24.5 0.3 fusion.11
  24.8 0.1 copy.20
  24.9 0.8 copy.21
  25.8 0.1 copy.18
  25.9 0.6 pad.9.clone
  26.5 0.1 pad.12.clone
  26.6 1.0 tile.16
  27.6 2.4 %copy.22.cq_ref = f32[512,384]{1,0:T(8,128)} copy(f32[512,384]{0,1:T(8,128)} %bitcast.62) | data formatting | bytes 1572864 | tf_op jit(solution)/shard_map/tile | solution.py:254
  30.0 1.0 tile.18
  31.0 2.3 %copy.23.sq_ref = f32[512,384]{1,0:T(8,128)} copy(f32[512,384]{0,1:T(8,128)} %bitcast.63) | data formatting | bytes 1572864 | tf_op jit(solution)/shard_map/tile | solution.py:255
  33.3 0.9 slice_bitcast_fusion
  34.2 2.1 %copy.24.kt_ref = bf16[2,64,1536]{2,1,0:T(8,128)(2,1)} copy(bf16[2,64,1536]{1,2,0:T(8,128)(2,1)} %slice_bitcast_fusion) | data formatting | bytes 786432 | tf_op jit(solution)/shard_map/transpose | solution.py:274
  36.4 0.1 maximum_maximum_fusion
  36.5 1.1 maximum_maximum_fusion.1
  37.6 0.2 tile.42
  37.8 0.2 tile.40
  38.0 1.1 copy_bitcast_fusion
  39.0 10.4 %all-gather.2.cloned.1.call-done = bf16[512,1,1536]{2,0,1:T(8,128)(2,1)} async-done(((bf16[128,1,1536]{2,0,1:T(8,128)(2,1)}), bf16[512,1,1536]{2,0,1:T(8,128)(2,1)}) %all-gather.2.cloned.1.call-update) | async-done | bytes 1572880 | tf_op jit(solution)/shard_map/all_gather | solution.py:246
  49.4 5.7 %shard_map.104 = (bf16[512,384]{1,0:T(8,128)(2,1)}, bf16[2,512,128]{2,1,0:T(8,128)(2,1)}, bf16[2,64,512]{2,1,0:T(8,128)(2,1)}) custom-call(bf16[512,1536]{1,0:T(8,128)(2,1)} %bitcast.67, f32[1536]{0:T(1024)} %gain_ref.1, bf16[1536,384]{1,0:T(8,128)(2,1)} %wq_ref.1, bf16[1536,256]{1,0:T(8,128)(2,1)} %wkv_ref.1, f32[512,384]{1,0:T(8,128)} %copy.22.cq_ref, ...), custom_call_target="tpu_custom_call" | custom-call | flops 1006632960 | bytes 6160384 | tf_op jit(solution)/shard_map/pallas_call | solution.py:78
  55.1 0.0 all-to-all-done
  55.1 14.5 %shard_map.105 = bf16[512,1536]{1,0:T(8,128)(2,1)} custom-call(s32[1]{0:T(128)} %dynamic_slice.3.length_ref, bf16[512,384]{1,0:T(8,128)(2,1)} %get-tuple-element.8.q_ref, bf16[2,64,1536]{2,1,0:T(8,128)(2,1)} %copy.24.kt_ref, bf16[2,1536,128]{2,1,0:T(8,128)(2,1)} %bitcast.59, bf16[2,64,512]{2,1,0:T(8,128)(2,1)} %get-tuple-element.9.ktf_ref, ...), custom_call_target="tpu_custom_call" | custom-call | flops 2214592512 | bytes 4718592 | tf_op jit(solution)/shard_map/pallas_call | solution.py:173
  69.6 0.0 reduce-scatter.2.cloned.1.call-update
  70.3 0.0 copy-done.2
  70.3 0.0 slice-start
  71.6 0.6 iota_compare_fusion.2
  72.2 1.4 %pad_select_fusion = bf16[2,2048,128]{2,1,0:T(8,128)(2,1)S(1)} fusion(bf16[2,1536,128]{2,1,0:T(8,128)(2,1)} %bitcast.60, pred[2048]{0:T(1024)(128)(4,1)S(1)} %iota_compare_fusion.2), kind=kLoop, calls=%fused_computation.9 | loop fusion | flops 524288 | bytes 1837056 | tf_op jit(solution)/shard_map/jit(_where)/select_n | solution.py:266
  73.6 0.9 dynamic_update_slice.3
  74.6 0.8 fusion.5
  75.4 0.4 copy.27
  75.8 18.8 %all_to_all.10 = bf16[8,512,128]{2,1,0:T(8,128)(2,1)S(1)} all-to-all(bf16[8,512,128]{2,1,0:T(8,128)(2,1)S(1)} %bitcast.57), channel_id=1, replica_groups=mesh['seq'=8,'dec'=4] {'seq'}, dimensions={0} | all-to-all | bytes 2097152 | tf_op jit(solution)/shard_map/all_to_all | solution.py:288
  94.6 0.3 maximum_bitcast_fusion
  94.9 2.1 %copy.28 = bf16[1,1,3,8,4,128,128]{6,5,4,3,2,1,0:T(8,128)(2,1)} copy(bf16[1,1,3,8,4,128,128]{6,5,4,2,3,1,0:T(8,128)(2,1)S(1)} %maximum_bitcast_fusion) | data formatting | bytes 6291456
  96.9 7.0 %reduce-scatter.2.cloned.1.call-done = bf16[128,1,1536]{2,0,1:T(8,128)(2,1)} async-done(((bf16[512,1,1536]{2,0,1:T(8,128)(2,1)}), bf16[128,1,1536]{2,0,1:T(8,128)(2,1)}) %reduce-scatter.2.cloned.1.call-update) | async-done | bytes 393232 | tf_op jit(solution)/shard_map/reduce_scatter | solution.py:281
  (19 shorter events, 0.1 us)
Async XLA Ops:
  7.2 42.2 %all-gather.2.cloned.1.call-start = ((), (), s32[]{:S(2)}) async-start(), calls=%async_computation.3 | async-start | bytes 1966080 | tf_op jit(solution)/shard_map/all_gather | solution.py:246
  10.2 60.0 %copy-start.2 = (pred[3,32,32]{2,1,0:T(8,128)(4,1)}, pred[3,32,32]{2,1,0:T(8,128)(4,1)S(1)}, u32[]{:S(2)}) copy-start(pred[3,32,32]{2,1,0:T(8,128)(4,1)S(1)} %iota_compare_fusion) | copy-start | bytes 9220
  18.6 36.5 %all-to-all-start = ((bf16[8,1024,128]{2,1,0:T(8,128)(2,1)}), bf16[8,1024,128]{2,1,0:T(8,128)(2,1)S(1)}, u32[]{:S(2)}, u32[]{:S(2)}) async-start(bf16[8,1024,128]{2,1,0:T(8,128)(2,1)} %bitcast.55), calls=%async_computation | async-start | bytes 4194304 | tf_op jit(solution)/shard_map/all_to_all | solution.py:243
  23.8 80.1 %reduce-scatter.2.cloned.1.call-start = ((), (), s32[]{:S(2)}) async-start(), calls=%async_computation.4 | async-start | bytes 1966080 | tf_op jit(solution)/shard_map/reduce_scatter | solution.py:281
  27.6 5.6 %copy-start = (bf16[1,2,1536,128]{3,2,1,0:T(8,128)(2,1)S(1)}, bf16[1,2,1536,128]{3,2,1,0:T(8,128)(2,1)}, u32[]{:S(2)}) copy-start(bf16[1,2,1536,128]{3,2,1,0:T(8,128)(2,1)} %param.15) | copy-start | bytes 2359300
  31.0 5.5 %copy-start.3 = (f32[128]{0:T(128)S(1)}, f32[128]{0:T(128)}, u32[]{:S(2)}) copy-start(f32[128]{0:T(128)} %pad.9.clone) | copy-start | bytes 1540
  69.6 4.1 %copy-start.1 = (bf16[2,512,128]{2,1,0:T(8,128)(2,1)S(1)}, bf16[2,512,128]{2,1,0:T(8,128)(2,1)}, u32[]{:S(2)}) copy-start(bf16[2,512,128]{2,1,0:T(8,128)(2,1)} %get-tuple-element.10.kvf_ref) | copy-start | bytes 786436
  70.3 4.3 %slice-start = ((pred[3,32,32]{2,1,0:T(8,128)(4,1)}), pred[1,32,32]{2,1,0:T(8,128)(4,1)S(1)}, s32[]{:S(2)}) async-start(pred[3,32,32]{2,1,0:T(8,128)(4,1)} %copy-done.2), calls=%async_computation.5 | async-start | bytes 8192 | tf_op jit(solution)/shard_map/slice | solution.py:289
Sparse Core Ops, SparseCore 0:
  9.6 39.7 all-gather.1
  69.7 34.1 reduce-scatter.1

commit v17 on v15

--- a/solution.py
+++ b/solution.py
@@ -58,11 +58,15 @@
     scale = lax.rsqrt(jnp.mean(widened * widened, axis=-1, keepdims=True) + EPSILON)
     x = (widened * scale * gain_ref[...]).astype(jnp.bfloat16)
     query = jnp.dot(x, wq_ref[...], preferred_element_type=jnp.float32)
-    q_out[...] = (query * cq_ref[...] + swap_halves(query, HD // 2) * sq_ref[...]).astype(
-        q_out.dtype
-    )
+    repeat = lambda ref, cols: jnp.concatenate([ref[...]] * (cols // ref.shape[1]), axis=1)
+    q_cols, kv_cols = query.shape[1], wkv_ref.shape[1]
+    q_out[...] = (
+        query * repeat(cq_ref, q_cols) + swap_halves(query, HD // 2) * repeat(sq_ref, q_cols)
+    ).astype(q_out.dtype)
     key_value = jnp.dot(x, wkv_ref[...], preferred_element_type=jnp.float32)
-    rotated = key_value * ckv_ref[...] + swap_halves(key_value, HD // 2) * skv_ref[...]
+    rotated = key_value * repeat(ckv_ref, kv_cols) + swap_halves(key_value, HD // 2) * repeat(
+        skv_ref, kv_cols
+    )
     width = kv_out.shape[2]
     for head_index in range(kv_out.shape[0]):
         block = rotated[:, head_index * width : (head_index + 1) * width].astype(kv_out.dtype)
@@ -88,10 +92,10 @@
             pl.BlockSpec((depth,), lambda i: (0,)),
             pl.BlockSpec((depth, q_cols), lambda i: (0, 0)),
             pl.BlockSpec((depth, kv_cols), lambda i: (0, 0)),
-            row_spec(q_cols),
-            row_spec(q_cols),
-            row_spec(kv_cols),
-            row_spec(kv_cols),
+            row_spec(cos_q.shape[1]),
+            row_spec(sin_q.shape[1]),
+            row_spec(cos_kv.shape[1]),
+            row_spec(sin_kv.shape[1]),
         ],
         out_specs=(
             row_spec(q_cols),
@@ -102,7 +106,7 @@
             flops=2 * tokens * depth * (q_cols + kv_cols),
             transcendentals=0,
             bytes_accessed=2 * (x.size + w_query.size + w_keyval.size)
-            + 8 * tokens * (q_cols + kv_cols),
+            + 4 * (cos_q.size + sin_q.size + cos_kv.size + sin_kv.size),
         ),
     )(x, gain, w_query, w_keyval, cos_q, sin_q, cos_kv, sin_kv)
 
@@ -251,12 +255,10 @@
     cosine, sine = jnp.cos(angles), jnp.sin(angles)
     signed_sine = jnp.concatenate([-sine, sine], axis=-1)
     head_cos = jnp.concatenate([cosine, cosine], axis=-1)
-    cos_q = jnp.tile(head_cos, (1, query_cols // HD))
-    sin_q = jnp.tile(signed_sine, (1, query_cols // HD))
-    cos_kv = jnp.tile(jnp.concatenate([head_cos, jnp.ones_like(head_cos)], axis=-1), (1, heads_here))
-    sin_kv = jnp.tile(
-        jnp.concatenate([signed_sine, jnp.zeros_like(signed_sine)], axis=-1), (1, heads_here)
-    )
+    cos_q = jnp.concatenate([head_cos, head_cos], axis=-1)
+    sin_q = jnp.concatenate([signed_sine, signed_sine], axis=-1)
+    cos_kv = jnp.concatenate([head_cos, jnp.ones_like(head_cos)], axis=-1)
+    sin_kv = jnp.concatenate([signed_sine, jnp.zeros_like(signed_sine)], axis=-1)
     queries, fresh_rows, fresh_keys_t = project(
         flattened, norm_gain, w_query, w_keyval, cos_q, sin_q, cos_kv, sin_kv
     )

time: 111 us -> 110 us (level)
  local copies, waits for them, and re-layouts: 21.2 us -> 11.4 us
  waiting for transfers between devices: 18 us -> 26.7 us
    all_gather x1, waiting for transfers between devices: 10.4 us -> 19 us  [local(): portion = lax.all_gather(tokens, 'dec', axis=0, tiled=True)]
    another operation x7 -> x0, local copies, waits for them, and re-layouts: 8.05 us -> none  [the longest x2 3.35 us: local(): cos_q = jnp.tile(head_cos, (1, query_cols // HD))]
    unnamed x10 -> x8, local copies, waits for them, and re-layouts: 2.61 us -> 2.61 us
  transfers between devices with their start and end apart: 3 -> 3, of which waited for: 2 -> 2; matrix products, arithmetic and copies ran while one was open for 29% -> 21% of each run, Pallas kernels for 5% -> 5%
where the time goes in v17:
time: 110 us
  waiting for transfers between devices  26.7 us (24%)
  Pallas kernels  19.4 us (18%)
  blocking collectives  18.8 us (17%)
  between operations  16.8 us (15%)
  local copies, waits for them, and re-layouts  11.4 us (10%)
  other arithmetic  7.15 us (6%)
  starting transfers between devices  5.38 us (5%)
  matrix products  4.31 us (4%)
    all_gather x1, waiting for transfers between devices, local(): portion = lax.all_gather(tokens, 'dec', axis=0, tiled=True)  19 us
    all_to_all x1, blocking collectives, local(): lax.all_to_all(route_blocks(dispatch[layer_count - 1:], current_rows), 's...  18.8 us
    pallas_call x1, Pallas kernels, attend(): pl.pallas_call(kernel, out_shape=jax.ShapeDtypeStruct((tokens, model), jn...  14.3 us
    reduce_scatter x1, waiting for transfers between devices, local(): lax.psum_scatter(product.reshape(NEW_TOK, 1, product.shape[-1]), 'dec', s...  6.94 us
    all_to_all x1, starting transfers between devices, local(): lax.all_to_all(route_blocks(dispatch[:layer_count - 1], earlier_rows), 's...  5.3 us
    pallas_call x1, Pallas kernels, project(): pl.pallas_call(project_kernel, out_shape=(jax.ShapeDtypeStruct((tokens, q...  5.12 us
    dot_general x2, matrix products, route_blocks(): jnp.einsum('locms,msbw->olcbw', spread, block_data, preferred_element_typ...  4.31 us
    transpose x2, local copies, waits for them, and re-layouts, local(): jnp.transpose(cached[:, :, :HD], (0, 2, 1))  3.11 us
  transfers between devices with their start and end apart: 3, of which 2 were waited for; matrix products, arithmetic and copies ran while one was open for 21% of the time, Pallas kernels for 5%

profile of v17, /device:TPU:0, one launch (start us, length us, event | category | flops | bytes accessed | tf_op | source)
XLA Modules:
  0.0 110.0 jit_solution(9607781452990030976)
XLA Ops:
  7.2 0.0 all-gather.2.cloned.1.call-start
  7.2 0.7 all-gather.2.cloned.1.call-update
  7.9 1.3 %dynamic_slice.3.length_ref = s32[1]{0:T(128)} dynamic-slice(s32[8]{0:T(128)} %param.11, s32[]{:T(128)S(6)} %select_n.15), dynamic_slice_sizes={1} | dynamic-slice | bytes 12 | tf_op jit(solution)/shard_map/dynamic_slice | solution.py:231
  9.9 0.1 copy.14
  10.0 0.5 broadcast.47
  10.5 1.3 %reduce.3 = s32[3,2,16]{2,1,0:T(2,128)S(1)} reduce(s32[1,3,2,16,1]{3,4,2,1,0:T(1,128)} %param.17, s32[]{:T(128)} %broadcast.47), dimensions={0,4}, to_apply=%param.17.reduce_sub_computation.3 | reduce | bytes 772 | tf_op args[8]
  11.9 0.1 reshape_squeeze.3
  12.0 0.1 fusion.11
  12.0 0.1 reduce_window_sum.11
  12.1 0.2 select_reduce_fusion
  12.4 0.0 copy-start.2
  12.4 3.6 %fusion.2 = bf16[8,2,4,128,128]{4,0,2,1,3:T(8,128)(2,1)S(1)} fusion(bf16[2,32,128,128]{3,2,1,0:T(8,128)(2,1)} %bitcast.59, pred[32,128]{0,1:T(8,128)(4,1)S(1)} %copy.14, bf16[2,2]{1,0:T(2,128)(2,1)S(1)} %compare_convert_fusion, bf16[2,8,4,32]{3,1,2,0:T(8,128)(2,1)S(1)} %copy.16), kind=kOutput, calls=%fused_computation.5 | convolution fusion | flops 136331264 | bytes 4202504 | tf_op jit(solution)/shard_map/locms,msbw->olcbw/dot_general | solution.py:37
  16.0 2.7 %copy.17 = bf16[8,2,4,128,128]{4,3,2,1,0:T(8,128)(2,1)} copy(bf16[8,2,4,128,128]{4,0,2,1,3:T(8,128)(2,1)S(1)} %fusion.2) | data formatting | bytes 4194304 | tf_op jit(solution)/shard_map/convert_element_type | solution.py:39
  18.6 0.0 copy-start
  18.6 5.3 %all-to-all-start = ((bf16[8,1024,128]{2,1,0:T(8,128)(2,1)}), bf16[8,1024,128]{2,1,0:T(8,128)(2,1)S(1)}, u32[]{:S(2)}, u32[]{:S(2)}) async-start(bf16[8,1024,128]{2,1,0:T(8,128)(2,1)} %bitcast.47), calls=%async_computation | async-start | bytes 4194304 | tf_op jit(solution)/shard_map/all_to_all | solution.py:247
  23.9 0.0 reduce-scatter.2.cloned.1.call-start
  24.0 0.1 pad.12.clone
  24.1 0.1 pad.9.clone
  24.2 0.0 copy-done
  24.2 1.0 slice_bitcast_fusion
  25.1 2.2 %copy.18.kt_ref = bf16[2,64,1536]{2,1,0:T(8,128)(2,1)} copy(bf16[2,64,1536]{1,2,0:T(8,128)(2,1)} %slice_bitcast_fusion) | data formatting | bytes 786432 | tf_op jit(solution)/shard_map/transpose | solution.py:276
  27.3 0.6 add_convert_fusion
  27.9 1.0 fusion.10
  28.9 1.4 %fusion.8 = (f32[512,128]{1,0:T(8,128)}, f32[512,128]{1,0:T(8,128)}, f32[512,128]{1,0:T(8,128)}, f32[512,128]{1,0:T(8,128)}) fusion(f32[512,32]{1,0:T(8,128)S(1)} %get-tuple-element.20, f32[128]{0:T(128)S(1)} %pad.12.clone, f32[512,32]{1,0:T(8,128)S(1)} %get-tuple-element.19, f32[512,32]{1,0:T(8,128)S(1)} %get-tuple-element.18, f32[128]{0:T(128)S(1)} %pad.9.clone), kind=kLoop, calls=%fused_computation.16 | loop fusion | flops 524288 | bytes 1246208 | tf_op jit(solution)/shard_map/concatenate | solution.py:260
  30.4 19.0 %all-gather.2.cloned.1.call-done = bf16[512,1,1536]{2,0,1:T(8,128)(2,1)} async-done(((bf16[128,1,1536]{2,0,1:T(8,128)(2,1)}), bf16[512,1,1536]{2,0,1:T(8,128)(2,1)}) %all-gather.2.cloned.1.call-update) | async-done | bytes 1572880 | tf_op jit(solution)/shard_map/all_gather | solution.py:250
  49.4 5.1 %shard_map.104 = (bf16[512,384]{1,0:T(8,128)(2,1)}, bf16[2,512,128]{2,1,0:T(8,128)(2,1)}, bf16[2,64,512]{2,1,0:T(8,128)(2,1)}) custom-call(bf16[512,1536]{1,0:T(8,128)(2,1)} %bitcast.54, f32[1536]{0:T(1024)} %gain_ref.1, bf16[1536,384]{1,0:T(8,128)(2,1)} %wq_ref.1, bf16[1536,256]{1,0:T(8,128)(2,1)} %wkv_ref.1, f32[512,128]{1,0:T(8,128)} %get-tuple-element.17.cq_ref, ...), custom_call_target="tpu_custom_call" | custom-call | flops 1006632960 | bytes 4587520 | tf_op jit(solution)/shard_map/pallas_call | solution.py:82
  54.5 0.0 all-to-all-done
  54.5 14.3 %shard_map.105 = bf16[512,1536]{1,0:T(8,128)(2,1)} custom-call(s32[1]{0:T(128)} %dynamic_slice.3.length_ref, bf16[512,384]{1,0:T(8,128)(2,1)} %get-tuple-element.8.q_ref, bf16[2,64,1536]{2,1,0:T(8,128)(2,1)} %copy.18.kt_ref, bf16[2,1536,128]{2,1,0:T(8,128)(2,1)} %bitcast.51, bf16[2,64,512]{2,1,0:T(8,128)(2,1)} %get-tuple-element.9.ktf_ref, ...), custom_call_target="tpu_custom_call" | custom-call | flops 2214592512 | bytes 4718592 | tf_op jit(solution)/shard_map/pallas_call | solution.py:177
  68.8 0.0 copy-start.1
  68.8 0.0 reduce-scatter.2.cloned.1.call-update
  69.5 0.0 copy-done.2
  69.5 0.0 slice-start
  70.8 0.6 iota_compare_fusion.2
  71.5 1.4 %pad_select_fusion = bf16[2,2048,128]{2,1,0:T(8,128)(2,1)S(1)} fusion(bf16[2,1536,128]{2,1,0:T(8,128)(2,1)} %bitcast.52, pred[2048]{0:T(1024)(128)(4,1)S(1)} %iota_compare_fusion.2), kind=kLoop, calls=%fused_computation.9 | loop fusion | flops 524288 | bytes 1837056 | tf_op jit(solution)/shard_map/jit(_where)/select_n | solution.py:268
  72.9 0.0 copy-done.1
  72.9 0.9 dynamic_update_slice.3
  73.8 0.0 slice-done
  73.9 0.8 fusion.5
  74.6 0.4 copy.21
  75.0 18.8 %all_to_all.10 = bf16[8,512,128]{2,1,0:T(8,128)(2,1)S(1)} all-to-all(bf16[8,512,128]{2,1,0:T(8,128)(2,1)S(1)} %bitcast.49), channel_id=1, replica_groups=mesh['seq'=8,'dec'=4] {'seq'}, dimensions={0} | all-to-all | bytes 2097152 | tf_op jit(solution)/shard_map/all_to_all | solution.py:290
  93.9 0.3 maximum_bitcast_fusion
  94.1 2.1 %copy.22 = bf16[1,1,3,8,4,128,128]{6,5,4,3,2,1,0:T(8,128)(2,1)} copy(bf16[1,1,3,8,4,128,128]{6,5,4,2,3,1,0:T(8,128)(2,1)S(1)} %maximum_bitcast_fusion) | data formatting | bytes 6291456
  96.2 6.9 %reduce-scatter.2.cloned.1.call-done = bf16[128,1,1536]{2,0,1:T(8,128)(2,1)} async-done(((bf16[512,1,1536]{2,0,1:T(8,128)(2,1)}), bf16[128,1,1536]{2,0,1:T(8,128)(2,1)}) %reduce-scatter.2.cloned.1.call-update) | async-done | bytes 393232 | tf_op jit(solution)/shard_map/reduce_scatter | solution.py:283
  (10 shorter events, 0.1 us)
Async XLA Ops:
  7.2 42.2 %all-gather.2.cloned.1.call-start = ((), (), s32[]{:S(2)}) async-start(), calls=%async_computation.3 | async-start | bytes 1966080 | tf_op jit(solution)/shard_map/all_gather | solution.py:250
  12.4 57.2 %copy-start.2 = (pred[3,32,32]{2,1,0:T(8,128)(4,1)}, pred[3,32,32]{2,1,0:T(8,128)(4,1)S(1)}, u32[]{:S(2)}) copy-start(pred[3,32,32]{2,1,0:T(8,128)(4,1)S(1)} %iota_compare_fusion) | copy-start | bytes 9220
  18.6 5.5 %copy-start = (bf16[1,2,1536,128]{3,2,1,0:T(8,128)(2,1)S(1)}, bf16[1,2,1536,128]{3,2,1,0:T(8,128)(2,1)}, u32[]{:S(2)}) copy-start(bf16[1,2,1536,128]{3,2,1,0:T(8,128)(2,1)} %param.15) | copy-start | bytes 2359300
  18.6 35.9 %all-to-all-start = ((bf16[8,1024,128]{2,1,0:T(8,128)(2,1)}), bf16[8,1024,128]{2,1,0:T(8,128)(2,1)S(1)}, u32[]{:S(2)}, u32[]{:S(2)}) async-start(bf16[8,1024,128]{2,1,0:T(8,128)(2,1)} %bitcast.47), calls=%async_computation | async-start | bytes 4194304 | tf_op jit(solution)/shard_map/all_to_all | solution.py:247
  23.9 79.2 %reduce-scatter.2.cloned.1.call-start = ((), (), s32[]{:S(2)}) async-start(), calls=%async_computation.4 | async-start | bytes 1966080 | tf_op jit(solution)/shard_map/reduce_scatter | solution.py:283
  68.8 4.1 %copy-start.1 = (bf16[2,512,128]{2,1,0:T(8,128)(2,1)S(1)}, bf16[2,512,128]{2,1,0:T(8,128)(2,1)}, u32[]{:S(2)}) copy-start(bf16[2,512,128]{2,1,0:T(8,128)(2,1)} %get-tuple-element.10.kvf_ref) | copy-start | bytes 786436
  69.5 4.3 %slice-start = ((pred[3,32,32]{2,1,0:T(8,128)(4,1)}), pred[1,32,32]{2,1,0:T(8,128)(4,1)S(1)}, s32[]{:S(2)}) async-start(pred[3,32,32]{2,1,0:T(8,128)(4,1)} %copy-done.2), calls=%async_computation.5 | async-start | bytes 8192 | tf_op jit(solution)/shard_map/slice | solution.py:291
Sparse Core Ops, SparseCore 0:
  9.6 39.7 all-gather.1
  69.0 34.1 reduce-scatter.1

commit v18 on v17

--- a/solution.py
+++ b/solution.py
@@ -201,6 +201,104 @@
     )(length, queries, keys_t, cache, fresh_keys_t, fresh, w_out)
 
 
+def fused_kernel(
+    length_ref, x_ref, gain_ref, wq_ref, wkv_ref, cq_ref, sq_ref, ckv_ref, skv_ref,
+    kt_ref, kv_ref, wo_ref, out_ref, kv_out, kt_out, ktf_ref, kvf_ref, ctx_ref,
+    *, tile, scale, group, q_tiles
+):
+    tile_index = pl.program_id(0)
+    widened = x_ref[...].astype(jnp.float32)
+    norm_scale = lax.rsqrt(jnp.mean(widened * widened, axis=-1, keepdims=True) + EPSILON)
+    x = (widened * norm_scale * gain_ref[...]).astype(jnp.bfloat16)
+    query = jnp.dot(x, wq_ref[...], preferred_element_type=jnp.float32)
+    repeat = lambda ref, cols: jnp.concatenate([ref[...]] * (cols // ref.shape[1]), axis=1)
+    q_cols, kv_cols = query.shape[1], wkv_ref.shape[1]
+    queries = (
+        query * repeat(cq_ref, q_cols) + swap_halves(query, HD // 2) * repeat(sq_ref, q_cols)
+    ).astype(jnp.bfloat16)
+    key_value = jnp.dot(x, wkv_ref[...], preferred_element_type=jnp.float32)
+    rotated = key_value * repeat(ckv_ref, kv_cols) + swap_halves(key_value, HD // 2) * repeat(
+        skv_ref, kv_cols
+    )
+    width = kv_out.shape[2]
+    start = pl.multiple_of(tile_index * tile, tile)
+    for head_index in range(kv_out.shape[0]):
+        block = rotated[:, head_index * width : (head_index + 1) * width].astype(kv_out.dtype)
+        keys_t = block[:, :HD].astype(jnp.float32).T.astype(kt_out.dtype)
+        kv_out[head_index] = block
+        kt_out[head_index] = keys_t
+        kvf_ref[head_index, pl.ds(start, tile), :] = block
+        ktf_ref[head_index, :, pl.ds(start, tile)] = keys_t
+    for static_tile in range(q_tiles):
+
+        @pl.when(tile_index == static_tile)
+        def _():
+            attend_tile(
+                length_ref, queries, kt_ref, kv_ref, ktf_ref, kvf_ref, ctx_ref,
+                tile=tile, scale=scale, group=group, tile_index=static_tile,
+            )
+
+    out_ref[...] = jnp.dot(ctx_ref[...], wo_ref[...], preferred_element_type=jnp.float32).astype(
+        out_ref.dtype
+    )
+
+
+def project_attend(length, x, gain, w_query, w_keyval, cos_q, sin_q, cos_kv, sin_kv, keys_t, cache, w_out, group, tile=256):
+    tokens, depth = x.shape
+    q_cols, kv_cols = w_query.shape[1], w_keyval.shape[1]
+    heads = kv_cols // (2 * HD)
+    model = w_out.shape[1]
+    span = cache.shape[1] + tokens
+    kernel = functools.partial(
+        fused_kernel, tile=tile, scale=HD ** (-0.5), group=group, q_tiles=tokens // tile
+    )
+    row_spec = lambda cols: pl.BlockSpec((tile, cols), lambda i, n: (i, 0))
+    whole = lambda shape: pl.BlockSpec(shape, lambda i, n: (0,) * len(shape))
+    return pl.pallas_call(
+        kernel,
+        out_shape=(
+            jax.ShapeDtypeStruct((tokens, model), jnp.bfloat16),
+            jax.ShapeDtypeStruct((heads, tokens, 2 * HD), jnp.bfloat16),
+            jax.ShapeDtypeStruct((heads, HD, tokens), jnp.bfloat16),
+        ),
+        grid_spec=pltpu.PrefetchScalarGridSpec(
+            num_scalar_prefetch=1,
+            grid=(tokens // tile,),
+            in_specs=[
+                row_spec(depth),
+                whole(gain.shape),
+                whole(w_query.shape),
+                whole(w_keyval.shape),
+                row_spec(cos_q.shape[1]),
+                row_spec(sin_q.shape[1]),
+                row_spec(cos_kv.shape[1]),
+                row_spec(sin_kv.shape[1]),
+                whole(keys_t.shape),
+                whole(cache.shape),
+                whole(w_out.shape),
+            ],
+            out_specs=(
+                row_spec(model),
+                pl.BlockSpec((heads, tile, 2 * HD), lambda i, n: (0, i, 0)),
+                pl.BlockSpec((heads, HD, tile), lambda i, n: (0, 0, i)),
+            ),
+            scratch_shapes=[
+                pltpu.VMEM((heads, HD, tokens), jnp.bfloat16),
+                pltpu.VMEM((heads, tokens, 2 * HD), jnp.bfloat16),
+                pltpu.VMEM((tile, q_cols), jnp.bfloat16),
+            ],
+        ),
+        cost_estimate=pl.CostEstimate(
+            flops=2 * tokens * depth * (q_cols + kv_cols)
+            + 4 * tokens * q_cols * span
+            + 2 * tokens * q_cols * model,
+            transcendentals=tokens * (q_cols // HD) * span,
+            bytes_accessed=2 * (x.size + w_query.size + w_keyval.size + keys_t.size + cache.size)
+            + 2 * (w_out.size + tokens * model),
+        ),
+    )(length, x, gain, w_query, w_keyval, cos_q, sin_q, cos_kv, sin_kv, keys_t, cache, w_out)
+
+
 def norm_kernel(x_ref, gain_ref, out_ref):
     widened = x_ref[...].astype(jnp.float32)
     scale = lax.rsqrt(jnp.mean(widened * widened, axis=-1, keepdims=True) + EPSILON)
@@ -259,26 +357,28 @@
     sin_q = jnp.concatenate([signed_sine, signed_sine], axis=-1)
     cos_kv = jnp.concatenate([head_cos, jnp.ones_like(head_cos)], axis=-1)
     sin_kv = jnp.concatenate([signed_sine, jnp.zeros_like(signed_sine)], axis=-1)
-    queries, fresh_rows, fresh_keys_t = project(
-        flattened, norm_gain, w_query, w_keyval, cos_q, sin_q, cos_kv, sin_kv
-    )
-    received_early, queries = lax.optimization_barrier((received_early, queries))
     cached = kv_cache[0]
+    group_size = query_cols // HD // heads_here
+    product, fresh_rows, fresh_keys_t = project_attend(
+        req_length.reshape(1),
+        flattened,
+        norm_gain,
+        w_query,
+        w_keyval,
+        cos_q,
+        sin_q,
+        cos_kv,
+        sin_kv,
+        jnp.transpose(cached[:, :, :HD], (0, 2, 1)),
+        cached,
+        w_out,
+        group_size,
+    )
+    received_early, product = lax.optimization_barrier((received_early, product))
     padded = jnp.pad(cached, ((0, 0), (0, span_len - cached.shape[1]), (0, 0)))
     kept_cache = jnp.where((slot_ids < req_length)[None, :, None], padded, jnp.zeros_like(padded))
     assembled = lax.dynamic_update_slice(
         kept_cache, fresh_rows, (zero_index, req_length, zero_index)
-    )
-    group_size = query_cols // HD // heads_here
-    product = attend(
-        req_length.reshape(1),
-        queries,
-        jnp.transpose(cached[:, :, :HD], (0, 2, 1)),
-        cached,
-        fresh_keys_t,
-        fresh_rows,
-        w_out,
-        group_size,
     )
     summed = lax.psum_scatter(
         product.reshape(NEW_TOK, 1, product.shape[-1]),

time: 110 us -> 109 us (level)
  Pallas kernels: 19.4 us -> 17.9 us
    pallas_call x2 -> x1, Pallas kernels: 19.4 us -> 17.9 us  [project_attend(): pl.pallas_call(kernel, out_shape=(jax.ShapeDtypeStruct((tokens, model), j...]
  transfers between devices with their start and end apart: 3 -> 3, of which waited for: 2 -> 2; matrix products, arithmetic and copies ran while one was open for 21% -> 22% of each run, Pallas kernels for 5% -> 17%
where the time goes in v18:
time: 109 us
  waiting for transfers between devices  26.1 us (24%)
  blocking collectives  18.4 us (17%)
  Pallas kernels  17.9 us (16%)
  between operations  17 us (16%)
  local copies, waits for them, and re-layouts  12.2 us (11%)
  other arithmetic  7.26 us (7%)
  starting transfers between devices  5.38 us (5%)
  matrix products  4.31 us (4%)
    all_gather x1, waiting for transfers between devices, local(): portion = lax.all_gather(tokens, 'dec', axis=0, tiled=True)  18.9 us
    all_to_all x1, blocking collectives, local(): lax.all_to_all(route_blocks(dispatch[layer_count - 1:], current_rows), 's...  18.4 us
    pallas_call x1, Pallas kernels, project_attend(): pl.pallas_call(kernel, out_shape=(jax.ShapeDtypeStruct((tokens, model), j...  17.9 us
    reduce_scatter x1, waiting for transfers between devices, local(): lax.psum_scatter(product.reshape(NEW_TOK, 1, product.shape[-1]), 'dec', s...  6.48 us
    all_to_all x1, starting transfers between devices, local(): lax.all_to_all(route_blocks(dispatch[:layer_count - 1], earlier_rows), 's...  5.3 us
    dot_general x2, matrix products, route_blocks(): jnp.einsum('locms,msbw->olcbw', spread, block_data, preferred_element_typ...  4.31 us
    transpose x2, local copies, waits for them, and re-layouts, local(): jnp.transpose(cached[:, :, :HD], (0, 2, 1))  3.1 us
    convert_element_type x2, local copies, waits for them, and re-layouts, route_blocks(): moved_blocks = jnp.einsum('locms,msbw->olcbw', spread, block_data, prefer...  3.08 us
  transfers between devices with their start and end apart: 3, of which 2 were waited for; matrix products, arithmetic and copies ran while one was open for 22% of the time, Pallas kernels for 17%

profile of v18, /device:TPU:0, one launch (start us, length us, event | category | flops | bytes accessed | tf_op | source)
XLA Modules:
  0.0 108.5 jit_solution(3438432579410446318)
XLA Ops:
  7.2 0.0 all-gather.2.cloned.1.call-start
  7.2 0.7 all-gather.2.cloned.1.call-update
  7.9 1.3 %dynamic_slice.3.length_ref = s32[1]{0:T(128)} dynamic-slice(s32[8]{0:T(128)} %param.11, s32[]{:T(128)S(6)} %select_n.15), dynamic_slice_sizes={1} | dynamic-slice | bytes 12 | tf_op jit(solution)/shard_map/dynamic_slice | solution.py:329
  9.9 0.1 copy.14
  10.0 0.5 broadcast.47
  10.6 1.3 %reduce.3 = s32[3,2,16]{2,1,0:T(2,128)S(1)} reduce(s32[1,3,2,16,1]{3,4,2,1,0:T(1,128)} %param.17, s32[]{:T(128)} %broadcast.47), dimensions={0,4}, to_apply=%param.17.reduce_sub_computation.3 | reduce | bytes 772 | tf_op args[8]
  11.9 0.1 reshape_squeeze.3
  12.0 0.1 fusion.11
  12.1 0.1 reduce_window_sum.11
  12.2 0.2 select_reduce_fusion
  12.4 0.0 copy-start.2
  12.4 3.6 %fusion.2 = bf16[8,2,4,128,128]{4,0,2,1,3:T(8,128)(2,1)S(1)} fusion(bf16[2,32,128,128]{3,2,1,0:T(8,128)(2,1)} %bitcast.58, pred[32,128]{0,1:T(8,128)(4,1)S(1)} %copy.14, bf16[2,2]{1,0:T(2,128)(2,1)S(1)} %compare_convert_fusion, bf16[2,8,4,32]{3,1,2,0:T(8,128)(2,1)S(1)} %copy.16), kind=kOutput, calls=%fused_computation.5 | convolution fusion | flops 136331264 | bytes 4202504 | tf_op jit(solution)/shard_map/locms,msbw->olcbw/dot_general | solution.py:37
  16.0 2.7 %copy.17 = bf16[8,2,4,128,128]{4,3,2,1,0:T(8,128)(2,1)} copy(bf16[8,2,4,128,128]{4,0,2,1,3:T(8,128)(2,1)S(1)} %fusion.2) | data formatting | bytes 4194304 | tf_op jit(solution)/shard_map/convert_element_type | solution.py:39
  18.7 0.0 copy-start
  18.7 5.3 %all-to-all-start = ((bf16[8,1024,128]{2,1,0:T(8,128)(2,1)}), bf16[8,1024,128]{2,1,0:T(8,128)(2,1)S(1)}, u32[]{:S(2)}, u32[]{:S(2)}) async-start(bf16[8,1024,128]{2,1,0:T(8,128)(2,1)} %bitcast.47), calls=%async_computation | async-start | bytes 4194304 | tf_op jit(solution)/shard_map/all_to_all | solution.py:345
  24.0 0.0 reduce-scatter.2.cloned.1.call-start
  24.0 0.1 pad.12.clone
  24.1 0.1 pad.9.clone
  24.2 0.0 copy-done
  24.2 1.0 slice_bitcast_fusion
  25.2 2.1 %copy.18.kt_ref = bf16[2,64,1536]{2,1,0:T(8,128)(2,1)} copy(bf16[2,64,1536]{1,2,0:T(8,128)(2,1)} %slice_bitcast_fusion) | data formatting | bytes 786432 | tf_op jit(solution)/shard_map/transpose | solution.py:372
  27.3 0.7 add_convert_fusion
  28.0 1.0 fusion.10
  29.0 1.4 %fusion.8 = (f32[512,128]{1,0:T(8,128)}, f32[512,128]{1,0:T(8,128)}, f32[512,128]{1,0:T(8,128)}, f32[512,128]{1,0:T(8,128)}) fusion(f32[512,32]{1,0:T(8,128)S(1)} %get-tuple-element.18, f32[128]{0:T(128)S(1)} %pad.12.clone, f32[512,32]{1,0:T(8,128)S(1)} %get-tuple-element.17, f32[512,32]{1,0:T(8,128)S(1)} %get-tuple-element.16, f32[128]{0:T(128)S(1)} %pad.9.clone), kind=kLoop, calls=%fused_computation.16 | loop fusion | flops 524288 | bytes 1246208 | tf_op jit(solution)/shard_map/concatenate | solution.py:358
  30.4 18.9 %all-gather.2.cloned.1.call-done = bf16[512,1,1536]{2,0,1:T(8,128)(2,1)} async-done(((bf16[128,1,1536]{2,0,1:T(8,128)(2,1)}), bf16[512,1,1536]{2,0,1:T(8,128)(2,1)}) %all-gather.2.cloned.1.call-update) | async-done | bytes 1572880 | tf_op jit(solution)/shard_map/all_gather | solution.py:348
  49.4 17.9 %shard_map.104 = (bf16[512,1536]{1,0:T(8,128)(2,1)}, bf16[2,512,128]{2,1,0:T(8,128)(2,1)}, bf16[2,64,512]{2,1,0:T(8,128)(2,1)}) custom-call(s32[1]{0:T(128)} %dynamic_slice.3.length_ref, bf16[512,1536]{1,0:T(8,128)(2,1)} %bitcast.59, f32[1536]{0:T(1024)} %gain_ref.1, bf16[1536,384]{1,0:T(8,128)(2,1)} %wq_ref.1, bf16[1536,256]{1,0:T(8,128)(2,1)} %wkv_ref.1, ...), custom_call_target="tpu_custom_call" | custom-call | flops 3221225472 | bytes 7471104 | tf_op jit(solution)/shard_map/pallas_call | solution.py:257
  67.3 0.0 copy-start.1
  67.3 0.0 all-to-all-done
  67.3 0.0 reduce-scatter.2.cloned.1.call-update
  68.1 0.0 copy-done.2
  68.1 0.0 slice-start
  69.4 0.7 iota_compare_fusion.2
  70.1 1.4 %pad_select_fusion = bf16[2,2048,128]{2,1,0:T(8,128)(2,1)S(1)} fusion(bf16[2,1536,128]{2,1,0:T(8,128)(2,1)} %bitcast.52, pred[2048]{0:T(1024)(128)(4,1)S(1)} %iota_compare_fusion.2), kind=kLoop, calls=%fused_computation.9 | loop fusion | flops 524288 | bytes 1837056 | tf_op jit(solution)/shard_map/jit(_where)/select_n | solution.py:379
  71.6 0.0 copy-done.1
  71.6 1.7 %dynamic_update_slice.3 = bf16[2,2048,128]{2,1,0:T(8,128)(2,1)S(1)} dynamic-update-slice(bf16[2,2048,128]{2,1,0:T(8,128)(2,1)S(1)} %pad_select_fusion, bf16[2,512,128]{2,1,0:T(8,128)(2,1)S(1)} %copy-done.1, s32[]{:T(128)} %constant.10.clone.1, s32[]{:T(128)S(6)} %select_n.18, s32[]{:T(128)} %constant.10.clone.1) | dynamic-update-slice | bytes 524292 | tf_op jit(solution)/shard_map/dynamic_update_slice | solution.py:380
  73.3 0.0 slice-done
  73.3 0.8 fusion.5
  74.0 0.4 copy.21
  74.5 18.4 %all_to_all.10 = bf16[8,512,128]{2,1,0:T(8,128)(2,1)S(1)} all-to-all(bf16[8,512,128]{2,1,0:T(8,128)(2,1)S(1)} %bitcast.49), channel_id=1, replica_groups=mesh['seq'=8,'dec'=4] {'seq'}, dimensions={0} | all-to-all | bytes 2097152 | tf_op jit(solution)/shard_map/all_to_all | solution.py:390
  92.8 0.3 maximum_bitcast_fusion
  93.1 2.1 %copy.22 = bf16[1,1,3,8,4,128,128]{6,5,4,3,2,1,0:T(8,128)(2,1)} copy(bf16[1,1,3,8,4,128,128]{6,5,4,2,3,1,0:T(8,128)(2,1)S(1)} %maximum_bitcast_fusion) | data formatting | bytes 6291456
  95.2 6.5 %reduce-scatter.2.cloned.1.call-done = bf16[128,1,1536]{2,0,1:T(8,128)(2,1)} async-done(((bf16[512,1,1536]{2,0,1:T(8,128)(2,1)}), bf16[128,1,1536]{2,0,1:T(8,128)(2,1)}) %reduce-scatter.2.cloned.1.call-update) | async-done | bytes 393232 | tf_op jit(solution)/shard_map/reduce_scatter | solution.py:383
  (10 shorter events, 0.1 us)
Async XLA Ops:
  7.2 42.2 %all-gather.2.cloned.1.call-start = ((), (), s32[]{:S(2)}) async-start(), calls=%async_computation.3 | async-start | bytes 1966080 | tf_op jit(solution)/shard_map/all_gather | solution.py:348
  12.4 55.7 %copy-start.2 = (pred[3,32,32]{2,1,0:T(8,128)(4,1)}, pred[3,32,32]{2,1,0:T(8,128)(4,1)S(1)}, u32[]{:S(2)}) copy-start(pred[3,32,32]{2,1,0:T(8,128)(4,1)S(1)} %iota_compare_fusion) | copy-start | bytes 9220
  18.7 5.5 %copy-start = (bf16[1,2,1536,128]{3,2,1,0:T(8,128)(2,1)S(1)}, bf16[1,2,1536,128]{3,2,1,0:T(8,128)(2,1)}, u32[]{:S(2)}) copy-start(bf16[1,2,1536,128]{3,2,1,0:T(8,128)(2,1)} %param.15) | copy-start | bytes 2359300
  18.7 48.6 %all-to-all-start = ((bf16[8,1024,128]{2,1,0:T(8,128)(2,1)}), bf16[8,1024,128]{2,1,0:T(8,128)(2,1)S(1)}, u32[]{:S(2)}, u32[]{:S(2)}) async-start(bf16[8,1024,128]{2,1,0:T(8,128)(2,1)} %bitcast.47), calls=%async_computation | async-start | bytes 4194304 | tf_op jit(solution)/shard_map/all_to_all | solution.py:345
  24.0 77.7 %reduce-scatter.2.cloned.1.call-start = ((), (), s32[]{:S(2)}) async-start(), calls=%async_computation.4 | async-start | bytes 1966080 | tf_op jit(solution)/shard_map/reduce_scatter | solution.py:383
  67.3 4.3 %copy-start.1 = (bf16[2,512,128]{2,1,0:T(8,128)(2,1)S(1)}, bf16[2,512,128]{2,1,0:T(8,128)(2,1)}, u32[]{:S(2)}) copy-start(bf16[2,512,128]{2,1,0:T(8,128)(2,1)} %get-tuple-element.9) | copy-start | bytes 786436
  68.1 5.2 %slice-start = ((pred[3,32,32]{2,1,0:T(8,128)(4,1)}), pred[1,32,32]{2,1,0:T(8,128)(4,1)S(1)}, s32[]{:S(2)}) async-start(pred[3,32,32]{2,1,0:T(8,128)(4,1)} %copy-done.2), calls=%async_computation.5 | async-start | bytes 8192 | tf_op jit(solution)/shard_map/slice | solution.py:391
Sparse Core Ops, SparseCore 0:
  9.6 39.7 all-gather.1
  67.5 34.1 reduce-scatter.1

commit v19 on v18

--- a/solution.py
+++ b/solution.py
@@ -203,10 +203,23 @@
 
 def fused_kernel(
     length_ref, x_ref, gain_ref, wq_ref, wkv_ref, cq_ref, sq_ref, ckv_ref, skv_ref,
-    kt_ref, kv_ref, wo_ref, out_ref, kv_out, kt_out, ktf_ref, kvf_ref, ctx_ref,
+    kt_hbm, kv_hbm, wo_hbm, out_ref, kv_out, kt_out, ktf_ref, kvf_ref, ctx_ref,
+    kt_ref, kv_ref, wo_ref, sems,
     *, tile, scale, group, q_tiles
 ):
     tile_index = pl.program_id(0)
+    copies = [
+        pltpu.make_async_copy(source, target, sems.at[index])
+        for index, (source, target) in enumerate(
+            ((kt_hbm, kt_ref), (kv_hbm, kv_ref), (wo_hbm, wo_ref))
+        )
+    ]
+
+    @pl.when(tile_index == 0)
+    def _():
+        for copy in copies:
+            copy.start()
+
     widened = x_ref[...].astype(jnp.float32)
     norm_scale = lax.rsqrt(jnp.mean(widened * widened, axis=-1, keepdims=True) + EPSILON)
     x = (widened * norm_scale * gain_ref[...]).astype(jnp.bfloat16)
@@ -229,6 +242,12 @@
         kt_out[head_index] = keys_t
         kvf_ref[head_index, pl.ds(start, tile), :] = block
         ktf_ref[head_index, :, pl.ds(start, tile)] = keys_t
+
+    @pl.when(tile_index == 0)
+    def _():
+        for copy in copies:
+            copy.wait()
+
     for static_tile in range(q_tiles):
 
         @pl.when(tile_index == static_tile)
@@ -273,9 +292,9 @@
                 row_spec(sin_q.shape[1]),
                 row_spec(cos_kv.shape[1]),
                 row_spec(sin_kv.shape[1]),
-                whole(keys_t.shape),
-                whole(cache.shape),
-                whole(w_out.shape),
+                pl.BlockSpec(memory_space=pl.ANY),
+                pl.BlockSpec(memory_space=pl.ANY),
+                pl.BlockSpec(memory_space=pl.ANY),
             ],
             out_specs=(
                 row_spec(model),
@@ -286,6 +305,10 @@
                 pltpu.VMEM((heads, HD, tokens), jnp.bfloat16),
                 pltpu.VMEM((heads, tokens, 2 * HD), jnp.bfloat16),
                 pltpu.VMEM((tile, q_cols), jnp.bfloat16),
+                pltpu.VMEM(keys_t.shape, keys_t.dtype),
+                pltpu.VMEM(cache.shape, cache.dtype),
+                pltpu.VMEM(w_out.shape, w_out.dtype),
+                pltpu.SemaphoreType.DMA((3,)),
             ],
         ),
         cost_estimate=pl.CostEstimate(

time: 109 us -> 110 us (level)
  transfers between devices with their start and end apart: 3 -> 3, of which waited for: 2 -> 2; matrix products, arithmetic and copies ran while one was open for 22% -> 21% of each run, Pallas kernels for 17% -> 17%
where the time goes in v19:
time: 110 us; the launch traced here: 109 us
  waiting for transfers between devices  26 us (24%)
  blocking collectives  19.3 us (18%)
  Pallas kernels  18.6 us (17%)
  between operations  17 us (15%)
  local copies, waits for them, and re-layouts  11.4 us (10%)
  other arithmetic  7.26 us (7%)
  starting transfers between devices  5.38 us (5%)
  matrix products  4.31 us (4%)
    all_to_all x1, blocking collectives, local(): lax.all_to_all(route_blocks(dispatch[layer_count - 1:], current_rows), 's...  19.3 us
    all_gather x1, waiting for transfers between devices, local(): portion = lax.all_gather(tokens, 'dec', axis=0, tiled=True)  18.9 us
    pallas_call x1, Pallas kernels, project_attend(): pl.pallas_call(kernel, out_shape=(jax.ShapeDtypeStruct((tokens, model), j...  18.6 us
    reduce_scatter x1, waiting for transfers between devices, local(): lax.psum_scatter(product.reshape(NEW_TOK, 1, product.shape[-1]), 'dec', s...  6.31 us
    all_to_all x1, starting transfers between devices, local(): lax.all_to_all(route_blocks(dispatch[:layer_count - 1], earlier_rows), 's...  5.3 us
    dot_general x2, matrix products, route_blocks(): jnp.einsum('locms,msbw->olcbw', spread, block_data, preferred_element_typ...  4.31 us
    transpose x2, local copies, waits for them, and re-layouts, local(): jnp.transpose(cached[:, :, :HD], (0, 2, 1))  3.1 us
    convert_element_type x2, local copies, waits for them, and re-layouts, route_blocks(): moved_blocks = jnp.einsum('locms,msbw->olcbw', spread, block_data, prefer...  3.08 us
  transfers between devices with their start and end apart: 3, of which 2 were waited for; matrix products, arithmetic and copies ran while one was open for 21% of the time, Pallas kernels for 17%

profile of v19, /device:TPU:0, one launch (start us, length us, event | category | flops | bytes accessed | tf_op | source)
XLA Modules:
  0.0 109.2 jit_solution(13353776140095430109)
XLA Ops:
  7.2 0.0 all-gather.2.cloned.1.call-start
  7.2 0.7 all-gather.2.cloned.1.call-update
  7.9 1.3 %dynamic_slice.3.length_ref = s32[1]{0:T(128)} dynamic-slice(s32[8]{0:T(128)} %param.11, s32[]{:T(128)S(6)} %select_n.15), dynamic_slice_sizes={1} | dynamic-slice | bytes 12 | tf_op jit(solution)/shard_map/dynamic_slice | solution.py:352
  9.9 0.1 copy.14
  10.0 0.5 broadcast.47
  10.6 1.3 %reduce.3 = s32[3,2,16]{2,1,0:T(2,128)S(1)} reduce(s32[1,3,2,16,1]{3,4,2,1,0:T(1,128)} %param.17, s32[]{:T(128)} %broadcast.47), dimensions={0,4}, to_apply=%param.17.reduce_sub_computation.3 | reduce | bytes 772 | tf_op args[8]
  11.9 0.1 reshape_squeeze.3
  12.0 0.1 fusion.11
  12.1 0.1 reduce_window_sum.11
  12.2 0.2 select_reduce_fusion
  12.4 0.0 copy-start.2
  12.4 3.6 %fusion.2 = bf16[8,2,4,128,128]{4,0,2,1,3:T(8,128)(2,1)S(1)} fusion(bf16[2,32,128,128]{3,2,1,0:T(8,128)(2,1)} %bitcast.58, pred[32,128]{0,1:T(8,128)(4,1)S(1)} %copy.14, bf16[2,2]{1,0:T(2,128)(2,1)S(1)} %compare_convert_fusion, bf16[2,8,4,32]{3,1,2,0:T(8,128)(2,1)S(1)} %copy.16), kind=kOutput, calls=%fused_computation.5 | convolution fusion | flops 136331264 | bytes 4202504 | tf_op jit(solution)/shard_map/locms,msbw->olcbw/dot_general | solution.py:37
  16.0 2.7 %copy.17 = bf16[8,2,4,128,128]{4,3,2,1,0:T(8,128)(2,1)} copy(bf16[8,2,4,128,128]{4,0,2,1,3:T(8,128)(2,1)S(1)} %fusion.2) | data formatting | bytes 4194304 | tf_op jit(solution)/shard_map/convert_element_type | solution.py:39
  18.7 0.0 copy-start
  18.7 5.3 %all-to-all-start = ((bf16[8,1024,128]{2,1,0:T(8,128)(2,1)}), bf16[8,1024,128]{2,1,0:T(8,128)(2,1)S(1)}, u32[]{:S(2)}, u32[]{:S(2)}) async-start(bf16[8,1024,128]{2,1,0:T(8,128)(2,1)} %bitcast.47), calls=%async_computation | async-start | bytes 4194304 | tf_op jit(solution)/shard_map/all_to_all | solution.py:368
  24.0 0.0 reduce-scatter.2.cloned.1.call-start
  24.0 0.1 pad.12.clone
  24.1 0.1 pad.9.clone
  24.2 0.0 copy-done
  24.2 1.0 slice_bitcast_fusion
  25.2 2.1 %copy.18.kt_hbm = bf16[2,64,1536]{2,1,0:T(8,128)(2,1)} copy(bf16[2,64,1536]{1,2,0:T(8,128)(2,1)} %slice_bitcast_fusion) | data formatting | bytes 786432 | tf_op jit(solution)/shard_map/transpose | solution.py:395
  27.3 0.7 add_convert_fusion
  28.0 1.0 fusion.10
  29.0 1.4 %fusion.8 = (f32[512,128]{1,0:T(8,128)}, f32[512,128]{1,0:T(8,128)}, f32[512,128]{1,0:T(8,128)}, f32[512,128]{1,0:T(8,128)}) fusion(f32[512,32]{1,0:T(8,128)S(1)} %get-tuple-element.18, f32[128]{0:T(128)S(1)} %pad.12.clone, f32[512,32]{1,0:T(8,128)S(1)} %get-tuple-element.17, f32[512,32]{1,0:T(8,128)S(1)} %get-tuple-element.16, f32[128]{0:T(128)S(1)} %pad.9.clone), kind=kLoop, calls=%fused_computation.16 | loop fusion | flops 524288 | bytes 1246208 | tf_op jit(solution)/shard_map/concatenate | solution.py:381
  30.4 18.9 %all-gather.2.cloned.1.call-done = bf16[512,1,1536]{2,0,1:T(8,128)(2,1)} async-done(((bf16[128,1,1536]{2,0,1:T(8,128)(2,1)}), bf16[512,1,1536]{2,0,1:T(8,128)(2,1)}) %all-gather.2.cloned.1.call-update) | async-done | bytes 1572880 | tf_op jit(solution)/shard_map/all_gather | solution.py:371
  49.4 18.6 %shard_map.104 = (bf16[512,1536]{1,0:T(8,128)(2,1)}, bf16[2,512,128]{2,1,0:T(8,128)(2,1)}, bf16[2,64,512]{2,1,0:T(8,128)(2,1)}) custom-call(s32[1]{0:T(128)} %dynamic_slice.3.length_ref, bf16[512,1536]{1,0:T(8,128)(2,1)} %bitcast.59, f32[1536]{0:T(1024)} %gain_ref.1, bf16[1536,384]{1,0:T(8,128)(2,1)} %wq_ref.1, bf16[1536,256]{1,0:T(8,128)(2,1)} %wkv_ref.1, ...), custom_call_target="tpu_custom_call" | custom-call | flops 3221225472 | bytes 7471104 | tf_op jit(solution)/shard_map/pallas_call | solution.py:276
  68.0 0.0 copy-start.1
  68.0 0.0 all-to-all-done
  68.0 0.0 reduce-scatter.2.cloned.1.call-update
  68.7 0.0 copy-done.2
  68.8 0.0 slice-start
  70.1 0.7 iota_compare_fusion.2
  70.8 1.4 %pad_select_fusion = bf16[2,2048,128]{2,1,0:T(8,128)(2,1)S(1)} fusion(bf16[2,1536,128]{2,1,0:T(8,128)(2,1)} %bitcast.52, pred[2048]{0:T(1024)(128)(4,1)S(1)} %iota_compare_fusion.2), kind=kLoop, calls=%fused_computation.9 | loop fusion | flops 524288 | bytes 1837056 | tf_op jit(solution)/shard_map/jit(_where)/select_n | solution.py:402
  72.3 0.0 copy-done.1
  72.3 0.9 dynamic_update_slice.3
  73.2 0.0 slice-done
  73.2 0.8 fusion.5
  74.0 0.4 copy.21
  74.4 19.3 %all_to_all.10 = bf16[8,512,128]{2,1,0:T(8,128)(2,1)S(1)} all-to-all(bf16[8,512,128]{2,1,0:T(8,128)(2,1)S(1)} %bitcast.49), channel_id=1, replica_groups=mesh['seq'=8,'dec'=4] {'seq'}, dimensions={0} | all-to-all | bytes 2097152 | tf_op jit(solution)/shard_map/all_to_all | solution.py:413
  93.7 0.3 maximum_bitcast_fusion
  93.9 2.1 %copy.22 = bf16[1,1,3,8,4,128,128]{6,5,4,3,2,1,0:T(8,128)(2,1)} copy(bf16[1,1,3,8,4,128,128]{6,5,4,2,3,1,0:T(8,128)(2,1)S(1)} %maximum_bitcast_fusion) | data formatting | bytes 6291456
  96.0 6.3 %reduce-scatter.2.cloned.1.call-done = bf16[128,1,1536]{2,0,1:T(8,128)(2,1)} async-done(((bf16[512,1,1536]{2,0,1:T(8,128)(2,1)}), bf16[128,1,1536]{2,0,1:T(8,128)(2,1)}) %reduce-scatter.2.cloned.1.call-update) | async-done | bytes 393232 | tf_op jit(solution)/shard_map/reduce_scatter | solution.py:406
  (10 shorter events, 0.1 us)
Async XLA Ops:
  7.2 42.2 %all-gather.2.cloned.1.call-start = ((), (), s32[]{:S(2)}) async-start(), calls=%async_computation.3 | async-start | bytes 1966080 | tf_op jit(solution)/shard_map/all_gather | solution.py:371
  12.4 56.4 %copy-start.2 = (pred[3,32,32]{2,1,0:T(8,128)(4,1)}, pred[3,32,32]{2,1,0:T(8,128)(4,1)S(1)}, u32[]{:S(2)}) copy-start(pred[3,32,32]{2,1,0:T(8,128)(4,1)S(1)} %iota_compare_fusion) | copy-start | bytes 9220
  18.7 5.5 %copy-start = (bf16[1,2,1536,128]{3,2,1,0:T(8,128)(2,1)S(1)}, bf16[1,2,1536,128]{3,2,1,0:T(8,128)(2,1)}, u32[]{:S(2)}) copy-start(bf16[1,2,1536,128]{3,2,1,0:T(8,128)(2,1)} %param.15) | copy-start | bytes 2359300
  18.7 49.3 %all-to-all-start = ((bf16[8,1024,128]{2,1,0:T(8,128)(2,1)}), bf16[8,1024,128]{2,1,0:T(8,128)(2,1)S(1)}, u32[]{:S(2)}, u32[]{:S(2)}) async-start(bf16[8,1024,128]{2,1,0:T(8,128)(2,1)} %bitcast.47), calls=%async_computation | async-start | bytes 4194304 | tf_op jit(solution)/shard_map/all_to_all | solution.py:368
  24.0 78.3 %reduce-scatter.2.cloned.1.call-start = ((), (), s32[]{:S(2)}) async-start(), calls=%async_computation.4 | async-start | bytes 1966080 | tf_op jit(solution)/shard_map/reduce_scatter | solution.py:406
  68.0 4.3 %copy-start.1 = (bf16[2,512,128]{2,1,0:T(8,128)(2,1)S(1)}, bf16[2,512,128]{2,1,0:T(8,128)(2,1)}, u32[]{:S(2)}) copy-start(bf16[2,512,128]{2,1,0:T(8,128)(2,1)} %get-tuple-element.9) | copy-start | bytes 786436
  68.8 4.4 %slice-start = ((pred[3,32,32]{2,1,0:T(8,128)(4,1)}), pred[1,32,32]{2,1,0:T(8,128)(4,1)S(1)}, s32[]{:S(2)}) async-start(pred[3,32,32]{2,1,0:T(8,128)(4,1)} %copy-done.2), calls=%async_computation.5 | async-start | bytes 8192 | tf_op jit(solution)/shard_map/slice | solution.py:414
Sparse Core Ops, SparseCore 0:
  9.6 39.7 all-gather.1
  68.1 34.1 reduce-scatter.1

commit v20 on v18

--- a/solution.py
+++ b/solution.py
@@ -243,7 +243,7 @@
     )
 
 
-def project_attend(length, x, gain, w_query, w_keyval, cos_q, sin_q, cos_kv, sin_kv, keys_t, cache, w_out, group, tile=256):
+def project_attend(length, x, gain, w_query, w_keyval, cos_q, sin_q, cos_kv, sin_kv, keys_t, cache, w_out, group, tile=128):
     tokens, depth = x.shape
     q_cols, kv_cols = w_query.shape[1], w_keyval.shape[1]
     heads = kv_cols // (2 * HD)

time: 109 us -> 112 us (1.028)
  Pallas kernels: 17.9 us -> 21 us
  blocking collectives: 18.4 us -> 20 us
    pallas_call x1, Pallas kernels: 17.9 us -> 21 us  [project_attend(): pl.pallas_call(kernel, out_shape=(jax.ShapeDtypeStruct((tokens, model), j...]
    all_to_all x1, blocking collectives: 18.4 us -> 20 us  [local(): lax.all_to_all(route_blocks(dispatch[layer_count - 1:], current_rows), 's...]
  transfers between devices with their start and end apart: 3 -> 3, of which waited for: 2 -> 2; matrix products, arithmetic and copies ran while one was open for 22% -> 21% of each run, Pallas kernels for 17% -> 19%
where the time goes in v20:
time: 112 us
  waiting for transfers between devices  25.2 us (22%)
  Pallas kernels  21 us (19%)
  blocking collectives  20 us (18%)
  between operations  17 us (15%)
  local copies, waits for them, and re-layouts  11.4 us (10%)
  other arithmetic  7.26 us (6%)
  starting transfers between devices  5.38 us (5%)
  matrix products  4.31 us (4%)
    pallas_call x1, Pallas kernels, project_attend(): pl.pallas_call(kernel, out_shape=(jax.ShapeDtypeStruct((tokens, model), j...  21 us
    all_to_all x1, blocking collectives, local(): lax.all_to_all(route_blocks(dispatch[layer_count - 1:], current_rows), 's...  20 us
    all_gather x1, waiting for transfers between devices, local(): portion = lax.all_gather(tokens, 'dec', axis=0, tiled=True)  18.9 us
    reduce_scatter x1, waiting for transfers between devices, local(): lax.psum_scatter(product.reshape(NEW_TOK, 1, product.shape[-1]), 'dec', s...  5.58 us
    all_to_all x1, starting transfers between devices, local(): lax.all_to_all(route_blocks(dispatch[:layer_count - 1], earlier_rows), 's...  5.3 us
    dot_general x2, matrix products, route_blocks(): jnp.einsum('locms,msbw->olcbw', spread, block_data, preferred_element_typ...  4.31 us
    transpose x2, local copies, waits for them, and re-layouts, local(): jnp.transpose(cached[:, :, :HD], (0, 2, 1))  3.1 us
    convert_element_type x2, local copies, waits for them, and re-layouts, route_blocks(): moved_blocks = jnp.einsum('locms,msbw->olcbw', spread, block_data, prefer...  3.08 us
  transfers between devices with their start and end apart: 3, of which 2 were waited for; matrix products, arithmetic and copies ran while one was open for 21% of the time, Pallas kernels for 19%

profile of v20, /device:TPU:0, one launch (start us, length us, event | category | flops | bytes accessed | tf_op | source)
XLA Modules:
  0.0 111.6 jit_solution(6605002397570527103)
XLA Ops:
  7.2 0.0 all-gather.2.cloned.1.call-start
  7.2 0.7 all-gather.2.cloned.1.call-update
  7.9 1.3 %dynamic_slice.3.length_ref = s32[1]{0:T(128)} dynamic-slice(s32[8]{0:T(128)} %param.11, s32[]{:T(128)S(6)} %select_n.15), dynamic_slice_sizes={1} | dynamic-slice | bytes 12 | tf_op jit(solution)/shard_map/dynamic_slice | solution.py:329
  9.9 0.1 copy.14
  10.0 0.5 broadcast.47
  10.6 1.3 %reduce.3 = s32[3,2,16]{2,1,0:T(2,128)S(1)} reduce(s32[1,3,2,16,1]{3,4,2,1,0:T(1,128)} %param.17, s32[]{:T(128)} %broadcast.47), dimensions={0,4}, to_apply=%param.17.reduce_sub_computation.3 | reduce | bytes 772 | tf_op args[8]
  11.9 0.1 reshape_squeeze.3
  12.0 0.1 fusion.11
  12.1 0.1 reduce_window_sum.11
  12.2 0.2 select_reduce_fusion
  12.4 0.0 copy-start.2
  12.4 3.6 %fusion.2 = bf16[8,2,4,128,128]{4,0,2,1,3:T(8,128)(2,1)S(1)} fusion(bf16[2,32,128,128]{3,2,1,0:T(8,128)(2,1)} %bitcast.58, pred[32,128]{0,1:T(8,128)(4,1)S(1)} %copy.14, bf16[2,2]{1,0:T(2,128)(2,1)S(1)} %compare_convert_fusion, bf16[2,8,4,32]{3,1,2,0:T(8,128)(2,1)S(1)} %copy.16), kind=kOutput, calls=%fused_computation.5 | convolution fusion | flops 136331264 | bytes 4202504 | tf_op jit(solution)/shard_map/locms,msbw->olcbw/dot_general | solution.py:37
  16.0 2.7 %copy.17 = bf16[8,2,4,128,128]{4,3,2,1,0:T(8,128)(2,1)} copy(bf16[8,2,4,128,128]{4,0,2,1,3:T(8,128)(2,1)S(1)} %fusion.2) | data formatting | bytes 4194304 | tf_op jit(solution)/shard_map/convert_element_type | solution.py:39
  18.7 0.0 copy-start
  18.7 5.3 %all-to-all-start = ((bf16[8,1024,128]{2,1,0:T(8,128)(2,1)}), bf16[8,1024,128]{2,1,0:T(8,128)(2,1)S(1)}, u32[]{:S(2)}, u32[]{:S(2)}) async-start(bf16[8,1024,128]{2,1,0:T(8,128)(2,1)} %bitcast.47), calls=%async_computation | async-start | bytes 4194304 | tf_op jit(solution)/shard_map/all_to_all | solution.py:345
  24.0 0.0 reduce-scatter.2.cloned.1.call-start
  24.0 0.1 pad.12.clone
  24.1 0.1 pad.9.clone
  24.2 0.0 copy-done
  24.2 1.0 slice_bitcast_fusion
  25.2 2.1 %copy.18.kt_ref = bf16[2,64,1536]{2,1,0:T(8,128)(2,1)} copy(bf16[2,64,1536]{1,2,0:T(8,128)(2,1)} %slice_bitcast_fusion) | data formatting | bytes 786432 | tf_op jit(solution)/shard_map/transpose | solution.py:372
  27.3 0.7 add_convert_fusion
  28.0 1.0 fusion.10
  29.0 1.4 %fusion.8 = (f32[512,128]{1,0:T(8,128)}, f32[512,128]{1,0:T(8,128)}, f32[512,128]{1,0:T(8,128)}, f32[512,128]{1,0:T(8,128)}) fusion(f32[512,32]{1,0:T(8,128)S(1)} %get-tuple-element.18, f32[128]{0:T(128)S(1)} %pad.12.clone, f32[512,32]{1,0:T(8,128)S(1)} %get-tuple-element.17, f32[512,32]{1,0:T(8,128)S(1)} %get-tuple-element.16, f32[128]{0:T(128)S(1)} %pad.9.clone), kind=kLoop, calls=%fused_computation.16 | loop fusion | flops 524288 | bytes 1246208 | tf_op jit(solution)/shard_map/concatenate | solution.py:358
  30.4 18.9 %all-gather.2.cloned.1.call-done = bf16[512,1,1536]{2,0,1:T(8,128)(2,1)} async-done(((bf16[128,1,1536]{2,0,1:T(8,128)(2,1)}), bf16[512,1,1536]{2,0,1:T(8,128)(2,1)}) %all-gather.2.cloned.1.call-update) | async-done | bytes 1572880 | tf_op jit(solution)/shard_map/all_gather | solution.py:348
  49.4 21.0 %shard_map.104 = (bf16[512,1536]{1,0:T(8,128)(2,1)}, bf16[2,512,128]{2,1,0:T(8,128)(2,1)}, bf16[2,64,512]{2,1,0:T(8,128)(2,1)}) custom-call(s32[1]{0:T(128)} %dynamic_slice.3.length_ref, bf16[512,1536]{1,0:T(8,128)(2,1)} %bitcast.59, f32[1536]{0:T(1024)} %gain_ref.1, bf16[1536,384]{1,0:T(8,128)(2,1)} %wq_ref.1, bf16[1536,256]{1,0:T(8,128)(2,1)} %wkv_ref.1, ...), custom_call_target="tpu_custom_call" | custom-call | flops 3221225472 | bytes 7471104 | tf_op jit(solution)/shard_map/pallas_call | solution.py:257
  70.4 0.0 copy-start.1
  70.4 0.0 all-to-all-done
  70.4 0.0 reduce-scatter.2.cloned.1.call-update
  71.2 0.0 copy-done.2
  71.2 0.0 slice-start
  72.6 0.7 iota_compare_fusion.2
  73.3 1.4 %pad_select_fusion = bf16[2,2048,128]{2,1,0:T(8,128)(2,1)S(1)} fusion(bf16[2,1536,128]{2,1,0:T(8,128)(2,1)} %bitcast.52, pred[2048]{0:T(1024)(128)(4,1)S(1)} %iota_compare_fusion.2), kind=kLoop, calls=%fused_computation.9 | loop fusion | flops 524288 | bytes 1837056 | tf_op jit(solution)/shard_map/jit(_where)/select_n | solution.py:379
  74.7 0.0 copy-done.1
  74.7 0.9 dynamic_update_slice.3
  75.6 0.0 slice-done
  75.6 0.8 fusion.5
  76.4 0.4 copy.21
  76.8 20.0 %all_to_all.10 = bf16[8,512,128]{2,1,0:T(8,128)(2,1)S(1)} all-to-all(bf16[8,512,128]{2,1,0:T(8,128)(2,1)S(1)} %bitcast.49), channel_id=1, replica_groups=mesh['seq'=8,'dec'=4] {'seq'}, dimensions={0} | all-to-all | bytes 2097152 | tf_op jit(solution)/shard_map/all_to_all | solution.py:390
  96.8 0.3 maximum_bitcast_fusion
  97.1 2.1 %copy.22 = bf16[1,1,3,8,4,128,128]{6,5,4,3,2,1,0:T(8,128)(2,1)} copy(bf16[1,1,3,8,4,128,128]{6,5,4,2,3,1,0:T(8,128)(2,1)S(1)} %maximum_bitcast_fusion) | data formatting | bytes 6291456
  99.2 5.6 %reduce-scatter.2.cloned.1.call-done = bf16[128,1,1536]{2,0,1:T(8,128)(2,1)} async-done(((bf16[512,1,1536]{2,0,1:T(8,128)(2,1)}), bf16[128,1,1536]{2,0,1:T(8,128)(2,1)}) %reduce-scatter.2.cloned.1.call-update) | async-done | bytes 393232 | tf_op jit(solution)/shard_map/reduce_scatter | solution.py:383
  (10 shorter events, 0.1 us)
Async XLA Ops:
  7.2 42.2 %all-gather.2.cloned.1.call-start = ((), (), s32[]{:S(2)}) async-start(), calls=%async_computation.3 | async-start | bytes 1966080 | tf_op jit(solution)/shard_map/all_gather | solution.py:348
  12.4 58.8 %copy-start.2 = (pred[3,32,32]{2,1,0:T(8,128)(4,1)}, pred[3,32,32]{2,1,0:T(8,128)(4,1)S(1)}, u32[]{:S(2)}) copy-start(pred[3,32,32]{2,1,0:T(8,128)(4,1)S(1)} %iota_compare_fusion) | copy-start | bytes 9220
  18.7 5.5 %copy-start = (bf16[1,2,1536,128]{3,2,1,0:T(8,128)(2,1)S(1)}, bf16[1,2,1536,128]{3,2,1,0:T(8,128)(2,1)}, u32[]{:S(2)}) copy-start(bf16[1,2,1536,128]{3,2,1,0:T(8,128)(2,1)} %param.15) | copy-start | bytes 2359300
  18.7 51.7 %all-to-all-start = ((bf16[8,1024,128]{2,1,0:T(8,128)(2,1)}), bf16[8,1024,128]{2,1,0:T(8,128)(2,1)S(1)}, u32[]{:S(2)}, u32[]{:S(2)}) async-start(bf16[8,1024,128]{2,1,0:T(8,128)(2,1)} %bitcast.47), calls=%async_computation | async-start | bytes 4194304 | tf_op jit(solution)/shard_map/all_to_all | solution.py:345
  24.0 80.8 %reduce-scatter.2.cloned.1.call-start = ((), (), s32[]{:S(2)}) async-start(), calls=%async_computation.4 | async-start | bytes 1966080 | tf_op jit(solution)/shard_map/reduce_scatter | solution.py:383
  70.4 4.3 %copy-start.1 = (bf16[2,512,128]{2,1,0:T(8,128)(2,1)S(1)}, bf16[2,512,128]{2,1,0:T(8,128)(2,1)}, u32[]{:S(2)}) copy-start(bf16[2,512,128]{2,1,0:T(8,128)(2,1)} %get-tuple-element.9) | copy-start | bytes 786436
  71.2 4.4 %slice-start = ((pred[3,32,32]{2,1,0:T(8,128)(4,1)}), pred[1,32,32]{2,1,0:T(8,128)(4,1)S(1)}, s32[]{:S(2)}) async-start(pred[3,32,32]{2,1,0:T(8,128)(4,1)} %copy-done.2), calls=%async_computation.5 | async-start | bytes 8192 | tf_op jit(solution)/shard_map/slice | solution.py:391
Sparse Core Ops, SparseCore 0:
  9.6 39.7 all-gather.1
  70.6 34.1 reduce-scatter.1
